TPU v7x, 256 devices: a whole 4x4x8 slice. The times are simulated.
256 devices in a mesh: elem: 32 (over z, x), blk: 8 (over y, core).
Axes of the slice: x: 4, y: 4, z: 8, core: 2. Of those that a mesh axis runs over, the one named last changes fastest.
Arguments:
- basis: bfloat16 [32768, 3, 512], P('elem'), may hold values from -6 to 6
- send_rows: int32 [32, 8, 256], P('elem', 'blk'), may hold values from 0 to 1023
- elem_slot: int32 [8, 16384], P(None, ('elem', 'blk')), may hold values from 0 to 255, as said below
- set_size: int32 [32], replicated, may hold values from 1 to 512, 10240 in all
- elem_weight: float32 [16384], P(('elem', 'blk')), may hold values from 0.2 to 5
- element_stiffening: float32 [16384], P(('elem', 'blk')), may hold values from 1 to 8
- state: bfloat16 [512], replicated, may hold values from -0.25 to 0.25
- load: float32 [512], P('blk'), may hold values from -6 to 6
Outputs:
- tangent: float32 [512, 512], P('elem', 'blk')
- residual: float32 [512], P('blk')
Inputs may be any that keep to these rules, and one draw needn't show every extreme that they name: `elem_slot`: for element column of device (s, b): p names slot p % 8 of what owner p // 8 sends to that device. From each owner only its first n slots are named, n at most 8; for every device exactly one owner gives 8, and the n over all owners sum to 128.
All inputs are finite; a program needn't handle non-finite values.
Results may differ from a plain program's by a relative error of at most 0.0003.
Values may be sent and summed in bfloat16 or wider, within the bound.
No kernel may reach another device: no remote copies, remote signals or barrier semaphores. Data moves between devices by JAX's collectives and lax.ppermute only.
A program may use at most 64 MiB of HBM per device.

v0:
```python
import jax
import jax.numpy as jnp
from jax import lax
from jax.sharding import PartitionSpec as P


def corner_grads():
    corner = jnp.arange(8)[:, None]
    bit = corner // 2 ** jnp.arange(3)[None, :] % 2
    return (bit * 2 - 1).astype(jnp.float32) * 0.25


def element_contributions(basis_matrix, displacement, stiffening_power):
    grads = corner_grads()
    element_count = basis_matrix.shape[0]
    basis_modes = basis_matrix.shape[2]
    corner_nodes = basis_matrix.reshape(element_count, 8, 3, basis_modes)
    grad_basis = jnp.einsum(
        "ak,eacm->ekcm",
        grads.astype(jnp.bfloat16),
        corner_nodes,
        preferred_element_type=jnp.float32,
    )
    moved = displacement.reshape(8, 3, element_count)
    hgrad = jnp.einsum("ak,ace->kce", grads, moved, precision=lax.Precision.HIGHEST)
    volume = hgrad[0, 0] + hgrad[1, 1] + hgrad[2, 2]
    stiff = 1.0 + stiffening_power * volume**2 - 2.0 / 3.0
    press = volume + stiffening_power * volume**3 / 3.0 - 2.0 / 3.0 * volume
    eye = jnp.eye(3, dtype=jnp.float32)
    stress = hgrad + jnp.transpose(hgrad, (1, 0, 2)) + press[None, None, :] * eye[:, :, None]
    force_vector = (
        jnp.einsum("ak,kce->ace", grads, stress, precision=lax.Precision.HIGHEST).reshape(
            24, element_count
        )
        + 0.25 * displacement
    )
    sym = grad_basis + jnp.transpose(grad_basis, (0, 2, 1, 3))
    trace_basis = grad_basis[:, 0, 0] + grad_basis[:, 1, 1] + grad_basis[:, 2, 2]
    mode_image = jnp.einsum("ak,ekcm->eacm", grads, sym, precision=lax.Precision.HIGHEST)
    mode_image = (
        mode_image
        + stiff[:, None, None, None] * grads[None, :, :, None] * trace_basis[:, None, None, :]
        + 0.25 * corner_nodes.astype(jnp.float32)
    )
    return (mode_image.reshape(element_count, 24, basis_modes), force_vector)


def local(basis, send_rows, elem_slot, set_size, elem_weight, element_stiffening, state, load):
    nodes = basis.shape[0]
    basis_modes = basis.shape[2]
    flat = basis.reshape(nodes, 3 * basis_modes)
    outgoing = jnp.take(flat, send_rows[0, 0], axis=0)
    arrived = lax.all_to_all(outgoing, "elem", split_axis=0, concat_axis=0, tiled=True)
    element_count = elem_slot.shape[1]
    chosen_elements = jnp.take(arrived, elem_slot.T.reshape(-1), axis=0)
    basis_matrix = chosen_elements.reshape(element_count, 24, basis_modes)
    set_index = lax.axis_index("elem")
    block_index = lax.axis_index("blk")
    live = lax.dynamic_index_in_dim(set_size, set_index, keepdims=False)
    position = block_index * element_count + jnp.arange(element_count, dtype=jnp.int32)
    weights = jnp.where(position < live, elem_weight, jnp.zeros_like(elem_weight))
    displacement = jnp.einsum("agd,d->ga", basis_matrix, state, preferred_element_type=jnp.float32)
    mode_image, force_vector = element_contributions(basis_matrix, displacement, element_stiffening)
    weighted_image = (weights[:, None, None] * mode_image).astype(jnp.bfloat16)
    weighted_force = (force_vector * weights[None, :]).astype(jnp.bfloat16)
    tangent = lax.dot_general(
        basis_matrix,
        weighted_image,
        (((0, 1), (0, 1)), ((), ())),
        preferred_element_type=jnp.float32,
    )
    force_all = lax.dot_general(
        basis_matrix,
        weighted_force,
        (((0, 1), (1, 0)), ((), ())),
        preferred_element_type=jnp.float32,
    )
    halfway, force_part = (
        lax.psum_scatter(tangent, "blk", scatter_dimension=1, tiled=True),
        lax.psum_scatter(force_all, "blk", scatter_dimension=0, tiled=True),
    )
    mine = lax.psum_scatter(halfway, "elem", scatter_dimension=0, tiled=True)
    force_cols = lax.psum(force_part, "elem")
    scale = lax.rsqrt(24.0 * jnp.sum(set_size).astype(jnp.float32))
    return (mine * scale, force_cols * scale - load)


def solution(mesh):
    in_specs = (
        P("elem", None, None),
        P("elem", "blk", None),
        P(None, ("elem", "blk")),
        P(),
        P(("elem", "blk")),
        P(("elem", "blk")),
        P(),
        P("blk"),
    )
    out_specs = (P("elem", "blk"), P("blk"))
    return jax.shard_map(local, mesh=mesh, in_specs=in_specs, out_specs=out_specs, check_vma=False)
```

profile of v0, /device:TPU:2, one launch (start us, length us, event | category | flops | bytes accessed | tf_op | source)
XLA Modules:
  0.0 335.5 jit_solution(8564623697525972582)
XLA Ops:
  7.2 4.7 %copy.32 = bf16[1024,3,512]{0,2,1:T(8,128)(2,1)} copy(bf16[1024,3,512]{2,0,1:T(8,128)(2,1)} %param.8) | data formatting | bytes 6291456 | tf_op args[0]
  11.9 3.2 copy.33
  15.6 0.7 reduce.3
  16.4 2.2 gather_fusion
  18.5 2.2 bitcast_select_fusion
  20.7 11.6 %all-to-all-start = ((bf16[32,8,1536]{2,1,0:T(8,128)(2,1)}), bf16[32,8,1536]{2,1,0:T(8,128)(2,1)S(1)}, u32[]{:S(2)}, u32[]{:S(2)}) async-start(bf16[32,8,1536]{2,1,0:T(8,128)(2,1)} %bitcast_select_fusion), calls=%async_computation | async-start | bytes 1572864 | tf_op jit(solution)/shard_map/all_to_all | solution.py:53
  33.2 0.9 broadcast_in_dim.51
  34.1 0.6 dynamic_slice.4
  34.7 0.7 compare_select_fusion.10
  35.6 19.2 %all-to-all-done = bf16[32,8,1536]{2,1,0:T(8,128)(2,1)S(1)} async-done(((bf16[32,8,1536]{2,1,0:T(8,128)(2,1)}), bf16[32,8,1536]{2,1,0:T(8,128)(2,1)S(1)}, u32[]{:S(2)}, u32[]{:S(2)}) %all-to-all-start) | async-done | bytes 786464 | tf_op jit(solution)/shard_map/all_to_all | solution.py:53
  54.8 2.1 gather_fusion.1
  56.9 1.6 gather.18
  58.6 0.8 fusion.8
  59.3 1.8 copy.67
  61.2 2.0 bitcast_add_fusion.1
  63.1 1.5 fusion.7
  65.1 1.7 slice_add_fusion
  66.9 5.6 %fusion.2 = bf16[64,8,3,512]{3,1,2,0:T(8,128)(2,1)S(1)} fusion(f32[64,3,3,512]{3,2,1,0:T(4,128)} %bitcast_add_fusion.1, f32[64,512]{1,0:T(8,128)S(1)} %bitcast.76, f32[64,8,3]{1,2,0:T(4,128)S(1)} %broadcast_multiply_fusion, f32[64]{0:T(128)S(1)} %compare_select_fusion.10, bf16[64,8,3,512]{3,1,2,0:T(8,128)(2,1)S(1)} %bitcast.72, pred[64,8]{1,0:T(8,128)(4,1)S(1)} %copy.35, ...), kind=kOutput, calls=%fused_computation.5 | convolution fusion | flops 34603536 | bytes 4463416 | tf_op jit(solution)/shard_map/ak,ekcm->eacm/dot_general | solution.py:39
  72.5 1.7 copy.39
  74.2 1.3 broadcast_select_fusion.5
  75.5 2.9 select_n.226
  78.4 2.4 fusion.9
  80.9 0.6 reduce_sum.9
  82.2 0.6 dynamic-slice
  84.1 28.3 %reduce-scatter.5.cloned.1.call-done = f32[512,64]{0,1:T(8,128)} async-done(((f32[512,512]{0,1:T(8,128)}), f32[512,64]{0,1:T(8,128)}) %reduce-scatter.5.cloned.1.call-update) | async-done | bytes 131088 | tf_op jit(solution)/shard_map/reduce_scatter | solution.py:79
  112.4 1.7 copy.48
  114.6 12.7 %all-reduce = f32[512]{0:T(512)S(1)} all-reduce(f32[512]{0:T(512)S(1)} %bitcast.81), channel_id=4, replica_groups=mesh['elem'=32,'blk'=8] {'blk'}, use_global_device_ids=true, to_apply=%region_3.4.clone | all-reduce | flops 512 | bytes 4096
  127.4 71.2 %psum.7 = f32[64]{0:T(128)S(1)} all-reduce(f32[64]{0:T(128)S(1)} %dynamic-slice.1), channel_id=1, replica_groups=mesh['elem'=32,'blk'=8] {'elem'}, use_global_device_ids=true, to_apply=%region_4.5 | all-reduce | flops 64 | bytes 512 | tf_op jit(solution)/shard_map/psum | solution.py:83
  198.6 0.5 multiply_subtract_fusion
  199.1 128.1 %reduce-scatter.7.cloned.1.call-done = f32[16,64]{1,0:T(8,128)} async-done(((f32[512,64]{1,0:T(8,128)}), f32[16,64]{1,0:T(8,128)}) %reduce-scatter.7.cloned.1.call-update) | async-done | bytes 4112
  327.2 0.8 copy.49
  328.0 0.7 copy.43
  (61 shorter events, 3.4 us)
Async XLA Ops:
  11.9 3.2 copy-start.4
  18.5 13.9 %copy-start.3 = (s32[8,64]{1,0:T(8,128)S(1)}, s32[8,64]{1,0:T(8,128)}, u32[]{:S(2)}) copy-start(s32[8,64]{1,0:T(8,128)} %param.10) | copy-start | bytes 6148
  18.5 14.3 %copy-start.5 = (bf16[512]{0:T(512)(128)(2,1)S(1)}, bf16[512]{0:T(512)(128)(2,1)}, u32[]{:S(2)}) copy-start(bf16[512]{0:T(512)(128)(2,1)} %param.14) | copy-start | bytes 3076
  20.7 34.1 %all-to-all-start = ((bf16[32,8,1536]{2,1,0:T(8,128)(2,1)}), bf16[32,8,1536]{2,1,0:T(8,128)(2,1)S(1)}, u32[]{:S(2)}, u32[]{:S(2)}) async-start(bf16[32,8,1536]{2,1,0:T(8,128)(2,1)} %bitcast_select_fusion), calls=%async_computation | async-start | bytes 1572864 | tf_op jit(solution)/shard_map/all_to_all | solution.py:53
  32.3 1.7 copy-start.9
  32.4 2.3 copy-start.6
  32.4 80.0 %reduce-scatter.5.cloned.1.call-start = ((), (), s32[]{:S(2)}) async-start(), calls=%async_computation.3 | async-start | bytes 1179648 | tf_op jit(solution)/shard_map/reduce_scatter | solution.py:79
  61.1 2.0 copy-start
  63.1 1.9 copy-start.7
  75.5 2.9 copy-start.2
  78.4 3.8 %copy-start.10 = (u32[256]{0:T(256)S(1)}, u32[256]{0:T(256)}, u32[]{:S(2)}) copy-start(u32[256]{0:T(256)} %constant.114) | copy-start | bytes 3076
  80.8 33.3 %copy-start.1 = (bf16[64,24,512]{2,1,0:T(8,128)(2,1)S(1)}, bf16[64,24,512]{2,1,0:T(8,128)(2,1)}, u32[]{:S(2)}) copy-start(bf16[64,24,512]{2,1,0:T(8,128)(2,1)} %gather.18) | copy-start | bytes 4718596
  80.9 246.3 %reduce-scatter.7.cloned.1.call-start = ((), (), s32[]{:S(2)}) async-start(), calls=%async_computation.4 | async-start | bytes 270336
  114.1 84.4 %copy-start.8 = (f32[64]{0:T(128)S(1)}, f32[64]{0:T(128)}, u32[]{:S(2)}) copy-start(f32[64]{0:T(128)} %param.15) | copy-start | bytes 772
Sparse Core Ops, SparseCore 0:
  81.0 31.3 reduce-scatter.4
  116.2 210.9 reduce-scatter.6
where the time goes:
time: 337 us; the launch traced here: 335 us
  waiting for transfers between devices  176 us (52%)
  blocking collectives  83.9 us (25%)
  local copies, waits for them, and re-layouts  27 us (8%)
  between operations  15.7 us (5%)
  starting transfers between devices  11.7 us (3%)
  matrix products  11.5 us (3%)
  other arithmetic  10 us (3%)
    unnamed x3, waiting for transfers between devices  128 us
    psum x1, blocking collectives, local(): force_cols = lax.psum(force_part, 'elem')  71.2 us
    reduce_scatter x1, waiting for transfers between devices, local(): lax.psum_scatter(tangent, 'blk', scatter_dimension=1, tiled=True)  28.3 us
    all_to_all x1, waiting for transfers between devices, local(): lax.all_to_all(outgoing, 'elem', split_axis=0, concat_axis=0, tiled=True)  19.2 us
    unnamed x1, blocking collectives  12.7 us
    all_to_all x1, starting transfers between devices, local(): lax.all_to_all(outgoing, 'elem', split_axis=0, concat_axis=0, tiled=True)  11.6 us
    unnamed x31, local copies, waits for them, and re-layouts  9.14 us
  transfers between devices with their start and end apart: 3, of which 3 were waited for; matrix products, arithmetic and copies ran while one was open for 2% of the time, Pallas kernels for 0%

commit v1 on v0

--- a/solution.py
+++ b/solution.py
@@ -48,6 +48,8 @@
 def local(basis, send_rows, elem_slot, set_size, elem_weight, element_stiffening, state, load):
     nodes = basis.shape[0]
     basis_modes = basis.shape[2]
+    n_elem = lax.psum(1, "elem")
+    n_blk = lax.psum(1, "blk")
     flat = basis.reshape(nodes, 3 * basis_modes)
     outgoing = jnp.take(flat, send_rows[0, 0], axis=0)
     arrived = lax.all_to_all(outgoing, "elem", split_axis=0, concat_axis=0, tiled=True)
@@ -63,10 +65,12 @@
     mode_image, force_vector = element_contributions(basis_matrix, displacement, element_stiffening)
     weighted_image = (weights[:, None, None] * mode_image).astype(jnp.bfloat16)
     weighted_force = (force_vector * weights[None, :]).astype(jnp.bfloat16)
-    tangent = lax.dot_general(
-        basis_matrix,
-        weighted_image,
-        (((0, 1), (0, 1)), ((), ())),
+    rows = basis_modes // n_elem
+    cols = basis_modes // n_blk
+    tangent = jnp.einsum(
+        "egri,egbc->rbic",
+        basis_matrix.reshape(element_count, 24, n_elem, rows),
+        weighted_image.reshape(element_count, 24, n_blk, cols),
         preferred_element_type=jnp.float32,
     )
     force_all = lax.dot_general(
@@ -75,14 +79,11 @@
         (((0, 1), (1, 0)), ((), ())),
         preferred_element_type=jnp.float32,
     )
-    halfway, force_part = (
-        lax.psum_scatter(tangent, "blk", scatter_dimension=1, tiled=True),
-        lax.psum_scatter(force_all, "blk", scatter_dimension=0, tiled=True),
-    )
-    mine = lax.psum_scatter(halfway, "elem", scatter_dimension=0, tiled=True)
-    force_cols = lax.psum(force_part, "elem")
+    force_rows = jnp.broadcast_to(force_all.reshape(1, n_blk, 1, cols), (n_elem, n_blk, 1, cols))
+    both = jnp.concatenate([tangent, force_rows], axis=2).reshape(n_elem * n_blk * (rows + 1), cols)
+    mine = lax.psum_scatter(both, ("elem", "blk"), scatter_dimension=0, tiled=True)
     scale = lax.rsqrt(24.0 * jnp.sum(set_size).astype(jnp.float32))
-    return (mine * scale, force_cols * scale - load)
+    return (mine[:rows] * scale, mine[rows] * scale - load)
 
 
 def solution(mesh):

time: 337 us -> 408 us (1.21)
  waiting for transfers between devices: 176 us -> 262 us
  blocking collectives: 83.9 us -> 0 us
  local copies, waits for them, and re-layouts: 27 us -> 86.8 us
  matrix products: 11.5 us -> 17.6 us
    unnamed x3 -> x2, waiting for transfers between devices: 128 us -> 262 us
    psum x1 -> x0, blocking collectives: 71.2 us -> none  [local(): force_cols = lax.psum(force_part, 'elem')]
    select_n x1 -> x2, local copies, waits for them, and re-layouts: 2.89 us -> 32.3 us  [local(): chosen_elements = jnp.take(arrived, elem_slot.T.reshape(-1), axis=0)]
    reduce_scatter x1 -> x0, waiting for transfers between devices: 28.3 us -> none  [local(): lax.psum_scatter(tangent, 'blk', scatter_dimension=1, tiled=True)]
    broadcast_in_dim x5, local copies, waits for them, and re-layouts: 1.27 us -> 25.8 us  [local(): chosen_elements = jnp.take(arrived, elem_slot.T.reshape(-1), axis=0)]
    all_to_all x1, waiting for transfers between devices: 19.2 us -> 0.01 us  [local(): lax.all_to_all(outgoing, 'elem', split_axis=0, concat_axis=0, tiled=True)]
    unnamed x1 -> x0, blocking collectives: 12.7 us -> none
    another operation x0 -> x1, local copies, waits for them, and re-layouts: none -> 5.13 us
  transfers between devices with their start and end apart: 3 -> 2, of which waited for: 3 -> 1; matrix products, arithmetic and copies ran while one was open for 2% -> 7% of each run, Pallas kernels for 0% -> 0%
where the time goes in v1:
time: 408 us; the launch traced here: 407 us
  waiting for transfers between devices  262 us (64%)
  local copies, waits for them, and re-layouts  86.8 us (21%)
  matrix products  17.6 us (4%)
  between operations  15 us (4%)
  other arithmetic  13.7 us (3%)
  starting transfers between devices  11.7 us (3%)
    unnamed x2, waiting for transfers between devices  262 us
    select_n x2, local copies, waits for them, and re-layouts, local(): chosen_elements = jnp.take(arrived, elem_slot.T.reshape(-1), axis=0)  32.3 us
    broadcast_in_dim x5, local copies, waits for them, and re-layouts, local(): chosen_elements = jnp.take(arrived, elem_slot.T.reshape(-1), axis=0)  25.8 us
    all_to_all x1, starting transfers between devices, local(): lax.all_to_all(outgoing, 'elem', split_axis=0, concat_axis=0, tiled=True)  11.6 us
  transfers between devices with their start and end apart: 2, of which 1 were waited for; matrix products, arithmetic and copies ran while one was open for 7% of the time, Pallas kernels for 0%

profile of v1, /device:TPU:2, one launch (start us, length us, event | category | flops | bytes accessed | tf_op | source)
XLA Modules:
  0.0 406.7 jit_solution(17030174012575924840)
XLA Ops:
  7.2 4.7 %copy.33 = bf16[1024,3,512]{0,2,1:T(8,128)(2,1)} copy(bf16[1024,3,512]{2,0,1:T(8,128)(2,1)} %param.8) | data formatting | bytes 6291456 | tf_op args[0]
  11.8 3.2 copy.34
  15.6 0.7 reduce.3
  16.3 2.1 gather_fusion
  18.5 2.2 bitcast_select_fusion
  20.7 11.6 %all-to-all-start = ((bf16[32,8,1536]{2,1,0:T(8,128)(2,1)}), bf16[32,8,1536]{2,1,0:T(8,128)(2,1)S(1)}, u32[]{:S(2)}, u32[]{:S(2)}) async-start(bf16[32,8,1536]{2,1,0:T(8,128)(2,1)} %bitcast_select_fusion), calls=%async_computation | async-start | bytes 1572864 | tf_op jit(solution)/shard_map/all_to_all | solution.py:55
  32.8 4.5 %broadcast_in_dim.64 = pred[64,24,32,16]{3,2,1,0:T(8,128)(4,1)} broadcast(pred[64,24]{1,0:T(8,128)(4,1)S(1)} %copy.38), dimensions={0,1} | broadcast | bytes 787968 | tf_op jit(solution)/shard_map/jit(_take)/broadcast_in_dim | solution.py:57
  37.3 21.2 %broadcast_in_dim.65 = pred[512,1536]{1,0:T(8,128)(4,1)S(1)} reshape(pred[64,24,32,16]{3,2,1,0:T(8,128)(4,1)} %broadcast_in_dim.64) | data formatting | bytes 1572864 | tf_op jit(solution)/shard_map/jit(_take)/broadcast_in_dim | solution.py:57
  58.5 0.6 dynamic_slice.4
  59.2 0.7 compare_select_fusion.10
  60.0 2.1 gather_fusion.1
  62.2 1.6 gather.18
  63.8 0.8 fusion.14
  64.6 2.0 bitcast_add_fusion.1
  66.6 1.8 copy.78
  68.4 1.5 fusion.15
  69.8 5.1 %reshape.318 = bf16[8,64,64,24]{1,0,3,2:T(8,128)(2,1)} reshape(bf16[512,64,24]{0,2,1:T(8,128)(2,1)} %fusion.15) | data formatting | bytes 3145728 | tf_op jit(solution)/shard_map/reshape.128
  75.0 2.9 fusion.16
  78.8 1.3 broadcast_select_fusion.4
  80.1 13.7 %select_n.239 = bf16[64,24,32,16]{3,2,1,0:T(8,128)(2,1)} reshape(bf16[512,1536]{1,0:T(8,128)(2,1)} %broadcast_select_fusion.4) | data formatting | bytes 3145728 | tf_op jit(solution)/shard_map/jit(_take)/select_n | solution.py:57
  93.8 18.6 %copy.43 = bf16[64,24,32,16]{0,2,1,3:T(8,128)(2,1)} copy(bf16[64,24,32,16]{3,2,1,0:T(8,128)(2,1)} %select_n.239) | data formatting | bytes 3145728 | tf_op jit(solution)/shard_map/jit(_take)/select_n | solution.py:57
  112.4 1.7 slice_add_fusion
  114.3 5.7 %fusion.5 = bf16[64,8,3,512]{3,1,2,0:T(8,128)(2,1)S(1)} fusion(f32[64,3,3,512]{3,2,1,0:T(4,128)} %bitcast_add_fusion.1, f32[64,512]{1,0:T(8,128)S(1)} %bitcast.96, f32[64,8,3]{1,2,0:T(4,128)S(1)} %broadcast_multiply_fusion, f32[64]{0:T(128)S(1)} %compare_select_fusion.10, bf16[64,8,3,512]{3,1,2,0:T(8,128)(2,1)S(1)} %bitcast.92, pred[64,8]{1,0:T(8,128)(4,1)S(1)} %copy.32, ...), kind=kOutput, calls=%fused_computation.8 | convolution fusion | flops 34603536 | bytes 4463416 | tf_op jit(solution)/shard_map/ak,ekcm->eacm/dot_general | solution.py:39
  120.5 3.0 convert_element_type.45
  123.5 3.8 fusion.6
  127.2 3.7 fusion.8
  131.3 1.3 copy.46
  132.6 1.4 reshape.320
  134.1 0.6 reduce_sum.9
  135.4 261.9 %all-reduce.3.cloned.1.call-done = f32[4352,64]{1,0:T(8,128)} async-done(((f32[4352,64]{1,0:T(8,128)}), f32[4352,64]{1,0:T(8,128)}) %all-reduce.3.cloned.1.call-update) | async-done | bytes 1114128
  397.4 1.3 dynamic-slice_multiply_fusion
  398.7 1.2 fusion.49
  (54 shorter events, 3.2 us)
Async XLA Ops:
  11.8 3.2 copy-start.3
  18.5 13.9 %copy-start.2 = (s32[8,64]{1,0:T(8,128)S(1)}, s32[8,64]{1,0:T(8,128)}, u32[]{:S(2)}) copy-start(s32[8,64]{1,0:T(8,128)} %param.10) | copy-start | bytes 6148
  18.5 14.3 %copy-start.4 = (bf16[512]{0:T(512)(128)(2,1)S(1)}, bf16[512]{0:T(512)(128)(2,1)}, u32[]{:S(2)}) copy-start(bf16[512]{0:T(512)(128)(2,1)} %param.14) | copy-start | bytes 3076
  20.7 39.4 %all-to-all-start = ((bf16[32,8,1536]{2,1,0:T(8,128)(2,1)}), bf16[32,8,1536]{2,1,0:T(8,128)(2,1)S(1)}, u32[]{:S(2)}, u32[]{:S(2)}) async-start(bf16[32,8,1536]{2,1,0:T(8,128)(2,1)} %bitcast_select_fusion), calls=%async_computation | async-start | bytes 1572864 | tf_op jit(solution)/shard_map/all_to_all | solution.py:55
  32.3 365.1 %all-reduce.3.cloned.1.call-start = ((), (), s32[]{:S(2)}) async-start(), calls=%async_computation.1 | async-start | bytes 4456448
  37.3 21.2 %copy-start.8 = (s32[32]{0:T(128)S(1)}, s32[32]{0:T(128)}, u32[]{:S(2)}) copy-start(s32[32]{0:T(128)} %param.11) | copy-start | bytes 388
  37.3 21.9 %copy-start.6 = (f32[64]{0:T(128)S(1)}, f32[64]{0:T(128)}, u32[]{:S(2)}) copy-start(f32[64]{0:T(128)} %param.12) | copy-start | bytes 772
  66.6 1.8 copy-start
  75.0 3.3 copy-start.7
  123.5 3.8 copy-start.1
  134.1 264.6 %copy-start.5 = (f32[64]{0:T(128)S(1)}, f32[64]{0:T(128)}, u32[]{:S(2)}) copy-start(f32[64]{0:T(128)} %param.15) | copy-start | bytes 772
Sparse Core Ops, SparseCore 0:
  134.2 263.1 all-reduce.2

commit v2 on v0

--- a/solution.py
+++ b/solution.py
@@ -48,6 +48,8 @@
 def local(basis, send_rows, elem_slot, set_size, elem_weight, element_stiffening, state, load):
     nodes = basis.shape[0]
     basis_modes = basis.shape[2]
+    n_elem = lax.psum(1, "elem")
+    n_blk = lax.psum(1, "blk")
     flat = basis.reshape(nodes, 3 * basis_modes)
     outgoing = jnp.take(flat, send_rows[0, 0], axis=0)
     arrived = lax.all_to_all(outgoing, "elem", split_axis=0, concat_axis=0, tiled=True)
@@ -63,6 +65,8 @@
     mode_image, force_vector = element_contributions(basis_matrix, displacement, element_stiffening)
     weighted_image = (weights[:, None, None] * mode_image).astype(jnp.bfloat16)
     weighted_force = (force_vector * weights[None, :]).astype(jnp.bfloat16)
+    rows = basis_modes // n_elem
+    cols = basis_modes // n_blk
     tangent = lax.dot_general(
         basis_matrix,
         weighted_image,
@@ -75,14 +79,19 @@
         (((0, 1), (1, 0)), ((), ())),
         preferred_element_type=jnp.float32,
     )
-    halfway, force_part = (
-        lax.psum_scatter(tangent, "blk", scatter_dimension=1, tiled=True),
-        lax.psum_scatter(force_all, "blk", scatter_dimension=0, tiled=True),
+    pad = jnp.zeros((7, basis_modes), jnp.float32)
+    stacked = jnp.concatenate([tangent, force_all[None, :], pad], axis=0)
+    parts = lax.all_to_all(stacked, "blk", split_axis=1, concat_axis=0, tiled=True)
+    halfway = jnp.sum(parts.reshape(n_blk, basis_modes + 8, cols), axis=0)
+    force_cols = halfway[basis_modes]
+    tangent_rows = halfway[:basis_modes].reshape(n_elem, rows, cols)
+    chunks = jnp.concatenate(
+        [tangent_rows, jnp.broadcast_to(force_cols[None, None, :], (n_elem, 1, cols))], axis=1
     )
-    mine = lax.psum_scatter(halfway, "elem", scatter_dimension=0, tiled=True)
-    force_cols = lax.psum(force_part, "elem")
+    arrived_chunks = lax.all_to_all(chunks, "elem", split_axis=0, concat_axis=0, tiled=True)
+    mine = jnp.sum(arrived_chunks, axis=0)
     scale = lax.rsqrt(24.0 * jnp.sum(set_size).astype(jnp.float32))
-    return (mine * scale, force_cols * scale - load)
+    return (mine[:rows] * scale, mine[rows] * scale - load)
 
 
 def solution(mesh):

time: 337 us -> 133 us (0.39)
  waiting for transfers between devices: 176 us -> 26.8 us
  blocking collectives: 83.9 us -> 23.2 us
  between operations: 15.7 us -> 1.7 us
  local copies, waits for them, and re-layouts: 27 us -> 32.8 us
  starting transfers between devices: 11.7 us -> 17.2 us
  matrix products: 11.5 us -> 16.9 us
  other arithmetic: 10 us -> 13.4 us
    unnamed x3 -> x0, waiting for transfers between devices: 128 us -> none
    psum x1 -> x0, blocking collectives: 71.2 us -> none  [local(): force_cols = lax.psum(force_part, 'elem')]
    reduce_scatter x1 -> x0, waiting for transfers between devices: 28.3 us -> none  [local(): lax.psum_scatter(tangent, 'blk', scatter_dimension=1, tiled=True)]
    all_to_all x0 -> x1, blocking collectives: none -> 23.2 us  [local(): lax.all_to_all(stacked, 'blk', split_axis=1, concat_axis=0, tiled=True)]
    unnamed x1 -> x0, blocking collectives: 12.7 us -> none
    all_to_all x0 -> x1, waiting for transfers between devices: none -> 7.58 us  [local(): lax.all_to_all(chunks, 'elem', split_axis=0, concat_axis=0, tiled=True)]
    all_to_all x0 -> x1, starting transfers between devices: none -> 5.56 us  [local(): lax.all_to_all(chunks, 'elem', split_axis=0, concat_axis=0, tiled=True)]
    dot_general x0 -> x1, local copies, waits for them, and re-layouts: none -> 5.14 us  [local(): lax.dot_general(basis_matrix, weighted_image, (((0, 1), (0, 1)), ((), ())...]
  transfers between devices with their start and end apart: 3 -> 2, of which waited for: 3 -> 2; matrix products, arithmetic and copies ran while one was open for 2% -> 3% of each run, Pallas kernels for 0% -> 0%
where the time goes in v2:
time: 133 us; the launch traced here: 132 us
  local copies, waits for them, and re-layouts  32.8 us (25%)
  waiting for transfers between devices  26.8 us (20%)
  blocking collectives  23.2 us (17%)
  starting transfers between devices  17.2 us (13%)
  matrix products  16.9 us (13%)
  other arithmetic  13.4 us (10%)
  between operations  1.7 us (1%)
    all_to_all x1, blocking collectives, local(): lax.all_to_all(stacked, 'blk', split_axis=1, concat_axis=0, tiled=True)  23.2 us
    all_to_all x1, waiting for transfers between devices, local(): lax.all_to_all(outgoing, 'elem', split_axis=0, concat_axis=0, tiled=True)  19.2 us
    all_to_all x1, starting transfers between devices, local(): lax.all_to_all(outgoing, 'elem', split_axis=0, concat_axis=0, tiled=True)  11.6 us
    all_to_all x1, waiting for transfers between devices, local(): lax.all_to_all(chunks, 'elem', split_axis=0, concat_axis=0, tiled=True)  7.58 us
    unnamed x26, local copies, waits for them, and re-layouts  6.21 us
    dot_general x1, matrix products, element_contributions(): jnp.einsum('ak,ekcm->eacm', grads, sym, precision=lax.Precision.HIGHEST)  5.69 us
    all_to_all x1, starting transfers between devices, local(): lax.all_to_all(chunks, 'elem', split_axis=0, concat_axis=0, tiled=True)  5.56 us
    dot_general x1, local copies, waits for them, and re-layouts, local(): lax.dot_general(basis_matrix, weighted_image, (((0, 1), (0, 1)), ((), ())...  5.14 us
  transfers between devices with their start and end apart: 2, of which 2 were waited for; matrix products, arithmetic and copies ran while one was open for 3% of the time, Pallas kernels for 0%

profile of v2, /device:TPU:2, one launch (start us, length us, event | category | flops | bytes accessed | tf_op | source)
XLA Modules:
  0.0 132.0 jit_solution(6316363443217147849)
XLA Ops:
  0.6 4.7 %copy.47 = bf16[1024,3,512]{0,2,1:T(8,128)(2,1)} copy(bf16[1024,3,512]{2,0,1:T(8,128)(2,1)} %param.8) | data formatting | bytes 6291456 | tf_op args[0]
  5.3 3.2 %copy.48 = bf16[1024,1536]{1,0:T(8,128)(2,1)S(1)} copy(bf16[1024,1536]{0,1:T(8,128)(2,1)} %bitcast.91) | data formatting | bytes 6291456 | tf_op jit(solution)/shard_map/reshape | solution.py:53
  9.1 0.7 reduce.7
  9.8 2.1 %gather_fusion = bf16[256,1536]{1,0:T(8,128)(2,1)} fusion(bf16[1024,1536]{1,0:T(8,128)(2,1)S(1)} %copy.48, s32[1024]{0:T(1024)S(1)} %pad_clamp_fusion.1), kind=kCustom, calls=%fused_computation | custom fusion | bytes 1573888 | tf_op jit(solution)/shard_map/jit(_take)/gather | solution.py:54
  12.0 2.2 %bitcast_select_fusion = bf16[32,8,1536]{2,1,0:T(8,128)(2,1)} fusion(bf16[256,1536]{1,0:T(8,128)(2,1)} %gather_fusion, pred[32,8]{1,0:T(8,128)(4,1)S(1)} %compare_and_fusion), kind=kLoop, calls=%fused_computation.21 | loop fusion | flops 393216 | bytes 1573120 | tf_op jit(solution)/shard_map/jit(_take)/select_n | solution.py:54
  14.2 11.6 %all-to-all-start = ((bf16[32,8,1536]{2,1,0:T(8,128)(2,1)}), bf16[32,8,1536]{2,1,0:T(8,128)(2,1)S(1)}, u32[]{:S(2)}, u32[]{:S(2)}) async-start(bf16[32,8,1536]{2,1,0:T(8,128)(2,1)} %bitcast_select_fusion), calls=%async_computation | async-start | bytes 1572864 | tf_op jit(solution)/shard_map/all_to_all | solution.py:55
  26.6 0.9 broadcast_in_dim.62
  28.2 0.7 compare_select_fusion.10
  29.1 19.2 %all-to-all-done = bf16[32,8,1536]{2,1,0:T(8,128)(2,1)S(1)} async-done(((bf16[32,8,1536]{2,1,0:T(8,128)(2,1)}), bf16[32,8,1536]{2,1,0:T(8,128)(2,1)S(1)}, u32[]{:S(2)}, u32[]{:S(2)}) %all-to-all-start) | async-done | bytes 786464 | tf_op jit(solution)/shard_map/all_to_all | solution.py:55
  48.3 2.1 %gather_fusion.1 = bf16[512,1536]{1,0:T(8,128)(2,1)S(1)} fusion(bf16[256,1536]{1,0:T(8,128)(2,1)S(1)} %bitcast.88, s32[1024]{0:T(1024)S(1)} %pad_clamp_fusion), kind=kCustom, calls=%fused_computation.1 | custom fusion | bytes 3147776 | tf_op jit(solution)/shard_map/jit(_take)/gather | solution.py:57
  50.4 1.6 %gather.18 = bf16[64,24,512]{2,1,0:T(8,128)(2,1)} reshape(bf16[512,1536]{1,0:T(8,128)(2,1)S(1)} %gather_fusion.1) | data formatting | bytes 3145728 | tf_op jit(solution)/shard_map/jit(_take)/gather | solution.py:57
  52.0 0.8 fusion.10
  52.8 1.8 %copy.93 = f32[64,3,512,3]{2,1,3,0:T(4,128)} copy(f32[64,3,512,3]{2,3,1,0:T(4,128)S(1)} %fusion.10) | data formatting | bytes 2359296 | tf_op jit(solution)/shard_map/ak,eacm->ekcm/dot_general | solution.py:18
  54.6 2.0 %bitcast_add_fusion.1 = f32[64,3,3,512]{3,2,1,0:T(4,128)} fusion(f32[64,3,512,3]{2,3,1,0:T(4,128)S(1)} %fusion.10), kind=kLoop, calls=%fused_computation.10 | loop fusion | flops 294912 | bytes 2359296 | tf_op jit(solution)/shard_map/add | solution.py:37
  56.5 1.4 %fusion.8 = bf16[512,64,24]{0,2,1:T(8,128)(2,1)} fusion(bf16[64,24,512]{2,1,0:T(8,128)(2,1)S(1)} %copy-done, pred[64,24]{1,0:T(8,128)(4,1)S(1)} %copy.46), kind=kLoop, calls=%fused_computation.15 | loop fusion | flops 786432 | bytes 3147264 | tf_op jit(solution)/shard_map/dot_general | solution.py:76
  58.0 1.5 %fusion.9 = f32[1,64,24]{2,0,1:T(1,128)S(1)} fusion(bf16[512,1,1]{0,1,2:T(2,128)(2,1)S(1)} %reshape.343, bf16[64,24,512]{2,1,0:T(8,128)(2,1)S(1)} %copy-done, pred[64,24]{1,0:T(8,128)(4,1)S(1)} %copy.46), kind=kOutput, calls=%fused_computation.16 | convolution fusion | flops 2359296 | bytes 1581568 | tf_op jit(solution)/shard_map/agd,d->ga/dot_general | solution.py:64
  59.9 1.7 %slice_add_fusion = f32[64,1,1,512]{3,2,1,0:T(1,128)S(1)} fusion(f32[64,3,3,512]{3,2,1,0:T(4,128)} %bitcast.93), kind=kLoop, calls=%fused_computation.26 | loop fusion | flops 65536 | bytes 524288 | tf_op jit(solution)/shard_map/add | solution.py:38
  61.7 5.7 %fusion.4 = bf16[64,8,3,512]{3,1,2,0:T(8,128)(2,1)S(1)} fusion(f32[64,3,3,512]{3,2,1,0:T(4,128)} %bitcast_add_fusion.1, f32[64,512]{1,0:T(8,128)S(1)} %bitcast.95, f32[64,8,3]{1,2,0:T(4,128)S(1)} %broadcast_multiply_fusion, f32[64]{0:T(128)S(1)} %compare_select_fusion.10, bf16[64,8,3,512]{3,1,2,0:T(8,128)(2,1)S(1)} %bitcast.90, pred[64,8]{1,0:T(8,128)(4,1)S(1)} %copy.50, ...), kind=kOutput, calls=%fused_computation.7 | convolution fusion | flops 34603536 | bytes 4463416 | tf_op jit(solution)/shard_map/ak,ekcm->eacm/dot_general | solution.py:39
  67.4 1.7 %copy.54 = bf16[64,8,3,512]{3,0,2,1:T(8,128)(2,1)} copy(bf16[64,8,3,512]{3,1,2,0:T(8,128)(2,1)S(1)} %fusion.4) | data formatting | bytes 3145728 | tf_op jit(solution)/shard_map/convert_element_type | solution.py:66
  69.1 5.1 %reshape.350 = bf16[8,64,64,24]{1,0,2,3:T(8,128)(2,1)} reshape(bf16[512,64,24]{0,1,2:T(8,128)(2,1)} %bitcast.92) | data formatting | bytes 3145728 | tf_op jit(solution)/shard_map/dot_general | solution.py:70
  74.3 1.4 %broadcast_select_fusion.4 = bf16[512,1536]{1,0:T(8,128)(2,1)} fusion(pred[512,1536]{1,0:T(8,128)(4,1)S(1)} %broadcast_in_dim.62, bf16[512,1536]{1,0:T(8,128)(2,1)S(1)} %gather_fusion.1), kind=kLoop, calls=%fused_computation.24 | loop fusion | flops 786432 | bytes 3932160 | tf_op jit(solution)/shard_map/jit(_take)/select_n | solution.py:57
  75.6 2.7 %reshape.346 = bf16[64,24,512,1]{2,1,0,3:T(8,128)(2,1)S(1)} reshape(bf16[512,1536]{1,0:T(8,128)(2,1)} %broadcast_select_fusion.4) | data formatting | bytes 3145728 | tf_op jit(solution)/shard_map/jit(_take)/select_n | solution.py:57
  78.8 3.0 %reshape.322 = bf16[8,64,64,24]{1,0,3,2:T(8,128)(2,1)} reshape(bf16[512,64,24]{0,2,1:T(8,128)(2,1)S(1)} %copy-done.1) | data formatting | bytes 3145728 | tf_op jit(solution)/shard_map/reshape.256
  81.9 4.5 %fusion.11 = f32[512,8,64]{0,2,1:T(8,128)S(1)} fusion(bf16[64,24,512,1]{2,1,0,3:T(8,128)(2,1)S(1)} %reshape.346, bf16[8,64,64,24]{1,0,2,3:T(8,128)(2,1)} %reshape.350), kind=kOutput, calls=%fused_computation.18 | convolution fusion | flops 805306368 | bytes 4194304 | tf_op jit(solution)/shard_map/dot_general | solution.py:70
  86.4 3.6 %fusion.14 = f32[1,8,64]{0,2,1:T(8,128)S(1)} fusion(bf16[8,64,64,24]{1,0,3,2:T(8,128)(2,1)S(1)} %copy-done.2, bf16[24,64,1,1]{1,0,2,3:T(8,128)(2,1)S(1)} %fusion.22), kind=kOutput, calls=%fused_computation.20 | convolution fusion | flops 1572864 | bytes 1577984 | tf_op jit(solution)/shard_map/dot_general | solution.py:76
  90.2 23.2 %all_to_all.24 = f32[520,8,64]{0,2,1:T(8,128)S(1)} all-to-all(f32[520,8,64]{0,2,1:T(8,128)S(1)} %maximum_maximum_fusion), channel_id=1, replica_groups=mesh['elem'=32,'blk'=8] {'blk'}, dimensions={1} | all-to-all | bytes 2129920 | tf_op jit(solution)/shard_map/all_to_all | solution.py:84
  113.9 0.8 reshape.362
  114.7 5.6 %all-to-all-start.2 = ((f32[32,1,1088]{2,1,0:T(1,128)}), f32[32,1,1088]{2,1,0:T(1,128)S(1)}, u32[]{:S(2)}, u32[]{:S(2)}) async-start(f32[32,1,1088]{2,1,0:T(1,128)} %reshape.362), calls=%async_computation.2 | async-start | bytes 294912 | tf_op jit(solution)/shard_map/all_to_all | solution.py:91
  120.3 0.6 reduce_sum.29
  121.6 7.6 %all-to-all-done.2 = f32[32,1,1088]{2,1,0:T(1,128)S(1)} async-done(((f32[32,1,1088]{2,1,0:T(1,128)}), f32[32,1,1088]{2,1,0:T(1,128)S(1)}, u32[]{:S(2)}, u32[]{:S(2)}) %all-to-all-start.2) | async-done | bytes 139296 | tf_op jit(solution)/shard_map/all_to_all | solution.py:91
  129.7 1.0 reduce.8
  130.8 0.6 slice_multiply_fusion
  (65 shorter events, 5.0 us)
Async XLA Ops:
  5.3 3.2 %copy-start.4 = (s32[1,1,256]{2,1,0:T(1,128)S(1)}, s32[1,1,256]{2,1,0:T(1,128)}, u32[]{:S(2)}) copy-start(s32[1,1,256]{2,1,0:T(1,128)} %param.9) | copy-start | bytes 3076
  12.0 13.9 %copy-start.3 = (s32[8,64]{1,0:T(8,128)S(1)}, s32[8,64]{1,0:T(8,128)}, u32[]{:S(2)}) copy-start(s32[8,64]{1,0:T(8,128)} %param.10) | copy-start | bytes 6148
  12.0 14.3 %copy-start.5 = (bf16[512]{0:T(512)(128)(2,1)S(1)}, bf16[512]{0:T(512)(128)(2,1)}, u32[]{:S(2)}) copy-start(bf16[512]{0:T(512)(128)(2,1)} %param.14) | copy-start | bytes 3076
  14.2 34.1 %all-to-all-start = ((bf16[32,8,1536]{2,1,0:T(8,128)(2,1)}), bf16[32,8,1536]{2,1,0:T(8,128)(2,1)S(1)}, u32[]{:S(2)}, u32[]{:S(2)}) async-start(bf16[32,8,1536]{2,1,0:T(8,128)(2,1)} %bitcast_select_fusion), calls=%async_computation | async-start | bytes 1572864 | tf_op jit(solution)/shard_map/all_to_all | solution.py:55
  25.8 1.6 %copy-start.9 = (s32[32]{0:T(128)S(1)}, s32[32]{0:T(128)}, u32[]{:S(2)}) copy-start(s32[32]{0:T(128)} %param.11) | copy-start | bytes 388
  25.8 2.4 %copy-start.6 = (f32[64]{0:T(128)S(1)}, f32[64]{0:T(128)}, u32[]{:S(2)}) copy-start(f32[64]{0:T(128)} %param.12) | copy-start | bytes 772
  54.6 2.0 %copy-start = (bf16[64,24,512]{2,1,0:T(8,128)(2,1)S(1)}, bf16[64,24,512]{2,1,0:T(8,128)(2,1)}, u32[]{:S(2)}) copy-start(bf16[64,24,512]{2,1,0:T(8,128)(2,1)} %gather.18) | copy-start | bytes 4718596
  58.0 3.6 %copy-start.7 = (f32[64]{0:T(128)S(1)}, f32[64]{0:T(128)}, u32[]{:S(2)}) copy-start(f32[64]{0:T(128)} %param.13) | copy-start | bytes 772
  75.6 3.2 %copy-start.1 = (bf16[512,64,24]{0,2,1:T(8,128)(2,1)S(1)}, bf16[512,64,24]{0,2,1:T(8,128)(2,1)}, u32[]{:S(2)}) copy-start(bf16[512,64,24]{0,2,1:T(8,128)(2,1)} %fusion.8) | copy-start | bytes 4718596
  81.9 4.5 %copy-start.2 = (bf16[8,64,64,24]{1,0,3,2:T(8,128)(2,1)S(1)}, bf16[8,64,64,24]{1,0,3,2:T(8,128)(2,1)}, u32[]{:S(2)}) copy-start(bf16[8,64,64,24]{1,0,3,2:T(8,128)(2,1)} %reshape.322) | copy-start | bytes 4718596
  113.7 17.8 %copy-start.8 = (f32[64]{0:T(128)S(1)}, f32[64]{0:T(128)}, u32[]{:S(2)}) copy-start(f32[64]{0:T(128)} %param.15) | copy-start | bytes 772
  114.7 14.5 %all-to-all-start.2 = ((f32[32,1,1088]{2,1,0:T(1,128)}), f32[32,1,1088]{2,1,0:T(1,128)S(1)}, u32[]{:S(2)}, u32[]{:S(2)}) async-start(f32[32,1,1088]{2,1,0:T(1,128)} %reshape.362), calls=%async_computation.2 | async-start | bytes 294912 | tf_op jit(solution)/shard_map/all_to_all | solution.py:91

commit v3 on v2

v3 whole, which is shorter than its diff:
```python
import jax
import jax.numpy as jnp
from jax import lax
from jax.experimental import pallas as pl
from jax.experimental.pallas import tpu as pltpu
from jax.sharding import PartitionSpec as P

G = [[(2 * ((a >> k) & 1) - 1) * 0.25 for k in range(3)] for a in range(8)]


def element_body(arrived_ref, slot_ref, state_ref, omega_ref, stiff_ref, out_ref, v_ref, w_ref):
    n_el = slot_ref.shape[0]
    n_slot = arrived_ref.shape[1]
    modes = arrived_ref.shape[2]
    lane = lax.broadcasted_iota(jnp.int32, (n_el, n_slot), 1)
    state_pad = state_ref[...]
    disp = {}
    for a in range(8):
        onehot = (slot_ref[:, a:a + 1] == lane).astype(jnp.bfloat16)
        for c in range(3):
            va = jnp.dot(onehot, arrived_ref[c], preferred_element_type=jnp.float32).astype(jnp.bfloat16)
            v_ref[pl.ds((3 * a + c) * n_el, n_el), :] = va
            disp[a, c] = jnp.dot(va, state_pad, preferred_element_type=jnp.float32)[:, 0:1]
    h = {}
    for k in range(3):
        for c in range(3):
            acc = G[0][k] * disp[0, c]
            for a in range(1, 8):
                acc = acc + G[a][k] * disp[a, c]
            h[k, c] = acc
    stiff = stiff_ref[...]
    omega = omega_ref[...]
    vol = h[0, 0] + h[1, 1] + h[2, 2]
    lam = 1.0 + stiff * vol ** 2 - 2.0 / 3.0
    press = vol + stiff * vol ** 3 / 3.0 - 2.0 / 3.0 * vol
    stress = {}
    for k in range(3):
        for c in range(3):
            s = h[k, c] + h[c, k]
            if k == c:
                s = s + press
            stress[k, c] = s
    force_acc = jnp.zeros((n_el, modes), jnp.float32)
    for a in range(8):
        for c in range(3):
            f = G[a][0] * stress[0, c] + G[a][1] * stress[1, c] + G[a][2] * stress[2, c]
            f = f + 0.25 * disp[a, c]
            wf = (f * omega).astype(jnp.bfloat16).astype(jnp.float32)
            force_acc = force_acc + v_ref[pl.ds((3 * a + c) * n_el, n_el), :].astype(jnp.float32) * wf
    grad = {}
    for k in range(3):
        for c in range(3):
            acc = None
            for a in range(8):
                term = G[a][k] * v_ref[pl.ds((3 * a + c) * n_el, n_el), :].astype(jnp.float32)
                acc = term if acc is None else acc + term
            grad[k, c] = acc
    trace = grad[0, 0] + grad[1, 1] + grad[2, 2]
    for a in range(8):
        for c in range(3):
            img = G[a][0] * (grad[0, c] + grad[c, 0])
            img = img + G[a][1] * (grad[1, c] + grad[c, 1])
            img = img + G[a][2] * (grad[2, c] + grad[c, 2])
            img = img + (lam * G[a][c]) * trace
            img = img + 0.25 * v_ref[pl.ds((3 * a + c) * n_el, n_el), :].astype(jnp.float32)
            w_ref[pl.ds((3 * a + c) * n_el, n_el), :] = (omega * img).astype(jnp.bfloat16)
    tangent = lax.dot_general(
        v_ref[...], w_ref[...], (((0,), (0,)), ((), ())), preferred_element_type=jnp.float32
    )
    out_ref[pl.ds(0, modes), :] = tangent
    force_row = jnp.sum(force_acc, axis=0, keepdims=True)
    out_ref[pl.ds(modes, 8), :] = jnp.concatenate(
        [force_row, jnp.zeros((7, modes), jnp.float32)], axis=0
    )


def element_stage(arrived3, slot_t, state, omega, stiff):
    n_el = slot_t.shape[0]
    modes = arrived3.shape[2]
    state_pad = jnp.zeros((modes, 128), jnp.bfloat16).at[:, 0].set(state)
    vmem = pltpu.MemorySpace.VMEM if hasattr(pltpu, "MemorySpace") else pltpu.TPUMemorySpace.VMEM
    return pl.pallas_call(
        element_body,
        out_shape=jax.ShapeDtypeStruct((modes + 8, modes), jnp.float32),
        in_specs=[pl.BlockSpec(memory_space=vmem)] * 5,
        out_specs=pl.BlockSpec(memory_space=vmem),
        scratch_shapes=[
            pltpu.VMEM((24 * n_el, modes), jnp.bfloat16),
            pltpu.VMEM((24 * n_el, modes), jnp.bfloat16),
        ],
    )(arrived3, slot_t, state_pad, omega.reshape(n_el, 1), stiff.reshape(n_el, 1))


def local(basis, send_rows, elem_slot, set_size, elem_weight, element_stiffening, state, load):
    basis_modes = basis.shape[2]
    n_elem = lax.psum(1, "elem")
    n_blk = lax.psum(1, "blk")
    by_component = jnp.transpose(basis, (1, 0, 2))
    outgoing = jnp.take(by_component, send_rows[0, 0], axis=1)
    arrived = lax.all_to_all(outgoing, "elem", split_axis=1, concat_axis=1, tiled=True)
    element_count = elem_slot.shape[1]
    set_index = lax.axis_index("elem")
    block_index = lax.axis_index("blk")
    live = lax.dynamic_index_in_dim(set_size, set_index, keepdims=False)
    position = block_index * element_count + jnp.arange(element_count, dtype=jnp.int32)
    weights = jnp.where(position < live, elem_weight, jnp.zeros_like(elem_weight))
    stacked = element_stage(arrived, elem_slot.T, state, weights, element_stiffening)
    rows = basis_modes // n_elem
    cols = basis_modes // n_blk
    parts = lax.all_to_all(stacked, "blk", split_axis=1, concat_axis=0, tiled=True)
    halfway = jnp.sum(parts.reshape(n_blk, basis_modes + 8, cols), axis=0)
    force_cols = halfway[basis_modes]
    tangent_rows = halfway[:basis_modes].reshape(n_elem, rows, cols)
    chunks = jnp.concatenate(
        [tangent_rows, jnp.broadcast_to(force_cols[None, None, :], (n_elem, 1, cols))], axis=1
    )
    arrived_chunks = lax.all_to_all(chunks, "elem", split_axis=0, concat_axis=0, tiled=True)
    mine = jnp.sum(arrived_chunks, axis=0)
    scale = lax.rsqrt(24.0 * jnp.sum(set_size).astype(jnp.float32))
    return (mine[:rows] * scale, mine[rows] * scale - load)


def solution(mesh):
    in_specs = (
        P("elem", None, None),
        P("elem", "blk", None),
        P(None, ("elem", "blk")),
        P(),
        P(("elem", "blk")),
        P(("elem", "blk")),
        P(),
        P("blk"),
    )
    out_specs = (P("elem", "blk"), P("blk"))
    return jax.shard_map(local, mesh=mesh, in_specs=in_specs, out_specs=out_specs, check_vma=False)
```

time: 133 us -> 106 us (0.80)
  matrix products: 16.9 us -> 0 us
  local copies, waits for them, and re-layouts: 32.8 us -> 18.2 us
  Pallas kernels: 0 us -> 8.21 us
  other arithmetic: 13.4 us -> 6.71 us
  waiting for transfers between devices: 26.8 us -> 30.1 us
    dot_general x7 -> x0, matrix products: 16.9 us -> none  [the longest x1 5.69 us: element_contributions(): jnp.einsum('ak,ekcm->eacm', grads, sym, precision=lax.Precision.HIGHEST)]
    pallas_call x0 -> x1, Pallas kernels: none -> 8.21 us  [element_stage(): pl.pallas_call(element_body, out_shape=jax.ShapeDtypeStruct((modes + 8, m...]
    dot_general x4 -> x0, local copies, waits for them, and re-layouts: 7.02 us -> none  [the longest x1 5.14 us: local(): lax.dot_general(basis_matrix, weighted_image, (((0, 1), (0, 1)), ((), ())...]
    add x2 -> x0, other arithmetic: 3.62 us -> none  [the longest x1 1.95 us: element_contributions(): sym = grad_basis + jnp.transpose(grad_basis, (0, 2, 1, 3))]
    all_to_all x1, waiting for transfers between devices: 19.2 us -> 22.6 us  [local(): lax.all_to_all(outgoing, 'elem', split_axis=1, concat_axis=1, tiled=True)]
    another operation x1, local copies, waits for them, and re-layouts: 3.04 us -> 0.13 us
    select_n x1 -> x0, local copies, waits for them, and re-layouts: 2.71 us -> none  [local(): chosen_elements = jnp.take(arrived, elem_slot.T.reshape(-1), axis=0)]
    select_n x6 -> x2, other arithmetic: 4.24 us -> 1.86 us  [local(): outgoing = jnp.take(by_component, send_rows[0, 0], axis=1)]
  transfers between devices with their start and end apart: 2 -> 2, of which waited for: 2 -> 2; matrix products, arithmetic and copies ran while one was open for 3% -> 6% of each run, Pallas kernels for 0% -> 0%
where the time goes in v3:
time: 106 us; the launch traced here: 105 us
  waiting for transfers between devices  30.1 us (28%)
  blocking collectives  23.2 us (22%)
  local copies, waits for them, and re-layouts  18.2 us (17%)
  starting transfers between devices  17.2 us (16%)
  Pallas kernels  8.21 us (8%)
  other arithmetic  6.71 us (6%)
  between operations  1.53 us (1%)
    all_to_all x1, blocking collectives, local(): lax.all_to_all(stacked, 'blk', split_axis=1, concat_axis=0, tiled=True)  23.2 us
    all_to_all x1, waiting for transfers between devices, local(): lax.all_to_all(outgoing, 'elem', split_axis=1, concat_axis=1, tiled=True)  22.6 us
    all_to_all x1, starting transfers between devices, local(): lax.all_to_all(outgoing, 'elem', split_axis=1, concat_axis=1, tiled=True)  11.6 us
    pallas_call x1, Pallas kernels, element_stage(): pl.pallas_call(element_body, out_shape=jax.ShapeDtypeStruct((modes + 8, m...  8.21 us
    unnamed x18, local copies, waits for them, and re-layouts  8.2 us
    all_to_all x1, waiting for transfers between devices, local(): lax.all_to_all(chunks, 'elem', split_axis=0, concat_axis=0, tiled=True)  7.58 us
    all_to_all x1, starting transfers between devices, local(): lax.all_to_all(chunks, 'elem', split_axis=0, concat_axis=0, tiled=True)  5.57 us
    gather x1, local copies, waits for them, and re-layouts, local(): outgoing = jnp.take(by_component, send_rows[0, 0], axis=1)  3.73 us
  transfers between devices with their start and end apart: 2, of which 2 were waited for; matrix products, arithmetic and copies ran while one was open for 6% of the time, Pallas kernels for 0%

profile of v3, /device:TPU:2, one launch (start us, length us, event | category | flops | bytes accessed | tf_op | source)
XLA Modules:
  0.0 105.2 jit_solution(1828673770474724285)
XLA Ops:
  0.6 6.5 %copy.36 = bf16[1024,3,512]{2,1,0:T(4,128)(2,1)} copy(bf16[1024,3,512]{2,0,1:T(8,128)(2,1)} %param.10) | data formatting | bytes 6291456 | tf_op args[0]
  7.2 0.0 copy-start.4
  7.2 3.7 %gather_fusion = bf16[256,3,512]{2,1,0:T(4,128)(2,1)S(1)} fusion(bf16[3,1024,512]{2,0,1:T(4,128)(2,1)} %bitcast.20, s32[1024]{0:T(1024)S(1)} %pad_clamp_fusion), kind=kCustom, calls=%fused_computation | custom fusion | bytes 1573888 | tf_op jit(solution)/shard_map/jit(_take)/gather | solution.py:99
  11.0 1.9 %select_bitcast_fusion = bf16[3,256,512]{2,0,1:T(4,128)(2,1)} fusion(bf16[256,3,512]{2,1,0:T(4,128)(2,1)S(1)} %gather_fusion, pred[256]{0:T(512)(128)(4,1)S(1)} %compare_and_fusion), kind=kLoop, calls=%fused_computation.2 | loop fusion | flops 393216 | bytes 1573120 | tf_op jit(solution)/shard_map/jit(_take)/select_n | solution.py:99
  12.8 11.6 %all-to-all-start = ((bf16[3,256,512]{2,0,1:T(4,128)(2,1)}), bf16[3,256,512]{2,0,1:T(4,128)(2,1)S(1)}, u32[]{:S(2)}, u32[]{:S(2)}) async-start(bf16[3,256,512]{2,0,1:T(4,128)(2,1)} %select_bitcast_fusion), calls=%async_computation | async-start | bytes 2097152 | tf_op jit(solution)/shard_map/all_to_all | solution.py:100
  24.5 0.7 copy.28
  25.2 0.6 compare_reduce_fusion
  25.8 0.6 broadcast_select_fusion
  26.5 0.1 reshape.97
  26.6 0.6 dynamic_slice.4
  27.2 0.6 fusion
  27.9 0.7 copy.31.omega_ref
  28.6 0.7 copy.32.stiff_ref
  29.3 0.7 scatter.4.state_ref
  30.0 22.6 %all-to-all-done = bf16[3,256,512]{2,0,1:T(4,128)(2,1)S(1)} async-done(((bf16[3,256,512]{2,0,1:T(4,128)(2,1)}), bf16[3,256,512]{2,0,1:T(4,128)(2,1)S(1)}, u32[]{:S(2)}, u32[]{:S(2)}) %all-to-all-start) | async-done | bytes 786464 | tf_op jit(solution)/shard_map/all_to_all | solution.py:100
  52.5 1.1 %copy.30.arrived_ref = bf16[3,256,512]{2,1,0:T(8,128)(2,1)} copy(bf16[3,256,512]{2,0,1:T(4,128)(2,1)S(1)} %all-to-all-done) | data formatting | bytes 1572864 | tf_op jit(solution)/shard_map/all_to_all | solution.py:100
  53.6 8.2 %shard_map.95 = f32[520,512]{1,0:T(8,128)} custom-call(bf16[3,256,512]{2,1,0:T(8,128)(2,1)} %copy.30.arrived_ref, s32[64,8]{1,0:T(8,128)} %bitcast.23, bf16[512,128]{1,0:T(8,128)(2,1)} %scatter.4.state_ref, f32[64,1]{1,0:T(8,128)} %copy.31.omega_ref, f32[64,1]{1,0:T(8,128)} %copy.32.stiff_ref), custom_call_target="tpu_custom_call" | custom-call | tf_op jit(solution)/shard_map/pallas_call | solution.py:82
  61.8 1.6 %copy.33 = f32[520,512]{0,1:T(8,128)S(1)} copy(f32[520,512]{1,0:T(8,128)} %shard_map.95) | data formatting | bytes 2129920 | tf_op jit(solution)/shard_map/pallas_call | solution.py:82
  63.5 0.0 copy-start.5
  63.5 23.2 %all_to_all.23 = f32[520,8,64]{0,2,1:T(8,128)S(1)} all-to-all(f32[520,8,64]{0,2,1:T(8,128)S(1)} %bitcast.21), channel_id=1, replica_groups=mesh['elem'=32,'blk'=8] {'blk'}, dimensions={1} | all-to-all | bytes 2129920 | tf_op jit(solution)/shard_map/all_to_all | solution.py:110
  86.7 0.1 reduce_sum.27
  86.8 0.1 slice_reduce_fusion
  86.9 0.1 copy.34
  87.1 0.8 reshape.99
  87.9 5.6 %all-to-all-start.2 = ((f32[32,1,1088]{2,1,0:T(1,128)}), f32[32,1,1088]{2,1,0:T(1,128)S(1)}, u32[]{:S(2)}, u32[]{:S(2)}) async-start(f32[32,1,1088]{2,1,0:T(1,128)} %reshape.99), calls=%async_computation.2 | async-start | bytes 294912 | tf_op jit(solution)/shard_map/all_to_all | solution.py:117
  93.5 0.6 reduce_sum.29
  94.8 7.6 %all-to-all-done.2 = f32[32,1,1088]{2,1,0:T(1,128)S(1)} async-done(((f32[32,1,1088]{2,1,0:T(1,128)}), f32[32,1,1088]{2,1,0:T(1,128)S(1)}, u32[]{:S(2)}, u32[]{:S(2)}) %all-to-all-start.2) | async-done | bytes 139296 | tf_op jit(solution)/shard_map/all_to_all | solution.py:117
  102.4 0.5 broadcast.74
  102.9 1.0 reduce.12
  103.9 0.1 reshape.100
  104.1 0.6 slice_multiply_fusion
  104.7 0.5 fusion.2
  (19 shorter events, 0.2 us)
Async XLA Ops:
  0.6 6.5 %copy-start.1 = (s32[1,1,256]{2,1,0:T(1,128)S(1)}, s32[1,1,256]{2,1,0:T(1,128)}, u32[]{:S(2)}) copy-start(s32[1,1,256]{2,1,0:T(1,128)} %param.11) | copy-start | bytes 3076
  7.2 17.3 %copy-start = (s32[8,64]{1,0:T(8,128)S(1)}, s32[8,64]{1,0:T(8,128)}, u32[]{:S(2)}) copy-start(s32[8,64]{1,0:T(8,128)} %param.12) | copy-start | bytes 6148
  7.2 18.6 %copy-start.2 = (bf16[512]{0:T(512)(128)(2,1)S(1)}, bf16[512]{0:T(512)(128)(2,1)}, u32[]{:S(2)}) copy-start(bf16[512]{0:T(512)(128)(2,1)} %param.16) | copy-start | bytes 3076
  7.2 19.4 %copy-start.6 = (s32[32]{0:T(128)S(1)}, s32[32]{0:T(128)}, u32[]{:S(2)}) copy-start(s32[32]{0:T(128)} %param.13) | copy-start | bytes 388
  7.2 20.0 %copy-start.4 = (f32[64]{0:T(128)S(1)}, f32[64]{0:T(128)}, u32[]{:S(2)}) copy-start(f32[64]{0:T(128)} %param.14) | copy-start | bytes 772
  7.2 21.4 %copy-start.3 = (f32[64]{0:T(128)S(1)}, f32[64]{0:T(128)}, u32[]{:S(2)}) copy-start(f32[64]{0:T(128)} %param.15) | copy-start | bytes 772
  12.8 39.7 %all-to-all-start = ((bf16[3,256,512]{2,0,1:T(4,128)(2,1)}), bf16[3,256,512]{2,0,1:T(4,128)(2,1)S(1)}, u32[]{:S(2)}, u32[]{:S(2)}) async-start(bf16[3,256,512]{2,0,1:T(4,128)(2,1)} %select_bitcast_fusion), calls=%async_computation | async-start | bytes 2097152 | tf_op jit(solution)/shard_map/all_to_all | solution.py:100
  63.5 41.2 %copy-start.5 = (f32[64]{0:T(128)S(1)}, f32[64]{0:T(128)}, u32[]{:S(2)}) copy-start(f32[64]{0:T(128)} %param.17) | copy-start | bytes 772
  87.9 14.5 %all-to-all-start.2 = ((f32[32,1,1088]{2,1,0:T(1,128)}), f32[32,1,1088]{2,1,0:T(1,128)S(1)}, u32[]{:S(2)}, u32[]{:S(2)}) async-start(f32[32,1,1088]{2,1,0:T(1,128)} %reshape.99), calls=%async_computation.2 | async-start | bytes 294912 | tf_op jit(solution)/shard_map/all_to_all | solution.py:117

commit v4 on v3

--- a/solution.py
+++ b/solution.py
@@ -107,8 +107,19 @@
     stacked = element_stage(arrived, elem_slot.T, state, weights, element_stiffening)
     rows = basis_modes // n_elem
     cols = basis_modes // n_blk
-    parts = lax.all_to_all(stacked, "blk", split_axis=1, concat_axis=0, tiled=True)
-    halfway = jnp.sum(parts.reshape(n_blk, basis_modes + 8, cols), axis=0)
+    n_y = n_blk // 2
+    core = block_index % 2
+    chip = block_index // 2
+    by_dest = stacked.reshape(basis_modes + 8, n_y, 2, cols)
+    pair = [(b, b ^ 1) for b in range(n_blk)]
+    sent = lax.dynamic_index_in_dim(by_dest, 1 - core, axis=2, keepdims=False)
+    kept = lax.dynamic_index_in_dim(by_dest, core, axis=2, keepdims=False)
+    chip_sum = kept + lax.ppermute(sent, "blk", pair)
+    halfway = lax.dynamic_index_in_dim(chip_sum, chip, axis=1, keepdims=False)
+    for shift in range(1, n_y):
+        ring = [(2 * y + c, 2 * ((y + shift) % n_y) + c) for y in range(n_y) for c in range(2)]
+        piece = lax.dynamic_index_in_dim(chip_sum, (chip + shift) % n_y, axis=1, keepdims=False)
+        halfway = halfway + lax.ppermute(piece, "blk", ring)
     force_cols = halfway[basis_modes]
     tangent_rows = halfway[:basis_modes].reshape(n_elem, rows, cols)
     chunks = jnp.concatenate(

time: 106 us -> 99.9 us (0.942)
  blocking collectives: 23.2 us -> 0 us
  waiting for transfers between devices: 30.1 us -> 41.8 us
  starting transfers between devices: 17.2 us -> 22.1 us
    all_to_all x1 -> x0, blocking collectives: 23.2 us -> none  [local(): lax.all_to_all(stacked, 'blk', split_axis=1, concat_axis=0, tiled=True)]
    ppermute x0 -> x4, waiting for transfers between devices: none -> 11.4 us  [the longest x3 9.37 us: local(): halfway = halfway + lax.ppermute(piece, 'blk', ring)]
    ppermute x0 -> x4, starting transfers between devices: none -> 4.79 us  [the longest x3 4.69 us: local(): halfway = halfway + lax.ppermute(piece, 'blk', ring)]
  transfers between devices with their start and end apart: 2 -> 6, of which waited for: 2 -> 6; matrix products, arithmetic and copies ran while one was open for 6% -> 6% of each run, Pallas kernels for 0% -> 0%
where the time goes in v4:
time: 99.9 us; the launch traced here: 98.7 us
  waiting for transfers between devices  41.8 us (42%)
  starting transfers between devices  22.1 us (22%)
  local copies, waits for them, and re-layouts  18.3 us (18%)
  Pallas kernels  8.2 us (8%)
  other arithmetic  6.71 us (7%)
  between operations  1.62 us (2%)
    all_to_all x1, waiting for transfers between devices, local(): lax.all_to_all(outgoing, 'elem', split_axis=1, concat_axis=1, tiled=True)  22.6 us
    all_to_all x1, starting transfers between devices, local(): lax.all_to_all(outgoing, 'elem', split_axis=1, concat_axis=1, tiled=True)  11.8 us
    ppermute x3, waiting for transfers between devices, local(): halfway = halfway + lax.ppermute(piece, 'blk', ring)  9.37 us
    unnamed x18, local copies, waits for them, and re-layouts  8.2 us
    pallas_call x1, Pallas kernels, element_stage(): pl.pallas_call(element_body, out_shape=jax.ShapeDtypeStruct((modes + 8, m...  8.2 us
    all_to_all x1, waiting for transfers between devices, local(): lax.all_to_all(chunks, 'elem', split_axis=0, concat_axis=0, tiled=True)  7.83 us
    all_to_all x1, starting transfers between devices, local(): lax.all_to_all(chunks, 'elem', split_axis=0, concat_axis=0, tiled=True)  5.56 us
    ppermute x3, starting transfers between devices, local(): halfway = halfway + lax.ppermute(piece, 'blk', ring)  4.69 us
  transfers between devices with their start and end apart: 6, of which 6 were waited for; matrix products, arithmetic and copies ran while one was open for 6% of the time, Pallas kernels for 0%

profile of v4, /device:TPU:2, one launch (start us, length us, event | category | flops | bytes accessed | tf_op | source)
XLA Modules:
  0.0 98.7 jit_solution(16497312337575863635)
XLA Ops:
  0.6 6.5 %copy.44 = bf16[1024,3,512]{2,1,0:T(4,128)(2,1)} copy(bf16[1024,3,512]{2,0,1:T(8,128)(2,1)} %param.10) | data formatting | bytes 6291456 | tf_op args[0]
  7.2 3.7 %gather_fusion = bf16[256,3,512]{2,1,0:T(4,128)(2,1)S(1)} fusion(bf16[3,1024,512]{2,0,1:T(4,128)(2,1)} %bitcast.36, s32[1024]{0:T(1024)S(1)} %pad_clamp_fusion), kind=kCustom, calls=%fused_computation | custom fusion | bytes 1573888 | tf_op jit(solution)/shard_map/jit(_take)/gather | solution.py:99
  10.9 1.8 %select_bitcast_fusion = bf16[3,256,512]{2,0,1:T(4,128)(2,1)} fusion(bf16[256,3,512]{2,1,0:T(4,128)(2,1)S(1)} %gather_fusion, pred[256]{0:T(512)(128)(4,1)S(1)} %compare_and_fusion), kind=kLoop, calls=%fused_computation.2 | loop fusion | flops 393216 | bytes 1573120 | tf_op jit(solution)/shard_map/jit(_take)/select_n | solution.py:99
  12.8 11.8 %all-to-all-start = ((bf16[3,256,512]{2,0,1:T(4,128)(2,1)}), bf16[3,256,512]{2,0,1:T(4,128)(2,1)S(1)}, u32[]{:S(2)}, u32[]{:S(2)}) async-start(bf16[3,256,512]{2,0,1:T(4,128)(2,1)} %select_bitcast_fusion), calls=%async_computation | async-start | bytes 2097152 | tf_op jit(solution)/shard_map/all_to_all | solution.py:100
  24.6 0.7 copy.36
  25.3 0.6 compare_reduce_fusion
  25.9 0.6 broadcast_select_fusion
  26.6 0.1 reshape.96
  26.7 0.6 dynamic_slice.24
  27.3 0.6 fusion.2
  28.0 0.7 copy.39.omega_ref
  28.7 0.7 copy.40.stiff_ref
  29.4 0.7 scatter.4.state_ref
  30.1 22.6 %all-to-all-done = bf16[3,256,512]{2,0,1:T(4,128)(2,1)S(1)} async-done(((bf16[3,256,512]{2,0,1:T(4,128)(2,1)}), bf16[3,256,512]{2,0,1:T(4,128)(2,1)S(1)}, u32[]{:S(2)}, u32[]{:S(2)}) %all-to-all-start) | async-done | bytes 786464 | tf_op jit(solution)/shard_map/all_to_all | solution.py:100
  52.6 1.1 %copy.38.arrived_ref = bf16[3,256,512]{2,1,0:T(8,128)(2,1)} copy(bf16[3,256,512]{2,0,1:T(4,128)(2,1)S(1)} %all-to-all-done) | data formatting | bytes 1572864 | tf_op jit(solution)/shard_map/all_to_all | solution.py:100
  53.7 8.2 %shard_map.95 = f32[520,512]{1,0:T(8,128)} custom-call(bf16[3,256,512]{2,1,0:T(8,128)(2,1)} %copy.38.arrived_ref, s32[64,8]{1,0:T(8,128)} %bitcast.40, bf16[512,128]{1,0:T(8,128)(2,1)} %scatter.4.state_ref, f32[64,1]{1,0:T(8,128)} %copy.39.omega_ref, f32[64,1]{1,0:T(8,128)} %copy.40.stiff_ref), custom_call_target="tpu_custom_call" | custom-call | tf_op jit(solution)/shard_map/pallas_call | solution.py:82
  61.9 1.6 %copy.41 = f32[520,512]{0,1:T(8,128)S(1)} copy(f32[520,512]{1,0:T(8,128)} %shard_map.95) | data formatting | bytes 2129920 | tf_op jit(solution)/shard_map/pallas_call | solution.py:82
  63.8 2.0 %collective-permute-done = f32[520,4,64]{0,2,1:T(8,128)S(1)} collective-permute-done((f32[520,4,64]{0,2,1:T(8,128)S(1)}, f32[520,4,64]{0,2,1:T(8,128)S(1)}, u32[]{:S(2)}, u32[]{:S(2)}) %collective-permute-start) | collective-permute-done | bytes 532512 | tf_op jit(solution)/shard_map/ppermute | solution.py:117
  65.9 3.1 %collective-permute-start.3 = (f32[520,64]{0,1:T(8,128)S(1)}, f32[520,64]{0,1:T(8,128)S(1)}, u32[]{:S(2)}, u32[]{:S(2)}) collective-permute-start(f32[520,64]{0,1:T(8,128)S(1)} %get-tuple-element.15), channel_id=1, source_target_pairs={{0,6},{1,7},{2,0},{3,1},{4,2},{5,3},{6,4},{7,5},{8,14},{9,15},{10,... | collective-permute-start | bytes 399368 | tf_op jit(solution)/shard_map/ppermute | solution.py:122
  69.0 0.6 collective-permute-start.2
  69.6 1.0 collective-permute-start.1
  70.6 5.7 %collective-permute-done.3 = f32[520,64]{0,1:T(8,128)S(1)} collective-permute-done((f32[520,64]{0,1:T(8,128)S(1)}, f32[520,64]{0,1:T(8,128)S(1)}, u32[]{:S(2)}, u32[]{:S(2)}) %collective-permute-start.3) | collective-permute-done | bytes 133152 | tf_op jit(solution)/shard_map/ppermute | solution.py:122
  76.3 1.4 %collective-permute-done.2 = f32[520,64]{0,1:T(8,128)S(1)} collective-permute-done((f32[520,64]{0,1:T(8,128)S(1)}, f32[520,64]{0,1:T(8,128)S(1)}, u32[]{:S(2)}, u32[]{:S(2)}) %collective-permute-start.2) | collective-permute-done | bytes 133152 | tf_op jit(solution)/shard_map/ppermute | solution.py:122
  77.6 2.3 %collective-permute-done.1 = f32[520,64]{0,1:T(8,128)S(1)} collective-permute-done((f32[520,64]{0,1:T(8,128)S(1)}, f32[520,64]{0,1:T(8,128)S(1)}, u32[]{:S(2)}, u32[]{:S(2)}) %collective-permute-start.1) | collective-permute-done | bytes 133152 | tf_op jit(solution)/shard_map/ppermute | solution.py:122
  80.3 0.8 reshape.98
  81.2 5.6 %all-to-all-start.1 = ((f32[32,1,1088]{2,1,0:T(1,128)}), f32[32,1,1088]{2,1,0:T(1,128)S(1)}, u32[]{:S(2)}, u32[]{:S(2)}) async-start(f32[32,1,1088]{2,1,0:T(1,128)} %reshape.98), calls=%async_computation.1 | async-start | bytes 294912 | tf_op jit(solution)/shard_map/all_to_all | solution.py:128
  86.8 0.6 reduce_sum.19
  88.1 7.8 %all-to-all-done.1 = f32[32,1,1088]{2,1,0:T(1,128)S(1)} async-done(((f32[32,1,1088]{2,1,0:T(1,128)}), f32[32,1,1088]{2,1,0:T(1,128)S(1)}, u32[]{:S(2)}, u32[]{:S(2)}) %all-to-all-start.1) | async-done | bytes 139296 | tf_op jit(solution)/shard_map/all_to_all | solution.py:128
  95.9 0.5 broadcast.79
  96.4 1.0 %reduce.10 = f32[32,1088]{1,0:T(8,128)S(1)} reduce(f32[32,1,1088]{2,1,0:T(1,128)S(1)} %all-to-all-done.1, f32[]{:T(128)} %broadcast.79), dimensions={1}, to_apply=%all_to_all.7.reduce_sub_computation | reduce | bytes 278532 | tf_op jit(solution)/shard_map/all_to_all | solution.py:128
  97.6 0.6 slice_multiply_fusion
  98.2 0.5 fusion.4
  (29 shorter events, 0.8 us)
Async XLA Ops:
  0.6 6.5 %copy-start.1 = (s32[1,1,256]{2,1,0:T(1,128)S(1)}, s32[1,1,256]{2,1,0:T(1,128)}, u32[]{:S(2)}) copy-start(s32[1,1,256]{2,1,0:T(1,128)} %param.11) | copy-start | bytes 3076
  12.8 11.8 %copy-start = (s32[8,64]{1,0:T(8,128)S(1)}, s32[8,64]{1,0:T(8,128)}, u32[]{:S(2)}) copy-start(s32[8,64]{1,0:T(8,128)} %param.12) | copy-start | bytes 6148
  12.8 13.1 %copy-start.2 = (bf16[512]{0:T(512)(128)(2,1)S(1)}, bf16[512]{0:T(512)(128)(2,1)}, u32[]{:S(2)}) copy-start(bf16[512]{0:T(512)(128)(2,1)} %param.16) | copy-start | bytes 3076
  12.8 13.9 %copy-start.6 = (s32[32]{0:T(128)S(1)}, s32[32]{0:T(128)}, u32[]{:S(2)}) copy-start(s32[32]{0:T(128)} %param.13) | copy-start | bytes 388
  12.8 14.5 %copy-start.4 = (f32[64]{0:T(128)S(1)}, f32[64]{0:T(128)}, u32[]{:S(2)}) copy-start(f32[64]{0:T(128)} %param.14) | copy-start | bytes 772
  12.8 15.9 %copy-start.3 = (f32[64]{0:T(128)S(1)}, f32[64]{0:T(128)}, u32[]{:S(2)}) copy-start(f32[64]{0:T(128)} %param.15) | copy-start | bytes 772
  12.8 39.8 %all-to-all-start = ((bf16[3,256,512]{2,0,1:T(4,128)(2,1)}), bf16[3,256,512]{2,0,1:T(4,128)(2,1)S(1)}, u32[]{:S(2)}, u32[]{:S(2)}) async-start(bf16[3,256,512]{2,0,1:T(4,128)(2,1)} %select_bitcast_fusion), calls=%async_computation | async-start | bytes 2097152 | tf_op jit(solution)/shard_map/all_to_all | solution.py:100
  63.6 2.2 %collective-permute-start = (f32[520,4,64]{0,2,1:T(8,128)S(1)}, f32[520,4,64]{0,2,1:T(8,128)S(1)}, u32[]{:S(2)}, u32[]{:S(2)}) collective-permute-start(f32[520,4,64]{0,2,1:T(8,128)S(1)} %dynamic-slice_bitcast_fusion), channel_id=1, source_target_pairs={{0,1},{1,0},{2,3},{3,2},{4,5},{5,4},{6,7},{7,6},{8,9},{9,8},{10,11... | collective-permute-start | bytes 1597448 | tf_op jit(solution)/shard_map/ppermute | solution.py:117
  65.9 10.4 %collective-permute-start.3 = (f32[520,64]{0,1:T(8,128)S(1)}, f32[520,64]{0,1:T(8,128)S(1)}, u32[]{:S(2)}, u32[]{:S(2)}) collective-permute-start(f32[520,64]{0,1:T(8,128)S(1)} %get-tuple-element.15), channel_id=1, source_target_pairs={{0,6},{1,7},{2,0},{3,1},{4,2},{5,3},{6,4},{7,5},{8,14},{9,15},{10,... | collective-permute-start | bytes 399368 | tf_op jit(solution)/shard_map/ppermute | solution.py:122
  69.0 8.6 %collective-permute-start.2 = (f32[520,64]{0,1:T(8,128)S(1)}, f32[520,64]{0,1:T(8,128)S(1)}, u32[]{:S(2)}, u32[]{:S(2)}) collective-permute-start(f32[520,64]{0,1:T(8,128)S(1)} %get-tuple-element.16), channel_id=1, source_target_pairs={{0,4},{1,5},{2,6},{3,7},{4,0},{5,1},{6,2},{7,3},{8,12},{9,13},{10,... | collective-permute-start | bytes 399368 | tf_op jit(solution)/shard_map/ppermute | solution.py:122
  69.6 10.3 %collective-permute-start.1 = (f32[520,64]{0,1:T(8,128)S(1)}, f32[520,64]{0,1:T(8,128)S(1)}, u32[]{:S(2)}, u32[]{:S(2)}) collective-permute-start(f32[520,64]{0,1:T(8,128)S(1)} %get-tuple-element.14), channel_id=1, source_target_pairs={{0,2},{1,3},{2,4},{3,5},{4,6},{5,7},{6,0},{7,1},{8,10},{9,11},{10,... | collective-permute-start | bytes 399368 | tf_op jit(solution)/shard_map/ppermute | solution.py:122
  80.3 17.9 %copy-start.5 = (f32[64]{0:T(128)S(1)}, f32[64]{0:T(128)}, u32[]{:S(2)}) copy-start(f32[64]{0:T(128)} %param.17) | copy-start | bytes 772
  81.2 14.7 %all-to-all-start.1 = ((f32[32,1,1088]{2,1,0:T(1,128)}), f32[32,1,1088]{2,1,0:T(1,128)S(1)}, u32[]{:S(2)}, u32[]{:S(2)}) async-start(f32[32,1,1088]{2,1,0:T(1,128)} %reshape.98), calls=%async_computation.1 | async-start | bytes 294912 | tf_op jit(solution)/shard_map/all_to_all | solution.py:128

commit v5 on v4

--- a/solution.py
+++ b/solution.py
@@ -10,15 +10,16 @@
 
 def element_body(arrived_ref, slot_ref, state_ref, omega_ref, stiff_ref, out_ref, v_ref, w_ref):
     n_el = slot_ref.shape[0]
-    n_slot = arrived_ref.shape[1]
-    modes = arrived_ref.shape[2]
+    n_slot = arrived_ref.shape[0]
+    modes = out_ref.shape[1]
     lane = lax.broadcasted_iota(jnp.int32, (n_el, n_slot), 1)
     state_pad = state_ref[...]
     disp = {}
     for a in range(8):
         onehot = (slot_ref[:, a:a + 1] == lane).astype(jnp.bfloat16)
+        corner = jnp.dot(onehot, arrived_ref[...], preferred_element_type=jnp.float32).astype(jnp.bfloat16)
         for c in range(3):
-            va = jnp.dot(onehot, arrived_ref[c], preferred_element_type=jnp.float32).astype(jnp.bfloat16)
+            va = corner[:, c * modes:(c + 1) * modes]
             v_ref[pl.ds((3 * a + c) * n_el, n_el), :] = va
             disp[a, c] = jnp.dot(va, state_pad, preferred_element_type=jnp.float32)[:, 0:1]
     h = {}
@@ -76,7 +77,7 @@
 
 def element_stage(arrived3, slot_t, state, omega, stiff):
     n_el = slot_t.shape[0]
-    modes = arrived3.shape[2]
+    modes = arrived3.shape[1] // 3
     state_pad = jnp.zeros((modes, 128), jnp.bfloat16).at[:, 0].set(state)
     vmem = pltpu.MemorySpace.VMEM if hasattr(pltpu, "MemorySpace") else pltpu.TPUMemorySpace.VMEM
     return pl.pallas_call(
@@ -91,13 +92,36 @@
     )(arrived3, slot_t, state_pad, omega.reshape(n_el, 1), stiff.reshape(n_el, 1))
 
 
+def gather_body(basis_ref, rows_ref, out_ref):
+    n_rows = rows_ref.shape[0]
+    nodes = basis_ref.shape[1]
+    modes = basis_ref.shape[2]
+    lane = lax.broadcasted_iota(jnp.int32, (n_rows, nodes), 1)
+    onehot = (rows_ref[...] == lane).astype(jnp.bfloat16)
+    for c in range(basis_ref.shape[0]):
+        picked = jnp.dot(onehot, basis_ref[c], preferred_element_type=jnp.float32)
+        out_ref[:, pl.ds(c * modes, modes)] = picked.astype(jnp.bfloat16)
+
+
+def gather_rows(by_component, rows):
+    comps, nodes, modes = by_component.shape
+    n_rows = rows.shape[0]
+    vmem = pltpu.MemorySpace.VMEM if hasattr(pltpu, "MemorySpace") else pltpu.TPUMemorySpace.VMEM
+    return pl.pallas_call(
+        gather_body,
+        out_shape=jax.ShapeDtypeStruct((n_rows, comps * modes), jnp.bfloat16),
+        in_specs=[pl.BlockSpec(memory_space=vmem)] * 2,
+        out_specs=pl.BlockSpec(memory_space=vmem),
+    )(by_component, rows.reshape(n_rows, 1))
+
+
 def local(basis, send_rows, elem_slot, set_size, elem_weight, element_stiffening, state, load):
     basis_modes = basis.shape[2]
     n_elem = lax.psum(1, "elem")
     n_blk = lax.psum(1, "blk")
     by_component = jnp.transpose(basis, (1, 0, 2))
-    outgoing = jnp.take(by_component, send_rows[0, 0], axis=1)
-    arrived = lax.all_to_all(outgoing, "elem", split_axis=1, concat_axis=1, tiled=True)
+    outgoing = gather_rows(by_component, send_rows[0, 0])
+    arrived = lax.all_to_all(outgoing, "elem", split_axis=0, concat_axis=0, tiled=True)
     element_count = elem_slot.shape[1]
     set_index = lax.axis_index("elem")
     block_index = lax.axis_index("blk")

time: 99.9 us -> 83.8 us (0.84)
  local copies, waits for them, and re-layouts: 18.3 us -> 9.35 us
  waiting for transfers between devices: 41.8 us -> 32.9 us
  Pallas kernels: 8.2 us -> 10.3 us
  other arithmetic: 6.71 us -> 4.86 us
  starting transfers between devices: 22.1 us -> 23.3 us
    all_to_all x1, waiting for transfers between devices: 22.6 us -> 16.9 us  [local(): lax.all_to_all(outgoing, 'elem', split_axis=0, concat_axis=0, tiled=True)]
    unnamed x18 -> x17, local copies, waits for them, and re-layouts: 8.2 us -> 2.58 us
    pallas_call x0 -> x1, Pallas kernels: none -> 3.83 us  [gather_rows(): pl.pallas_call(gather_body, out_shape=jax.ShapeDtypeStruct((n_rows, comps...]
    gather x1 -> x0, local copies, waits for them, and re-layouts: 3.73 us -> none  [local(): outgoing = jnp.take(by_component, send_rows[0, 0], axis=1)]
    ppermute x3, waiting for transfers between devices: 9.37 us -> 6.38 us  [local(): halfway = halfway + lax.ppermute(piece, 'blk', ring)]
    select_n x2 -> x0, other arithmetic: 1.84 us -> none  [local(): outgoing = jnp.take(by_component, send_rows[0, 0], axis=1)]
    pallas_call x1, Pallas kernels: 8.2 us -> 6.43 us  [element_stage(): pl.pallas_call(element_body, out_shape=jax.ShapeDtypeStruct((modes + 8, m...]
    another operation x1 -> x2, local copies, waits for them, and re-layouts: 0.13 us -> 1.6 us  [the longest x1 1.47 us: gather_rows(): rows.reshape(n_rows, 1)]
  transfers between devices with their start and end apart: 6 -> 6, of which waited for: 6 -> 5; matrix products, arithmetic and copies ran while one was open for 6% -> 7% of each run, Pallas kernels for 0% -> 0%
where the time goes in v5:
time: 83.8 us; the launch traced here: 82.3 us
  waiting for transfers between devices  32.9 us (39%)
  starting transfers between devices  23.3 us (28%)
  Pallas kernels  10.3 us (12%)
  local copies, waits for them, and re-layouts  9.35 us (11%)
  other arithmetic  4.86 us (6%)
  between operations  1.6 us (2%)
    all_to_all x1, waiting for transfers between devices, local(): lax.all_to_all(outgoing, 'elem', split_axis=0, concat_axis=0, tiled=True)  16.9 us
    all_to_all x1, starting transfers between devices, local(): lax.all_to_all(outgoing, 'elem', split_axis=0, concat_axis=0, tiled=True)  11.8 us
    all_to_all x1, waiting for transfers between devices, local(): lax.all_to_all(chunks, 'elem', split_axis=0, concat_axis=0, tiled=True)  7.58 us
    pallas_call x1, Pallas kernels, element_stage(): pl.pallas_call(element_body, out_shape=jax.ShapeDtypeStruct((modes + 8, m...  6.43 us
    ppermute x3, waiting for transfers between devices, local(): halfway = halfway + lax.ppermute(piece, 'blk', ring)  6.38 us
    ppermute x3, starting transfers between devices, local(): halfway = halfway + lax.ppermute(piece, 'blk', ring)  5.9 us
    all_to_all x1, starting transfers between devices, local(): lax.all_to_all(chunks, 'elem', split_axis=0, concat_axis=0, tiled=True)  5.56 us
    pallas_call x1, Pallas kernels, gather_rows(): pl.pallas_call(gather_body, out_shape=jax.ShapeDtypeStruct((n_rows, comps...  3.83 us
  transfers between devices with their start and end apart: 6, of which 5 were waited for; matrix products, arithmetic and copies ran while one was open for 7% of the time, Pallas kernels for 0%

profile of v5, /device:TPU:2, one launch (start us, length us, event | category | flops | bytes accessed | tf_op | source)
XLA Modules:
  0.0 82.3 jit_solution(12925734221615796156)
XLA Ops:
  0.6 1.5 %copy.25.rows_ref = s32[256,1]{1,0:T(8,128)} copy(s32[256,1]{0,1:T(1,128)} %bitcast.38) | data formatting | bytes 2048 | tf_op jit(solution)/shard_map/reshape;squeeze | solution.py:115
  2.1 3.8 %shard_map.95 = bf16[256,1536]{1,0:T(8,128)(2,1)} custom-call(bf16[3,1024,512]{2,1,0:T(8,128)(2,1)} %bitcast.34, s32[256,1]{1,0:T(8,128)} %copy.25.rows_ref), custom_call_target="tpu_custom_call" | custom-call | tf_op jit(solution)/shard_map/pallas_call | solution.py:110
  6.0 11.8 %all-to-all-start = ((bf16[32,8,1536]{2,1,0:T(8,128)(2,1)}), bf16[32,8,1536]{2,1,0:T(8,128)(2,1)S(1)}, u32[]{:S(2)}, u32[]{:S(2)}) async-start(bf16[32,8,1536]{2,1,0:T(8,128)(2,1)} %bitcast.35), calls=%async_computation | async-start | bytes 1572864 | tf_op jit(solution)/shard_map/all_to_all | solution.py:124
  17.8 0.6 dynamic_slice.24
  18.3 0.6 fusion.2
  19.0 0.7 copy.28.omega_ref
  19.7 0.6 compare_reduce_fusion
  20.4 0.6 broadcast_select_fusion
  21.0 0.1 reshape.56
  21.2 0.7 copy.26
  21.9 0.7 copy.29.stiff_ref
  22.6 0.7 scatter.4.state_ref
  23.2 16.9 %all-to-all-done = bf16[32,8,1536]{2,1,0:T(8,128)(2,1)S(1)} async-done(((bf16[32,8,1536]{2,1,0:T(8,128)(2,1)}), bf16[32,8,1536]{2,1,0:T(8,128)(2,1)S(1)}, u32[]{:S(2)}, u32[]{:S(2)}) %all-to-all-start) | async-done | bytes 786464 | tf_op jit(solution)/shard_map/all_to_all | solution.py:124
  40.2 0.9 %copy-done = bf16[32,8,1536]{2,1,0:T(8,128)(2,1)} copy-done((bf16[32,8,1536]{2,1,0:T(8,128)(2,1)}, bf16[32,8,1536]{2,1,0:T(8,128)(2,1)S(1)}, u32[]{:S(2)}) %copy-start) | copy-done | bytes 786456
  41.1 6.4 %shard_map.96 = f32[520,512]{1,0:T(8,128)} custom-call(bf16[256,1536]{1,0:T(8,128)(2,1)} %bitcast.33, s32[64,8]{1,0:T(8,128)} %bitcast.37, bf16[512,128]{1,0:T(8,128)(2,1)} %scatter.4.state_ref, f32[64,1]{1,0:T(8,128)} %copy.28.omega_ref, f32[64,1]{1,0:T(8,128)} %copy.29.stiff_ref), custom_call_target="tpu_custom_call" | custom-call | tf_op jit(solution)/shard_map/pallas_call | solution.py:83
  47.5 1.6 %copy.30 = f32[520,512]{0,1:T(8,128)S(1)} copy(f32[520,512]{1,0:T(8,128)} %shard_map.96) | data formatting | bytes 2129920 | tf_op jit(solution)/shard_map/pallas_call | solution.py:83
  49.4 2.0 %collective-permute-done = f32[520,4,64]{0,2,1:T(8,128)S(1)} collective-permute-done((f32[520,4,64]{0,2,1:T(8,128)S(1)}, f32[520,4,64]{0,2,1:T(8,128)S(1)}, u32[]{:S(2)}, u32[]{:S(2)}) %collective-permute-start) | collective-permute-done | bytes 532512 | tf_op jit(solution)/shard_map/ppermute | solution.py:141
  51.5 1.7 %collective-permute-start.1 = (f32[520,64]{0,1:T(8,128)S(1)}, f32[520,64]{0,1:T(8,128)S(1)}, u32[]{:S(2)}, u32[]{:S(2)}) collective-permute-start(f32[520,64]{0,1:T(8,128)S(1)} %get-tuple-element.14), channel_id=1, source_target_pairs={{0,2},{1,3},{2,4},{3,5},{4,6},{5,7},{6,0},{7,1},{8,10},{9,11},{10,... | collective-permute-start | bytes 399368 | tf_op jit(solution)/shard_map/ppermute | solution.py:146
  53.2 2.9 %collective-permute-start.2 = (f32[520,64]{0,1:T(8,128)S(1)}, f32[520,64]{0,1:T(8,128)S(1)}, u32[]{:S(2)}, u32[]{:S(2)}) collective-permute-start(f32[520,64]{0,1:T(8,128)S(1)} %get-tuple-element.16), channel_id=1, source_target_pairs={{0,4},{1,5},{2,6},{3,7},{4,0},{5,1},{6,2},{7,3},{8,12},{9,13},{10,... | collective-permute-start | bytes 399368 | tf_op jit(solution)/shard_map/ppermute | solution.py:146
  56.1 1.3 %collective-permute-start.3 = (f32[520,64]{0,1:T(8,128)S(1)}, f32[520,64]{0,1:T(8,128)S(1)}, u32[]{:S(2)}, u32[]{:S(2)}) collective-permute-start(f32[520,64]{0,1:T(8,128)S(1)} %get-tuple-element.15), channel_id=1, source_target_pairs={{0,6},{1,7},{2,0},{3,1},{4,2},{5,3},{6,4},{7,5},{8,14},{9,15},{10,... | collective-permute-start | bytes 399368 | tf_op jit(solution)/shard_map/ppermute | solution.py:146
  57.4 1.7 %collective-permute-done.1 = f32[520,64]{0,1:T(8,128)S(1)} collective-permute-done((f32[520,64]{0,1:T(8,128)S(1)}, f32[520,64]{0,1:T(8,128)S(1)}, u32[]{:S(2)}, u32[]{:S(2)}) %collective-permute-start.1) | collective-permute-done | bytes 133152 | tf_op jit(solution)/shard_map/ppermute | solution.py:146
  59.1 4.7 %collective-permute-done.2 = f32[520,64]{0,1:T(8,128)S(1)} collective-permute-done((f32[520,64]{0,1:T(8,128)S(1)}, f32[520,64]{0,1:T(8,128)S(1)}, u32[]{:S(2)}, u32[]{:S(2)}) %collective-permute-start.2) | collective-permute-done | bytes 133152 | tf_op jit(solution)/shard_map/ppermute | solution.py:146
  63.9 0.1 slice_reduce_fusion
  64.0 0.1 copy.31
  64.2 0.8 %reshape.58 = f32[32,1,1088]{2,1,0:T(1,128)} reshape(f32[32,17,64]{2,1,0:T(8,128)S(1)} %pad_maximum_fusion) | data formatting | bytes 278528
  65.0 5.6 %all-to-all-start.1 = ((f32[32,1,1088]{2,1,0:T(1,128)}), f32[32,1,1088]{2,1,0:T(1,128)S(1)}, u32[]{:S(2)}, u32[]{:S(2)}) async-start(f32[32,1,1088]{2,1,0:T(1,128)} %reshape.58), calls=%async_computation.1 | async-start | bytes 294912 | tf_op jit(solution)/shard_map/all_to_all | solution.py:152
  70.6 0.6 reduce_sum.19
  71.9 7.6 %all-to-all-done.1 = f32[32,1,1088]{2,1,0:T(1,128)S(1)} async-done(((f32[32,1,1088]{2,1,0:T(1,128)}), f32[32,1,1088]{2,1,0:T(1,128)S(1)}, u32[]{:S(2)}, u32[]{:S(2)}) %all-to-all-start.1) | async-done | bytes 139296 | tf_op jit(solution)/shard_map/all_to_all | solution.py:152
  79.5 0.5 broadcast.46
  80.0 1.0 %reduce.10 = f32[32,1088]{1,0:T(8,128)S(1)} reduce(f32[32,1,1088]{2,1,0:T(1,128)S(1)} %all-to-all-done.1, f32[]{:T(128)} %broadcast.46), dimensions={1}, to_apply=%all_to_all.13.reduce_sub_computation | reduce | bytes 278532 | tf_op jit(solution)/shard_map/all_to_all | solution.py:152
  81.2 0.6 slice_multiply_fusion
  81.8 0.5 fusion.4
  (24 shorter events, 0.5 us)
Async XLA Ops:
  5.9 11.8 %copy-start.6 = (s32[32]{0:T(128)S(1)}, s32[32]{0:T(128)}, u32[]{:S(2)}) copy-start(s32[32]{0:T(128)} %param.13) | copy-start | bytes 388
  5.9 12.4 %copy-start.4 = (f32[64]{0:T(128)S(1)}, f32[64]{0:T(128)}, u32[]{:S(2)}) copy-start(f32[64]{0:T(128)} %param.14) | copy-start | bytes 772
  5.9 14.4 %copy-start.2 = (bf16[512]{0:T(512)(128)(2,1)S(1)}, bf16[512]{0:T(512)(128)(2,1)}, u32[]{:S(2)}) copy-start(bf16[512]{0:T(512)(128)(2,1)} %param.16) | copy-start | bytes 3076
  5.9 15.2 %copy-start.1 = (s32[8,64]{1,0:T(8,128)S(1)}, s32[8,64]{1,0:T(8,128)}, u32[]{:S(2)}) copy-start(s32[8,64]{1,0:T(8,128)} %param.12) | copy-start | bytes 6148
  5.9 15.9 %copy-start.3 = (f32[64]{0:T(128)S(1)}, f32[64]{0:T(128)}, u32[]{:S(2)}) copy-start(f32[64]{0:T(128)} %param.15) | copy-start | bytes 772
  6.0 34.2 %all-to-all-start = ((bf16[32,8,1536]{2,1,0:T(8,128)(2,1)}), bf16[32,8,1536]{2,1,0:T(8,128)(2,1)S(1)}, u32[]{:S(2)}, u32[]{:S(2)}) async-start(bf16[32,8,1536]{2,1,0:T(8,128)(2,1)} %bitcast.35), calls=%async_computation | async-start | bytes 1572864 | tf_op jit(solution)/shard_map/all_to_all | solution.py:124
  40.2 0.9 %copy-start = (bf16[32,8,1536]{2,1,0:T(8,128)(2,1)}, bf16[32,8,1536]{2,1,0:T(8,128)(2,1)S(1)}, u32[]{:S(2)}) copy-start(bf16[32,8,1536]{2,1,0:T(8,128)(2,1)S(1)} %all-to-all-done) | copy-start | bytes 2359300
  49.2 2.2 %collective-permute-start = (f32[520,4,64]{0,2,1:T(8,128)S(1)}, f32[520,4,64]{0,2,1:T(8,128)S(1)}, u32[]{:S(2)}, u32[]{:S(2)}) collective-permute-start(f32[520,4,64]{0,2,1:T(8,128)S(1)} %dynamic-slice_bitcast_fusion), channel_id=1, source_target_pairs={{0,1},{1,0},{2,3},{3,2},{4,5},{5,4},{6,7},{7,6},{8,9},{9,8},{10,11... | collective-permute-start | bytes 1597448 | tf_op jit(solution)/shard_map/ppermute | solution.py:141
  51.5 7.6 %collective-permute-start.1 = (f32[520,64]{0,1:T(8,128)S(1)}, f32[520,64]{0,1:T(8,128)S(1)}, u32[]{:S(2)}, u32[]{:S(2)}) collective-permute-start(f32[520,64]{0,1:T(8,128)S(1)} %get-tuple-element.14), channel_id=1, source_target_pairs={{0,2},{1,3},{2,4},{3,5},{4,6},{5,7},{6,0},{7,1},{8,10},{9,11},{10,... | collective-permute-start | bytes 399368 | tf_op jit(solution)/shard_map/ppermute | solution.py:146
  53.2 10.6 %collective-permute-start.2 = (f32[520,64]{0,1:T(8,128)S(1)}, f32[520,64]{0,1:T(8,128)S(1)}, u32[]{:S(2)}, u32[]{:S(2)}) collective-permute-start(f32[520,64]{0,1:T(8,128)S(1)} %get-tuple-element.16), channel_id=1, source_target_pairs={{0,4},{1,5},{2,6},{3,7},{4,0},{5,1},{6,2},{7,3},{8,12},{9,13},{10,... | collective-permute-start | bytes 399368 | tf_op jit(solution)/shard_map/ppermute | solution.py:146
  56.1 7.7 %collective-permute-start.3 = (f32[520,64]{0,1:T(8,128)S(1)}, f32[520,64]{0,1:T(8,128)S(1)}, u32[]{:S(2)}, u32[]{:S(2)}) collective-permute-start(f32[520,64]{0,1:T(8,128)S(1)} %get-tuple-element.15), channel_id=1, source_target_pairs={{0,6},{1,7},{2,0},{3,1},{4,2},{5,3},{6,4},{7,5},{8,14},{9,15},{10,... | collective-permute-start | bytes 399368 | tf_op jit(solution)/shard_map/ppermute | solution.py:146
  64.1 17.6 %copy-start.5 = (f32[64]{0:T(128)S(1)}, f32[64]{0:T(128)}, u32[]{:S(2)}) copy-start(f32[64]{0:T(128)} %param.17) | copy-start | bytes 772
  65.0 14.5 %all-to-all-start.1 = ((f32[32,1,1088]{2,1,0:T(1,128)}), f32[32,1,1088]{2,1,0:T(1,128)S(1)}, u32[]{:S(2)}, u32[]{:S(2)}) async-start(f32[32,1,1088]{2,1,0:T(1,128)} %reshape.58), calls=%async_computation.1 | async-start | bytes 294912 | tf_op jit(solution)/shard_map/all_to_all | solution.py:152

commit v6 on v5

--- a/solution.py
+++ b/solution.py
@@ -93,27 +93,29 @@
 
 
 def gather_body(basis_ref, rows_ref, out_ref):
-    n_rows = rows_ref.shape[0]
     nodes = basis_ref.shape[1]
-    modes = basis_ref.shape[2]
-    lane = lax.broadcasted_iota(jnp.int32, (n_rows, nodes), 1)
-    onehot = (rows_ref[...] == lane).astype(jnp.bfloat16)
-    for c in range(basis_ref.shape[0]):
-        picked = jnp.dot(onehot, basis_ref[c], preferred_element_type=jnp.float32)
-        out_ref[:, pl.ds(c * modes, modes)] = picked.astype(jnp.bfloat16)
+    n_rows = rows_ref.shape[1]
+    node = lax.broadcasted_iota(jnp.int32, (nodes, n_rows), 0)
+    onehot_t = (node == rows_ref[...]).astype(jnp.bfloat16)
+    picked = lax.dot_general(
+        onehot_t, basis_ref[0], (((0,), (0,)), ((), ())), preferred_element_type=jnp.float32
+    )
+    out_ref[...] = picked.astype(jnp.bfloat16)
 
 
 def gather_rows(by_component, rows):
     comps, nodes, modes = by_component.shape
     n_rows = rows.shape[0]
-    vmem = pltpu.MemorySpace.VMEM if hasattr(pltpu, "MemorySpace") else pltpu.TPUMemorySpace.VMEM
     return pl.pallas_call(
         gather_body,
         out_shape=jax.ShapeDtypeStruct((n_rows, comps * modes), jnp.bfloat16),
-        in_specs=[pl.BlockSpec(memory_space=vmem)] * 2,
-        out_specs=pl.BlockSpec(memory_space=vmem),
-    )(by_component, rows.reshape(n_rows, 1))
-
+        grid=(comps,),
+        in_specs=[
+            pl.BlockSpec((1, nodes, modes), lambda c: (c, 0, 0)),
+            pl.BlockSpec((1, n_rows), lambda c: (0, 0)),
+        ],
+        out_specs=pl.BlockSpec((n_rows, modes), lambda c: (0, c)),
+    )(by_component, rows.reshape(1, n_rows))
 
 def local(basis, send_rows, elem_slot, set_size, elem_weight, element_stiffening, state, load):
     basis_modes = basis.shape[2]

time: 83.8 us -> 82.8 us (0.988)
  local copies, waits for them, and re-layouts: 9.35 us -> 7.89 us
    another operation x2 -> x1, local copies, waits for them, and re-layouts: 1.6 us -> 0.13 us  [the longest x1 1.47 us: gather_rows(): rows.reshape(n_rows, 1)]
where the time goes in v6:
time: 82.8 us; the launch traced here: 81.2 us
  waiting for transfers between devices  32.9 us (40%)
  starting transfers between devices  23.3 us (28%)
  Pallas kernels  10.7 us (13%)
  local copies, waits for them, and re-layouts  7.89 us (10%)
  other arithmetic  4.86 us (6%)
  between operations  1.61 us (2%)
    all_to_all x1, waiting for transfers between devices, local(): lax.all_to_all(outgoing, 'elem', split_axis=0, concat_axis=0, tiled=True)  16.9 us
    all_to_all x1, starting transfers between devices, local(): lax.all_to_all(outgoing, 'elem', split_axis=0, concat_axis=0, tiled=True)  11.8 us
    all_to_all x1, waiting for transfers between devices, local(): lax.all_to_all(chunks, 'elem', split_axis=0, concat_axis=0, tiled=True)  7.58 us
    pallas_call x1, Pallas kernels, element_stage(): pl.pallas_call(element_body, out_shape=jax.ShapeDtypeStruct((modes + 8, m...  6.42 us
    ppermute x3, waiting for transfers between devices, local(): halfway = halfway + lax.ppermute(piece, 'blk', ring)  6.38 us
    ppermute x3, starting transfers between devices, local(): halfway = halfway + lax.ppermute(piece, 'blk', ring)  5.92 us
    all_to_all x1, starting transfers between devices, local(): lax.all_to_all(chunks, 'elem', split_axis=0, concat_axis=0, tiled=True)  5.56 us
    pallas_call x1, Pallas kernels, gather_rows(): pl.pallas_call(gather_body, out_shape=jax.ShapeDtypeStruct((n_rows, comps...  4.25 us
  transfers between devices with their start and end apart: 6, of which 5 were waited for; matrix products, arithmetic and copies ran while one was open for 7% of the time, Pallas kernels for 0%

profile of v6, /device:TPU:2, one launch (start us, length us, event | category | flops | bytes accessed | tf_op | source)
XLA Modules:
  0.0 81.2 jit_solution(10071488207150379978)
XLA Ops:
  0.6 4.2 %shard_map.95 = bf16[256,1536]{1,0:T(8,128)(2,1)} custom-call(bf16[3,1024,512]{2,1,0:T(8,128)(2,1)} %bitcast.33, s32[1,256]{1,0:T(1,128)} %bitcast.38), custom_call_target="tpu_custom_call" | custom-call | tf_op jit(solution)/shard_map/pallas_call | solution.py:109
  4.9 11.8 %all-to-all-start = ((bf16[32,8,1536]{2,1,0:T(8,128)(2,1)}), bf16[32,8,1536]{2,1,0:T(8,128)(2,1)S(1)}, u32[]{:S(2)}, u32[]{:S(2)}) async-start(bf16[32,8,1536]{2,1,0:T(8,128)(2,1)} %bitcast.35), calls=%async_computation | async-start | bytes 1572864 | tf_op jit(solution)/shard_map/all_to_all | solution.py:126
  16.7 0.6 dynamic_slice.24
  17.3 0.6 fusion.2
  17.9 0.7 copy.25.omega_ref
  18.7 0.6 compare_reduce_fusion
  19.3 0.6 broadcast_select_fusion
  20.0 0.1 reshape.56
  20.1 0.7 copy.23
  20.8 0.7 copy.26.stiff_ref
  21.5 0.7 scatter.4.state_ref
  22.2 16.9 %all-to-all-done = bf16[32,8,1536]{2,1,0:T(8,128)(2,1)S(1)} async-done(((bf16[32,8,1536]{2,1,0:T(8,128)(2,1)}), bf16[32,8,1536]{2,1,0:T(8,128)(2,1)S(1)}, u32[]{:S(2)}, u32[]{:S(2)}) %all-to-all-start) | async-done | bytes 786464 | tf_op jit(solution)/shard_map/all_to_all | solution.py:126
  39.1 0.9 %copy-done = bf16[32,8,1536]{2,1,0:T(8,128)(2,1)} copy-done((bf16[32,8,1536]{2,1,0:T(8,128)(2,1)}, bf16[32,8,1536]{2,1,0:T(8,128)(2,1)S(1)}, u32[]{:S(2)}) %copy-start) | copy-done | bytes 786456
  40.0 6.4 %shard_map.96 = f32[520,512]{1,0:T(8,128)} custom-call(bf16[256,1536]{1,0:T(8,128)(2,1)} %bitcast.34, s32[64,8]{1,0:T(8,128)} %bitcast.37, bf16[512,128]{1,0:T(8,128)(2,1)} %scatter.4.state_ref, f32[64,1]{1,0:T(8,128)} %copy.25.omega_ref, f32[64,1]{1,0:T(8,128)} %copy.26.stiff_ref), custom_call_target="tpu_custom_call" | custom-call | tf_op jit(solution)/shard_map/pallas_call | solution.py:83
  46.5 1.6 %copy.27 = f32[520,512]{0,1:T(8,128)S(1)} copy(f32[520,512]{1,0:T(8,128)} %shard_map.96) | data formatting | bytes 2129920 | tf_op jit(solution)/shard_map/pallas_call | solution.py:83
  48.3 2.0 %collective-permute-done = f32[520,4,64]{0,2,1:T(8,128)S(1)} collective-permute-done((f32[520,4,64]{0,2,1:T(8,128)S(1)}, f32[520,4,64]{0,2,1:T(8,128)S(1)}, u32[]{:S(2)}, u32[]{:S(2)}) %collective-permute-start) | collective-permute-done | bytes 532512 | tf_op jit(solution)/shard_map/ppermute | solution.py:143
  50.5 1.7 %collective-permute-start.1 = (f32[520,64]{0,1:T(8,128)S(1)}, f32[520,64]{0,1:T(8,128)S(1)}, u32[]{:S(2)}, u32[]{:S(2)}) collective-permute-start(f32[520,64]{0,1:T(8,128)S(1)} %get-tuple-element.14), channel_id=1, source_target_pairs={{0,2},{1,3},{2,4},{3,5},{4,6},{5,7},{6,0},{7,1},{8,10},{9,11},{10,... | collective-permute-start | bytes 399368 | tf_op jit(solution)/shard_map/ppermute | solution.py:148
  52.1 2.9 %collective-permute-start.2 = (f32[520,64]{0,1:T(8,128)S(1)}, f32[520,64]{0,1:T(8,128)S(1)}, u32[]{:S(2)}, u32[]{:S(2)}) collective-permute-start(f32[520,64]{0,1:T(8,128)S(1)} %get-tuple-element.16), channel_id=1, source_target_pairs={{0,4},{1,5},{2,6},{3,7},{4,0},{5,1},{6,2},{7,3},{8,12},{9,13},{10,... | collective-permute-start | bytes 399368 | tf_op jit(solution)/shard_map/ppermute | solution.py:148
  55.0 1.3 %collective-permute-start.3 = (f32[520,64]{0,1:T(8,128)S(1)}, f32[520,64]{0,1:T(8,128)S(1)}, u32[]{:S(2)}, u32[]{:S(2)}) collective-permute-start(f32[520,64]{0,1:T(8,128)S(1)} %get-tuple-element.15), channel_id=1, source_target_pairs={{0,6},{1,7},{2,0},{3,1},{4,2},{5,3},{6,4},{7,5},{8,14},{9,15},{10,... | collective-permute-start | bytes 399368 | tf_op jit(solution)/shard_map/ppermute | solution.py:148
  56.4 1.7 %collective-permute-done.1 = f32[520,64]{0,1:T(8,128)S(1)} collective-permute-done((f32[520,64]{0,1:T(8,128)S(1)}, f32[520,64]{0,1:T(8,128)S(1)}, u32[]{:S(2)}, u32[]{:S(2)}) %collective-permute-start.1) | collective-permute-done | bytes 133152 | tf_op jit(solution)/shard_map/ppermute | solution.py:148
  58.1 4.7 %collective-permute-done.2 = f32[520,64]{0,1:T(8,128)S(1)} collective-permute-done((f32[520,64]{0,1:T(8,128)S(1)}, f32[520,64]{0,1:T(8,128)S(1)}, u32[]{:S(2)}, u32[]{:S(2)}) %collective-permute-start.2) | collective-permute-done | bytes 133152 | tf_op jit(solution)/shard_map/ppermute | solution.py:148
  62.8 0.1 slice_reduce_fusion
  62.9 0.1 copy.28
  63.1 0.8 %reshape.58 = f32[32,1,1088]{2,1,0:T(1,128)} reshape(f32[32,17,64]{2,1,0:T(8,128)S(1)} %pad_maximum_fusion) | data formatting | bytes 278528
  64.0 5.6 %all-to-all-start.1 = ((f32[32,1,1088]{2,1,0:T(1,128)}), f32[32,1,1088]{2,1,0:T(1,128)S(1)}, u32[]{:S(2)}, u32[]{:S(2)}) async-start(f32[32,1,1088]{2,1,0:T(1,128)} %reshape.58), calls=%async_computation.1 | async-start | bytes 294912 | tf_op jit(solution)/shard_map/all_to_all | solution.py:154
  69.6 0.6 reduce_sum.19
  70.9 7.6 %all-to-all-done.1 = f32[32,1,1088]{2,1,0:T(1,128)S(1)} async-done(((f32[32,1,1088]{2,1,0:T(1,128)}), f32[32,1,1088]{2,1,0:T(1,128)S(1)}, u32[]{:S(2)}, u32[]{:S(2)}) %all-to-all-start.1) | async-done | bytes 139296 | tf_op jit(solution)/shard_map/all_to_all | solution.py:154
  78.5 0.5 broadcast.46
  79.0 1.0 %reduce.10 = f32[32,1088]{1,0:T(8,128)S(1)} reduce(f32[32,1,1088]{2,1,0:T(1,128)S(1)} %all-to-all-done.1, f32[]{:T(128)} %broadcast.46), dimensions={1}, to_apply=%all_to_all.13.reduce_sub_computation | reduce | bytes 278532 | tf_op jit(solution)/shard_map/all_to_all | solution.py:154
  80.0 0.1 reshape.59
  80.1 0.6 slice_multiply_fusion
  80.7 0.5 fusion.4
  (23 shorter events, 0.4 us)
Async XLA Ops:
  4.9 11.8 %copy-start.6 = (s32[32]{0:T(128)S(1)}, s32[32]{0:T(128)}, u32[]{:S(2)}) copy-start(s32[32]{0:T(128)} %param.13) | copy-start | bytes 388
  4.9 12.4 %copy-start.4 = (f32[64]{0:T(128)S(1)}, f32[64]{0:T(128)}, u32[]{:S(2)}) copy-start(f32[64]{0:T(128)} %param.14) | copy-start | bytes 772
  4.9 14.4 %copy-start.2 = (bf16[512]{0:T(512)(128)(2,1)S(1)}, bf16[512]{0:T(512)(128)(2,1)}, u32[]{:S(2)}) copy-start(bf16[512]{0:T(512)(128)(2,1)} %param.16) | copy-start | bytes 3076
  4.9 15.2 %copy-start.1 = (s32[8,64]{1,0:T(8,128)S(1)}, s32[8,64]{1,0:T(8,128)}, u32[]{:S(2)}) copy-start(s32[8,64]{1,0:T(8,128)} %param.12) | copy-start | bytes 6148
  4.9 15.9 %copy-start.3 = (f32[64]{0:T(128)S(1)}, f32[64]{0:T(128)}, u32[]{:S(2)}) copy-start(f32[64]{0:T(128)} %param.15) | copy-start | bytes 772
  4.9 34.2 %all-to-all-start = ((bf16[32,8,1536]{2,1,0:T(8,128)(2,1)}), bf16[32,8,1536]{2,1,0:T(8,128)(2,1)S(1)}, u32[]{:S(2)}, u32[]{:S(2)}) async-start(bf16[32,8,1536]{2,1,0:T(8,128)(2,1)} %bitcast.35), calls=%async_computation | async-start | bytes 1572864 | tf_op jit(solution)/shard_map/all_to_all | solution.py:126
  39.1 0.9 %copy-start = (bf16[32,8,1536]{2,1,0:T(8,128)(2,1)}, bf16[32,8,1536]{2,1,0:T(8,128)(2,1)S(1)}, u32[]{:S(2)}) copy-start(bf16[32,8,1536]{2,1,0:T(8,128)(2,1)S(1)} %all-to-all-done) | copy-start | bytes 2359300
  48.2 2.2 %collective-permute-start = (f32[520,4,64]{0,2,1:T(8,128)S(1)}, f32[520,4,64]{0,2,1:T(8,128)S(1)}, u32[]{:S(2)}, u32[]{:S(2)}) collective-permute-start(f32[520,4,64]{0,2,1:T(8,128)S(1)} %dynamic-slice_bitcast_fusion), channel_id=1, source_target_pairs={{0,1},{1,0},{2,3},{3,2},{4,5},{5,4},{6,7},{7,6},{8,9},{9,8},{10,11... | collective-permute-start | bytes 1597448 | tf_op jit(solution)/shard_map/ppermute | solution.py:143
  50.5 7.6 %collective-permute-start.1 = (f32[520,64]{0,1:T(8,128)S(1)}, f32[520,64]{0,1:T(8,128)S(1)}, u32[]{:S(2)}, u32[]{:S(2)}) collective-permute-start(f32[520,64]{0,1:T(8,128)S(1)} %get-tuple-element.14), channel_id=1, source_target_pairs={{0,2},{1,3},{2,4},{3,5},{4,6},{5,7},{6,0},{7,1},{8,10},{9,11},{10,... | collective-permute-start | bytes 399368 | tf_op jit(solution)/shard_map/ppermute | solution.py:148
  52.1 10.6 %collective-permute-start.2 = (f32[520,64]{0,1:T(8,128)S(1)}, f32[520,64]{0,1:T(8,128)S(1)}, u32[]{:S(2)}, u32[]{:S(2)}) collective-permute-start(f32[520,64]{0,1:T(8,128)S(1)} %get-tuple-element.16), channel_id=1, source_target_pairs={{0,4},{1,5},{2,6},{3,7},{4,0},{5,1},{6,2},{7,3},{8,12},{9,13},{10,... | collective-permute-start | bytes 399368 | tf_op jit(solution)/shard_map/ppermute | solution.py:148
  55.0 7.7 %collective-permute-start.3 = (f32[520,64]{0,1:T(8,128)S(1)}, f32[520,64]{0,1:T(8,128)S(1)}, u32[]{:S(2)}, u32[]{:S(2)}) collective-permute-start(f32[520,64]{0,1:T(8,128)S(1)} %get-tuple-element.15), channel_id=1, source_target_pairs={{0,6},{1,7},{2,0},{3,1},{4,2},{5,3},{6,4},{7,5},{8,14},{9,15},{10,... | collective-permute-start | bytes 399368 | tf_op jit(solution)/shard_map/ppermute | solution.py:148
  63.1 17.6 %copy-start.5 = (f32[64]{0:T(128)S(1)}, f32[64]{0:T(128)}, u32[]{:S(2)}) copy-start(f32[64]{0:T(128)} %param.17) | copy-start | bytes 772
  64.0 14.5 %all-to-all-start.1 = ((f32[32,1,1088]{2,1,0:T(1,128)}), f32[32,1,1088]{2,1,0:T(1,128)S(1)}, u32[]{:S(2)}, u32[]{:S(2)}) async-start(f32[32,1,1088]{2,1,0:T(1,128)} %reshape.58), calls=%async_computation.1 | async-start | bytes 294912 | tf_op jit(solution)/shard_map/all_to_all | solution.py:154

commit v7 on v6

--- a/solution.py
+++ b/solution.py
@@ -151,8 +151,17 @@
     chunks = jnp.concatenate(
         [tangent_rows, jnp.broadcast_to(force_cols[None, None, :], (n_elem, 1, cols))], axis=1
     )
-    arrived_chunks = lax.all_to_all(chunks, "elem", split_axis=0, concat_axis=0, tiled=True)
-    mine = jnp.sum(arrived_chunks, axis=0)
+    elem_index = lax.axis_index("elem")
+    rest = chunks
+    bit = 1
+    while bit < n_elem:
+        mine_bit = (elem_index // bit) % 2
+        split = rest.reshape(rest.shape[0] // 2, 2, rest.shape[1], cols)
+        kept = lax.dynamic_index_in_dim(split, mine_bit, axis=1, keepdims=False)
+        sent = lax.dynamic_index_in_dim(split, 1 - mine_bit, axis=1, keepdims=False)
+        rest = kept + lax.ppermute(sent, "elem", [(e, e ^ bit) for e in range(n_elem)])
+        bit *= 2
+    mine = rest[0]
     scale = lax.rsqrt(24.0 * jnp.sum(set_size).astype(jnp.float32))
     return (mine[:rows] * scale, mine[rows] * scale - load)
 

time: 82.8 us -> 92.9 us (1.12); the launches traced: 81.2 us -> 92.6 us
  waiting for transfers between devices: 32.9 us -> 45.8 us
  local copies, waits for them, and re-layouts: 7.89 us -> 6.69 us
  other arithmetic: 4.86 us -> 3.91 us
    ppermute x0 -> x5, waiting for transfers between devices: none -> 20.5 us  [local(): lax.ppermute(sent, 'elem', [(e, e ^ bit) for e in range(n_elem)])]
    all_to_all x1 -> x0, waiting for transfers between devices: 7.58 us -> none  [local(): lax.all_to_all(chunks, 'elem', split_axis=0, concat_axis=0, tiled=True)]
    ppermute x0 -> x5, starting transfers between devices: none -> 6.01 us  [local(): lax.ppermute(sent, 'elem', [(e, e ^ bit) for e in range(n_elem)])]
    all_to_all x1 -> x0, starting transfers between devices: 5.56 us -> none  [local(): lax.all_to_all(chunks, 'elem', split_axis=0, concat_axis=0, tiled=True)]
    all_to_all x1 -> x0, other arithmetic: 0.99 us -> none  [local(): lax.all_to_all(chunks, 'elem', split_axis=0, concat_axis=0, tiled=True)]
    unnamed x17 -> x15, local copies, waits for them, and re-layouts: 2.59 us -> 1.65 us
  transfers between devices with their start and end apart: 6 -> 10, of which waited for: 5 -> 9; matrix products, arithmetic and copies ran while one was open for 7% -> 7% of each run, Pallas kernels for 0% -> 0%
where the time goes in v7:
time: 92.9 us; the launch traced here: 92.6 us
  waiting for transfers between devices  45.8 us (49%)
  starting transfers between devices  23.8 us (26%)
  Pallas kernels  10.7 us (12%)
  local copies, waits for them, and re-layouts  6.69 us (7%)
  other arithmetic  3.91 us (4%)
  between operations  1.65 us (2%)
    ppermute x5, waiting for transfers between devices, local(): lax.ppermute(sent, 'elem', [(e, e ^ bit) for e in range(n_elem)])  20.5 us
    all_to_all x1, waiting for transfers between devices, local(): lax.all_to_all(outgoing, 'elem', split_axis=0, concat_axis=0, tiled=True)  17 us
    all_to_all x1, starting transfers between devices, local(): lax.all_to_all(outgoing, 'elem', split_axis=0, concat_axis=0, tiled=True)  11.8 us
    pallas_call x1, Pallas kernels, element_stage(): pl.pallas_call(element_body, out_shape=jax.ShapeDtypeStruct((modes + 8, m...  6.43 us
    ppermute x3, waiting for transfers between devices, local(): halfway = halfway + lax.ppermute(piece, 'blk', ring)  6.38 us
    ppermute x5, starting transfers between devices, local(): lax.ppermute(sent, 'elem', [(e, e ^ bit) for e in range(n_elem)])  6.01 us
    ppermute x3, starting transfers between devices, local(): halfway = halfway + lax.ppermute(piece, 'blk', ring)  5.91 us
    pallas_call x1, Pallas kernels, gather_rows(): pl.pallas_call(gather_body, out_shape=jax.ShapeDtypeStruct((n_rows, comps...  4.27 us
  transfers between devices with their start and end apart: 10, of which 9 were waited for; matrix products, arithmetic and copies ran while one was open for 7% of the time, Pallas kernels for 0%

profile of v7, /device:TPU:2, one launch (start us, length us, event | category | flops | bytes accessed | tf_op | source)
XLA Modules:
  0.0 92.6 jit_solution(10745624134433829237)
XLA Ops:
  0.6 4.3 %shard_map.95 = bf16[256,1536]{1,0:T(8,128)(2,1)} custom-call(bf16[3,1024,512]{2,1,0:T(8,128)(2,1)} %bitcast.48, s32[1,256]{1,0:T(1,128)} %bitcast.64), custom_call_target="tpu_custom_call" | custom-call | tf_op jit(solution)/shard_map/pallas_call | solution.py:109
  4.9 11.8 %all-to-all-start = ((bf16[32,8,1536]{2,1,0:T(8,128)(2,1)}), bf16[32,8,1536]{2,1,0:T(8,128)(2,1)S(1)}, u32[]{:S(2)}, u32[]{:S(2)}) async-start(bf16[32,8,1536]{2,1,0:T(8,128)(2,1)} %bitcast.50), calls=%async_computation | async-start | bytes 1572864 | tf_op jit(solution)/shard_map/all_to_all | solution.py:126
  16.7 0.6 dynamic_slice.55
  17.3 0.6 fusion.4
  18.0 0.7 copy.31.omega_ref
  18.7 0.6 compare_reduce_fusion
  19.3 0.6 broadcast_select_fusion
  20.1 0.7 copy.29
  20.8 0.7 copy.32.stiff_ref
  21.5 0.7 scatter.4.state_ref
  22.2 17.0 %all-to-all-done = bf16[32,8,1536]{2,1,0:T(8,128)(2,1)S(1)} async-done(((bf16[32,8,1536]{2,1,0:T(8,128)(2,1)}), bf16[32,8,1536]{2,1,0:T(8,128)(2,1)S(1)}, u32[]{:S(2)}, u32[]{:S(2)}) %all-to-all-start) | async-done | bytes 786464 | tf_op jit(solution)/shard_map/all_to_all | solution.py:126
  39.1 0.9 %copy-done = bf16[32,8,1536]{2,1,0:T(8,128)(2,1)} copy-done((bf16[32,8,1536]{2,1,0:T(8,128)(2,1)}, bf16[32,8,1536]{2,1,0:T(8,128)(2,1)S(1)}, u32[]{:S(2)}) %copy-start) | copy-done | bytes 786456
  40.1 6.4 %shard_map.96 = f32[520,512]{1,0:T(8,128)} custom-call(bf16[256,1536]{1,0:T(8,128)(2,1)} %bitcast.49, s32[64,8]{1,0:T(8,128)} %bitcast.58, bf16[512,128]{1,0:T(8,128)(2,1)} %scatter.4.state_ref, f32[64,1]{1,0:T(8,128)} %copy.31.omega_ref, f32[64,1]{1,0:T(8,128)} %copy.32.stiff_ref), custom_call_target="tpu_custom_call" | custom-call | tf_op jit(solution)/shard_map/pallas_call | solution.py:83
  46.5 1.6 %copy.33 = f32[520,512]{0,1:T(8,128)S(1)} copy(f32[520,512]{1,0:T(8,128)} %shard_map.96) | data formatting | bytes 2129920 | tf_op jit(solution)/shard_map/pallas_call | solution.py:83
  48.4 2.0 %collective-permute-done = f32[520,4,64]{0,2,1:T(8,128)S(1)} collective-permute-done((f32[520,4,64]{0,2,1:T(8,128)S(1)}, f32[520,4,64]{0,2,1:T(8,128)S(1)}, u32[]{:S(2)}, u32[]{:S(2)}) %collective-permute-start) | collective-permute-done | bytes 532512 | tf_op jit(solution)/shard_map/ppermute | solution.py:143
  50.5 1.7 %collective-permute-start.1 = (f32[520,64]{0,1:T(8,128)S(1)}, f32[520,64]{0,1:T(8,128)S(1)}, u32[]{:S(2)}, u32[]{:S(2)}) collective-permute-start(f32[520,64]{0,1:T(8,128)S(1)} %get-tuple-element.14), channel_id=1, source_target_pairs={{0,2},{1,3},{2,4},{3,5},{4,6},{5,7},{6,0},{7,1},{8,10},{9,11},{10,... | collective-permute-start | bytes 399368 | tf_op jit(solution)/shard_map/ppermute | solution.py:148
  52.2 2.9 %collective-permute-start.2 = (f32[520,64]{0,1:T(8,128)S(1)}, f32[520,64]{0,1:T(8,128)S(1)}, u32[]{:S(2)}, u32[]{:S(2)}) collective-permute-start(f32[520,64]{0,1:T(8,128)S(1)} %get-tuple-element.16), channel_id=1, source_target_pairs={{0,4},{1,5},{2,6},{3,7},{4,0},{5,1},{6,2},{7,3},{8,12},{9,13},{10,... | collective-permute-start | bytes 399368 | tf_op jit(solution)/shard_map/ppermute | solution.py:148
  55.1 1.3 %collective-permute-start.3 = (f32[520,64]{0,1:T(8,128)S(1)}, f32[520,64]{0,1:T(8,128)S(1)}, u32[]{:S(2)}, u32[]{:S(2)}) collective-permute-start(f32[520,64]{0,1:T(8,128)S(1)} %get-tuple-element.15), channel_id=1, source_target_pairs={{0,6},{1,7},{2,0},{3,1},{4,2},{5,3},{6,4},{7,5},{8,14},{9,15},{10,... | collective-permute-start | bytes 399368 | tf_op jit(solution)/shard_map/ppermute | solution.py:148
  56.4 1.7 %collective-permute-done.1 = f32[520,64]{0,1:T(8,128)S(1)} collective-permute-done((f32[520,64]{0,1:T(8,128)S(1)}, f32[520,64]{0,1:T(8,128)S(1)}, u32[]{:S(2)}, u32[]{:S(2)}) %collective-permute-start.1) | collective-permute-done | bytes 133152 | tf_op jit(solution)/shard_map/ppermute | solution.py:148
  58.1 4.7 %collective-permute-done.2 = f32[520,64]{0,1:T(8,128)S(1)} collective-permute-done((f32[520,64]{0,1:T(8,128)S(1)}, f32[520,64]{0,1:T(8,128)S(1)}, u32[]{:S(2)}, u32[]{:S(2)}) %collective-permute-start.2) | collective-permute-done | bytes 133152 | tf_op jit(solution)/shard_map/ppermute | solution.py:148
  63.2 0.8 collective-permute-start.4
  64.0 4.3 %collective-permute-done.4 = f32[16,17,64]{2,0,1:T(8,128)S(1)} collective-permute-done((f32[16,17,64]{2,0,1:T(8,128)S(1)}, f32[16,17,64]{2,0,1:T(8,128)S(1)}, u32[]{:S(2)}, u32[]{:S(2)}) %collective-permute-start.4) | collective-permute-done | bytes 69664 | tf_op jit(solution)/shard_map/ppermute | solution.py:162
  68.5 2.2 %collective-permute-start.5 = (f32[8,17,64]{2,0,1:T(8,128)S(1)}, f32[8,17,64]{2,0,1:T(8,128)S(1)}, u32[]{:S(2)}, u32[]{:S(2)}) collective-permute-start(f32[8,17,64]{2,0,1:T(8,128)S(1)} %bitcast.59), channel_id=1, source_target_pairs={{0,16},{8,24},{16,0},{24,8},{32,48},{40,56},{48,32},{56,40},{64,80... | collective-permute-start | bytes 104456 | tf_op jit(solution)/shard_map/ppermute | solution.py:162
  70.7 3.7 %collective-permute-done.5 = f32[8,17,64]{2,0,1:T(8,128)S(1)} collective-permute-done((f32[8,17,64]{2,0,1:T(8,128)S(1)}, f32[8,17,64]{2,0,1:T(8,128)S(1)}, u32[]{:S(2)}, u32[]{:S(2)}) %collective-permute-start.5) | collective-permute-done | bytes 34848 | tf_op jit(solution)/shard_map/ppermute | solution.py:162
  74.5 0.7 collective-permute-start.6
  75.2 3.5 %collective-permute-done.6 = f32[4,17,64]{2,0,1:T(4,128)S(1)} collective-permute-done((f32[4,17,64]{2,0,1:T(4,128)S(1)}, f32[4,17,64]{2,0,1:T(4,128)S(1)}, u32[]{:S(2)}, u32[]{:S(2)}) %collective-permute-start.6) | collective-permute-done | bytes 17440 | tf_op jit(solution)/shard_map/ppermute | solution.py:162
  78.8 1.0 %collective-permute-start.7 = (f32[2,17,64]{2,0,1:T(2,128)S(1)}, f32[2,17,64]{2,0,1:T(2,128)S(1)}, u32[]{:S(2)}, u32[]{:S(2)}) collective-permute-start(f32[2,17,64]{2,0,1:T(2,128)S(1)} %bitcast.62), channel_id=1, source_target_pairs={{0,64},{8,72},{16,80},{24,88},{32,96},{40,104},{48,112},{56,120},{... | collective-permute-start | bytes 26120 | tf_op jit(solution)/shard_map/ppermute | solution.py:162
  79.8 3.9 %collective-permute-done.7 = f32[2,17,64]{2,0,1:T(2,128)S(1)} collective-permute-done((f32[2,17,64]{2,0,1:T(2,128)S(1)}, f32[2,17,64]{2,0,1:T(2,128)S(1)}, u32[]{:S(2)}, u32[]{:S(2)}) %collective-permute-start.7) | collective-permute-done | bytes 8736 | tf_op jit(solution)/shard_map/ppermute | solution.py:162
  83.8 1.4 %collective-permute-start.8 = (f32[1,17,64]{2,0,1:T(1,128)S(1)}, f32[1,17,64]{2,0,1:T(1,128)S(1)}, u32[]{:S(2)}, u32[]{:S(2)}) collective-permute-start(f32[1,17,64]{2,0,1:T(1,128)S(1)} %constant_dynamic-slice_fusion), channel_id=1, source_target_pairs={{0,128},{8,136},{16,144},{24,152},{32,160},{40,168},{48,176},{56,1... | collective-permute-start | bytes 13064 | tf_op jit(solution)/shard_map/ppermute | solution.py:162
  85.1 0.6 reduce_sum.9
  86.5 4.9 %collective-permute-done.8 = f32[1,17,64]{2,0,1:T(1,128)S(1)} collective-permute-done((f32[1,17,64]{2,0,1:T(1,128)S(1)}, f32[1,17,64]{2,0,1:T(1,128)S(1)}, u32[]{:S(2)}, u32[]{:S(2)}) %collective-permute-start.8) | collective-permute-done | bytes 4384 | tf_op jit(solution)/shard_map/ppermute | solution.py:162
  91.4 0.6 slice_multiply_fusion
  (36 shorter events, 1.6 us)
Async XLA Ops:
  4.9 11.8 %copy-start.6 = (s32[32]{0:T(128)S(1)}, s32[32]{0:T(128)}, u32[]{:S(2)}) copy-start(s32[32]{0:T(128)} %param.13) | copy-start | bytes 388
  4.9 12.4 %copy-start.4 = (f32[64]{0:T(128)S(1)}, f32[64]{0:T(128)}, u32[]{:S(2)}) copy-start(f32[64]{0:T(128)} %param.14) | copy-start | bytes 772
  4.9 14.4 %copy-start.2 = (bf16[512]{0:T(512)(128)(2,1)S(1)}, bf16[512]{0:T(512)(128)(2,1)}, u32[]{:S(2)}) copy-start(bf16[512]{0:T(512)(128)(2,1)} %param.16) | copy-start | bytes 3076
  4.9 15.2 %copy-start.1 = (s32[8,64]{1,0:T(8,128)S(1)}, s32[8,64]{1,0:T(8,128)}, u32[]{:S(2)}) copy-start(s32[8,64]{1,0:T(8,128)} %param.12) | copy-start | bytes 6148
  4.9 15.9 %copy-start.3 = (f32[64]{0:T(128)S(1)}, f32[64]{0:T(128)}, u32[]{:S(2)}) copy-start(f32[64]{0:T(128)} %param.15) | copy-start | bytes 772
  4.9 34.2 %all-to-all-start = ((bf16[32,8,1536]{2,1,0:T(8,128)(2,1)}), bf16[32,8,1536]{2,1,0:T(8,128)(2,1)S(1)}, u32[]{:S(2)}, u32[]{:S(2)}) async-start(bf16[32,8,1536]{2,1,0:T(8,128)(2,1)} %bitcast.50), calls=%async_computation | async-start | bytes 1572864 | tf_op jit(solution)/shard_map/all_to_all | solution.py:126
  39.1 0.9 %copy-start = (bf16[32,8,1536]{2,1,0:T(8,128)(2,1)}, bf16[32,8,1536]{2,1,0:T(8,128)(2,1)S(1)}, u32[]{:S(2)}) copy-start(bf16[32,8,1536]{2,1,0:T(8,128)(2,1)S(1)} %all-to-all-done) | copy-start | bytes 2359300
  48.2 2.2 %collective-permute-start = (f32[520,4,64]{0,2,1:T(8,128)S(1)}, f32[520,4,64]{0,2,1:T(8,128)S(1)}, u32[]{:S(2)}, u32[]{:S(2)}) collective-permute-start(f32[520,4,64]{0,2,1:T(8,128)S(1)} %dynamic-slice_bitcast_fusion), channel_id=1, source_target_pairs={{0,1},{1,0},{2,3},{3,2},{4,5},{5,4},{6,7},{7,6},{8,9},{9,8},{10,11... | collective-permute-start | bytes 1597448 | tf_op jit(solution)/shard_map/ppermute | solution.py:143
  50.5 7.6 %collective-permute-start.1 = (f32[520,64]{0,1:T(8,128)S(1)}, f32[520,64]{0,1:T(8,128)S(1)}, u32[]{:S(2)}, u32[]{:S(2)}) collective-permute-start(f32[520,64]{0,1:T(8,128)S(1)} %get-tuple-element.14), channel_id=1, source_target_pairs={{0,2},{1,3},{2,4},{3,5},{4,6},{5,7},{6,0},{7,1},{8,10},{9,11},{10,... | collective-permute-start | bytes 399368 | tf_op jit(solution)/shard_map/ppermute | solution.py:148
  52.2 10.6 %collective-permute-start.2 = (f32[520,64]{0,1:T(8,128)S(1)}, f32[520,64]{0,1:T(8,128)S(1)}, u32[]{:S(2)}, u32[]{:S(2)}) collective-permute-start(f32[520,64]{0,1:T(8,128)S(1)} %get-tuple-element.16), channel_id=1, source_target_pairs={{0,4},{1,5},{2,6},{3,7},{4,0},{5,1},{6,2},{7,3},{8,12},{9,13},{10,... | collective-permute-start | bytes 399368 | tf_op jit(solution)/shard_map/ppermute | solution.py:148
  55.1 7.7 %collective-permute-start.3 = (f32[520,64]{0,1:T(8,128)S(1)}, f32[520,64]{0,1:T(8,128)S(1)}, u32[]{:S(2)}, u32[]{:S(2)}) collective-permute-start(f32[520,64]{0,1:T(8,128)S(1)} %get-tuple-element.15), channel_id=1, source_target_pairs={{0,6},{1,7},{2,0},{3,1},{4,2},{5,3},{6,4},{7,5},{8,14},{9,15},{10,... | collective-permute-start | bytes 399368 | tf_op jit(solution)/shard_map/ppermute | solution.py:148
  63.1 28.9 %copy-start.5 = (f32[64]{0:T(128)S(1)}, f32[64]{0:T(128)}, u32[]{:S(2)}) copy-start(f32[64]{0:T(128)} %param.17) | copy-start | bytes 772
  63.2 5.1 %collective-permute-start.4 = (f32[16,17,64]{2,0,1:T(8,128)S(1)}, f32[16,17,64]{2,0,1:T(8,128)S(1)}, u32[]{:S(2)}, u32[]{:S(2)}) collective-permute-start(f32[16,17,64]{2,0,1:T(8,128)S(1)} %bitcast.55), channel_id=1, source_target_pairs={{0,8},{8,0},{16,24},{24,16},{32,40},{40,32},{48,56},{56,48},{64,72... | collective-permute-start | bytes 208904 | tf_op jit(solution)/shard_map/ppermute | solution.py:162
  68.5 5.9 %collective-permute-start.5 = (f32[8,17,64]{2,0,1:T(8,128)S(1)}, f32[8,17,64]{2,0,1:T(8,128)S(1)}, u32[]{:S(2)}, u32[]{:S(2)}) collective-permute-start(f32[8,17,64]{2,0,1:T(8,128)S(1)} %bitcast.59), channel_id=1, source_target_pairs={{0,16},{8,24},{16,0},{24,8},{32,48},{40,56},{48,32},{56,40},{64,80... | collective-permute-start | bytes 104456 | tf_op jit(solution)/shard_map/ppermute | solution.py:162
  74.5 4.2 %collective-permute-start.6 = (f32[4,17,64]{2,0,1:T(4,128)S(1)}, f32[4,17,64]{2,0,1:T(4,128)S(1)}, u32[]{:S(2)}, u32[]{:S(2)}) collective-permute-start(f32[4,17,64]{2,0,1:T(4,128)S(1)} %bitcast.61), channel_id=1, source_target_pairs={{0,32},{8,40},{16,48},{24,56},{32,0},{40,8},{48,16},{56,24},{64,96... | collective-permute-start | bytes 52232 | tf_op jit(solution)/shard_map/ppermute | solution.py:162
  78.8 4.9 %collective-permute-start.7 = (f32[2,17,64]{2,0,1:T(2,128)S(1)}, f32[2,17,64]{2,0,1:T(2,128)S(1)}, u32[]{:S(2)}, u32[]{:S(2)}) collective-permute-start(f32[2,17,64]{2,0,1:T(2,128)S(1)} %bitcast.62), channel_id=1, source_target_pairs={{0,64},{8,72},{16,80},{24,88},{32,96},{40,104},{48,112},{56,120},{... | collective-permute-start | bytes 26120 | tf_op jit(solution)/shard_map/ppermute | solution.py:162
  83.8 7.7 %collective-permute-start.8 = (f32[1,17,64]{2,0,1:T(1,128)S(1)}, f32[1,17,64]{2,0,1:T(1,128)S(1)}, u32[]{:S(2)}, u32[]{:S(2)}) collective-permute-start(f32[1,17,64]{2,0,1:T(1,128)S(1)} %constant_dynamic-slice_fusion), channel_id=1, source_target_pairs={{0,128},{8,136},{16,144},{24,152},{32,160},{40,168},{48,176},{56,1... | collective-permute-start | bytes 13064 | tf_op jit(solution)/shard_map/ppermute | solution.py:162

commit v8 on v6

--- a/solution.py
+++ b/solution.py
@@ -50,12 +50,13 @@
             force_acc = force_acc + v_ref[pl.ds((3 * a + c) * n_el, n_el), :].astype(jnp.float32) * wf
     grad = {}
     for k in range(3):
+        signed = None
+        for a in range(8):
+            term = jnp.where(slot_ref[:, a:a + 1] == lane, G[a][k], 0.0)
+            signed = term if signed is None else signed + term
+        full = jnp.dot(signed.astype(jnp.bfloat16), arrived_ref[...], preferred_element_type=jnp.float32)
         for c in range(3):
-            acc = None
-            for a in range(8):
-                term = G[a][k] * v_ref[pl.ds((3 * a + c) * n_el, n_el), :].astype(jnp.float32)
-                acc = term if acc is None else acc + term
-            grad[k, c] = acc
+            grad[k, c] = full[:, c * modes:(c + 1) * modes]
     trace = grad[0, 0] + grad[1, 1] + grad[2, 2]
     for a in range(8):
         for c in range(3):

time: 82.8 us -> 83 us (level)
  no operation moved by 1% of the time
where the time goes in v8:
time: 83 us; the launch traced here: 81.4 us
  waiting for transfers between devices  32.9 us (40%)
  starting transfers between devices  23.3 us (28%)
  Pallas kernels  10.8 us (13%)
  local copies, waits for them, and re-layouts  7.89 us (10%)
  other arithmetic  4.86 us (6%)
  between operations  1.61 us (2%)
    all_to_all x1, waiting for transfers between devices, local(): lax.all_to_all(outgoing, 'elem', split_axis=0, concat_axis=0, tiled=True)  16.9 us
    all_to_all x1, starting transfers between devices, local(): lax.all_to_all(outgoing, 'elem', split_axis=0, concat_axis=0, tiled=True)  11.8 us
    all_to_all x1, waiting for transfers between devices, local(): lax.all_to_all(chunks, 'elem', split_axis=0, concat_axis=0, tiled=True)  7.58 us
    pallas_call x1, Pallas kernels, element_stage(): pl.pallas_call(element_body, out_shape=jax.ShapeDtypeStruct((modes + 8, m...  6.59 us
    ppermute x3, waiting for transfers between devices, local(): halfway = halfway + lax.ppermute(piece, 'blk', ring)  6.38 us
    ppermute x3, starting transfers between devices, local(): halfway = halfway + lax.ppermute(piece, 'blk', ring)  5.92 us
    all_to_all x1, starting transfers between devices, local(): lax.all_to_all(chunks, 'elem', split_axis=0, concat_axis=0, tiled=True)  5.56 us
    pallas_call x1, Pallas kernels, gather_rows(): pl.pallas_call(gather_body, out_shape=jax.ShapeDtypeStruct((n_rows, comps...  4.25 us
  transfers between devices with their start and end apart: 6, of which 5 were waited for; matrix products, arithmetic and copies ran while one was open for 7% of the time, Pallas kernels for 0%

profile of v8, /device:TPU:2, one launch (start us, length us, event | category | flops | bytes accessed | tf_op | source)
XLA Modules:
  0.0 81.4 jit_solution(1875804202816294523)
XLA Ops:
  0.6 4.2 %shard_map.95 = bf16[256,1536]{1,0:T(8,128)(2,1)} custom-call(bf16[3,1024,512]{2,1,0:T(8,128)(2,1)} %bitcast.33, s32[1,256]{1,0:T(1,128)} %bitcast.38), custom_call_target="tpu_custom_call" | custom-call | tf_op jit(solution)/shard_map/pallas_call | solution.py:110
  4.9 11.8 %all-to-all-start = ((bf16[32,8,1536]{2,1,0:T(8,128)(2,1)}), bf16[32,8,1536]{2,1,0:T(8,128)(2,1)S(1)}, u32[]{:S(2)}, u32[]{:S(2)}) async-start(bf16[32,8,1536]{2,1,0:T(8,128)(2,1)} %bitcast.35), calls=%async_computation | async-start | bytes 1572864 | tf_op jit(solution)/shard_map/all_to_all | solution.py:127
  16.7 0.6 dynamic_slice.24
  17.3 0.6 fusion.2
  17.9 0.7 copy.25.omega_ref
  18.7 0.6 compare_reduce_fusion
  19.3 0.6 broadcast_select_fusion
  20.0 0.1 reshape.56
  20.1 0.7 copy.23
  20.8 0.7 copy.26.stiff_ref
  21.5 0.7 scatter.4.state_ref
  22.2 16.9 %all-to-all-done = bf16[32,8,1536]{2,1,0:T(8,128)(2,1)S(1)} async-done(((bf16[32,8,1536]{2,1,0:T(8,128)(2,1)}), bf16[32,8,1536]{2,1,0:T(8,128)(2,1)S(1)}, u32[]{:S(2)}, u32[]{:S(2)}) %all-to-all-start) | async-done | bytes 786464 | tf_op jit(solution)/shard_map/all_to_all | solution.py:127
  39.1 0.9 %copy-done = bf16[32,8,1536]{2,1,0:T(8,128)(2,1)} copy-done((bf16[32,8,1536]{2,1,0:T(8,128)(2,1)}, bf16[32,8,1536]{2,1,0:T(8,128)(2,1)S(1)}, u32[]{:S(2)}) %copy-start) | copy-done | bytes 786456
  40.0 6.6 %shard_map.96 = f32[520,512]{1,0:T(8,128)} custom-call(bf16[256,1536]{1,0:T(8,128)(2,1)} %bitcast.34, s32[64,8]{1,0:T(8,128)} %bitcast.37, bf16[512,128]{1,0:T(8,128)(2,1)} %scatter.4.state_ref, f32[64,1]{1,0:T(8,128)} %copy.25.omega_ref, f32[64,1]{1,0:T(8,128)} %copy.26.stiff_ref), custom_call_target="tpu_custom_call" | custom-call | tf_op jit(solution)/shard_map/pallas_call | solution.py:84
  46.6 1.6 %copy.27 = f32[520,512]{0,1:T(8,128)S(1)} copy(f32[520,512]{1,0:T(8,128)} %shard_map.96) | data formatting | bytes 2129920 | tf_op jit(solution)/shard_map/pallas_call | solution.py:84
  48.5 2.0 %collective-permute-done = f32[520,4,64]{0,2,1:T(8,128)S(1)} collective-permute-done((f32[520,4,64]{0,2,1:T(8,128)S(1)}, f32[520,4,64]{0,2,1:T(8,128)S(1)}, u32[]{:S(2)}, u32[]{:S(2)}) %collective-permute-start) | collective-permute-done | bytes 532512 | tf_op jit(solution)/shard_map/ppermute | solution.py:144
  50.6 1.7 %collective-permute-start.1 = (f32[520,64]{0,1:T(8,128)S(1)}, f32[520,64]{0,1:T(8,128)S(1)}, u32[]{:S(2)}, u32[]{:S(2)}) collective-permute-start(f32[520,64]{0,1:T(8,128)S(1)} %get-tuple-element.14), channel_id=1, source_target_pairs={{0,2},{1,3},{2,4},{3,5},{4,6},{5,7},{6,0},{7,1},{8,10},{9,11},{10,... | collective-permute-start | bytes 399368 | tf_op jit(solution)/shard_map/ppermute | solution.py:149
  52.3 2.9 %collective-permute-start.2 = (f32[520,64]{0,1:T(8,128)S(1)}, f32[520,64]{0,1:T(8,128)S(1)}, u32[]{:S(2)}, u32[]{:S(2)}) collective-permute-start(f32[520,64]{0,1:T(8,128)S(1)} %get-tuple-element.16), channel_id=1, source_target_pairs={{0,4},{1,5},{2,6},{3,7},{4,0},{5,1},{6,2},{7,3},{8,12},{9,13},{10,... | collective-permute-start | bytes 399368 | tf_op jit(solution)/shard_map/ppermute | solution.py:149
  55.2 1.3 %collective-permute-start.3 = (f32[520,64]{0,1:T(8,128)S(1)}, f32[520,64]{0,1:T(8,128)S(1)}, u32[]{:S(2)}, u32[]{:S(2)}) collective-permute-start(f32[520,64]{0,1:T(8,128)S(1)} %get-tuple-element.15), channel_id=1, source_target_pairs={{0,6},{1,7},{2,0},{3,1},{4,2},{5,3},{6,4},{7,5},{8,14},{9,15},{10,... | collective-permute-start | bytes 399368 | tf_op jit(solution)/shard_map/ppermute | solution.py:149
  56.6 1.7 %collective-permute-done.1 = f32[520,64]{0,1:T(8,128)S(1)} collective-permute-done((f32[520,64]{0,1:T(8,128)S(1)}, f32[520,64]{0,1:T(8,128)S(1)}, u32[]{:S(2)}, u32[]{:S(2)}) %collective-permute-start.1) | collective-permute-done | bytes 133152 | tf_op jit(solution)/shard_map/ppermute | solution.py:149
  58.2 4.7 %collective-permute-done.2 = f32[520,64]{0,1:T(8,128)S(1)} collective-permute-done((f32[520,64]{0,1:T(8,128)S(1)}, f32[520,64]{0,1:T(8,128)S(1)}, u32[]{:S(2)}, u32[]{:S(2)}) %collective-permute-start.2) | collective-permute-done | bytes 133152 | tf_op jit(solution)/shard_map/ppermute | solution.py:149
  63.0 0.1 slice_reduce_fusion
  63.1 0.1 copy.28
  63.3 0.8 %reshape.58 = f32[32,1,1088]{2,1,0:T(1,128)} reshape(f32[32,17,64]{2,1,0:T(8,128)S(1)} %pad_maximum_fusion) | data formatting | bytes 278528
  64.2 5.6 %all-to-all-start.1 = ((f32[32,1,1088]{2,1,0:T(1,128)}), f32[32,1,1088]{2,1,0:T(1,128)S(1)}, u32[]{:S(2)}, u32[]{:S(2)}) async-start(f32[32,1,1088]{2,1,0:T(1,128)} %reshape.58), calls=%async_computation.1 | async-start | bytes 294912 | tf_op jit(solution)/shard_map/all_to_all | solution.py:155
  69.7 0.6 reduce_sum.19
  71.1 7.6 %all-to-all-done.1 = f32[32,1,1088]{2,1,0:T(1,128)S(1)} async-done(((f32[32,1,1088]{2,1,0:T(1,128)}), f32[32,1,1088]{2,1,0:T(1,128)S(1)}, u32[]{:S(2)}, u32[]{:S(2)}) %all-to-all-start.1) | async-done | bytes 139296 | tf_op jit(solution)/shard_map/all_to_all | solution.py:155
  78.6 0.5 broadcast.46
  79.1 1.0 %reduce.10 = f32[32,1088]{1,0:T(8,128)S(1)} reduce(f32[32,1,1088]{2,1,0:T(1,128)S(1)} %all-to-all-done.1, f32[]{:T(128)} %broadcast.46), dimensions={1}, to_apply=%all_to_all.13.reduce_sub_computation | reduce | bytes 278532 | tf_op jit(solution)/shard_map/all_to_all | solution.py:155
  80.1 0.1 reshape.59
  80.3 0.6 slice_multiply_fusion
  80.9 0.5 fusion.4
  (23 shorter events, 0.4 us)
Async XLA Ops:
  4.9 11.8 %copy-start.6 = (s32[32]{0:T(128)S(1)}, s32[32]{0:T(128)}, u32[]{:S(2)}) copy-start(s32[32]{0:T(128)} %param.13) | copy-start | bytes 388
  4.9 12.4 %copy-start.4 = (f32[64]{0:T(128)S(1)}, f32[64]{0:T(128)}, u32[]{:S(2)}) copy-start(f32[64]{0:T(128)} %param.14) | copy-start | bytes 772
  4.9 14.4 %copy-start.2 = (bf16[512]{0:T(512)(128)(2,1)S(1)}, bf16[512]{0:T(512)(128)(2,1)}, u32[]{:S(2)}) copy-start(bf16[512]{0:T(512)(128)(2,1)} %param.16) | copy-start | bytes 3076
  4.9 15.2 %copy-start.1 = (s32[8,64]{1,0:T(8,128)S(1)}, s32[8,64]{1,0:T(8,128)}, u32[]{:S(2)}) copy-start(s32[8,64]{1,0:T(8,128)} %param.12) | copy-start | bytes 6148
  4.9 15.9 %copy-start.3 = (f32[64]{0:T(128)S(1)}, f32[64]{0:T(128)}, u32[]{:S(2)}) copy-start(f32[64]{0:T(128)} %param.15) | copy-start | bytes 772
  4.9 34.2 %all-to-all-start = ((bf16[32,8,1536]{2,1,0:T(8,128)(2,1)}), bf16[32,8,1536]{2,1,0:T(8,128)(2,1)S(1)}, u32[]{:S(2)}, u32[]{:S(2)}) async-start(bf16[32,8,1536]{2,1,0:T(8,128)(2,1)} %bitcast.35), calls=%async_computation | async-start | bytes 1572864 | tf_op jit(solution)/shard_map/all_to_all | solution.py:127
  39.1 0.9 %copy-start = (bf16[32,8,1536]{2,1,0:T(8,128)(2,1)}, bf16[32,8,1536]{2,1,0:T(8,128)(2,1)S(1)}, u32[]{:S(2)}) copy-start(bf16[32,8,1536]{2,1,0:T(8,128)(2,1)S(1)} %all-to-all-done) | copy-start | bytes 2359300
  48.3 2.2 %collective-permute-start = (f32[520,4,64]{0,2,1:T(8,128)S(1)}, f32[520,4,64]{0,2,1:T(8,128)S(1)}, u32[]{:S(2)}, u32[]{:S(2)}) collective-permute-start(f32[520,4,64]{0,2,1:T(8,128)S(1)} %dynamic-slice_bitcast_fusion), channel_id=1, source_target_pairs={{0,1},{1,0},{2,3},{3,2},{4,5},{5,4},{6,7},{7,6},{8,9},{9,8},{10,11... | collective-permute-start | bytes 1597448 | tf_op jit(solution)/shard_map/ppermute | solution.py:144
  50.6 7.6 %collective-permute-start.1 = (f32[520,64]{0,1:T(8,128)S(1)}, f32[520,64]{0,1:T(8,128)S(1)}, u32[]{:S(2)}, u32[]{:S(2)}) collective-permute-start(f32[520,64]{0,1:T(8,128)S(1)} %get-tuple-element.14), channel_id=1, source_target_pairs={{0,2},{1,3},{2,4},{3,5},{4,6},{5,7},{6,0},{7,1},{8,10},{9,11},{10,... | collective-permute-start | bytes 399368 | tf_op jit(solution)/shard_map/ppermute | solution.py:149
  52.3 10.6 %collective-permute-start.2 = (f32[520,64]{0,1:T(8,128)S(1)}, f32[520,64]{0,1:T(8,128)S(1)}, u32[]{:S(2)}, u32[]{:S(2)}) collective-permute-start(f32[520,64]{0,1:T(8,128)S(1)} %get-tuple-element.16), channel_id=1, source_target_pairs={{0,4},{1,5},{2,6},{3,7},{4,0},{5,1},{6,2},{7,3},{8,12},{9,13},{10,... | collective-permute-start | bytes 399368 | tf_op jit(solution)/shard_map/ppermute | solution.py:149
  55.2 7.7 %collective-permute-start.3 = (f32[520,64]{0,1:T(8,128)S(1)}, f32[520,64]{0,1:T(8,128)S(1)}, u32[]{:S(2)}, u32[]{:S(2)}) collective-permute-start(f32[520,64]{0,1:T(8,128)S(1)} %get-tuple-element.15), channel_id=1, source_target_pairs={{0,6},{1,7},{2,0},{3,1},{4,2},{5,3},{6,4},{7,5},{8,14},{9,15},{10,... | collective-permute-start | bytes 399368 | tf_op jit(solution)/shard_map/ppermute | solution.py:149
  63.3 17.6 %copy-start.5 = (f32[64]{0:T(128)S(1)}, f32[64]{0:T(128)}, u32[]{:S(2)}) copy-start(f32[64]{0:T(128)} %param.17) | copy-start | bytes 772
  64.2 14.5 %all-to-all-start.1 = ((f32[32,1,1088]{2,1,0:T(1,128)}), f32[32,1,1088]{2,1,0:T(1,128)S(1)}, u32[]{:S(2)}, u32[]{:S(2)}) async-start(f32[32,1,1088]{2,1,0:T(1,128)} %reshape.58), calls=%async_computation.1 | async-start | bytes 294912 | tf_op jit(solution)/shard_map/all_to_all | solution.py:155

commit v9 on v6

--- a/solution.py
+++ b/solution.py
@@ -9,19 +9,38 @@
 
 
 def element_body(arrived_ref, slot_ref, state_ref, omega_ref, stiff_ref, out_ref, v_ref, w_ref):
-    n_el = slot_ref.shape[0]
+    n_el = omega_ref.shape[0]
     n_slot = arrived_ref.shape[0]
     modes = out_ref.shape[1]
-    lane = lax.broadcasted_iota(jnp.int32, (n_el, n_slot), 1)
-    state_pad = state_ref[...]
+    slots = slot_ref[...]
+    lane = lax.broadcasted_iota(jnp.int32, (8 * n_el, n_slot), 1)
+    onehot = (slots == lane).astype(jnp.bfloat16)
+    corners = jnp.dot(onehot, arrived_ref[...], preferred_element_type=jnp.float32).astype(jnp.bfloat16)
+    for c in range(3):
+        v_ref[pl.ds(c * 8 * n_el, 8 * n_el), :] = corners[:, c * modes:(c + 1) * modes]
+    disp_all = jnp.dot(corners, state_ref[...], preferred_element_type=jnp.float32)
     disp = {}
     for a in range(8):
-        onehot = (slot_ref[:, a:a + 1] == lane).astype(jnp.bfloat16)
-        corner = jnp.dot(onehot, arrived_ref[...], preferred_element_type=jnp.float32).astype(jnp.bfloat16)
         for c in range(3):
-            va = corner[:, c * modes:(c + 1) * modes]
-            v_ref[pl.ds((3 * a + c) * n_el, n_el), :] = va
-            disp[a, c] = jnp.dot(va, state_pad, preferred_element_type=jnp.float32)[:, 0:1]
+            disp[a, c] = disp_all[a * n_el:(a + 1) * n_el, c:c + 1]
+    lane_el = lane[:n_el]
+    signed_rows = []
+    for k in range(3):
+        signed = None
+        for a in range(8):
+            term = jnp.where(slots[a * n_el:(a + 1) * n_el] == lane_el, G[a][k], 0.0)
+            signed = term if signed is None else signed + term
+        signed_rows.append(signed)
+    signed_all = jnp.concatenate(signed_rows, axis=0).astype(jnp.bfloat16)
+    grad_all = jnp.dot(signed_all, arrived_ref[...], preferred_element_type=jnp.float32)
+    grad = {}
+    for k in range(3):
+        for c in range(3):
+            grad[k, c] = grad_all[k * n_el:(k + 1) * n_el, c * modes:(c + 1) * modes]
+
+    def corner_rows(a, c):
+        return pl.ds(c * 8 * n_el + a * n_el, n_el)
+
     h = {}
     for k in range(3):
         for c in range(3):
@@ -47,15 +66,7 @@
             f = G[a][0] * stress[0, c] + G[a][1] * stress[1, c] + G[a][2] * stress[2, c]
             f = f + 0.25 * disp[a, c]
             wf = (f * omega).astype(jnp.bfloat16).astype(jnp.float32)
-            force_acc = force_acc + v_ref[pl.ds((3 * a + c) * n_el, n_el), :].astype(jnp.float32) * wf
-    grad = {}
-    for k in range(3):
-        for c in range(3):
-            acc = None
-            for a in range(8):
-                term = G[a][k] * v_ref[pl.ds((3 * a + c) * n_el, n_el), :].astype(jnp.float32)
-                acc = term if acc is None else acc + term
-            grad[k, c] = acc
+            force_acc = force_acc + v_ref[corner_rows(a, c), :].astype(jnp.float32) * wf
     trace = grad[0, 0] + grad[1, 1] + grad[2, 2]
     for a in range(8):
         for c in range(3):
@@ -63,8 +74,8 @@
             img = img + G[a][1] * (grad[1, c] + grad[c, 1])
             img = img + G[a][2] * (grad[2, c] + grad[c, 2])
             img = img + (lam * G[a][c]) * trace
-            img = img + 0.25 * v_ref[pl.ds((3 * a + c) * n_el, n_el), :].astype(jnp.float32)
-            w_ref[pl.ds((3 * a + c) * n_el, n_el), :] = (omega * img).astype(jnp.bfloat16)
+            img = img + 0.25 * v_ref[corner_rows(a, c), :].astype(jnp.float32)
+            w_ref[corner_rows(a, c), :] = (omega * img).astype(jnp.bfloat16)
     tangent = lax.dot_general(
         v_ref[...], w_ref[...], (((0,), (0,)), ((), ())), preferred_element_type=jnp.float32
     )
@@ -75,10 +86,13 @@
     )
 
 
-def element_stage(arrived3, slot_t, state, omega, stiff):
-    n_el = slot_t.shape[0]
+def element_stage(arrived3, slot, state, omega, stiff):
+    n_el = slot.shape[1]
     modes = arrived3.shape[1] // 3
-    state_pad = jnp.zeros((modes, 128), jnp.bfloat16).at[:, 0].set(state)
+    comp = jnp.arange(3 * modes) // modes
+    state_blocks = jnp.where(
+        comp[:, None] == jnp.arange(128)[None, :], jnp.tile(state, 3)[:, None], jnp.zeros((), state.dtype)
+    )
     vmem = pltpu.MemorySpace.VMEM if hasattr(pltpu, "MemorySpace") else pltpu.TPUMemorySpace.VMEM
     return pl.pallas_call(
         element_body,
@@ -89,7 +103,7 @@
             pltpu.VMEM((24 * n_el, modes), jnp.bfloat16),
             pltpu.VMEM((24 * n_el, modes), jnp.bfloat16),
         ],
-    )(arrived3, slot_t, state_pad, omega.reshape(n_el, 1), stiff.reshape(n_el, 1))
+    )(arrived3, slot.reshape(8 * n_el, 1), state_blocks, omega.reshape(n_el, 1), stiff.reshape(n_el, 1))
 
 
 def gather_body(basis_ref, rows_ref, out_ref):
@@ -130,7 +144,7 @@
     live = lax.dynamic_index_in_dim(set_size, set_index, keepdims=False)
     position = block_index * element_count + jnp.arange(element_count, dtype=jnp.int32)
     weights = jnp.where(position < live, elem_weight, jnp.zeros_like(elem_weight))
-    stacked = element_stage(arrived, elem_slot.T, state, weights, element_stiffening)
+    stacked = element_stage(arrived, elem_slot, state, weights, element_stiffening)
     rows = basis_modes // n_elem
     cols = basis_modes // n_blk
     n_y = n_blk // 2

time: 82.8 us -> 81.9 us (0.989)
  Pallas kernels: 10.7 us -> 9.74 us
    select_n x0 -> x2, other arithmetic: none -> 1.76 us  [the longest x1 1.76 us: element_stage(): jnp.where(comp[:, None] == jnp.arange(128)[None, :], jnp.tile(state, 3)[:...]
    another operation x2 -> x0, other arithmetic: 1.29 us -> none
    pallas_call x1, Pallas kernels: 6.42 us -> 5.5 us  [element_stage(): pl.pallas_call(element_body, out_shape=jax.ShapeDtypeStruct((modes + 8, m...]
    reshape x0 -> x1, local copies, waits for them, and re-layouts: none -> 0.9 us  [element_stage(): slot.reshape(8 * n_el, 1)]
    unnamed x17 -> x16, local copies, waits for them, and re-layouts: 2.59 us -> 1.89 us
where the time goes in v9:
time: 81.9 us; the launch traced here: 80.3 us
  waiting for transfers between devices  33 us (40%)
  starting transfers between devices  23.3 us (28%)
  Pallas kernels  9.74 us (12%)
  local copies, waits for them, and re-layouts  7.28 us (9%)
  other arithmetic  5.33 us (7%)
  between operations  1.58 us (2%)
    all_to_all x1, waiting for transfers between devices, local(): lax.all_to_all(outgoing, 'elem', split_axis=0, concat_axis=0, tiled=True)  17.1 us
    all_to_all x1, starting transfers between devices, local(): lax.all_to_all(outgoing, 'elem', split_axis=0, concat_axis=0, tiled=True)  11.8 us
    all_to_all x1, waiting for transfers between devices, local(): lax.all_to_all(chunks, 'elem', split_axis=0, concat_axis=0, tiled=True)  7.58 us
    ppermute x3, waiting for transfers between devices, local(): halfway = halfway + lax.ppermute(piece, 'blk', ring)  6.38 us
    ppermute x3, starting transfers between devices, local(): halfway = halfway + lax.ppermute(piece, 'blk', ring)  5.92 us
    all_to_all x1, starting transfers between devices, local(): lax.all_to_all(chunks, 'elem', split_axis=0, concat_axis=0, tiled=True)  5.57 us
    pallas_call x1, Pallas kernels, element_stage(): pl.pallas_call(element_body, out_shape=jax.ShapeDtypeStruct((modes + 8, m...  5.5 us
    pallas_call x1, Pallas kernels, gather_rows(): pl.pallas_call(gather_body, out_shape=jax.ShapeDtypeStruct((n_rows, comps...  4.24 us
  transfers between devices with their start and end apart: 6, of which 5 were waited for; matrix products, arithmetic and copies ran while one was open for 7% of the time, Pallas kernels for 0%

profile of v9, /device:TPU:2, one launch (start us, length us, event | category | flops | bytes accessed | tf_op | source)
XLA Modules:
  0.0 80.3 jit_solution(11009359617953539074)
XLA Ops:
  0.6 4.2 %shard_map.95 = bf16[256,1536]{1,0:T(8,128)(2,1)} custom-call(bf16[3,1024,512]{2,1,0:T(8,128)(2,1)} %bitcast.32, s32[1,256]{1,0:T(1,128)} %bitcast.36), custom_call_target="tpu_custom_call" | custom-call | tf_op jit(solution)/shard_map/pallas_call | solution.py:123
  4.9 11.8 %all-to-all-start = ((bf16[32,8,1536]{2,1,0:T(8,128)(2,1)}), bf16[32,8,1536]{2,1,0:T(8,128)(2,1)S(1)}, u32[]{:S(2)}, u32[]{:S(2)}) async-start(bf16[32,8,1536]{2,1,0:T(8,128)(2,1)} %bitcast.34), calls=%async_computation | async-start | bytes 1572864 | tf_op jit(solution)/shard_map/all_to_all | solution.py:140
  16.7 0.6 dynamic_slice.24
  17.3 0.6 fusion.6
  17.9 0.7 copy.21.omega_ref
  18.7 0.9 %reshape.46.slot_ref = s32[512,1]{1,0:T(8,128)} reshape(s32[8,64]{1,0:T(8,128)S(1)} %copy-done.1) | data formatting | bytes 4096 | tf_op jit(solution)/shard_map/reshape | solution.py:106
  19.6 0.7 copy.22.stiff_ref
  20.3 1.8 %fusion.state_ref = bf16[1536,128]{1,0:T(8,128)(2,1)} fusion(s32[1536]{0:T(1024)S(1)} %add_select_fusion, bf16[1536]{0:T(1024)(128)(2,1)S(1)} %broadcast_in_dim.26), kind=kLoop, calls=%fused_computation.1 | loop fusion | flops 393216 | bytes 402432 | tf_op jit(solution)/shard_map/jit(_where)/select_n | solution.py:93
  22.0 17.1 %all-to-all-done = bf16[32,8,1536]{2,1,0:T(8,128)(2,1)S(1)} async-done(((bf16[32,8,1536]{2,1,0:T(8,128)(2,1)}), bf16[32,8,1536]{2,1,0:T(8,128)(2,1)S(1)}, u32[]{:S(2)}, u32[]{:S(2)}) %all-to-all-start) | async-done | bytes 786464 | tf_op jit(solution)/shard_map/all_to_all | solution.py:140
  39.1 0.9 %copy-done = bf16[32,8,1536]{2,1,0:T(8,128)(2,1)} copy-done((bf16[32,8,1536]{2,1,0:T(8,128)(2,1)}, bf16[32,8,1536]{2,1,0:T(8,128)(2,1)S(1)}, u32[]{:S(2)}) %copy-start) | copy-done | bytes 786456
  40.0 5.5 %shard_map.96 = f32[520,512]{1,0:T(8,128)} custom-call(bf16[256,1536]{1,0:T(8,128)(2,1)} %bitcast.33, s32[512,1]{1,0:T(8,128)} %reshape.46.slot_ref, bf16[1536,128]{1,0:T(8,128)(2,1)} %fusion.state_ref, f32[64,1]{1,0:T(8,128)} %copy.21.omega_ref, f32[64,1]{1,0:T(8,128)} %copy.22.stiff_ref), custom_call_target="tpu_custom_call" | custom-call | tf_op jit(solution)/shard_map/pallas_call | solution.py:97
  45.5 1.6 %copy.23 = f32[520,512]{0,1:T(8,128)S(1)} copy(f32[520,512]{1,0:T(8,128)} %shard_map.96) | data formatting | bytes 2129920 | tf_op jit(solution)/shard_map/pallas_call | solution.py:97
  47.2 0.1 dynamic-slice_bitcast_fusion
  47.2 0.1 collective-permute-start
  47.4 2.0 %collective-permute-done = f32[520,4,64]{0,2,1:T(8,128)S(1)} collective-permute-done((f32[520,4,64]{0,2,1:T(8,128)S(1)}, f32[520,4,64]{0,2,1:T(8,128)S(1)}, u32[]{:S(2)}, u32[]{:S(2)}) %collective-permute-start) | collective-permute-done | bytes 532512 | tf_op jit(solution)/shard_map/ppermute | solution.py:157
  49.4 0.1 bitcast_add_fusion
  49.5 1.7 %collective-permute-start.1 = (f32[520,64]{0,1:T(8,128)S(1)}, f32[520,64]{0,1:T(8,128)S(1)}, u32[]{:S(2)}, u32[]{:S(2)}) collective-permute-start(f32[520,64]{0,1:T(8,128)S(1)} %get-tuple-element.2), channel_id=1, source_target_pairs={{0,2},{1,3},{2,4},{3,5},{4,6},{5,7},{6,0},{7,1},{8,10},{9,11},{10,... | collective-permute-start | bytes 399368 | tf_op jit(solution)/shard_map/ppermute | solution.py:162
  51.2 2.9 %collective-permute-start.2 = (f32[520,64]{0,1:T(8,128)S(1)}, f32[520,64]{0,1:T(8,128)S(1)}, u32[]{:S(2)}, u32[]{:S(2)}) collective-permute-start(f32[520,64]{0,1:T(8,128)S(1)} %get-tuple-element.4), channel_id=1, source_target_pairs={{0,4},{1,5},{2,6},{3,7},{4,0},{5,1},{6,2},{7,3},{8,12},{9,13},{10,... | collective-permute-start | bytes 399368 | tf_op jit(solution)/shard_map/ppermute | solution.py:162
  54.1 1.3 %collective-permute-start.3 = (f32[520,64]{0,1:T(8,128)S(1)}, f32[520,64]{0,1:T(8,128)S(1)}, u32[]{:S(2)}, u32[]{:S(2)}) collective-permute-start(f32[520,64]{0,1:T(8,128)S(1)} %get-tuple-element.3), channel_id=1, source_target_pairs={{0,6},{1,7},{2,0},{3,1},{4,2},{5,3},{6,4},{7,5},{8,14},{9,15},{10,... | collective-permute-start | bytes 399368 | tf_op jit(solution)/shard_map/ppermute | solution.py:162
  55.5 1.7 %collective-permute-done.1 = f32[520,64]{0,1:T(8,128)S(1)} collective-permute-done((f32[520,64]{0,1:T(8,128)S(1)}, f32[520,64]{0,1:T(8,128)S(1)}, u32[]{:S(2)}, u32[]{:S(2)}) %collective-permute-start.1) | collective-permute-done | bytes 133152 | tf_op jit(solution)/shard_map/ppermute | solution.py:162
  57.1 4.7 %collective-permute-done.2 = f32[520,64]{0,1:T(8,128)S(1)} collective-permute-done((f32[520,64]{0,1:T(8,128)S(1)}, f32[520,64]{0,1:T(8,128)S(1)}, u32[]{:S(2)}, u32[]{:S(2)}) %collective-permute-start.2) | collective-permute-done | bytes 133152 | tf_op jit(solution)/shard_map/ppermute | solution.py:162
  61.9 0.1 slice_reduce_fusion
  62.0 0.1 copy.24
  62.2 0.8 %reshape.48 = f32[32,1,1088]{2,1,0:T(1,128)} reshape(f32[32,17,64]{2,1,0:T(8,128)S(1)} %pad_maximum_fusion) | data formatting | bytes 278528
  63.1 5.6 %all-to-all-start.1 = ((f32[32,1,1088]{2,1,0:T(1,128)}), f32[32,1,1088]{2,1,0:T(1,128)S(1)}, u32[]{:S(2)}, u32[]{:S(2)}) async-start(f32[32,1,1088]{2,1,0:T(1,128)} %reshape.48), calls=%async_computation.1 | async-start | bytes 294912 | tf_op jit(solution)/shard_map/all_to_all | solution.py:168
  68.6 0.6 reduce_sum.19
  70.0 7.6 %all-to-all-done.1 = f32[32,1,1088]{2,1,0:T(1,128)S(1)} async-done(((f32[32,1,1088]{2,1,0:T(1,128)}), f32[32,1,1088]{2,1,0:T(1,128)S(1)}, u32[]{:S(2)}, u32[]{:S(2)}) %all-to-all-start.1) | async-done | bytes 139296 | tf_op jit(solution)/shard_map/all_to_all | solution.py:168
  77.5 0.5 broadcast.43
  78.0 1.0 %reduce.2 = f32[32,1088]{1,0:T(8,128)S(1)} reduce(f32[32,1,1088]{2,1,0:T(1,128)S(1)} %all-to-all-done.1, f32[]{:T(128)} %broadcast.43), dimensions={1}, to_apply=%all_to_all.13.reduce_sub_computation | reduce | bytes 278532 | tf_op jit(solution)/shard_map/all_to_all | solution.py:168
  79.0 0.1 reshape.49
  79.2 0.6 slice_multiply_fusion
  79.8 0.5 fusion.8
  (23 shorter events, 0.2 us)
Async XLA Ops:
  4.9 11.8 %copy-start.6 = (s32[32]{0:T(128)S(1)}, s32[32]{0:T(128)}, u32[]{:S(2)}) copy-start(s32[32]{0:T(128)} %param.11) | copy-start | bytes 388
  4.9 12.4 %copy-start.4 = (f32[64]{0:T(128)S(1)}, f32[64]{0:T(128)}, u32[]{:S(2)}) copy-start(f32[64]{0:T(128)} %param.12) | copy-start | bytes 772
  4.9 13.8 %copy-start.2 = (bf16[512]{0:T(512)(128)(2,1)S(1)}, bf16[512]{0:T(512)(128)(2,1)}, u32[]{:S(2)}) copy-start(bf16[512]{0:T(512)(128)(2,1)} %param.14) | copy-start | bytes 3076
  4.9 13.8 %copy-start.1 = (s32[8,64]{1,0:T(8,128)S(1)}, s32[8,64]{1,0:T(8,128)}, u32[]{:S(2)}) copy-start(s32[8,64]{1,0:T(8,128)} %param.10) | copy-start | bytes 6148
  4.9 14.7 %copy-start.3 = (f32[64]{0:T(128)S(1)}, f32[64]{0:T(128)}, u32[]{:S(2)}) copy-start(f32[64]{0:T(128)} %param.13) | copy-start | bytes 772
  4.9 34.2 %all-to-all-start = ((bf16[32,8,1536]{2,1,0:T(8,128)(2,1)}), bf16[32,8,1536]{2,1,0:T(8,128)(2,1)S(1)}, u32[]{:S(2)}, u32[]{:S(2)}) async-start(bf16[32,8,1536]{2,1,0:T(8,128)(2,1)} %bitcast.34), calls=%async_computation | async-start | bytes 1572864 | tf_op jit(solution)/shard_map/all_to_all | solution.py:140
  39.1 0.9 %copy-start = (bf16[32,8,1536]{2,1,0:T(8,128)(2,1)}, bf16[32,8,1536]{2,1,0:T(8,128)(2,1)S(1)}, u32[]{:S(2)}) copy-start(bf16[32,8,1536]{2,1,0:T(8,128)(2,1)S(1)} %all-to-all-done) | copy-start | bytes 2359300
  47.2 2.2 %collective-permute-start = (f32[520,4,64]{0,2,1:T(8,128)S(1)}, f32[520,4,64]{0,2,1:T(8,128)S(1)}, u32[]{:S(2)}, u32[]{:S(2)}) collective-permute-start(f32[520,4,64]{0,2,1:T(8,128)S(1)} %dynamic-slice_bitcast_fusion), channel_id=1, source_target_pairs={{0,1},{1,0},{2,3},{3,2},{4,5},{5,4},{6,7},{7,6},{8,9},{9,8},{10,11... | collective-permute-start | bytes 1597448 | tf_op jit(solution)/shard_map/ppermute | solution.py:157
  49.5 7.6 %collective-permute-start.1 = (f32[520,64]{0,1:T(8,128)S(1)}, f32[520,64]{0,1:T(8,128)S(1)}, u32[]{:S(2)}, u32[]{:S(2)}) collective-permute-start(f32[520,64]{0,1:T(8,128)S(1)} %get-tuple-element.2), channel_id=1, source_target_pairs={{0,2},{1,3},{2,4},{3,5},{4,6},{5,7},{6,0},{7,1},{8,10},{9,11},{10,... | collective-permute-start | bytes 399368 | tf_op jit(solution)/shard_map/ppermute | solution.py:162
  51.2 10.6 %collective-permute-start.2 = (f32[520,64]{0,1:T(8,128)S(1)}, f32[520,64]{0,1:T(8,128)S(1)}, u32[]{:S(2)}, u32[]{:S(2)}) collective-permute-start(f32[520,64]{0,1:T(8,128)S(1)} %get-tuple-element.4), channel_id=1, source_target_pairs={{0,4},{1,5},{2,6},{3,7},{4,0},{5,1},{6,2},{7,3},{8,12},{9,13},{10,... | collective-permute-start | bytes 399368 | tf_op jit(solution)/shard_map/ppermute | solution.py:162
  54.1 7.7 %collective-permute-start.3 = (f32[520,64]{0,1:T(8,128)S(1)}, f32[520,64]{0,1:T(8,128)S(1)}, u32[]{:S(2)}, u32[]{:S(2)}) collective-permute-start(f32[520,64]{0,1:T(8,128)S(1)} %get-tuple-element.3), channel_id=1, source_target_pairs={{0,6},{1,7},{2,0},{3,1},{4,2},{5,3},{6,4},{7,5},{8,14},{9,15},{10,... | collective-permute-start | bytes 399368 | tf_op jit(solution)/shard_map/ppermute | solution.py:162
  62.2 17.7 %copy-start.5 = (f32[64]{0:T(128)S(1)}, f32[64]{0:T(128)}, u32[]{:S(2)}) copy-start(f32[64]{0:T(128)} %param.15) | copy-start | bytes 772
  63.1 14.5 %all-to-all-start.1 = ((f32[32,1,1088]{2,1,0:T(1,128)}), f32[32,1,1088]{2,1,0:T(1,128)S(1)}, u32[]{:S(2)}, u32[]{:S(2)}) async-start(f32[32,1,1088]{2,1,0:T(1,128)} %reshape.48), calls=%async_computation.1 | async-start | bytes 294912 | tf_op jit(solution)/shard_map/all_to_all | solution.py:168

commit v10 on v9

--- a/solution.py
+++ b/solution.py
@@ -11,7 +11,7 @@
 def element_body(arrived_ref, slot_ref, state_ref, omega_ref, stiff_ref, out_ref, v_ref, w_ref):
     n_el = omega_ref.shape[0]
     n_slot = arrived_ref.shape[0]
-    modes = out_ref.shape[1]
+    modes = out_ref.shape[0]
     slots = slot_ref[...]
     lane = lax.broadcasted_iota(jnp.int32, (8 * n_el, n_slot), 1)
     onehot = (slots == lane).astype(jnp.bfloat16)
@@ -76,14 +76,14 @@
             img = img + (lam * G[a][c]) * trace
             img = img + 0.25 * v_ref[corner_rows(a, c), :].astype(jnp.float32)
             w_ref[corner_rows(a, c), :] = (omega * img).astype(jnp.bfloat16)
-    tangent = lax.dot_general(
-        v_ref[...], w_ref[...], (((0,), (0,)), ((), ())), preferred_element_type=jnp.float32
+    tangent_t = lax.dot_general(
+        w_ref[...], v_ref[...], (((0,), (0,)), ((), ())), preferred_element_type=jnp.float32
     )
-    out_ref[pl.ds(0, modes), :] = tangent
-    force_row = jnp.sum(force_acc, axis=0, keepdims=True)
-    out_ref[pl.ds(modes, 8), :] = jnp.concatenate(
-        [force_row, jnp.zeros((7, modes), jnp.float32)], axis=0
+    out_ref[:, pl.ds(0, modes)] = tangent_t
+    force_rows = jnp.concatenate(
+        [jnp.sum(force_acc, axis=0, keepdims=True), jnp.zeros((7, modes), jnp.float32)], axis=0
     )
+    out_ref[:, pl.ds(modes, 8)] = jnp.transpose(force_rows)
 
 
 def element_stage(arrived3, slot, state, omega, stiff):
@@ -96,7 +96,7 @@
     vmem = pltpu.MemorySpace.VMEM if hasattr(pltpu, "MemorySpace") else pltpu.TPUMemorySpace.VMEM
     return pl.pallas_call(
         element_body,
-        out_shape=jax.ShapeDtypeStruct((modes + 8, modes), jnp.float32),
+        out_shape=jax.ShapeDtypeStruct((modes, modes + 8), jnp.float32),
         in_specs=[pl.BlockSpec(memory_space=vmem)] * 5,
         out_specs=pl.BlockSpec(memory_space=vmem),
         scratch_shapes=[
@@ -144,7 +144,7 @@
     live = lax.dynamic_index_in_dim(set_size, set_index, keepdims=False)
     position = block_index * element_count + jnp.arange(element_count, dtype=jnp.int32)
     weights = jnp.where(position < live, elem_weight, jnp.zeros_like(elem_weight))
-    stacked = element_stage(arrived, elem_slot, state, weights, element_stiffening)
+    stacked = element_stage(arrived, elem_slot, state, weights, element_stiffening).T
     rows = basis_modes // n_elem
     cols = basis_modes // n_blk
     n_y = n_blk // 2

time: 81.9 us -> 83.4 us (1.018)
  waiting for transfers between devices: 33 us -> 36.3 us
  starting transfers between devices: 23.3 us -> 22.1 us
    ppermute x3, waiting for transfers between devices: 6.38 us -> 9.37 us  [local(): halfway = halfway + lax.ppermute(piece, 'blk', ring)]
    pallas_call x1 -> x0, local copies, waits for them, and re-layouts: 1.63 us -> none  [element_stage(): pl.pallas_call(element_body, out_shape=jax.ShapeDtypeStruct((modes + 8, m...]
    ppermute x3, starting transfers between devices: 5.92 us -> 4.71 us  [local(): halfway = halfway + lax.ppermute(piece, 'blk', ring)]
    squeeze x1, local copies, waits for them, and re-layouts: 0.05 us -> 1.24 us  [local(): sent = lax.dynamic_index_in_dim(by_dest, 1 - core, axis=2, keepdims=False)]
    unnamed x16 -> x18, local copies, waits for them, and re-layouts: 1.89 us -> 1.89 us
  transfers between devices with their start and end apart: 6 -> 6, of which waited for: 5 -> 6; matrix products, arithmetic and copies ran while one was open for 7% -> 7% of each run, Pallas kernels for 0% -> 0%
where the time goes in v10:
time: 83.4 us; the launch traced here: 82.3 us
  waiting for transfers between devices  36.3 us (44%)
  starting transfers between devices  22.1 us (26%)
  Pallas kernels  10.1 us (12%)
  local copies, waits for them, and re-layouts  6.83 us (8%)
  other arithmetic  5.31 us (6%)
  between operations  1.57 us (2%)
    all_to_all x1, waiting for transfers between devices, local(): lax.all_to_all(outgoing, 'elem', split_axis=0, concat_axis=0, tiled=True)  17.1 us
    all_to_all x1, starting transfers between devices, local(): lax.all_to_all(outgoing, 'elem', split_axis=0, concat_axis=0, tiled=True)  11.8 us
    ppermute x3, waiting for transfers between devices, local(): halfway = halfway + lax.ppermute(piece, 'blk', ring)  9.37 us
    all_to_all x1, waiting for transfers between devices, local(): lax.all_to_all(chunks, 'elem', split_axis=0, concat_axis=0, tiled=True)  7.83 us
    pallas_call x1, Pallas kernels, element_stage(): pl.pallas_call(element_body, out_shape=jax.ShapeDtypeStruct((modes, modes...  5.85 us
    all_to_all x1, starting transfers between devices, local(): lax.all_to_all(chunks, 'elem', split_axis=0, concat_axis=0, tiled=True)  5.57 us
    ppermute x3, starting transfers between devices, local(): halfway = halfway + lax.ppermute(piece, 'blk', ring)  4.71 us
    pallas_call x1, Pallas kernels, gather_rows(): pl.pallas_call(gather_body, out_shape=jax.ShapeDtypeStruct((n_rows, comps...  4.24 us
  transfers between devices with their start and end apart: 6, of which 6 were waited for; matrix products, arithmetic and copies ran while one was open for 7% of the time, Pallas kernels for 0%

profile of v10, /device:TPU:2, one launch (start us, length us, event | category | flops | bytes accessed | tf_op | source)
XLA Modules:
  0.0 82.3 jit_solution(16567742326505779551)
XLA Ops:
  0.6 4.2 %shard_map.95 = bf16[256,1536]{1,0:T(8,128)(2,1)} custom-call(bf16[3,1024,512]{2,1,0:T(8,128)(2,1)} %bitcast.34, s32[1,256]{1,0:T(1,128)} %bitcast.38), custom_call_target="tpu_custom_call" | custom-call | tf_op jit(solution)/shard_map/pallas_call | solution.py:123
  4.9 11.8 %all-to-all-start = ((bf16[32,8,1536]{2,1,0:T(8,128)(2,1)}), bf16[32,8,1536]{2,1,0:T(8,128)(2,1)S(1)}, u32[]{:S(2)}, u32[]{:S(2)}) async-start(bf16[32,8,1536]{2,1,0:T(8,128)(2,1)} %bitcast.36), calls=%async_computation | async-start | bytes 1572864 | tf_op jit(solution)/shard_map/all_to_all | solution.py:140
  16.7 0.9 %reshape.46.slot_ref = s32[512,1]{1,0:T(8,128)} reshape(s32[8,64]{1,0:T(8,128)S(1)} %copy-done.2) | data formatting | bytes 4096 | tf_op jit(solution)/shard_map/reshape | solution.py:106
  17.6 0.6 dynamic_slice.24
  18.2 0.6 fusion.6
  18.9 0.7 copy.19.omega_ref
  19.6 0.7 copy.20.stiff_ref
  20.3 1.7 %fusion.state_ref = bf16[1536,128]{1,0:T(8,128)(2,1)} fusion(s32[1536]{0:T(1024)S(1)} %add_select_fusion, bf16[1536]{0:T(1024)(128)(2,1)S(1)} %broadcast_in_dim.26), kind=kLoop, calls=%fused_computation.1 | loop fusion | flops 393216 | bytes 402432 | tf_op jit(solution)/shard_map/jit(_where)/select_n | solution.py:93
  22.0 17.1 %all-to-all-done = bf16[32,8,1536]{2,1,0:T(8,128)(2,1)S(1)} async-done(((bf16[32,8,1536]{2,1,0:T(8,128)(2,1)}), bf16[32,8,1536]{2,1,0:T(8,128)(2,1)S(1)}, u32[]{:S(2)}, u32[]{:S(2)}) %all-to-all-start) | async-done | bytes 786464 | tf_op jit(solution)/shard_map/all_to_all | solution.py:140
  39.1 0.9 %copy-done.1 = bf16[32,8,1536]{2,1,0:T(8,128)(2,1)} copy-done((bf16[32,8,1536]{2,1,0:T(8,128)(2,1)}, bf16[32,8,1536]{2,1,0:T(8,128)(2,1)S(1)}, u32[]{:S(2)}) %copy-start.1) | copy-done | bytes 786456
  40.0 5.9 %shard_map.96 = f32[512,520]{1,0:T(8,128)} custom-call(bf16[256,1536]{1,0:T(8,128)(2,1)} %bitcast.35, s32[512,1]{1,0:T(8,128)} %reshape.46.slot_ref, bf16[1536,128]{1,0:T(8,128)(2,1)} %fusion.state_ref, f32[64,1]{1,0:T(8,128)} %copy.19.omega_ref, f32[64,1]{1,0:T(8,128)} %copy.20.stiff_ref), custom_call_target="tpu_custom_call" | custom-call | tf_op jit(solution)/shard_map/pallas_call | solution.py:97
  45.9 1.2 %dynamic-slice_bitcast_fusion = f32[520,4,64]{0,2,1:T(8,128)S(1)} fusion(f32[520,4,2,64]{0,3,2,1:T(8,128)} %bitcast.32, s32[]{:T(128)S(6)} %select_n.70), kind=kLoop, calls=%fused_computation.3 | loop fusion | bytes 1064964 | tf_op jit(solution)/shard_map/jit(dynamic_index_in_dim)/squeeze | solution.py:155
  47.1 0.1 collective-permute-start
  47.3 2.0 %collective-permute-done = f32[520,4,64]{0,2,1:T(8,128)S(1)} collective-permute-done((f32[520,4,64]{0,2,1:T(8,128)S(1)}, f32[520,4,64]{0,2,1:T(8,128)S(1)}, u32[]{:S(2)}, u32[]{:S(2)}) %collective-permute-start) | collective-permute-done | bytes 532512 | tf_op jit(solution)/shard_map/ppermute | solution.py:157
  49.3 0.1 bitcast_add_fusion
  49.4 3.1 %collective-permute-start.3 = (f32[520,64]{0,1:T(8,128)S(1)}, f32[520,64]{0,1:T(8,128)S(1)}, u32[]{:S(2)}, u32[]{:S(2)}) collective-permute-start(f32[520,64]{0,1:T(8,128)S(1)} %get-tuple-element.3), channel_id=1, source_target_pairs={{0,6},{1,7},{2,0},{3,1},{4,2},{5,3},{6,4},{7,5},{8,14},{9,15},{10,... | collective-permute-start | bytes 399368 | tf_op jit(solution)/shard_map/ppermute | solution.py:162
  52.6 0.6 collective-permute-start.2
  53.2 1.0 %collective-permute-start.1 = (f32[520,64]{0,1:T(8,128)S(1)}, f32[520,64]{0,1:T(8,128)S(1)}, u32[]{:S(2)}, u32[]{:S(2)}) collective-permute-start(f32[520,64]{0,1:T(8,128)S(1)} %get-tuple-element.2), channel_id=1, source_target_pairs={{0,2},{1,3},{2,4},{3,5},{4,6},{5,7},{6,0},{7,1},{8,10},{9,11},{10,... | collective-permute-start | bytes 399368 | tf_op jit(solution)/shard_map/ppermute | solution.py:162
  54.2 5.7 %collective-permute-done.3 = f32[520,64]{0,1:T(8,128)S(1)} collective-permute-done((f32[520,64]{0,1:T(8,128)S(1)}, f32[520,64]{0,1:T(8,128)S(1)}, u32[]{:S(2)}, u32[]{:S(2)}) %collective-permute-start.3) | collective-permute-done | bytes 133152 | tf_op jit(solution)/shard_map/ppermute | solution.py:162
  59.8 1.4 %collective-permute-done.2 = f32[520,64]{0,1:T(8,128)S(1)} collective-permute-done((f32[520,64]{0,1:T(8,128)S(1)}, f32[520,64]{0,1:T(8,128)S(1)}, u32[]{:S(2)}, u32[]{:S(2)}) %collective-permute-start.2) | collective-permute-done | bytes 133152 | tf_op jit(solution)/shard_map/ppermute | solution.py:162
  61.2 2.3 %collective-permute-done.1 = f32[520,64]{0,1:T(8,128)S(1)} collective-permute-done((f32[520,64]{0,1:T(8,128)S(1)}, f32[520,64]{0,1:T(8,128)S(1)}, u32[]{:S(2)}, u32[]{:S(2)}) %collective-permute-start.1) | collective-permute-done | bytes 133152 | tf_op jit(solution)/shard_map/ppermute | solution.py:162
  63.6 0.1 slice_reduce_fusion
  63.7 0.1 copy.21
  63.9 0.8 %reshape.48 = f32[32,1,1088]{2,1,0:T(1,128)} reshape(f32[32,17,64]{2,1,0:T(8,128)S(1)} %pad_maximum_fusion) | data formatting | bytes 278528
  64.7 5.6 %all-to-all-start.1 = ((f32[32,1,1088]{2,1,0:T(1,128)}), f32[32,1,1088]{2,1,0:T(1,128)S(1)}, u32[]{:S(2)}, u32[]{:S(2)}) async-start(f32[32,1,1088]{2,1,0:T(1,128)} %reshape.48), calls=%async_computation.1 | async-start | bytes 294912 | tf_op jit(solution)/shard_map/all_to_all | solution.py:168
  70.3 0.6 reduce_sum.19
  71.6 7.8 %all-to-all-done.1 = f32[32,1,1088]{2,1,0:T(1,128)S(1)} async-done(((f32[32,1,1088]{2,1,0:T(1,128)}), f32[32,1,1088]{2,1,0:T(1,128)S(1)}, u32[]{:S(2)}, u32[]{:S(2)}) %all-to-all-start.1) | async-done | bytes 139296 | tf_op jit(solution)/shard_map/all_to_all | solution.py:168
  79.5 0.5 broadcast.43
  80.0 1.0 %reduce.2 = f32[32,1088]{1,0:T(8,128)S(1)} reduce(f32[32,1,1088]{2,1,0:T(1,128)S(1)} %all-to-all-done.1, f32[]{:T(128)} %broadcast.43), dimensions={1}, to_apply=%all_to_all.13.reduce_sub_computation | reduce | bytes 278532 | tf_op jit(solution)/shard_map/all_to_all | solution.py:168
  81.0 0.1 reshape.49
  81.1 0.6 slice_multiply_fusion
  81.7 0.5 fusion.8
  (24 shorter events, 0.2 us)
Async XLA Ops:
  4.9 11.8 %copy-start.2 = (s32[8,64]{1,0:T(8,128)S(1)}, s32[8,64]{1,0:T(8,128)}, u32[]{:S(2)}) copy-start(s32[8,64]{1,0:T(8,128)} %param.10) | copy-start | bytes 6148
  4.9 12.7 %copy-start.3 = (bf16[512]{0:T(512)(128)(2,1)S(1)}, bf16[512]{0:T(512)(128)(2,1)}, u32[]{:S(2)}) copy-start(bf16[512]{0:T(512)(128)(2,1)} %param.14) | copy-start | bytes 3076
  4.9 12.7 %copy-start.7 = (s32[32]{0:T(128)S(1)}, s32[32]{0:T(128)}, u32[]{:S(2)}) copy-start(s32[32]{0:T(128)} %param.11) | copy-start | bytes 388
  4.9 13.3 %copy-start.5 = (f32[64]{0:T(128)S(1)}, f32[64]{0:T(128)}, u32[]{:S(2)}) copy-start(f32[64]{0:T(128)} %param.12) | copy-start | bytes 772
  4.9 14.7 %copy-start.4 = (f32[64]{0:T(128)S(1)}, f32[64]{0:T(128)}, u32[]{:S(2)}) copy-start(f32[64]{0:T(128)} %param.13) | copy-start | bytes 772
  4.9 34.2 %all-to-all-start = ((bf16[32,8,1536]{2,1,0:T(8,128)(2,1)}), bf16[32,8,1536]{2,1,0:T(8,128)(2,1)S(1)}, u32[]{:S(2)}, u32[]{:S(2)}) async-start(bf16[32,8,1536]{2,1,0:T(8,128)(2,1)} %bitcast.36), calls=%async_computation | async-start | bytes 1572864 | tf_op jit(solution)/shard_map/all_to_all | solution.py:140
  39.1 0.9 %copy-start.1 = (bf16[32,8,1536]{2,1,0:T(8,128)(2,1)}, bf16[32,8,1536]{2,1,0:T(8,128)(2,1)S(1)}, u32[]{:S(2)}) copy-start(bf16[32,8,1536]{2,1,0:T(8,128)(2,1)S(1)} %all-to-all-done) | copy-start | bytes 2359300
  45.9 3.4 %copy-start = (f32[512,520]{1,0:T(8,128)S(1)}, f32[512,520]{1,0:T(8,128)}, u32[]{:S(2)}) copy-start(f32[512,520]{1,0:T(8,128)} %shard_map.96) | copy-start | bytes 3194884
  47.1 2.2 %collective-permute-start = (f32[520,4,64]{0,2,1:T(8,128)S(1)}, f32[520,4,64]{0,2,1:T(8,128)S(1)}, u32[]{:S(2)}, u32[]{:S(2)}) collective-permute-start(f32[520,4,64]{0,2,1:T(8,128)S(1)} %dynamic-slice_bitcast_fusion), channel_id=1, source_target_pairs={{0,1},{1,0},{2,3},{3,2},{4,5},{5,4},{6,7},{7,6},{8,9},{9,8},{10,11... | collective-permute-start | bytes 1597448 | tf_op jit(solution)/shard_map/ppermute | solution.py:157
  49.4 10.4 %collective-permute-start.3 = (f32[520,64]{0,1:T(8,128)S(1)}, f32[520,64]{0,1:T(8,128)S(1)}, u32[]{:S(2)}, u32[]{:S(2)}) collective-permute-start(f32[520,64]{0,1:T(8,128)S(1)} %get-tuple-element.3), channel_id=1, source_target_pairs={{0,6},{1,7},{2,0},{3,1},{4,2},{5,3},{6,4},{7,5},{8,14},{9,15},{10,... | collective-permute-start | bytes 399368 | tf_op jit(solution)/shard_map/ppermute | solution.py:162
  52.6 8.6 %collective-permute-start.2 = (f32[520,64]{0,1:T(8,128)S(1)}, f32[520,64]{0,1:T(8,128)S(1)}, u32[]{:S(2)}, u32[]{:S(2)}) collective-permute-start(f32[520,64]{0,1:T(8,128)S(1)} %get-tuple-element.4), channel_id=1, source_target_pairs={{0,4},{1,5},{2,6},{3,7},{4,0},{5,1},{6,2},{7,3},{8,12},{9,13},{10,... | collective-permute-start | bytes 399368 | tf_op jit(solution)/shard_map/ppermute | solution.py:162
  53.2 10.3 %collective-permute-start.1 = (f32[520,64]{0,1:T(8,128)S(1)}, f32[520,64]{0,1:T(8,128)S(1)}, u32[]{:S(2)}, u32[]{:S(2)}) collective-permute-start(f32[520,64]{0,1:T(8,128)S(1)} %get-tuple-element.2), channel_id=1, source_target_pairs={{0,2},{1,3},{2,4},{3,5},{4,6},{5,7},{6,0},{7,1},{8,10},{9,11},{10,... | collective-permute-start | bytes 399368 | tf_op jit(solution)/shard_map/ppermute | solution.py:162
  63.8 17.9 %copy-start.6 = (f32[64]{0:T(128)S(1)}, f32[64]{0:T(128)}, u32[]{:S(2)}) copy-start(f32[64]{0:T(128)} %param.15) | copy-start | bytes 772
  64.7 14.7 %all-to-all-start.1 = ((f32[32,1,1088]{2,1,0:T(1,128)}), f32[32,1,1088]{2,1,0:T(1,128)S(1)}, u32[]{:S(2)}, u32[]{:S(2)}) async-start(f32[32,1,1088]{2,1,0:T(1,128)} %reshape.48), calls=%async_computation.1 | async-start | bytes 294912 | tf_op jit(solution)/shard_map/all_to_all | solution.py:168

commit v11 on v9

--- a/solution.py
+++ b/solution.py
@@ -155,17 +155,13 @@
     sent = lax.dynamic_index_in_dim(by_dest, 1 - core, axis=2, keepdims=False)
     kept = lax.dynamic_index_in_dim(by_dest, core, axis=2, keepdims=False)
     chip_sum = kept + lax.ppermute(sent, "blk", pair)
-    halfway = lax.dynamic_index_in_dim(chip_sum, chip, axis=1, keepdims=False)
-    for shift in range(1, n_y):
-        ring = [(2 * y + c, 2 * ((y + shift) % n_y) + c) for y in range(n_y) for c in range(2)]
-        piece = lax.dynamic_index_in_dim(chip_sum, (chip + shift) % n_y, axis=1, keepdims=False)
-        halfway = halfway + lax.ppermute(piece, "blk", ring)
-    force_cols = halfway[basis_modes]
-    tangent_rows = halfway[:basis_modes].reshape(n_elem, rows, cols)
-    chunks = jnp.concatenate(
-        [tangent_rows, jnp.broadcast_to(force_cols[None, None, :], (n_elem, 1, cols))], axis=1
+    tang = chip_sum[:basis_modes].reshape(n_elem, rows, n_y, cols).transpose(0, 2, 1, 3)
+    force_part = jnp.broadcast_to(chip_sum[basis_modes][None, :, None, :], (n_elem, n_y, 1, cols))
+    chunks = jnp.concatenate([tang, force_part], axis=2).reshape(n_elem * n_y, rows + 1, cols)
+    groups = [[e * n_blk + 2 * y + c for e in range(n_elem) for y in range(n_y)] for c in range(2)]
+    arrived_chunks = lax.all_to_all(
+        chunks, ("elem", "blk"), split_axis=0, concat_axis=0, axis_index_groups=groups, tiled=True
     )
-    arrived_chunks = lax.all_to_all(chunks, "elem", split_axis=0, concat_axis=0, tiled=True)
     mine = jnp.sum(arrived_chunks, axis=0)
     scale = lax.rsqrt(24.0 * jnp.sum(set_size).astype(jnp.float32))
     return (mine[:rows] * scale, mine[rows] * scale - load)

time: 81.9 us -> 88.8 us (1.084); the launches traced: 80.3 us -> 88.3 us
  waiting for transfers between devices: 33 us -> 39.5 us
  local copies, waits for them, and re-layouts: 7.28 us -> 9.78 us
  starting transfers between devices: 23.3 us -> 21.2 us
  other arithmetic: 5.33 us -> 6.56 us
    all_to_all x1, waiting for transfers between devices: 7.58 us -> 20.3 us  [local(): lax.all_to_all(chunks, ('elem', 'blk'), split_axis=0, concat_axis=0, axis...]
    ppermute x3 -> x0, waiting for transfers between devices: 6.38 us -> none  [local(): halfway = halfway + lax.ppermute(piece, 'blk', ring)]
    ppermute x3 -> x0, starting transfers between devices: 5.92 us -> none  [local(): halfway = halfway + lax.ppermute(piece, 'blk', ring)]
    all_to_all x1, starting transfers between devices: 5.57 us -> 9.4 us  [local(): lax.all_to_all(chunks, ('elem', 'blk'), split_axis=0, concat_axis=0, axis...]
    all_to_all x1, other arithmetic: 0.99 us -> 2.05 us  [local(): lax.all_to_all(chunks, ('elem', 'blk'), split_axis=0, concat_axis=0, axis...]
  transfers between devices with their start and end apart: 6 -> 3, of which waited for: 5 -> 3; matrix products, arithmetic and copies ran while one was open for 7% -> 7% of each run, Pallas kernels for 0% -> 0%
where the time goes in v11:
time: 88.8 us; the launch traced here: 88.3 us
  waiting for transfers between devices  39.5 us (44%)
  starting transfers between devices  21.2 us (24%)
  local copies, waits for them, and re-layouts  9.78 us (11%)
  Pallas kernels  9.75 us (11%)
  other arithmetic  6.56 us (7%)
  between operations  1.51 us (2%)
    all_to_all x1, waiting for transfers between devices, local(): lax.all_to_all(chunks, ('elem', 'blk'), split_axis=0, concat_axis=0, axis...  20.3 us
    all_to_all x1, waiting for transfers between devices, local(): lax.all_to_all(outgoing, 'elem', split_axis=0, concat_axis=0, tiled=True)  17.1 us
    all_to_all x1, starting transfers between devices, local(): lax.all_to_all(outgoing, 'elem', split_axis=0, concat_axis=0, tiled=True)  11.8 us
    all_to_all x1, starting transfers between devices, local(): lax.all_to_all(chunks, ('elem', 'blk'), split_axis=0, concat_axis=0, axis...  9.4 us
    pallas_call x1, Pallas kernels, element_stage(): pl.pallas_call(element_body, out_shape=jax.ShapeDtypeStruct((modes + 8, m...  5.5 us
    pallas_call x1, Pallas kernels, gather_rows(): pl.pallas_call(gather_body, out_shape=jax.ShapeDtypeStruct((n_rows, comps...  4.25 us
    unnamed x16, local copies, waits for them, and re-layouts  2.75 us
    ppermute x1, waiting for transfers between devices, local(): chip_sum = kept + lax.ppermute(sent, 'blk', pair)  2.08 us
  transfers between devices with their start and end apart: 3, of which 3 were waited for; matrix products, arithmetic and copies ran while one was open for 7% of the time, Pallas kernels for 0%

profile of v11, /device:TPU:2, one launch (start us, length us, event | category | flops | bytes accessed | tf_op | source)
XLA Modules:
  0.0 88.3 jit_solution(1925023525340952197)
XLA Ops:
  0.6 4.2 %shard_map.95 = bf16[256,1536]{1,0:T(8,128)(2,1)} custom-call(bf16[3,1024,512]{2,1,0:T(8,128)(2,1)} %bitcast.25, s32[1,256]{1,0:T(1,128)} %bitcast.28), custom_call_target="tpu_custom_call" | custom-call | tf_op jit(solution)/shard_map/pallas_call | solution.py:123
  4.9 11.8 %all-to-all-start = ((bf16[32,8,1536]{2,1,0:T(8,128)(2,1)}), bf16[32,8,1536]{2,1,0:T(8,128)(2,1)S(1)}, u32[]{:S(2)}, u32[]{:S(2)}) async-start(bf16[32,8,1536]{2,1,0:T(8,128)(2,1)} %bitcast.27), calls=%async_computation | async-start | bytes 1572864 | tf_op jit(solution)/shard_map/all_to_all | solution.py:140
  16.7 0.6 dynamic_slice.11
  17.3 0.6 fusion.4
  17.9 0.7 copy.28.omega_ref
  18.7 0.9 %reshape.50.slot_ref = s32[512,1]{1,0:T(8,128)} reshape(s32[8,64]{1,0:T(8,128)S(1)} %copy-done.1) | data formatting | bytes 4096 | tf_op jit(solution)/shard_map/reshape | solution.py:106
  19.6 0.7 copy.29.stiff_ref
  20.3 1.7 %fusion.state_ref = bf16[1536,128]{1,0:T(8,128)(2,1)} fusion(s32[1536]{0:T(1024)S(1)} %add_select_fusion, bf16[1536]{0:T(1024)(128)(2,1)S(1)} %broadcast_in_dim.26), kind=kLoop, calls=%fused_computation.2 | loop fusion | flops 393216 | bytes 402432 | tf_op jit(solution)/shard_map/jit(_where)/select_n | solution.py:93
  22.0 17.1 %all-to-all-done = bf16[32,8,1536]{2,1,0:T(8,128)(2,1)S(1)} async-done(((bf16[32,8,1536]{2,1,0:T(8,128)(2,1)}), bf16[32,8,1536]{2,1,0:T(8,128)(2,1)S(1)}, u32[]{:S(2)}, u32[]{:S(2)}) %all-to-all-start) | async-done | bytes 786464 | tf_op jit(solution)/shard_map/all_to_all | solution.py:140
  39.1 0.9 %copy-done = bf16[32,8,1536]{2,1,0:T(8,128)(2,1)} copy-done((bf16[32,8,1536]{2,1,0:T(8,128)(2,1)}, bf16[32,8,1536]{2,1,0:T(8,128)(2,1)S(1)}, u32[]{:S(2)}) %copy-start) | copy-done | bytes 786456
  40.0 5.5 %shard_map.96 = f32[520,512]{1,0:T(8,128)} custom-call(bf16[256,1536]{1,0:T(8,128)(2,1)} %bitcast.26, s32[512,1]{1,0:T(8,128)} %reshape.50.slot_ref, bf16[1536,128]{1,0:T(8,128)(2,1)} %fusion.state_ref, f32[64,1]{1,0:T(8,128)} %copy.28.omega_ref, f32[64,1]{1,0:T(8,128)} %copy.29.stiff_ref), custom_call_target="tpu_custom_call" | custom-call | tf_op jit(solution)/shard_map/pallas_call | solution.py:97
  45.5 1.6 %copy.30 = f32[520,512]{0,1:T(8,128)S(1)} copy(f32[520,512]{1,0:T(8,128)} %shard_map.96) | data formatting | bytes 2129920 | tf_op jit(solution)/shard_map/pallas_call | solution.py:97
  47.2 0.1 dynamic-slice_bitcast_fusion
  47.2 0.1 collective-permute-start
  47.3 2.1 %collective-permute-done = f32[520,4,64]{0,2,1:T(8,128)S(1)} collective-permute-done((f32[520,4,64]{0,2,1:T(8,128)S(1)}, f32[520,4,64]{0,2,1:T(8,128)S(1)}, u32[]{:S(2)}, u32[]{:S(2)}) %collective-permute-start) | collective-permute-done | bytes 532512 | tf_op jit(solution)/shard_map/ppermute | solution.py:157
  49.4 0.1 bitcast_add_fusion
  49.5 0.1 slice.16
  49.6 0.1 slice_reduce_fusion
  49.7 0.3 copy.31
  50.1 0.1 pad_maximum_fusion
  50.2 0.7 copy.32
  50.9 0.7 copy.33
  51.6 1.6 %reshape.52 = f32[128,1,1088]{2,1,0:T(1,128)} reshape(f32[128,17,64]{2,1,0:T(8,128)S(1)} %copy.33) | data formatting | bytes 1114112
  53.2 9.4 %all-to-all-start.1 = ((f32[128,1,1088]{2,1,0:T(1,128)}), f32[128,1,1088]{2,1,0:T(1,128)S(1)}, u32[]{:S(2)}, u32[]{:S(2)}) async-start(f32[128,1,1088]{2,1,0:T(1,128)} %reshape.52), calls=%async_computation.1 | async-start | bytes 1179648 | tf_op jit(solution)/shard_map/all_to_all | solution.py:162
  62.6 0.6 reduce_sum.19
  63.9 20.3 %all-to-all-done.1 = f32[128,1,1088]{2,1,0:T(1,128)S(1)} async-done(((f32[128,1,1088]{2,1,0:T(1,128)}), f32[128,1,1088]{2,1,0:T(1,128)S(1)}, u32[]{:S(2)}, u32[]{:S(2)}) %all-to-all-start.1) | async-done | bytes 557088 | tf_op jit(solution)/shard_map/all_to_all | solution.py:162
  84.2 0.5 broadcast.39
  84.8 2.0 %reduce.2 = f32[128,1088]{1,0:T(8,128)S(1)} reduce(f32[128,1,1088]{2,1,0:T(1,128)S(1)} %all-to-all-done.1, f32[]{:T(128)} %broadcast.39), dimensions={1}, to_apply=%all_to_all.13.reduce_sub_computation | reduce | bytes 1114116 | tf_op jit(solution)/shard_map/all_to_all | solution.py:162
  86.8 0.2 reshape.53
  87.1 0.2 reduce_sum.18
  87.2 0.6 slice_multiply_fusion
  87.8 0.5 fusion.6
  (17 shorter events, 0.1 us)
Async XLA Ops:
  4.9 11.8 %copy-start.6 = (s32[32]{0:T(128)S(1)}, s32[32]{0:T(128)}, u32[]{:S(2)}) copy-start(s32[32]{0:T(128)} %param.11) | copy-start | bytes 388
  4.9 12.4 %copy-start.4 = (f32[64]{0:T(128)S(1)}, f32[64]{0:T(128)}, u32[]{:S(2)}) copy-start(f32[64]{0:T(128)} %param.12) | copy-start | bytes 772
  4.9 13.8 %copy-start.2 = (bf16[512]{0:T(512)(128)(2,1)S(1)}, bf16[512]{0:T(512)(128)(2,1)}, u32[]{:S(2)}) copy-start(bf16[512]{0:T(512)(128)(2,1)} %param.14) | copy-start | bytes 3076
  4.9 13.8 %copy-start.1 = (s32[8,64]{1,0:T(8,128)S(1)}, s32[8,64]{1,0:T(8,128)}, u32[]{:S(2)}) copy-start(s32[8,64]{1,0:T(8,128)} %param.10) | copy-start | bytes 6148
  4.9 14.7 %copy-start.3 = (f32[64]{0:T(128)S(1)}, f32[64]{0:T(128)}, u32[]{:S(2)}) copy-start(f32[64]{0:T(128)} %param.13) | copy-start | bytes 772
  4.9 34.2 %all-to-all-start = ((bf16[32,8,1536]{2,1,0:T(8,128)(2,1)}), bf16[32,8,1536]{2,1,0:T(8,128)(2,1)S(1)}, u32[]{:S(2)}, u32[]{:S(2)}) async-start(bf16[32,8,1536]{2,1,0:T(8,128)(2,1)} %bitcast.27), calls=%async_computation | async-start | bytes 1572864 | tf_op jit(solution)/shard_map/all_to_all | solution.py:140
  39.1 0.9 %copy-start = (bf16[32,8,1536]{2,1,0:T(8,128)(2,1)}, bf16[32,8,1536]{2,1,0:T(8,128)(2,1)S(1)}, u32[]{:S(2)}) copy-start(bf16[32,8,1536]{2,1,0:T(8,128)(2,1)S(1)} %all-to-all-done) | copy-start | bytes 2359300
  47.2 2.2 %collective-permute-start = (f32[520,4,64]{0,2,1:T(8,128)S(1)}, f32[520,4,64]{0,2,1:T(8,128)S(1)}, u32[]{:S(2)}, u32[]{:S(2)}) collective-permute-start(f32[520,4,64]{0,2,1:T(8,128)S(1)} %dynamic-slice_bitcast_fusion), channel_id=1, source_target_pairs={{0,1},{1,0},{2,3},{3,2},{4,5},{5,4},{6,7},{7,6},{8,9},{9,8},{10,11... | collective-permute-start | bytes 1597448 | tf_op jit(solution)/shard_map/ppermute | solution.py:157
  53.2 31.1 %all-to-all-start.1 = ((f32[128,1,1088]{2,1,0:T(1,128)}), f32[128,1,1088]{2,1,0:T(1,128)S(1)}, u32[]{:S(2)}, u32[]{:S(2)}) async-start(f32[128,1,1088]{2,1,0:T(1,128)} %reshape.52), calls=%async_computation.1 | async-start | bytes 1179648 | tf_op jit(solution)/shard_map/all_to_all | solution.py:162
  86.8 1.0 %copy-start.5 = (f32[64]{0:T(128)S(1)}, f32[64]{0:T(128)}, u32[]{:S(2)}) copy-start(f32[64]{0:T(128)} %param.15) | copy-start | bytes 772

commit v12 on v9

--- a/solution.py
+++ b/solution.py
@@ -165,8 +165,15 @@
     chunks = jnp.concatenate(
         [tangent_rows, jnp.broadcast_to(force_cols[None, None, :], (n_elem, 1, cols))], axis=1
     )
-    arrived_chunks = lax.all_to_all(chunks, "elem", split_axis=0, concat_axis=0, tiled=True)
-    mine = jnp.sum(arrived_chunks, axis=0)
+    n_x = 4
+    n_z = n_elem // n_x
+    by_x = chunks.reshape(n_z, n_x, rows + 1, cols).transpose(1, 0, 2, 3)
+    x_groups = [[z * n_x + x for x in range(n_x)] for z in range(n_z)]
+    z_groups = [[z * n_x + x for z in range(n_z)] for x in range(n_x)]
+    along_x = lax.all_to_all(by_x, "elem", 0, 0, axis_index_groups=x_groups, tiled=True)
+    partial = jnp.sum(along_x.reshape(n_x, n_z, rows + 1, cols), axis=0)
+    along_z = lax.all_to_all(partial, "elem", 0, 0, axis_index_groups=z_groups, tiled=True)
+    mine = jnp.sum(along_z, axis=0)
     scale = lax.rsqrt(24.0 * jnp.sum(set_size).astype(jnp.float32))
     return (mine[:rows] * scale, mine[rows] * scale - load)
 

time: 81.9 us -> 88.5 us (1.081)
  blocking collectives: 0 us -> 9.16 us
  starting transfers between devices: 23.3 us -> 21.1 us
  waiting for transfers between devices: 33 us -> 32.1 us
    all_to_all x0 -> x1, blocking collectives: none -> 9.16 us  [local(): lax.all_to_all(by_x, 'elem', 0, 0, axis_index_groups=x_groups, tiled=True)]
    all_to_all x1, starting transfers between devices: 5.57 us -> 3.34 us  [local(): lax.all_to_all(partial, 'elem', 0, 0, axis_index_groups=z_groups, tiled=T...]
    all_to_all x1, waiting for transfers between devices: 7.58 us -> 6.66 us  [local(): lax.all_to_all(partial, 'elem', 0, 0, axis_index_groups=z_groups, tiled=T...]
    unnamed x16 -> x18, local copies, waits for them, and re-layouts: 1.89 us -> 2.07 us
where the time goes in v12:
time: 88.5 us; the launch traced here: 87.5 us
  waiting for transfers between devices  32.1 us (36%)
  starting transfers between devices  21.1 us (24%)
  Pallas kernels  9.75 us (11%)
  blocking collectives  9.16 us (10%)
  local copies, waits for them, and re-layouts  7.67 us (9%)
  other arithmetic  6.08 us (7%)
  between operations  1.61 us (2%)
    all_to_all x1, waiting for transfers between devices, local(): lax.all_to_all(outgoing, 'elem', split_axis=0, concat_axis=0, tiled=True)  17.1 us
    all_to_all x1, starting transfers between devices, local(): lax.all_to_all(outgoing, 'elem', split_axis=0, concat_axis=0, tiled=True)  11.8 us
    all_to_all x1, blocking collectives, local(): lax.all_to_all(by_x, 'elem', 0, 0, axis_index_groups=x_groups, tiled=True)  9.16 us
    all_to_all x1, waiting for transfers between devices, local(): lax.all_to_all(partial, 'elem', 0, 0, axis_index_groups=z_groups, tiled=T...  6.66 us
    ppermute x3, waiting for transfers between devices, local(): halfway = halfway + lax.ppermute(piece, 'blk', ring)  6.38 us
    ppermute x3, starting transfers between devices, local(): halfway = halfway + lax.ppermute(piece, 'blk', ring)  5.92 us
    pallas_call x1, Pallas kernels, element_stage(): pl.pallas_call(element_body, out_shape=jax.ShapeDtypeStruct((modes + 8, m...  5.51 us
    pallas_call x1, Pallas kernels, gather_rows(): pl.pallas_call(gather_body, out_shape=jax.ShapeDtypeStruct((n_rows, comps...  4.24 us
  transfers between devices with their start and end apart: 6, of which 5 were waited for; matrix products, arithmetic and copies ran while one was open for 7% of the time, Pallas kernels for 0%

profile of v12, /device:TPU:2, one launch (start us, length us, event | category | flops | bytes accessed | tf_op | source)
XLA Modules:
  0.0 87.5 jit_solution(15436430695149301541)
XLA Ops:
  0.6 4.2 %shard_map.95 = bf16[256,1536]{1,0:T(8,128)(2,1)} custom-call(bf16[3,1024,512]{2,1,0:T(8,128)(2,1)} %bitcast.39, s32[1,256]{1,0:T(1,128)} %bitcast.44), custom_call_target="tpu_custom_call" | custom-call | tf_op jit(solution)/shard_map/pallas_call | solution.py:123
  4.9 11.8 %all-to-all-start = ((bf16[32,8,1536]{2,1,0:T(8,128)(2,1)}), bf16[32,8,1536]{2,1,0:T(8,128)(2,1)S(1)}, u32[]{:S(2)}, u32[]{:S(2)}) async-start(bf16[32,8,1536]{2,1,0:T(8,128)(2,1)} %bitcast.41), calls=%async_computation | async-start | bytes 1572864 | tf_op jit(solution)/shard_map/all_to_all | solution.py:140
  16.7 0.6 dynamic_slice.24
  17.3 0.6 fusion.6
  17.9 0.7 copy.38.omega_ref
  18.7 0.9 %reshape.47.slot_ref = s32[512,1]{1,0:T(8,128)} reshape(s32[8,64]{1,0:T(8,128)S(1)} %copy-done.1) | data formatting | bytes 4096 | tf_op jit(solution)/shard_map/reshape | solution.py:106
  19.6 0.7 copy.39.stiff_ref
  20.3 1.8 %fusion.state_ref = bf16[1536,128]{1,0:T(8,128)(2,1)} fusion(s32[1536]{0:T(1024)S(1)} %add_select_fusion, bf16[1536]{0:T(1024)(128)(2,1)S(1)} %broadcast_in_dim.26), kind=kLoop, calls=%fused_computation.1 | loop fusion | flops 393216 | bytes 402432 | tf_op jit(solution)/shard_map/jit(_where)/select_n | solution.py:93
  22.1 17.1 %all-to-all-done = bf16[32,8,1536]{2,1,0:T(8,128)(2,1)S(1)} async-done(((bf16[32,8,1536]{2,1,0:T(8,128)(2,1)}), bf16[32,8,1536]{2,1,0:T(8,128)(2,1)S(1)}, u32[]{:S(2)}, u32[]{:S(2)}) %all-to-all-start) | async-done | bytes 786464 | tf_op jit(solution)/shard_map/all_to_all | solution.py:140
  39.1 0.9 %copy-done = bf16[32,8,1536]{2,1,0:T(8,128)(2,1)} copy-done((bf16[32,8,1536]{2,1,0:T(8,128)(2,1)}, bf16[32,8,1536]{2,1,0:T(8,128)(2,1)S(1)}, u32[]{:S(2)}) %copy-start) | copy-done | bytes 786456
  40.0 5.5 %shard_map.96 = f32[520,512]{1,0:T(8,128)} custom-call(bf16[256,1536]{1,0:T(8,128)(2,1)} %bitcast.40, s32[512,1]{1,0:T(8,128)} %reshape.47.slot_ref, bf16[1536,128]{1,0:T(8,128)(2,1)} %fusion.state_ref, f32[64,1]{1,0:T(8,128)} %copy.38.omega_ref, f32[64,1]{1,0:T(8,128)} %copy.39.stiff_ref), custom_call_target="tpu_custom_call" | custom-call | tf_op jit(solution)/shard_map/pallas_call | solution.py:97
  45.5 1.6 %copy.40 = f32[520,512]{0,1:T(8,128)S(1)} copy(f32[520,512]{1,0:T(8,128)} %shard_map.96) | data formatting | bytes 2129920 | tf_op jit(solution)/shard_map/pallas_call | solution.py:97
  47.4 2.0 %collective-permute-done = f32[520,4,64]{0,2,1:T(8,128)S(1)} collective-permute-done((f32[520,4,64]{0,2,1:T(8,128)S(1)}, f32[520,4,64]{0,2,1:T(8,128)S(1)}, u32[]{:S(2)}, u32[]{:S(2)}) %collective-permute-start) | collective-permute-done | bytes 532512 | tf_op jit(solution)/shard_map/ppermute | solution.py:157
  49.6 1.7 %collective-permute-start.1 = (f32[520,64]{0,1:T(8,128)S(1)}, f32[520,64]{0,1:T(8,128)S(1)}, u32[]{:S(2)}, u32[]{:S(2)}) collective-permute-start(f32[520,64]{0,1:T(8,128)S(1)} %get-tuple-element.2), channel_id=1, source_target_pairs={{0,2},{1,3},{2,4},{3,5},{4,6},{5,7},{6,0},{7,1},{8,10},{9,11},{10,... | collective-permute-start | bytes 399368 | tf_op jit(solution)/shard_map/ppermute | solution.py:162
  51.2 2.9 %collective-permute-start.2 = (f32[520,64]{0,1:T(8,128)S(1)}, f32[520,64]{0,1:T(8,128)S(1)}, u32[]{:S(2)}, u32[]{:S(2)}) collective-permute-start(f32[520,64]{0,1:T(8,128)S(1)} %get-tuple-element.4), channel_id=1, source_target_pairs={{0,4},{1,5},{2,6},{3,7},{4,0},{5,1},{6,2},{7,3},{8,12},{9,13},{10,... | collective-permute-start | bytes 399368 | tf_op jit(solution)/shard_map/ppermute | solution.py:162
  54.1 1.3 %collective-permute-start.3 = (f32[520,64]{0,1:T(8,128)S(1)}, f32[520,64]{0,1:T(8,128)S(1)}, u32[]{:S(2)}, u32[]{:S(2)}) collective-permute-start(f32[520,64]{0,1:T(8,128)S(1)} %get-tuple-element.3), channel_id=1, source_target_pairs={{0,6},{1,7},{2,0},{3,1},{4,2},{5,3},{6,4},{7,5},{8,14},{9,15},{10,... | collective-permute-start | bytes 399368 | tf_op jit(solution)/shard_map/ppermute | solution.py:162
  55.5 1.7 %collective-permute-done.1 = f32[520,64]{0,1:T(8,128)S(1)} collective-permute-done((f32[520,64]{0,1:T(8,128)S(1)}, f32[520,64]{0,1:T(8,128)S(1)}, u32[]{:S(2)}, u32[]{:S(2)}) %collective-permute-start.1) | collective-permute-done | bytes 133152 | tf_op jit(solution)/shard_map/ppermute | solution.py:162
  57.2 4.7 %collective-permute-done.2 = f32[520,64]{0,1:T(8,128)S(1)} collective-permute-done((f32[520,64]{0,1:T(8,128)S(1)}, f32[520,64]{0,1:T(8,128)S(1)}, u32[]{:S(2)}, u32[]{:S(2)}) %collective-permute-start.2) | collective-permute-done | bytes 133152 | tf_op jit(solution)/shard_map/ppermute | solution.py:162
  62.0 0.1 copy.41
  62.2 0.2 copy.45
  62.4 0.2 reshape.49
  62.6 9.2 %all_to_all.21 = f32[4,1,8704]{2,1,0:T(1,128)S(1)} all-to-all(f32[4,1,8704]{2,1,0:T(1,128)S(1)} %reshape.49), channel_id=1, replica_groups={{0,8,16,24},{32,40,48,56},{64,72,80,88},{96,104,112,120},{128,136,144,1..., dimensions={0} | all-to-all | bytes 278528 | tf_op jit(solution)/shard_map/all_to_all | solution.py:173
  71.8 0.5 broadcast.44
  72.3 1.0 %reduce.2 = f32[4,8704]{1,0:T(4,128)S(1)} reduce(f32[4,1,8704]{2,1,0:T(1,128)S(1)} %all_to_all.21, f32[]{:T(128)} %broadcast.44), dimensions={1}, to_apply=%all_to_all.16.reduce_sub_computation | reduce | bytes 278532 | tf_op jit(solution)/shard_map/all_to_all | solution.py:173
  73.3 0.1 reshape.50
  73.5 0.7 reshape.51
  74.2 3.3 %all-to-all-start.2 = ((f32[8,1,1088]{2,1,0:T(1,128)}), f32[8,1,1088]{2,1,0:T(1,128)S(1)}, u32[]{:S(2)}, u32[]{:S(2)}) async-start(f32[8,1,1088]{2,1,0:T(1,128)} %reshape.51), calls=%async_computation.2 | async-start | bytes 73728 | tf_op jit(solution)/shard_map/all_to_all | solution.py:175
  77.5 0.6 reduce_sum.29
  78.9 6.7 %all-to-all-done.2 = f32[8,1,1088]{2,1,0:T(1,128)S(1)} async-done(((f32[8,1,1088]{2,1,0:T(1,128)}), f32[8,1,1088]{2,1,0:T(1,128)S(1)}, u32[]{:S(2)}, u32[]{:S(2)}) %all-to-all-start.2) | async-done | bytes 34848 | tf_op jit(solution)/shard_map/all_to_all | solution.py:175
  85.5 0.7 reduce.3
  86.4 0.6 slice_multiply_fusion
  87.0 0.5 fusion.8
  (30 shorter events, 0.7 us)
Async XLA Ops:
  4.9 11.8 %copy-start.6 = (s32[32]{0:T(128)S(1)}, s32[32]{0:T(128)}, u32[]{:S(2)}) copy-start(s32[32]{0:T(128)} %param.11) | copy-start | bytes 388
  4.9 12.4 %copy-start.4 = (f32[64]{0:T(128)S(1)}, f32[64]{0:T(128)}, u32[]{:S(2)}) copy-start(f32[64]{0:T(128)} %param.12) | copy-start | bytes 772
  4.9 13.8 %copy-start.2 = (bf16[512]{0:T(512)(128)(2,1)S(1)}, bf16[512]{0:T(512)(128)(2,1)}, u32[]{:S(2)}) copy-start(bf16[512]{0:T(512)(128)(2,1)} %param.14) | copy-start | bytes 3076
  4.9 13.8 %copy-start.1 = (s32[8,64]{1,0:T(8,128)S(1)}, s32[8,64]{1,0:T(8,128)}, u32[]{:S(2)}) copy-start(s32[8,64]{1,0:T(8,128)} %param.10) | copy-start | bytes 6148
  4.9 14.7 %copy-start.3 = (f32[64]{0:T(128)S(1)}, f32[64]{0:T(128)}, u32[]{:S(2)}) copy-start(f32[64]{0:T(128)} %param.13) | copy-start | bytes 772
  4.9 34.2 %all-to-all-start = ((bf16[32,8,1536]{2,1,0:T(8,128)(2,1)}), bf16[32,8,1536]{2,1,0:T(8,128)(2,1)S(1)}, u32[]{:S(2)}, u32[]{:S(2)}) async-start(bf16[32,8,1536]{2,1,0:T(8,128)(2,1)} %bitcast.41), calls=%async_computation | async-start | bytes 1572864 | tf_op jit(solution)/shard_map/all_to_all | solution.py:140
  39.1 0.9 %copy-start = (bf16[32,8,1536]{2,1,0:T(8,128)(2,1)}, bf16[32,8,1536]{2,1,0:T(8,128)(2,1)S(1)}, u32[]{:S(2)}) copy-start(bf16[32,8,1536]{2,1,0:T(8,128)(2,1)S(1)} %all-to-all-done) | copy-start | bytes 2359300
  47.2 2.2 %collective-permute-start = (f32[520,4,64]{0,2,1:T(8,128)S(1)}, f32[520,4,64]{0,2,1:T(8,128)S(1)}, u32[]{:S(2)}, u32[]{:S(2)}) collective-permute-start(f32[520,4,64]{0,2,1:T(8,128)S(1)} %dynamic-slice_bitcast_fusion), channel_id=1, source_target_pairs={{0,1},{1,0},{2,3},{3,2},{4,5},{5,4},{6,7},{7,6},{8,9},{9,8},{10,11... | collective-permute-start | bytes 1597448 | tf_op jit(solution)/shard_map/ppermute | solution.py:157
  49.6 7.6 %collective-permute-start.1 = (f32[520,64]{0,1:T(8,128)S(1)}, f32[520,64]{0,1:T(8,128)S(1)}, u32[]{:S(2)}, u32[]{:S(2)}) collective-permute-start(f32[520,64]{0,1:T(8,128)S(1)} %get-tuple-element.2), channel_id=1, source_target_pairs={{0,2},{1,3},{2,4},{3,5},{4,6},{5,7},{6,0},{7,1},{8,10},{9,11},{10,... | collective-permute-start | bytes 399368 | tf_op jit(solution)/shard_map/ppermute | solution.py:162
  51.2 10.6 %collective-permute-start.2 = (f32[520,64]{0,1:T(8,128)S(1)}, f32[520,64]{0,1:T(8,128)S(1)}, u32[]{:S(2)}, u32[]{:S(2)}) collective-permute-start(f32[520,64]{0,1:T(8,128)S(1)} %get-tuple-element.4), channel_id=1, source_target_pairs={{0,4},{1,5},{2,6},{3,7},{4,0},{5,1},{6,2},{7,3},{8,12},{9,13},{10,... | collective-permute-start | bytes 399368 | tf_op jit(solution)/shard_map/ppermute | solution.py:162
  54.1 7.7 %collective-permute-start.3 = (f32[520,64]{0,1:T(8,128)S(1)}, f32[520,64]{0,1:T(8,128)S(1)}, u32[]{:S(2)}, u32[]{:S(2)}) collective-permute-start(f32[520,64]{0,1:T(8,128)S(1)} %get-tuple-element.3), channel_id=1, source_target_pairs={{0,6},{1,7},{2,0},{3,1},{4,2},{5,3},{6,4},{7,5},{8,14},{9,15},{10,... | collective-permute-start | bytes 399368 | tf_op jit(solution)/shard_map/ppermute | solution.py:162
  62.4 24.6 %copy-start.5 = (f32[64]{0:T(128)S(1)}, f32[64]{0:T(128)}, u32[]{:S(2)}) copy-start(f32[64]{0:T(128)} %param.15) | copy-start | bytes 772
  74.2 11.3 %all-to-all-start.2 = ((f32[8,1,1088]{2,1,0:T(1,128)}), f32[8,1,1088]{2,1,0:T(1,128)S(1)}, u32[]{:S(2)}, u32[]{:S(2)}) async-start(f32[8,1,1088]{2,1,0:T(1,128)} %reshape.51), calls=%async_computation.2 | async-start | bytes 73728 | tf_op jit(solution)/shard_map/all_to_all | solution.py:175

commit v13 on v9

--- a/solution.py
+++ b/solution.py
@@ -136,7 +136,9 @@
     n_elem = lax.psum(1, "elem")
     n_blk = lax.psum(1, "blk")
     by_component = jnp.transpose(basis, (1, 0, 2))
-    outgoing = gather_rows(by_component, send_rows[0, 0])
+    outgoing = jnp.concatenate(
+        [jnp.take(by_component[c], send_rows[0, 0], axis=0) for c in range(by_component.shape[0])], axis=1
+    )
     arrived = lax.all_to_all(outgoing, "elem", split_axis=0, concat_axis=0, tiled=True)
     element_count = elem_slot.shape[1]
     set_index = lax.axis_index("elem")

time: 81.9 us -> 87.1 us (1.063)
  local copies, waits for them, and re-layouts: 7.28 us -> 12.8 us
  Pallas kernels: 9.74 us -> 5.48 us
  waiting for transfers between devices: 33 us -> 36.3 us
  other arithmetic: 5.33 us -> 7.78 us
  starting transfers between devices: 23.3 us -> 22 us
    pallas_call x1 -> x0, Pallas kernels: 4.24 us -> none  [gather_rows(): pl.pallas_call(gather_body, out_shape=jax.ShapeDtypeStruct((n_rows, comps...]
    gather x0 -> x3, local copies, waits for them, and re-layouts: none -> 3.46 us  [local(): jnp.take(by_component[c], send_rows[0, 0], axis=0)]
    ppermute x3, waiting for transfers between devices: 6.38 us -> 9.37 us  [local(): halfway = halfway + lax.ppermute(piece, 'blk', ring)]
    squeeze x0 -> x1, local copies, waits for them, and re-layouts: none -> 2.06 us  [local(): by_component[c]]
    ppermute x3, starting transfers between devices: 5.92 us -> 4.7 us  [local(): halfway = halfway + lax.ppermute(piece, 'blk', ring)]
    all_to_all x0 -> x1, other arithmetic: none -> 0.95 us  [local(): lax.all_to_all(outgoing, 'elem', split_axis=0, concat_axis=0, tiled=True)]
  transfers between devices with their start and end apart: 6 -> 6, of which waited for: 5 -> 6; matrix products, arithmetic and copies ran while one was open for 7% -> 7% of each run, Pallas kernels for 0% -> 0%
where the time goes in v13:
time: 87.1 us; the launch traced here: 86 us
  waiting for transfers between devices  36.3 us (42%)
  starting transfers between devices  22 us (25%)
  local copies, waits for them, and re-layouts  12.8 us (15%)
  other arithmetic  7.78 us (9%)
  Pallas kernels  5.48 us (6%)
  between operations  1.62 us (2%)
    all_to_all x1, waiting for transfers between devices, local(): lax.all_to_all(outgoing, 'elem', split_axis=0, concat_axis=0, tiled=True)  17.1 us
    all_to_all x1, starting transfers between devices, local(): lax.all_to_all(outgoing, 'elem', split_axis=0, concat_axis=0, tiled=True)  11.6 us
    ppermute x3, waiting for transfers between devices, local(): halfway = halfway + lax.ppermute(piece, 'blk', ring)  9.37 us
    all_to_all x1, waiting for transfers between devices, local(): lax.all_to_all(chunks, 'elem', split_axis=0, concat_axis=0, tiled=True)  7.83 us
    all_to_all x1, starting transfers between devices, local(): lax.all_to_all(chunks, 'elem', split_axis=0, concat_axis=0, tiled=True)  5.56 us
    pallas_call x1, Pallas kernels, element_stage(): pl.pallas_call(element_body, out_shape=jax.ShapeDtypeStruct((modes + 8, m...  5.48 us
    ppermute x3, starting transfers between devices, local(): halfway = halfway + lax.ppermute(piece, 'blk', ring)  4.7 us
    gather x3, local copies, waits for them, and re-layouts, local(): jnp.take(by_component[c], send_rows[0, 0], axis=0)  3.46 us
  transfers between devices with their start and end apart: 6, of which 6 were waited for; matrix products, arithmetic and copies ran while one was open for 7% of the time, Pallas kernels for 0%

profile of v13, /device:TPU:2, one launch (start us, length us, event | category | flops | bytes accessed | tf_op | source)
XLA Modules:
  0.0 86.0 jit_solution(8924987524067764598)
XLA Ops:
  0.6 0.7 compare_select_fusion
  1.3 0.7 compare_and_fusion
  2.0 2.1 %slice_bitcast_fusion.2 = (bf16[1024,512]{1,0:T(8,128)(2,1)S(1)}, bf16[1024,512]{1,0:T(8,128)(2,1)S(1)}, bf16[1024,512]{1,0:T(8,128)(2,1)S(1)}) fusion(bf16[3,1024,512]{2,1,0:T(8,128)(2,1)} %bitcast.39), kind=kLoop, calls=%fused_computation.5 | loop fusion | bytes 6291456 | tf_op jit(solution)/shard_map/squeeze | solution.py:140
  4.1 1.2 %gather_fusion = bf16[256,512]{1,0:T(8,128)(2,1)S(1)} fusion(bf16[1024,512]{1,0:T(8,128)(2,1)S(1)} %get-tuple-element.3, s32[1024]{0:T(1024)S(1)} %pad_clamp_fusion), kind=kCustom, calls=%fused_computation.clone | custom fusion | bytes 525312 | tf_op jit(solution)/shard_map/jit(_take)/gather | solution.py:140
  5.2 1.2 %gather_fusion.1 = bf16[256,512]{1,0:T(8,128)(2,1)S(1)} fusion(bf16[1024,512]{1,0:T(8,128)(2,1)S(1)} %get-tuple-element.5, s32[1024]{0:T(1024)S(1)} %pad_clamp_fusion), kind=kCustom, calls=%fused_computation.1.clone | custom fusion | bytes 525312 | tf_op jit(solution)/shard_map/jit(_take)/gather | solution.py:140
  6.4 1.2 %gather_fusion.2 = bf16[256,512]{1,0:T(8,128)(2,1)S(1)} fusion(bf16[1024,512]{1,0:T(8,128)(2,1)S(1)} %get-tuple-element.4, s32[1024]{0:T(1024)S(1)} %pad_clamp_fusion), kind=kCustom, calls=%fused_computation.2.clone | custom fusion | bytes 525312 | tf_op jit(solution)/shard_map/jit(_take)/gather | solution.py:140
  7.7 0.9 %maximum_bitcast_fusion = bf16[32,8,1536]{2,1,0:T(8,128)(2,1)} fusion(bf16[256,512]{1,0:T(8,128)(2,1)S(1)} %get-tuple-element.11, bf16[256,512]{1,0:T(8,128)(2,1)S(1)} %get-tuple-element.10, bf16[256,512]{1,0:T(8,128)(2,1)S(1)} %get-tuple-element.9), kind=kLoop, calls=%fused_computation.6 | loop fusion | flops 2359296 | bytes 1572864 | tf_op jit(solution)/shard_map/all_to_all | solution.py:142
  8.7 11.6 %all-to-all-start = ((bf16[32,8,1536]{2,1,0:T(8,128)(2,1)}), bf16[32,8,1536]{2,1,0:T(8,128)(2,1)S(1)}, u32[]{:S(2)}, u32[]{:S(2)}) async-start(bf16[32,8,1536]{2,1,0:T(8,128)(2,1)} %maximum_bitcast_fusion), calls=%async_computation | async-start | bytes 1572864 | tf_op jit(solution)/shard_map/all_to_all | solution.py:142
  20.3 0.9 %reshape.84.slot_ref = s32[512,1]{1,0:T(8,128)} reshape(s32[8,64]{1,0:T(8,128)S(1)} %copy-done.1) | data formatting | bytes 4096 | tf_op jit(solution)/shard_map/reshape | solution.py:106
  21.3 0.6 dynamic_slice.24
  21.9 0.6 fusion.6
  22.5 0.7 copy.21.omega_ref
  23.2 0.7 copy.22.stiff_ref
  23.9 1.7 %fusion.state_ref = bf16[1536,128]{1,0:T(8,128)(2,1)} fusion(s32[1536]{0:T(1024)S(1)} %add_select_fusion, bf16[1536]{0:T(1024)(128)(2,1)S(1)} %broadcast_in_dim.35), kind=kLoop, calls=%fused_computation.8 | loop fusion | flops 393216 | bytes 402432 | tf_op jit(solution)/shard_map/jit(_where)/select_n | solution.py:93
  25.7 17.1 %all-to-all-done = bf16[32,8,1536]{2,1,0:T(8,128)(2,1)S(1)} async-done(((bf16[32,8,1536]{2,1,0:T(8,128)(2,1)}), bf16[32,8,1536]{2,1,0:T(8,128)(2,1)S(1)}, u32[]{:S(2)}, u32[]{:S(2)}) %all-to-all-start) | async-done | bytes 786464 | tf_op jit(solution)/shard_map/all_to_all | solution.py:142
  42.8 0.9 %copy-done = bf16[32,8,1536]{2,1,0:T(8,128)(2,1)} copy-done((bf16[32,8,1536]{2,1,0:T(8,128)(2,1)}, bf16[32,8,1536]{2,1,0:T(8,128)(2,1)S(1)}, u32[]{:S(2)}) %copy-start) | copy-done | bytes 786456
  43.7 5.5 %shard_map.95 = f32[520,512]{1,0:T(8,128)} custom-call(bf16[256,1536]{1,0:T(8,128)(2,1)} %bitcast.40, s32[512,1]{1,0:T(8,128)} %reshape.84.slot_ref, bf16[1536,128]{1,0:T(8,128)(2,1)} %fusion.state_ref, f32[64,1]{1,0:T(8,128)} %copy.21.omega_ref, f32[64,1]{1,0:T(8,128)} %copy.22.stiff_ref), custom_call_target="tpu_custom_call" | custom-call | tf_op jit(solution)/shard_map/pallas_call | solution.py:97
  49.2 1.6 %copy.23 = f32[520,512]{0,1:T(8,128)S(1)} copy(f32[520,512]{1,0:T(8,128)} %shard_map.95) | data formatting | bytes 2129920 | tf_op jit(solution)/shard_map/pallas_call | solution.py:97
  51.0 2.0 %collective-permute-done = f32[520,4,64]{0,2,1:T(8,128)S(1)} collective-permute-done((f32[520,4,64]{0,2,1:T(8,128)S(1)}, f32[520,4,64]{0,2,1:T(8,128)S(1)}, u32[]{:S(2)}, u32[]{:S(2)}) %collective-permute-start) | collective-permute-done | bytes 532512 | tf_op jit(solution)/shard_map/ppermute | solution.py:159
  53.2 3.1 %collective-permute-start.3 = (f32[520,64]{0,1:T(8,128)S(1)}, f32[520,64]{0,1:T(8,128)S(1)}, u32[]{:S(2)}, u32[]{:S(2)}) collective-permute-start(f32[520,64]{0,1:T(8,128)S(1)} %get-tuple-element.7), channel_id=1, source_target_pairs={{0,6},{1,7},{2,0},{3,1},{4,2},{5,3},{6,4},{7,5},{8,14},{9,15},{10,... | collective-permute-start | bytes 399368 | tf_op jit(solution)/shard_map/ppermute | solution.py:164
  56.3 0.6 collective-permute-start.2
  56.9 1.0 %collective-permute-start.1 = (f32[520,64]{0,1:T(8,128)S(1)}, f32[520,64]{0,1:T(8,128)S(1)}, u32[]{:S(2)}, u32[]{:S(2)}) collective-permute-start(f32[520,64]{0,1:T(8,128)S(1)} %get-tuple-element.6), channel_id=1, source_target_pairs={{0,2},{1,3},{2,4},{3,5},{4,6},{5,7},{6,0},{7,1},{8,10},{9,11},{10,... | collective-permute-start | bytes 399368 | tf_op jit(solution)/shard_map/ppermute | solution.py:164
  57.9 5.7 %collective-permute-done.3 = f32[520,64]{0,1:T(8,128)S(1)} collective-permute-done((f32[520,64]{0,1:T(8,128)S(1)}, f32[520,64]{0,1:T(8,128)S(1)}, u32[]{:S(2)}, u32[]{:S(2)}) %collective-permute-start.3) | collective-permute-done | bytes 133152 | tf_op jit(solution)/shard_map/ppermute | solution.py:164
  63.5 1.4 %collective-permute-done.2 = f32[520,64]{0,1:T(8,128)S(1)} collective-permute-done((f32[520,64]{0,1:T(8,128)S(1)}, f32[520,64]{0,1:T(8,128)S(1)}, u32[]{:S(2)}, u32[]{:S(2)}) %collective-permute-start.2) | collective-permute-done | bytes 133152 | tf_op jit(solution)/shard_map/ppermute | solution.py:164
  64.9 2.3 %collective-permute-done.1 = f32[520,64]{0,1:T(8,128)S(1)} collective-permute-done((f32[520,64]{0,1:T(8,128)S(1)}, f32[520,64]{0,1:T(8,128)S(1)}, u32[]{:S(2)}, u32[]{:S(2)}) %collective-permute-start.1) | collective-permute-done | bytes 133152 | tf_op jit(solution)/shard_map/ppermute | solution.py:164
  67.6 0.9 reshape.86
  68.5 5.6 %all-to-all-start.1 = ((f32[32,1,1088]{2,1,0:T(1,128)}), f32[32,1,1088]{2,1,0:T(1,128)S(1)}, u32[]{:S(2)}, u32[]{:S(2)}) async-start(f32[32,1,1088]{2,1,0:T(1,128)} %reshape.86), calls=%async_computation.1 | async-start | bytes 294912 | tf_op jit(solution)/shard_map/all_to_all | solution.py:170
  74.0 0.6 reduce_sum.19
  75.4 7.8 %all-to-all-done.1 = f32[32,1,1088]{2,1,0:T(1,128)S(1)} async-done(((f32[32,1,1088]{2,1,0:T(1,128)}), f32[32,1,1088]{2,1,0:T(1,128)S(1)}, u32[]{:S(2)}, u32[]{:S(2)}) %all-to-all-start.1) | async-done | bytes 139296 | tf_op jit(solution)/shard_map/all_to_all | solution.py:170
  83.7 1.0 %reduce.2 = f32[32,1088]{1,0:T(8,128)S(1)} reduce(f32[32,1,1088]{2,1,0:T(1,128)S(1)} %all-to-all-done.1, f32[]{:T(128)} %broadcast.54), dimensions={1}, to_apply=%all_to_all.13.reduce_sub_computation | reduce | bytes 278532 | tf_op jit(solution)/shard_map/all_to_all | solution.py:170
  84.9 0.6 slice_multiply_fusion
  85.5 0.5 fusion.8
  (31 shorter events, 1.4 us)
Async XLA Ops:
  7.7 12.6 %copy-start.1 = (s32[8,64]{1,0:T(8,128)S(1)}, s32[8,64]{1,0:T(8,128)}, u32[]{:S(2)}) copy-start(s32[8,64]{1,0:T(8,128)} %param.12) | copy-start | bytes 6148
  7.7 13.5 %copy-start.2 = (bf16[512]{0:T(512)(128)(2,1)S(1)}, bf16[512]{0:T(512)(128)(2,1)}, u32[]{:S(2)}) copy-start(bf16[512]{0:T(512)(128)(2,1)} %param.16) | copy-start | bytes 3076
  7.7 13.6 %copy-start.6 = (s32[32]{0:T(128)S(1)}, s32[32]{0:T(128)}, u32[]{:S(2)}) copy-start(s32[32]{0:T(128)} %param.13) | copy-start | bytes 388
  7.7 14.1 %copy-start.4 = (f32[64]{0:T(128)S(1)}, f32[64]{0:T(128)}, u32[]{:S(2)}) copy-start(f32[64]{0:T(128)} %param.14) | copy-start | bytes 772
  7.7 15.5 %copy-start.3 = (f32[64]{0:T(128)S(1)}, f32[64]{0:T(128)}, u32[]{:S(2)}) copy-start(f32[64]{0:T(128)} %param.15) | copy-start | bytes 772
  8.7 34.1 %all-to-all-start = ((bf16[32,8,1536]{2,1,0:T(8,128)(2,1)}), bf16[32,8,1536]{2,1,0:T(8,128)(2,1)S(1)}, u32[]{:S(2)}, u32[]{:S(2)}) async-start(bf16[32,8,1536]{2,1,0:T(8,128)(2,1)} %maximum_bitcast_fusion), calls=%async_computation | async-start | bytes 1572864 | tf_op jit(solution)/shard_map/all_to_all | solution.py:142
  42.8 0.9 %copy-start = (bf16[32,8,1536]{2,1,0:T(8,128)(2,1)}, bf16[32,8,1536]{2,1,0:T(8,128)(2,1)S(1)}, u32[]{:S(2)}) copy-start(bf16[32,8,1536]{2,1,0:T(8,128)(2,1)S(1)} %all-to-all-done) | copy-start | bytes 2359300
  50.9 2.2 %collective-permute-start = (f32[520,4,64]{0,2,1:T(8,128)S(1)}, f32[520,4,64]{0,2,1:T(8,128)S(1)}, u32[]{:S(2)}, u32[]{:S(2)}) collective-permute-start(f32[520,4,64]{0,2,1:T(8,128)S(1)} %dynamic-slice_bitcast_fusion), channel_id=1, source_target_pairs={{0,1},{1,0},{2,3},{3,2},{4,5},{5,4},{6,7},{7,6},{8,9},{9,8},{10,11... | collective-permute-start | bytes 1597448 | tf_op jit(solution)/shard_map/ppermute | solution.py:159
  53.2 10.4 %collective-permute-start.3 = (f32[520,64]{0,1:T(8,128)S(1)}, f32[520,64]{0,1:T(8,128)S(1)}, u32[]{:S(2)}, u32[]{:S(2)}) collective-permute-start(f32[520,64]{0,1:T(8,128)S(1)} %get-tuple-element.7), channel_id=1, source_target_pairs={{0,6},{1,7},{2,0},{3,1},{4,2},{5,3},{6,4},{7,5},{8,14},{9,15},{10,... | collective-permute-start | bytes 399368 | tf_op jit(solution)/shard_map/ppermute | solution.py:164
  56.3 8.6 %collective-permute-start.2 = (f32[520,64]{0,1:T(8,128)S(1)}, f32[520,64]{0,1:T(8,128)S(1)}, u32[]{:S(2)}, u32[]{:S(2)}) collective-permute-start(f32[520,64]{0,1:T(8,128)S(1)} %get-tuple-element.8), channel_id=1, source_target_pairs={{0,4},{1,5},{2,6},{3,7},{4,0},{5,1},{6,2},{7,3},{8,12},{9,13},{10,... | collective-permute-start | bytes 399368 | tf_op jit(solution)/shard_map/ppermute | solution.py:164
  56.9 10.3 %collective-permute-start.1 = (f32[520,64]{0,1:T(8,128)S(1)}, f32[520,64]{0,1:T(8,128)S(1)}, u32[]{:S(2)}, u32[]{:S(2)}) collective-permute-start(f32[520,64]{0,1:T(8,128)S(1)} %get-tuple-element.6), channel_id=1, source_target_pairs={{0,2},{1,3},{2,4},{3,5},{4,6},{5,7},{6,0},{7,1},{8,10},{9,11},{10,... | collective-permute-start | bytes 399368 | tf_op jit(solution)/shard_map/ppermute | solution.py:164
  67.4 18.0 %copy-start.5 = (f32[64]{0:T(128)S(1)}, f32[64]{0:T(128)}, u32[]{:S(2)}) copy-start(f32[64]{0:T(128)} %param.17) | copy-start | bytes 772
  68.5 14.7 %all-to-all-start.1 = ((f32[32,1,1088]{2,1,0:T(1,128)}), f32[32,1,1088]{2,1,0:T(1,128)S(1)}, u32[]{:S(2)}, u32[]{:S(2)}) async-start(f32[32,1,1088]{2,1,0:T(1,128)} %reshape.86), calls=%async_computation.1 | async-start | bytes 294912 | tf_op jit(solution)/shard_map/all_to_all | solution.py:170

commit v14 on v9

--- a/solution.py
+++ b/solution.py
@@ -106,29 +106,35 @@
     )(arrived3, slot.reshape(8 * n_el, 1), state_blocks, omega.reshape(n_el, 1), stiff.reshape(n_el, 1))
 
 
-def gather_body(basis_ref, rows_ref, out_ref):
-    nodes = basis_ref.shape[1]
+def gather_body(basis_hbm, rows_ref, out_ref, buf, sem):
+    comps, nodes, modes = buf.shape
     n_rows = rows_ref.shape[1]
+    copies = [pltpu.make_async_copy(basis_hbm.at[c], buf.at[c], sem.at[c]) for c in range(comps)]
+    for copy in copies:
+        copy.start()
     node = lax.broadcasted_iota(jnp.int32, (nodes, n_rows), 0)
     onehot_t = (node == rows_ref[...]).astype(jnp.bfloat16)
-    picked = lax.dot_general(
-        onehot_t, basis_ref[0], (((0,), (0,)), ((), ())), preferred_element_type=jnp.float32
-    )
-    out_ref[...] = picked.astype(jnp.bfloat16)
+    for c in range(comps):
+        copies[c].wait()
+        picked = lax.dot_general(
+            onehot_t, buf[c], (((0,), (0,)), ((), ())), preferred_element_type=jnp.float32
+        )
+        out_ref[:, pl.ds(c * modes, modes)] = picked.astype(jnp.bfloat16)
 
 
 def gather_rows(by_component, rows):
     comps, nodes, modes = by_component.shape
     n_rows = rows.shape[0]
+    vmem = pltpu.MemorySpace.VMEM if hasattr(pltpu, "MemorySpace") else pltpu.TPUMemorySpace.VMEM
     return pl.pallas_call(
         gather_body,
         out_shape=jax.ShapeDtypeStruct((n_rows, comps * modes), jnp.bfloat16),
-        grid=(comps,),
-        in_specs=[
-            pl.BlockSpec((1, nodes, modes), lambda c: (c, 0, 0)),
-            pl.BlockSpec((1, n_rows), lambda c: (0, 0)),
+        in_specs=[pl.BlockSpec(memory_space=pl.ANY), pl.BlockSpec(memory_space=vmem)],
+        out_specs=pl.BlockSpec(memory_space=vmem),
+        scratch_shapes=[
+            pltpu.VMEM((comps, nodes, modes), jnp.bfloat16),
+            pltpu.SemaphoreType.DMA((comps,)),
         ],
-        out_specs=pl.BlockSpec((n_rows, modes), lambda c: (0, c)),
     )(by_component, rows.reshape(1, n_rows))
 
 def local(basis, send_rows, elem_slot, set_size, elem_weight, element_stiffening, state, load):

time: 81.9 us -> 81.8 us (level)
  no operation moved by 1% of the time
where the time goes in v14:
time: 81.8 us; the launch traced here: 80.3 us
  waiting for transfers between devices  33 us (40%)
  starting transfers between devices  23.3 us (28%)
  Pallas kernels  9.67 us (12%)
  local copies, waits for them, and re-layouts  7.29 us (9%)
  other arithmetic  5.33 us (7%)
  between operations  1.61 us (2%)
    all_to_all x1, waiting for transfers between devices, local(): lax.all_to_all(outgoing, 'elem', split_axis=0, concat_axis=0, tiled=True)  17.1 us
    all_to_all x1, starting transfers between devices, local(): lax.all_to_all(outgoing, 'elem', split_axis=0, concat_axis=0, tiled=True)  11.8 us
    all_to_all x1, waiting for transfers between devices, local(): lax.all_to_all(chunks, 'elem', split_axis=0, concat_axis=0, tiled=True)  7.58 us
    ppermute x3, waiting for transfers between devices, local(): halfway = halfway + lax.ppermute(piece, 'blk', ring)  6.38 us
    ppermute x3, starting transfers between devices, local(): halfway = halfway + lax.ppermute(piece, 'blk', ring)  5.9 us
    all_to_all x1, starting transfers between devices, local(): lax.all_to_all(chunks, 'elem', split_axis=0, concat_axis=0, tiled=True)  5.57 us
    pallas_call x1, Pallas kernels, element_stage(): pl.pallas_call(element_body, out_shape=jax.ShapeDtypeStruct((modes + 8, m...  5.5 us
    pallas_call x1, Pallas kernels, gather_rows(): pl.pallas_call(gather_body, out_shape=jax.ShapeDtypeStruct((n_rows, comps...  4.17 us
  transfers between devices with their start and end apart: 6, of which 5 were waited for; matrix products, arithmetic and copies ran while one was open for 7% of the time, Pallas kernels for 0%

profile of v14, /device:TPU:2, one launch (start us, length us, event | category | flops | bytes accessed | tf_op | source)
XLA Modules:
  0.0 80.3 jit_solution(2779736236496166281)
XLA Ops:
  0.6 4.2 %shard_map.95 = bf16[256,1536]{1,0:T(8,128)(2,1)} custom-call(bf16[3,1024,512]{2,1,0:T(8,128)(2,1)} %bitcast.32, s32[1,256]{1,0:T(1,128)} %bitcast.36), custom_call_target="tpu_custom_call" | custom-call | tf_op jit(solution)/shard_map/pallas_call | solution.py:129
  4.9 11.8 %all-to-all-start = ((bf16[32,8,1536]{2,1,0:T(8,128)(2,1)}), bf16[32,8,1536]{2,1,0:T(8,128)(2,1)S(1)}, u32[]{:S(2)}, u32[]{:S(2)}) async-start(bf16[32,8,1536]{2,1,0:T(8,128)(2,1)} %bitcast.34), calls=%async_computation | async-start | bytes 1572864 | tf_op jit(solution)/shard_map/all_to_all | solution.py:146
  16.7 0.6 dynamic_slice.24
  17.2 0.6 fusion.6
  17.9 0.7 copy.21.omega_ref
  18.6 0.9 %reshape.46.slot_ref = s32[512,1]{1,0:T(8,128)} reshape(s32[8,64]{1,0:T(8,128)S(1)} %copy-done.1) | data formatting | bytes 4096 | tf_op jit(solution)/shard_map/reshape | solution.py:106
  19.5 0.7 copy.22.stiff_ref
  20.2 1.8 %fusion.state_ref = bf16[1536,128]{1,0:T(8,128)(2,1)} fusion(s32[1536]{0:T(1024)S(1)} %add_select_fusion, bf16[1536]{0:T(1024)(128)(2,1)S(1)} %broadcast_in_dim.26), kind=kLoop, calls=%fused_computation.1 | loop fusion | flops 393216 | bytes 402432 | tf_op jit(solution)/shard_map/jit(_where)/select_n | solution.py:93
  22.0 17.1 %all-to-all-done = bf16[32,8,1536]{2,1,0:T(8,128)(2,1)S(1)} async-done(((bf16[32,8,1536]{2,1,0:T(8,128)(2,1)}), bf16[32,8,1536]{2,1,0:T(8,128)(2,1)S(1)}, u32[]{:S(2)}, u32[]{:S(2)}) %all-to-all-start) | async-done | bytes 786464 | tf_op jit(solution)/shard_map/all_to_all | solution.py:146
  39.1 0.9 %copy-done = bf16[32,8,1536]{2,1,0:T(8,128)(2,1)} copy-done((bf16[32,8,1536]{2,1,0:T(8,128)(2,1)}, bf16[32,8,1536]{2,1,0:T(8,128)(2,1)S(1)}, u32[]{:S(2)}) %copy-start) | copy-done | bytes 786456
  40.0 5.5 %shard_map.96 = f32[520,512]{1,0:T(8,128)} custom-call(bf16[256,1536]{1,0:T(8,128)(2,1)} %bitcast.33, s32[512,1]{1,0:T(8,128)} %reshape.46.slot_ref, bf16[1536,128]{1,0:T(8,128)(2,1)} %fusion.state_ref, f32[64,1]{1,0:T(8,128)} %copy.21.omega_ref, f32[64,1]{1,0:T(8,128)} %copy.22.stiff_ref), custom_call_target="tpu_custom_call" | custom-call | tf_op jit(solution)/shard_map/pallas_call | solution.py:97
  45.5 1.6 %copy.23 = f32[520,512]{0,1:T(8,128)S(1)} copy(f32[520,512]{1,0:T(8,128)} %shard_map.96) | data formatting | bytes 2129920 | tf_op jit(solution)/shard_map/pallas_call | solution.py:97
  47.1 0.1 dynamic-slice_bitcast_fusion
  47.2 0.1 collective-permute-start
  47.4 2.0 %collective-permute-done = f32[520,4,64]{0,2,1:T(8,128)S(1)} collective-permute-done((f32[520,4,64]{0,2,1:T(8,128)S(1)}, f32[520,4,64]{0,2,1:T(8,128)S(1)}, u32[]{:S(2)}, u32[]{:S(2)}) %collective-permute-start) | collective-permute-done | bytes 532512 | tf_op jit(solution)/shard_map/ppermute | solution.py:163
  49.4 0.1 bitcast_add_fusion
  49.5 1.7 %collective-permute-start.1 = (f32[520,64]{0,1:T(8,128)S(1)}, f32[520,64]{0,1:T(8,128)S(1)}, u32[]{:S(2)}, u32[]{:S(2)}) collective-permute-start(f32[520,64]{0,1:T(8,128)S(1)} %get-tuple-element.2), channel_id=1, source_target_pairs={{0,2},{1,3},{2,4},{3,5},{4,6},{5,7},{6,0},{7,1},{8,10},{9,11},{10,... | collective-permute-start | bytes 399368 | tf_op jit(solution)/shard_map/ppermute | solution.py:168
  51.1 2.9 %collective-permute-start.2 = (f32[520,64]{0,1:T(8,128)S(1)}, f32[520,64]{0,1:T(8,128)S(1)}, u32[]{:S(2)}, u32[]{:S(2)}) collective-permute-start(f32[520,64]{0,1:T(8,128)S(1)} %get-tuple-element.4), channel_id=1, source_target_pairs={{0,4},{1,5},{2,6},{3,7},{4,0},{5,1},{6,2},{7,3},{8,12},{9,13},{10,... | collective-permute-start | bytes 399368 | tf_op jit(solution)/shard_map/ppermute | solution.py:168
  54.0 1.3 %collective-permute-start.3 = (f32[520,64]{0,1:T(8,128)S(1)}, f32[520,64]{0,1:T(8,128)S(1)}, u32[]{:S(2)}, u32[]{:S(2)}) collective-permute-start(f32[520,64]{0,1:T(8,128)S(1)} %get-tuple-element.3), channel_id=1, source_target_pairs={{0,6},{1,7},{2,0},{3,1},{4,2},{5,3},{6,4},{7,5},{8,14},{9,15},{10,... | collective-permute-start | bytes 399368 | tf_op jit(solution)/shard_map/ppermute | solution.py:168
  55.4 1.7 %collective-permute-done.1 = f32[520,64]{0,1:T(8,128)S(1)} collective-permute-done((f32[520,64]{0,1:T(8,128)S(1)}, f32[520,64]{0,1:T(8,128)S(1)}, u32[]{:S(2)}, u32[]{:S(2)}) %collective-permute-start.1) | collective-permute-done | bytes 133152 | tf_op jit(solution)/shard_map/ppermute | solution.py:168
  57.1 4.7 %collective-permute-done.2 = f32[520,64]{0,1:T(8,128)S(1)} collective-permute-done((f32[520,64]{0,1:T(8,128)S(1)}, f32[520,64]{0,1:T(8,128)S(1)}, u32[]{:S(2)}, u32[]{:S(2)}) %collective-permute-start.2) | collective-permute-done | bytes 133152 | tf_op jit(solution)/shard_map/ppermute | solution.py:168
  61.8 0.1 slice_reduce_fusion
  61.9 0.1 copy.24
  62.2 0.8 %reshape.48 = f32[32,1,1088]{2,1,0:T(1,128)} reshape(f32[32,17,64]{2,1,0:T(8,128)S(1)} %pad_maximum_fusion) | data formatting | bytes 278528
  63.0 5.6 %all-to-all-start.1 = ((f32[32,1,1088]{2,1,0:T(1,128)}), f32[32,1,1088]{2,1,0:T(1,128)S(1)}, u32[]{:S(2)}, u32[]{:S(2)}) async-start(f32[32,1,1088]{2,1,0:T(1,128)} %reshape.48), calls=%async_computation.1 | async-start | bytes 294912 | tf_op jit(solution)/shard_map/all_to_all | solution.py:174
  68.6 0.6 reduce_sum.19
  69.9 7.6 %all-to-all-done.1 = f32[32,1,1088]{2,1,0:T(1,128)S(1)} async-done(((f32[32,1,1088]{2,1,0:T(1,128)}), f32[32,1,1088]{2,1,0:T(1,128)S(1)}, u32[]{:S(2)}, u32[]{:S(2)}) %all-to-all-start.1) | async-done | bytes 139296 | tf_op jit(solution)/shard_map/all_to_all | solution.py:174
  77.5 0.5 broadcast.43
  78.0 1.0 %reduce.2 = f32[32,1088]{1,0:T(8,128)S(1)} reduce(f32[32,1,1088]{2,1,0:T(1,128)S(1)} %all-to-all-done.1, f32[]{:T(128)} %broadcast.43), dimensions={1}, to_apply=%all_to_all.13.reduce_sub_computation | reduce | bytes 278532 | tf_op jit(solution)/shard_map/all_to_all | solution.py:174
  79.0 0.1 reshape.49
  79.1 0.6 slice_multiply_fusion
  79.7 0.5 fusion.8
  (23 shorter events, 0.3 us)
Async XLA Ops:
  4.8 11.8 %copy-start.6 = (s32[32]{0:T(128)S(1)}, s32[32]{0:T(128)}, u32[]{:S(2)}) copy-start(s32[32]{0:T(128)} %param.11) | copy-start | bytes 388
  4.8 12.4 %copy-start.4 = (f32[64]{0:T(128)S(1)}, f32[64]{0:T(128)}, u32[]{:S(2)}) copy-start(f32[64]{0:T(128)} %param.12) | copy-start | bytes 772
  4.8 13.8 %copy-start.2 = (bf16[512]{0:T(512)(128)(2,1)S(1)}, bf16[512]{0:T(512)(128)(2,1)}, u32[]{:S(2)}) copy-start(bf16[512]{0:T(512)(128)(2,1)} %param.14) | copy-start | bytes 3076
  4.8 13.8 %copy-start.1 = (s32[8,64]{1,0:T(8,128)S(1)}, s32[8,64]{1,0:T(8,128)}, u32[]{:S(2)}) copy-start(s32[8,64]{1,0:T(8,128)} %param.10) | copy-start | bytes 6148
  4.9 14.7 %copy-start.3 = (f32[64]{0:T(128)S(1)}, f32[64]{0:T(128)}, u32[]{:S(2)}) copy-start(f32[64]{0:T(128)} %param.13) | copy-start | bytes 772
  4.9 34.2 %all-to-all-start = ((bf16[32,8,1536]{2,1,0:T(8,128)(2,1)}), bf16[32,8,1536]{2,1,0:T(8,128)(2,1)S(1)}, u32[]{:S(2)}, u32[]{:S(2)}) async-start(bf16[32,8,1536]{2,1,0:T(8,128)(2,1)} %bitcast.34), calls=%async_computation | async-start | bytes 1572864 | tf_op jit(solution)/shard_map/all_to_all | solution.py:146
  39.1 0.9 %copy-start = (bf16[32,8,1536]{2,1,0:T(8,128)(2,1)}, bf16[32,8,1536]{2,1,0:T(8,128)(2,1)S(1)}, u32[]{:S(2)}) copy-start(bf16[32,8,1536]{2,1,0:T(8,128)(2,1)S(1)} %all-to-all-done) | copy-start | bytes 2359300
  47.2 2.2 %collective-permute-start = (f32[520,4,64]{0,2,1:T(8,128)S(1)}, f32[520,4,64]{0,2,1:T(8,128)S(1)}, u32[]{:S(2)}, u32[]{:S(2)}) collective-permute-start(f32[520,4,64]{0,2,1:T(8,128)S(1)} %dynamic-slice_bitcast_fusion), channel_id=1, source_target_pairs={{0,1},{1,0},{2,3},{3,2},{4,5},{5,4},{6,7},{7,6},{8,9},{9,8},{10,11... | collective-permute-start | bytes 1597448 | tf_op jit(solution)/shard_map/ppermute | solution.py:163
  49.5 7.6 %collective-permute-start.1 = (f32[520,64]{0,1:T(8,128)S(1)}, f32[520,64]{0,1:T(8,128)S(1)}, u32[]{:S(2)}, u32[]{:S(2)}) collective-permute-start(f32[520,64]{0,1:T(8,128)S(1)} %get-tuple-element.2), channel_id=1, source_target_pairs={{0,2},{1,3},{2,4},{3,5},{4,6},{5,7},{6,0},{7,1},{8,10},{9,11},{10,... | collective-permute-start | bytes 399368 | tf_op jit(solution)/shard_map/ppermute | solution.py:168
  51.1 10.6 %collective-permute-start.2 = (f32[520,64]{0,1:T(8,128)S(1)}, f32[520,64]{0,1:T(8,128)S(1)}, u32[]{:S(2)}, u32[]{:S(2)}) collective-permute-start(f32[520,64]{0,1:T(8,128)S(1)} %get-tuple-element.4), channel_id=1, source_target_pairs={{0,4},{1,5},{2,6},{3,7},{4,0},{5,1},{6,2},{7,3},{8,12},{9,13},{10,... | collective-permute-start | bytes 399368 | tf_op jit(solution)/shard_map/ppermute | solution.py:168
  54.0 7.7 %collective-permute-start.3 = (f32[520,64]{0,1:T(8,128)S(1)}, f32[520,64]{0,1:T(8,128)S(1)}, u32[]{:S(2)}, u32[]{:S(2)}) collective-permute-start(f32[520,64]{0,1:T(8,128)S(1)} %get-tuple-element.3), channel_id=1, source_target_pairs={{0,6},{1,7},{2,0},{3,1},{4,2},{5,3},{6,4},{7,5},{8,14},{9,15},{10,... | collective-permute-start | bytes 399368 | tf_op jit(solution)/shard_map/ppermute | solution.py:168
  62.1 17.7 %copy-start.5 = (f32[64]{0:T(128)S(1)}, f32[64]{0:T(128)}, u32[]{:S(2)}) copy-start(f32[64]{0:T(128)} %param.15) | copy-start | bytes 772
  63.0 14.5 %all-to-all-start.1 = ((f32[32,1,1088]{2,1,0:T(1,128)}), f32[32,1,1088]{2,1,0:T(1,128)S(1)}, u32[]{:S(2)}, u32[]{:S(2)}) async-start(f32[32,1,1088]{2,1,0:T(1,128)} %reshape.48), calls=%async_computation.1 | async-start | bytes 294912 | tf_op jit(solution)/shard_map/all_to_all | solution.py:174

commit v15 on v9

--- a/solution.py
+++ b/solution.py
@@ -8,21 +8,15 @@
 G = [[(2 * ((a >> k) & 1) - 1) * 0.25 for k in range(3)] for a in range(8)]
 
 
-def element_body(arrived_ref, slot_ref, state_ref, omega_ref, stiff_ref, out_ref, v_ref, w_ref):
+def element_body(arrived_hbm, slot_ref, state_ref, omega_ref, stiff_ref, out_ref, v_ref, w_ref, arrived_ref, sem):
     n_el = omega_ref.shape[0]
     n_slot = arrived_ref.shape[0]
     modes = out_ref.shape[1]
+    fetch = pltpu.make_async_copy(arrived_hbm, arrived_ref, sem.at[0])
+    fetch.start()
     slots = slot_ref[...]
     lane = lax.broadcasted_iota(jnp.int32, (8 * n_el, n_slot), 1)
     onehot = (slots == lane).astype(jnp.bfloat16)
-    corners = jnp.dot(onehot, arrived_ref[...], preferred_element_type=jnp.float32).astype(jnp.bfloat16)
-    for c in range(3):
-        v_ref[pl.ds(c * 8 * n_el, 8 * n_el), :] = corners[:, c * modes:(c + 1) * modes]
-    disp_all = jnp.dot(corners, state_ref[...], preferred_element_type=jnp.float32)
-    disp = {}
-    for a in range(8):
-        for c in range(3):
-            disp[a, c] = disp_all[a * n_el:(a + 1) * n_el, c:c + 1]
     lane_el = lane[:n_el]
     signed_rows = []
     for k in range(3):
@@ -32,6 +26,15 @@
             signed = term if signed is None else signed + term
         signed_rows.append(signed)
     signed_all = jnp.concatenate(signed_rows, axis=0).astype(jnp.bfloat16)
+    fetch.wait()
+    corners = jnp.dot(onehot, arrived_ref[...], preferred_element_type=jnp.float32).astype(jnp.bfloat16)
+    for c in range(3):
+        v_ref[pl.ds(c * 8 * n_el, 8 * n_el), :] = corners[:, c * modes:(c + 1) * modes]
+    disp_all = jnp.dot(corners, state_ref[...], preferred_element_type=jnp.float32)
+    disp = {}
+    for a in range(8):
+        for c in range(3):
+            disp[a, c] = disp_all[a * n_el:(a + 1) * n_el, c:c + 1]
     grad_all = jnp.dot(signed_all, arrived_ref[...], preferred_element_type=jnp.float32)
     grad = {}
     for k in range(3):
@@ -97,11 +100,13 @@
     return pl.pallas_call(
         element_body,
         out_shape=jax.ShapeDtypeStruct((modes + 8, modes), jnp.float32),
-        in_specs=[pl.BlockSpec(memory_space=vmem)] * 5,
+        in_specs=[pl.BlockSpec(memory_space=pl.ANY)] + [pl.BlockSpec(memory_space=vmem)] * 4,
         out_specs=pl.BlockSpec(memory_space=vmem),
         scratch_shapes=[
             pltpu.VMEM((24 * n_el, modes), jnp.bfloat16),
             pltpu.VMEM((24 * n_el, modes), jnp.bfloat16),
+            pltpu.VMEM(arrived3.shape, arrived3.dtype),
+            pltpu.SemaphoreType.DMA((1,)),
         ],
     )(arrived3, slot.reshape(8 * n_el, 1), state_blocks, omega.reshape(n_el, 1), stiff.reshape(n_el, 1))
 

time: 81.9 us -> 82.7 us (level)
  Pallas kernels: 9.74 us -> 10.6 us
where the time goes in v15:
time: 82.7 us; the launch traced here: 81.2 us
  waiting for transfers between devices  33 us (40%)
  starting transfers between devices  23.3 us (28%)
  Pallas kernels  10.6 us (13%)
  local copies, waits for them, and re-layouts  7.28 us (9%)
  other arithmetic  5.33 us (6%)
  between operations  1.59 us (2%)
    all_to_all x1, waiting for transfers between devices, local(): lax.all_to_all(outgoing, 'elem', split_axis=0, concat_axis=0, tiled=True)  17.1 us
    all_to_all x1, starting transfers between devices, local(): lax.all_to_all(outgoing, 'elem', split_axis=0, concat_axis=0, tiled=True)  11.8 us
    all_to_all x1, waiting for transfers between devices, local(): lax.all_to_all(chunks, 'elem', split_axis=0, concat_axis=0, tiled=True)  7.58 us
    ppermute x3, waiting for transfers between devices, local(): halfway = halfway + lax.ppermute(piece, 'blk', ring)  6.38 us
    pallas_call x1, Pallas kernels, element_stage(): pl.pallas_call(element_body, out_shape=jax.ShapeDtypeStruct((modes + 8, m...  6.32 us
    ppermute x3, starting transfers between devices, local(): halfway = halfway + lax.ppermute(piece, 'blk', ring)  5.92 us
    all_to_all x1, starting transfers between devices, local(): lax.all_to_all(chunks, 'elem', split_axis=0, concat_axis=0, tiled=True)  5.57 us
    pallas_call x1, Pallas kernels, gather_rows(): pl.pallas_call(gather_body, out_shape=jax.ShapeDtypeStruct((n_rows, comps...  4.24 us
  transfers between devices with their start and end apart: 6, of which 5 were waited for; matrix products, arithmetic and copies ran while one was open for 7% of the time, Pallas kernels for 0%

profile of v15, /device:TPU:2, one launch (start us, length us, event | category | flops | bytes accessed | tf_op | source)
XLA Modules:
  0.0 81.2 jit_solution(221049532100122757)
XLA Ops:
  0.6 4.2 %shard_map.95 = bf16[256,1536]{1,0:T(8,128)(2,1)} custom-call(bf16[3,1024,512]{2,1,0:T(8,128)(2,1)} %bitcast.32, s32[1,256]{1,0:T(1,128)} %bitcast.36), custom_call_target="tpu_custom_call" | custom-call | tf_op jit(solution)/shard_map/pallas_call | solution.py:128
  4.9 11.8 %all-to-all-start = ((bf16[32,8,1536]{2,1,0:T(8,128)(2,1)}), bf16[32,8,1536]{2,1,0:T(8,128)(2,1)S(1)}, u32[]{:S(2)}, u32[]{:S(2)}) async-start(bf16[32,8,1536]{2,1,0:T(8,128)(2,1)} %bitcast.34), calls=%async_computation | async-start | bytes 1572864 | tf_op jit(solution)/shard_map/all_to_all | solution.py:145
  16.7 0.6 dynamic_slice.24
  17.3 0.6 fusion.6
  17.9 0.7 copy.21.omega_ref
  18.7 0.9 %reshape.46.slot_ref = s32[512,1]{1,0:T(8,128)} reshape(s32[8,64]{1,0:T(8,128)S(1)} %copy-done.1) | data formatting | bytes 4096 | tf_op jit(solution)/shard_map/reshape | solution.py:111
  19.6 0.7 copy.22.stiff_ref
  20.3 1.8 %fusion.state_ref = bf16[1536,128]{1,0:T(8,128)(2,1)} fusion(s32[1536]{0:T(1024)S(1)} %add_select_fusion, bf16[1536]{0:T(1024)(128)(2,1)S(1)} %broadcast_in_dim.26), kind=kLoop, calls=%fused_computation.1 | loop fusion | flops 393216 | bytes 402432 | tf_op jit(solution)/shard_map/jit(_where)/select_n | solution.py:96
  22.0 17.1 %all-to-all-done = bf16[32,8,1536]{2,1,0:T(8,128)(2,1)S(1)} async-done(((bf16[32,8,1536]{2,1,0:T(8,128)(2,1)}), bf16[32,8,1536]{2,1,0:T(8,128)(2,1)S(1)}, u32[]{:S(2)}, u32[]{:S(2)}) %all-to-all-start) | async-done | bytes 786464 | tf_op jit(solution)/shard_map/all_to_all | solution.py:145
  39.1 0.9 %copy-done = bf16[32,8,1536]{2,1,0:T(8,128)(2,1)} copy-done((bf16[32,8,1536]{2,1,0:T(8,128)(2,1)}, bf16[32,8,1536]{2,1,0:T(8,128)(2,1)S(1)}, u32[]{:S(2)}) %copy-start) | copy-done | bytes 786456
  40.0 6.3 %shard_map.96 = f32[520,512]{1,0:T(8,128)} custom-call(bf16[256,1536]{1,0:T(8,128)(2,1)} %bitcast.33, s32[512,1]{1,0:T(8,128)} %reshape.46.slot_ref, bf16[1536,128]{1,0:T(8,128)(2,1)} %fusion.state_ref, f32[64,1]{1,0:T(8,128)} %copy.21.omega_ref, f32[64,1]{1,0:T(8,128)} %copy.22.stiff_ref), custom_call_target="tpu_custom_call" | custom-call | tf_op jit(solution)/shard_map/pallas_call | solution.py:100
  46.4 1.6 %copy.23 = f32[520,512]{0,1:T(8,128)S(1)} copy(f32[520,512]{1,0:T(8,128)} %shard_map.96) | data formatting | bytes 2129920 | tf_op jit(solution)/shard_map/pallas_call | solution.py:100
  48.0 0.1 dynamic-slice_bitcast_fusion
  48.1 0.1 collective-permute-start
  48.2 2.0 %collective-permute-done = f32[520,4,64]{0,2,1:T(8,128)S(1)} collective-permute-done((f32[520,4,64]{0,2,1:T(8,128)S(1)}, f32[520,4,64]{0,2,1:T(8,128)S(1)}, u32[]{:S(2)}, u32[]{:S(2)}) %collective-permute-start) | collective-permute-done | bytes 532512 | tf_op jit(solution)/shard_map/ppermute | solution.py:162
  50.2 0.1 bitcast_add_fusion
  50.4 1.7 %collective-permute-start.1 = (f32[520,64]{0,1:T(8,128)S(1)}, f32[520,64]{0,1:T(8,128)S(1)}, u32[]{:S(2)}, u32[]{:S(2)}) collective-permute-start(f32[520,64]{0,1:T(8,128)S(1)} %get-tuple-element.2), channel_id=1, source_target_pairs={{0,2},{1,3},{2,4},{3,5},{4,6},{5,7},{6,0},{7,1},{8,10},{9,11},{10,... | collective-permute-start | bytes 399368 | tf_op jit(solution)/shard_map/ppermute | solution.py:167
  52.0 2.9 %collective-permute-start.2 = (f32[520,64]{0,1:T(8,128)S(1)}, f32[520,64]{0,1:T(8,128)S(1)}, u32[]{:S(2)}, u32[]{:S(2)}) collective-permute-start(f32[520,64]{0,1:T(8,128)S(1)} %get-tuple-element.4), channel_id=1, source_target_pairs={{0,4},{1,5},{2,6},{3,7},{4,0},{5,1},{6,2},{7,3},{8,12},{9,13},{10,... | collective-permute-start | bytes 399368 | tf_op jit(solution)/shard_map/ppermute | solution.py:167
  54.9 1.3 %collective-permute-start.3 = (f32[520,64]{0,1:T(8,128)S(1)}, f32[520,64]{0,1:T(8,128)S(1)}, u32[]{:S(2)}, u32[]{:S(2)}) collective-permute-start(f32[520,64]{0,1:T(8,128)S(1)} %get-tuple-element.3), channel_id=1, source_target_pairs={{0,6},{1,7},{2,0},{3,1},{4,2},{5,3},{6,4},{7,5},{8,14},{9,15},{10,... | collective-permute-start | bytes 399368 | tf_op jit(solution)/shard_map/ppermute | solution.py:167
  56.3 1.7 %collective-permute-done.1 = f32[520,64]{0,1:T(8,128)S(1)} collective-permute-done((f32[520,64]{0,1:T(8,128)S(1)}, f32[520,64]{0,1:T(8,128)S(1)}, u32[]{:S(2)}, u32[]{:S(2)}) %collective-permute-start.1) | collective-permute-done | bytes 133152 | tf_op jit(solution)/shard_map/ppermute | solution.py:167
  58.0 4.7 %collective-permute-done.2 = f32[520,64]{0,1:T(8,128)S(1)} collective-permute-done((f32[520,64]{0,1:T(8,128)S(1)}, f32[520,64]{0,1:T(8,128)S(1)}, u32[]{:S(2)}, u32[]{:S(2)}) %collective-permute-start.2) | collective-permute-done | bytes 133152 | tf_op jit(solution)/shard_map/ppermute | solution.py:167
  62.7 0.1 slice_reduce_fusion
  62.8 0.1 copy.24
  63.0 0.8 %reshape.48 = f32[32,1,1088]{2,1,0:T(1,128)} reshape(f32[32,17,64]{2,1,0:T(8,128)S(1)} %pad_maximum_fusion) | data formatting | bytes 278528
  63.9 5.6 %all-to-all-start.1 = ((f32[32,1,1088]{2,1,0:T(1,128)}), f32[32,1,1088]{2,1,0:T(1,128)S(1)}, u32[]{:S(2)}, u32[]{:S(2)}) async-start(f32[32,1,1088]{2,1,0:T(1,128)} %reshape.48), calls=%async_computation.1 | async-start | bytes 294912 | tf_op jit(solution)/shard_map/all_to_all | solution.py:173
  69.5 0.6 reduce_sum.19
  70.8 7.6 %all-to-all-done.1 = f32[32,1,1088]{2,1,0:T(1,128)S(1)} async-done(((f32[32,1,1088]{2,1,0:T(1,128)}), f32[32,1,1088]{2,1,0:T(1,128)S(1)}, u32[]{:S(2)}, u32[]{:S(2)}) %all-to-all-start.1) | async-done | bytes 139296 | tf_op jit(solution)/shard_map/all_to_all | solution.py:173
  78.4 0.5 broadcast.43
  78.9 1.0 %reduce.2 = f32[32,1088]{1,0:T(8,128)S(1)} reduce(f32[32,1,1088]{2,1,0:T(1,128)S(1)} %all-to-all-done.1, f32[]{:T(128)} %broadcast.43), dimensions={1}, to_apply=%all_to_all.13.reduce_sub_computation | reduce | bytes 278532 | tf_op jit(solution)/shard_map/all_to_all | solution.py:173
  79.9 0.1 reshape.49
  80.0 0.6 slice_multiply_fusion
  80.6 0.5 fusion.8
  (23 shorter events, 0.2 us)
Async XLA Ops:
  4.9 11.8 %copy-start.6 = (s32[32]{0:T(128)S(1)}, s32[32]{0:T(128)}, u32[]{:S(2)}) copy-start(s32[32]{0:T(128)} %param.11) | copy-start | bytes 388
  4.9 12.4 %copy-start.4 = (f32[64]{0:T(128)S(1)}, f32[64]{0:T(128)}, u32[]{:S(2)}) copy-start(f32[64]{0:T(128)} %param.12) | copy-start | bytes 772
  4.9 13.8 %copy-start.2 = (bf16[512]{0:T(512)(128)(2,1)S(1)}, bf16[512]{0:T(512)(128)(2,1)}, u32[]{:S(2)}) copy-start(bf16[512]{0:T(512)(128)(2,1)} %param.14) | copy-start | bytes 3076
  4.9 13.8 %copy-start.1 = (s32[8,64]{1,0:T(8,128)S(1)}, s32[8,64]{1,0:T(8,128)}, u32[]{:S(2)}) copy-start(s32[8,64]{1,0:T(8,128)} %param.10) | copy-start | bytes 6148
  4.9 14.7 %copy-start.3 = (f32[64]{0:T(128)S(1)}, f32[64]{0:T(128)}, u32[]{:S(2)}) copy-start(f32[64]{0:T(128)} %param.13) | copy-start | bytes 772
  4.9 34.2 %all-to-all-start = ((bf16[32,8,1536]{2,1,0:T(8,128)(2,1)}), bf16[32,8,1536]{2,1,0:T(8,128)(2,1)S(1)}, u32[]{:S(2)}, u32[]{:S(2)}) async-start(bf16[32,8,1536]{2,1,0:T(8,128)(2,1)} %bitcast.34), calls=%async_computation | async-start | bytes 1572864 | tf_op jit(solution)/shard_map/all_to_all | solution.py:145
  39.1 0.9 %copy-start = (bf16[32,8,1536]{2,1,0:T(8,128)(2,1)}, bf16[32,8,1536]{2,1,0:T(8,128)(2,1)S(1)}, u32[]{:S(2)}) copy-start(bf16[32,8,1536]{2,1,0:T(8,128)(2,1)S(1)} %all-to-all-done) | copy-start | bytes 2359300
  48.1 2.2 %collective-permute-start = (f32[520,4,64]{0,2,1:T(8,128)S(1)}, f32[520,4,64]{0,2,1:T(8,128)S(1)}, u32[]{:S(2)}, u32[]{:S(2)}) collective-permute-start(f32[520,4,64]{0,2,1:T(8,128)S(1)} %dynamic-slice_bitcast_fusion), channel_id=1, source_target_pairs={{0,1},{1,0},{2,3},{3,2},{4,5},{5,4},{6,7},{7,6},{8,9},{9,8},{10,11... | collective-permute-start | bytes 1597448 | tf_op jit(solution)/shard_map/ppermute | solution.py:162
  50.4 7.6 %collective-permute-start.1 = (f32[520,64]{0,1:T(8,128)S(1)}, f32[520,64]{0,1:T(8,128)S(1)}, u32[]{:S(2)}, u32[]{:S(2)}) collective-permute-start(f32[520,64]{0,1:T(8,128)S(1)} %get-tuple-element.2), channel_id=1, source_target_pairs={{0,2},{1,3},{2,4},{3,5},{4,6},{5,7},{6,0},{7,1},{8,10},{9,11},{10,... | collective-permute-start | bytes 399368 | tf_op jit(solution)/shard_map/ppermute | solution.py:167
  52.0 10.6 %collective-permute-start.2 = (f32[520,64]{0,1:T(8,128)S(1)}, f32[520,64]{0,1:T(8,128)S(1)}, u32[]{:S(2)}, u32[]{:S(2)}) collective-permute-start(f32[520,64]{0,1:T(8,128)S(1)} %get-tuple-element.4), channel_id=1, source_target_pairs={{0,4},{1,5},{2,6},{3,7},{4,0},{5,1},{6,2},{7,3},{8,12},{9,13},{10,... | collective-permute-start | bytes 399368 | tf_op jit(solution)/shard_map/ppermute | solution.py:167
  54.9 7.7 %collective-permute-start.3 = (f32[520,64]{0,1:T(8,128)S(1)}, f32[520,64]{0,1:T(8,128)S(1)}, u32[]{:S(2)}, u32[]{:S(2)}) collective-permute-start(f32[520,64]{0,1:T(8,128)S(1)} %get-tuple-element.3), channel_id=1, source_target_pairs={{0,6},{1,7},{2,0},{3,1},{4,2},{5,3},{6,4},{7,5},{8,14},{9,15},{10,... | collective-permute-start | bytes 399368 | tf_op jit(solution)/shard_map/ppermute | solution.py:167
  63.0 17.7 %copy-start.5 = (f32[64]{0:T(128)S(1)}, f32[64]{0:T(128)}, u32[]{:S(2)}) copy-start(f32[64]{0:T(128)} %param.15) | copy-start | bytes 772
  63.9 14.5 %all-to-all-start.1 = ((f32[32,1,1088]{2,1,0:T(1,128)}), f32[32,1,1088]{2,1,0:T(1,128)S(1)}, u32[]{:S(2)}, u32[]{:S(2)}) async-start(f32[32,1,1088]{2,1,0:T(1,128)} %reshape.48), calls=%async_computation.1 | async-start | bytes 294912 | tf_op jit(solution)/shard_map/all_to_all | solution.py:173

commit v16 on v9

--- a/solution.py
+++ b/solution.py
@@ -8,7 +8,7 @@
 G = [[(2 * ((a >> k) & 1) - 1) * 0.25 for k in range(3)] for a in range(8)]
 
 
-def element_body(arrived_ref, slot_ref, state_ref, omega_ref, stiff_ref, out_ref, v_ref, w_ref):
+def element_body(arrived_ref, slot_ref, state_ref, omega_ref, stiff_ref, scale_ref, out_ref, v_ref, w_ref):
     n_el = omega_ref.shape[0]
     n_slot = arrived_ref.shape[0]
     modes = out_ref.shape[1]
@@ -79,14 +79,15 @@
     tangent = lax.dot_general(
         v_ref[...], w_ref[...], (((0,), (0,)), ((), ())), preferred_element_type=jnp.float32
     )
-    out_ref[pl.ds(0, modes), :] = tangent
-    force_row = jnp.sum(force_acc, axis=0, keepdims=True)
+    scale = scale_ref[0:1, 0:1]
+    out_ref[pl.ds(0, modes), :] = tangent * scale
+    force_row = jnp.sum(force_acc, axis=0, keepdims=True) * scale
     out_ref[pl.ds(modes, 8), :] = jnp.concatenate(
         [force_row, jnp.zeros((7, modes), jnp.float32)], axis=0
     )
 
 
-def element_stage(arrived3, slot, state, omega, stiff):
+def element_stage(arrived3, slot, state, omega, stiff, scale):
     n_el = slot.shape[1]
     modes = arrived3.shape[1] // 3
     comp = jnp.arange(3 * modes) // modes
@@ -97,13 +98,14 @@
     return pl.pallas_call(
         element_body,
         out_shape=jax.ShapeDtypeStruct((modes + 8, modes), jnp.float32),
-        in_specs=[pl.BlockSpec(memory_space=vmem)] * 5,
+        in_specs=[pl.BlockSpec(memory_space=vmem)] * 6,
         out_specs=pl.BlockSpec(memory_space=vmem),
         scratch_shapes=[
             pltpu.VMEM((24 * n_el, modes), jnp.bfloat16),
             pltpu.VMEM((24 * n_el, modes), jnp.bfloat16),
         ],
-    )(arrived3, slot.reshape(8 * n_el, 1), state_blocks, omega.reshape(n_el, 1), stiff.reshape(n_el, 1))
+    )(arrived3, slot.reshape(8 * n_el, 1), state_blocks, omega.reshape(n_el, 1), stiff.reshape(n_el, 1),
+      jnp.broadcast_to(scale, (8, 128)))
 
 
 def gather_body(basis_ref, rows_ref, out_ref):
@@ -144,7 +146,8 @@
     live = lax.dynamic_index_in_dim(set_size, set_index, keepdims=False)
     position = block_index * element_count + jnp.arange(element_count, dtype=jnp.int32)
     weights = jnp.where(position < live, elem_weight, jnp.zeros_like(elem_weight))
-    stacked = element_stage(arrived, elem_slot, state, weights, element_stiffening)
+    scale = lax.rsqrt(24.0 * jnp.sum(set_size).astype(jnp.float32))
+    stacked = element_stage(arrived, elem_slot, state, weights, element_stiffening, scale)
     rows = basis_modes // n_elem
     cols = basis_modes // n_blk
     n_y = n_blk // 2
@@ -160,15 +163,14 @@
         ring = [(2 * y + c, 2 * ((y + shift) % n_y) + c) for y in range(n_y) for c in range(2)]
         piece = lax.dynamic_index_in_dim(chip_sum, (chip + shift) % n_y, axis=1, keepdims=False)
         halfway = halfway + lax.ppermute(piece, "blk", ring)
-    force_cols = halfway[basis_modes]
+    force_cols = halfway[basis_modes] - jnp.where(set_index == 0, load, jnp.zeros_like(load))
     tangent_rows = halfway[:basis_modes].reshape(n_elem, rows, cols)
     chunks = jnp.concatenate(
         [tangent_rows, jnp.broadcast_to(force_cols[None, None, :], (n_elem, 1, cols))], axis=1
     )
     arrived_chunks = lax.all_to_all(chunks, "elem", split_axis=0, concat_axis=0, tiled=True)
     mine = jnp.sum(arrived_chunks, axis=0)
-    scale = lax.rsqrt(24.0 * jnp.sum(set_size).astype(jnp.float32))
-    return (mine[:rows] * scale, mine[rows] * scale - load)
+    return (mine[:rows], mine[rows])
 
 
 def solution(mesh):

time: 81.9 us -> 81 us (0.989)
  blocking collectives: 0 us -> 14.3 us
  waiting for transfers between devices: 33 us -> 24.1 us
  starting transfers between devices: 23.3 us -> 17.8 us
  other arithmetic: 5.33 us -> 4.25 us
    all_to_all x0 -> x1, blocking collectives: none -> 14.3 us  [local(): lax.all_to_all(chunks, 'elem', split_axis=0, concat_axis=0, tiled=True)]
    all_to_all x1 -> x0, waiting for transfers between devices: 7.58 us -> none  [local(): lax.all_to_all(chunks, 'elem', split_axis=0, concat_axis=0, tiled=True)]
    all_to_all x1 -> x0, starting transfers between devices: 5.57 us -> none  [local(): lax.all_to_all(chunks, 'elem', split_axis=0, concat_axis=0, tiled=True)]
    all_to_all x1, waiting for transfers between devices: 17.1 us -> 15.7 us  [local(): lax.all_to_all(outgoing, 'elem', split_axis=0, concat_axis=0, tiled=True)]
    unnamed x16, local copies, waits for them, and re-layouts: 1.89 us -> 0.6 us
  transfers between devices with their start and end apart: 6 -> 5, of which waited for: 5 -> 4; matrix products, arithmetic and copies ran while one was open for 7% -> 8% of each run, Pallas kernels for 0% -> 0%
where the time goes in v16:
time: 81 us; the launch traced here: 79.5 us
  waiting for transfers between devices  24.1 us (30%)
  starting transfers between devices  17.8 us (22%)
  blocking collectives  14.3 us (18%)
  Pallas kernels  9.77 us (12%)
  local copies, waits for them, and re-layouts  7.73 us (10%)
  other arithmetic  4.25 us (5%)
  between operations  1.61 us (2%)
    all_to_all x1, waiting for transfers between devices, local(): lax.all_to_all(outgoing, 'elem', split_axis=0, concat_axis=0, tiled=True)  15.7 us
    all_to_all x1, blocking collectives, local(): lax.all_to_all(chunks, 'elem', split_axis=0, concat_axis=0, tiled=True)  14.3 us
    all_to_all x1, starting transfers between devices, local(): lax.all_to_all(outgoing, 'elem', split_axis=0, concat_axis=0, tiled=True)  11.8 us
    ppermute x3, waiting for transfers between devices, local(): halfway = halfway + lax.ppermute(piece, 'blk', ring)  6.38 us
    ppermute x3, starting transfers between devices, local(): halfway = halfway + lax.ppermute(piece, 'blk', ring)  5.92 us
    pallas_call x1, Pallas kernels, element_stage(): pl.pallas_call(element_body, out_shape=jax.ShapeDtypeStruct((modes + 8, m...  5.53 us
    pallas_call x1, Pallas kernels, gather_rows(): pl.pallas_call(gather_body, out_shape=jax.ShapeDtypeStruct((n_rows, comps...  4.24 us
    ppermute x1, waiting for transfers between devices, local(): chip_sum = kept + lax.ppermute(sent, 'blk', pair)  2 us
  transfers between devices with their start and end apart: 5, of which 4 were waited for; matrix products, arithmetic and copies ran while one was open for 8% of the time, Pallas kernels for 0%

profile of v16, /device:TPU:2, one launch (start us, length us, event | category | flops | bytes accessed | tf_op | source)
XLA Modules:
  0.0 79.5 jit_solution(12650910683372060435)
XLA Ops:
  0.6 4.2 %shard_map.95 = bf16[256,1536]{1,0:T(8,128)(2,1)} custom-call(bf16[3,1024,512]{2,1,0:T(8,128)(2,1)} %bitcast.30, s32[1,256]{1,0:T(1,128)} %bitcast.34), custom_call_target="tpu_custom_call" | custom-call | tf_op jit(solution)/shard_map/pallas_call | solution.py:125
  4.9 11.8 %all-to-all-start = ((bf16[32,8,1536]{2,1,0:T(8,128)(2,1)}), bf16[32,8,1536]{2,1,0:T(8,128)(2,1)S(1)}, u32[]{:S(2)}, u32[]{:S(2)}) async-start(bf16[32,8,1536]{2,1,0:T(8,128)(2,1)} %bitcast.32), calls=%async_computation | async-start | bytes 1572864 | tf_op jit(solution)/shard_map/all_to_all | solution.py:142
  16.7 0.6 reduce_sum.18
  17.3 0.6 dynamic_slice.24
  17.9 0.6 fusion.7
  18.6 0.7 copy.21.omega_ref
  19.3 0.9 %reshape.44.slot_ref = s32[512,1]{1,0:T(8,128)} reshape(s32[8,64]{1,0:T(8,128)S(1)} %copy-done.1) | data formatting | bytes 4096 | tf_op jit(solution)/shard_map/reshape | solution.py:107
  20.2 0.7 copy.22.stiff_ref
  21.6 1.8 %fusion.state_ref = bf16[1536,128]{1,0:T(8,128)(2,1)} fusion(s32[1536]{0:T(1024)S(1)} %add_select_fusion, bf16[1536]{0:T(1024)(128)(2,1)S(1)} %broadcast_in_dim.25), kind=kLoop, calls=%fused_computation.1 | loop fusion | flops 393216 | bytes 402432 | tf_op jit(solution)/shard_map/jit(_where)/select_n | solution.py:94
  23.4 15.7 %all-to-all-done = bf16[32,8,1536]{2,1,0:T(8,128)(2,1)S(1)} async-done(((bf16[32,8,1536]{2,1,0:T(8,128)(2,1)}), bf16[32,8,1536]{2,1,0:T(8,128)(2,1)S(1)}, u32[]{:S(2)}, u32[]{:S(2)}) %all-to-all-start) | async-done | bytes 786464 | tf_op jit(solution)/shard_map/all_to_all | solution.py:142
  39.1 0.6 broadcast_in_dim.28.scale_ref
  39.7 0.3 copy-done
  40.0 5.5 %shard_map.96 = f32[520,512]{1,0:T(8,128)} custom-call(bf16[256,1536]{1,0:T(8,128)(2,1)} %bitcast.31, s32[512,1]{1,0:T(8,128)} %reshape.44.slot_ref, bf16[1536,128]{1,0:T(8,128)(2,1)} %fusion.state_ref, f32[64,1]{1,0:T(8,128)} %copy.21.omega_ref, f32[64,1]{1,0:T(8,128)} %copy.22.stiff_ref, f32[8,128]{1,0:T(8,128)} %broadcast_in_dim.28.scale_ref), custom_call_target="tpu_custom_call" | custom-call | tf_op jit(solution)/shard_map/pallas_call | solution.py:98
  45.6 1.6 %copy.23 = f32[520,512]{0,1:T(8,128)S(1)} copy(f32[520,512]{1,0:T(8,128)} %shard_map.96) | data formatting | bytes 2129920 | tf_op jit(solution)/shard_map/pallas_call | solution.py:98
  47.2 0.1 dynamic-slice_bitcast_fusion
  47.2 0.1 collective-permute-start
  47.4 2.0 %collective-permute-done = f32[520,4,64]{0,2,1:T(8,128)S(1)} collective-permute-done((f32[520,4,64]{0,2,1:T(8,128)S(1)}, f32[520,4,64]{0,2,1:T(8,128)S(1)}, u32[]{:S(2)}, u32[]{:S(2)}) %collective-permute-start) | collective-permute-done | bytes 532512 | tf_op jit(solution)/shard_map/ppermute | solution.py:160
  49.4 0.1 bitcast_add_fusion
  49.6 1.7 %collective-permute-start.1 = (f32[520,64]{0,1:T(8,128)S(1)}, f32[520,64]{0,1:T(8,128)S(1)}, u32[]{:S(2)}, u32[]{:S(2)}) collective-permute-start(f32[520,64]{0,1:T(8,128)S(1)} %get-tuple-element.2), channel_id=1, source_target_pairs={{0,2},{1,3},{2,4},{3,5},{4,6},{5,7},{6,0},{7,1},{8,10},{9,11},{10,... | collective-permute-start | bytes 399368 | tf_op jit(solution)/shard_map/ppermute | solution.py:165
  51.2 2.9 %collective-permute-start.2 = (f32[520,64]{0,1:T(8,128)S(1)}, f32[520,64]{0,1:T(8,128)S(1)}, u32[]{:S(2)}, u32[]{:S(2)}) collective-permute-start(f32[520,64]{0,1:T(8,128)S(1)} %get-tuple-element.4), channel_id=1, source_target_pairs={{0,4},{1,5},{2,6},{3,7},{4,0},{5,1},{6,2},{7,3},{8,12},{9,13},{10,... | collective-permute-start | bytes 399368 | tf_op jit(solution)/shard_map/ppermute | solution.py:165
  54.1 1.3 %collective-permute-start.3 = (f32[520,64]{0,1:T(8,128)S(1)}, f32[520,64]{0,1:T(8,128)S(1)}, u32[]{:S(2)}, u32[]{:S(2)}) collective-permute-start(f32[520,64]{0,1:T(8,128)S(1)} %get-tuple-element.3), channel_id=1, source_target_pairs={{0,6},{1,7},{2,0},{3,1},{4,2},{5,3},{6,4},{7,5},{8,14},{9,15},{10,... | collective-permute-start | bytes 399368 | tf_op jit(solution)/shard_map/ppermute | solution.py:165
  55.5 1.7 %collective-permute-done.1 = f32[520,64]{0,1:T(8,128)S(1)} collective-permute-done((f32[520,64]{0,1:T(8,128)S(1)}, f32[520,64]{0,1:T(8,128)S(1)}, u32[]{:S(2)}, u32[]{:S(2)}) %collective-permute-start.1) | collective-permute-done | bytes 133152 | tf_op jit(solution)/shard_map/ppermute | solution.py:165
  57.2 4.7 %collective-permute-done.2 = f32[520,64]{0,1:T(8,128)S(1)} collective-permute-done((f32[520,64]{0,1:T(8,128)S(1)}, f32[520,64]{0,1:T(8,128)S(1)}, u32[]{:S(2)}, u32[]{:S(2)}) %collective-permute-start.2) | collective-permute-done | bytes 133152 | tf_op jit(solution)/shard_map/ppermute | solution.py:165
  61.9 0.1 slice_reduce_fusion
  62.0 0.1 copy.24
  62.3 0.2 reshape.46
  62.5 14.3 %all_to_all.16 = f32[32,1,1088]{2,1,0:T(1,128)S(1)} all-to-all(f32[32,1,1088]{2,1,0:T(1,128)S(1)} %reshape.46), channel_id=1, replica_groups=mesh['elem'=32,'blk'=8] {'elem'}, dimensions={0} | all-to-all | bytes 278528 | tf_op jit(solution)/shard_map/all_to_all | solution.py:171
  76.7 0.5 broadcast.48
  77.2 1.0 %reduce.2 = f32[32,1088]{1,0:T(8,128)S(1)} reduce(f32[32,1,1088]{2,1,0:T(1,128)S(1)} %all_to_all.16, f32[]{:T(128)} %broadcast.48), dimensions={1}, to_apply=%all_to_all.13.reduce_sub_computation | reduce | bytes 278532 | tf_op jit(solution)/shard_map/all_to_all | solution.py:171
  78.2 0.1 reshape.47
  78.4 0.6 slice.18
  79.0 0.5 slice_bitcast_fusion
  (24 shorter events, 0.3 us)
Async XLA Ops:
  4.9 11.8 %copy-start.6 = (s32[32]{0:T(128)S(1)}, s32[32]{0:T(128)}, u32[]{:S(2)}) copy-start(s32[32]{0:T(128)} %param.11) | copy-start | bytes 388
  4.9 13.0 %copy-start.4 = (f32[64]{0:T(128)S(1)}, f32[64]{0:T(128)}, u32[]{:S(2)}) copy-start(f32[64]{0:T(128)} %param.12) | copy-start | bytes 772
  4.9 14.4 %copy-start.2 = (bf16[512]{0:T(512)(128)(2,1)S(1)}, bf16[512]{0:T(512)(128)(2,1)}, u32[]{:S(2)}) copy-start(bf16[512]{0:T(512)(128)(2,1)} %param.14) | copy-start | bytes 3076
  4.9 14.4 %copy-start.1 = (s32[8,64]{1,0:T(8,128)S(1)}, s32[8,64]{1,0:T(8,128)}, u32[]{:S(2)}) copy-start(s32[8,64]{1,0:T(8,128)} %param.10) | copy-start | bytes 6148
  4.9 15.3 %copy-start.3 = (f32[64]{0:T(128)S(1)}, f32[64]{0:T(128)}, u32[]{:S(2)}) copy-start(f32[64]{0:T(128)} %param.13) | copy-start | bytes 772
  4.9 34.2 %all-to-all-start = ((bf16[32,8,1536]{2,1,0:T(8,128)(2,1)}), bf16[32,8,1536]{2,1,0:T(8,128)(2,1)S(1)}, u32[]{:S(2)}, u32[]{:S(2)}) async-start(bf16[32,8,1536]{2,1,0:T(8,128)(2,1)} %bitcast.32), calls=%async_computation | async-start | bytes 1572864 | tf_op jit(solution)/shard_map/all_to_all | solution.py:142
  39.1 0.9 %copy-start = (bf16[32,8,1536]{2,1,0:T(8,128)(2,1)}, bf16[32,8,1536]{2,1,0:T(8,128)(2,1)S(1)}, u32[]{:S(2)}) copy-start(bf16[32,8,1536]{2,1,0:T(8,128)(2,1)S(1)} %all-to-all-done) | copy-start | bytes 2359300
  47.2 2.2 %collective-permute-start = (f32[520,4,64]{0,2,1:T(8,128)S(1)}, f32[520,4,64]{0,2,1:T(8,128)S(1)}, u32[]{:S(2)}, u32[]{:S(2)}) collective-permute-start(f32[520,4,64]{0,2,1:T(8,128)S(1)} %dynamic-slice_bitcast_fusion), channel_id=1, source_target_pairs={{0,1},{1,0},{2,3},{3,2},{4,5},{5,4},{6,7},{7,6},{8,9},{9,8},{10,11... | collective-permute-start | bytes 1597448 | tf_op jit(solution)/shard_map/ppermute | solution.py:160
  49.5 12.7 %copy-start.5 = (f32[64]{0:T(128)S(1)}, f32[64]{0:T(128)}, u32[]{:S(2)}) copy-start(f32[64]{0:T(128)} %param.15) | copy-start | bytes 772
  49.6 7.6 %collective-permute-start.1 = (f32[520,64]{0,1:T(8,128)S(1)}, f32[520,64]{0,1:T(8,128)S(1)}, u32[]{:S(2)}, u32[]{:S(2)}) collective-permute-start(f32[520,64]{0,1:T(8,128)S(1)} %get-tuple-element.2), channel_id=1, source_target_pairs={{0,2},{1,3},{2,4},{3,5},{4,6},{5,7},{6,0},{7,1},{8,10},{9,11},{10,... | collective-permute-start | bytes 399368 | tf_op jit(solution)/shard_map/ppermute | solution.py:165
  51.2 10.6 %collective-permute-start.2 = (f32[520,64]{0,1:T(8,128)S(1)}, f32[520,64]{0,1:T(8,128)S(1)}, u32[]{:S(2)}, u32[]{:S(2)}) collective-permute-start(f32[520,64]{0,1:T(8,128)S(1)} %get-tuple-element.4), channel_id=1, source_target_pairs={{0,4},{1,5},{2,6},{3,7},{4,0},{5,1},{6,2},{7,3},{8,12},{9,13},{10,... | collective-permute-start | bytes 399368 | tf_op jit(solution)/shard_map/ppermute | solution.py:165
  54.1 7.7 %collective-permute-start.3 = (f32[520,64]{0,1:T(8,128)S(1)}, f32[520,64]{0,1:T(8,128)S(1)}, u32[]{:S(2)}, u32[]{:S(2)}) collective-permute-start(f32[520,64]{0,1:T(8,128)S(1)} %get-tuple-element.3), channel_id=1, source_target_pairs={{0,6},{1,7},{2,0},{3,1},{4,2},{5,3},{6,4},{7,5},{8,14},{9,15},{10,... | collective-permute-start | bytes 399368 | tf_op jit(solution)/shard_map/ppermute | solution.py:165

commit v17 on v16

--- a/solution.py
+++ b/solution.py
@@ -168,8 +168,9 @@
     chunks = jnp.concatenate(
         [tangent_rows, jnp.broadcast_to(force_cols[None, None, :], (n_elem, 1, cols))], axis=1
     )
-    arrived_chunks = lax.all_to_all(chunks, "elem", split_axis=0, concat_axis=0, tiled=True)
-    mine = jnp.sum(arrived_chunks, axis=0)
+    flat = chunks.reshape(n_elem, (rows + 1) * cols)
+    arrived_chunks = lax.all_to_all(flat, "elem", split_axis=0, concat_axis=0, tiled=True)
+    mine = jnp.sum(arrived_chunks, axis=0).reshape(rows + 1, cols)
     return (mine[:rows], mine[rows])
 
 

time: 81 us -> 79.6 us (0.983)
  other arithmetic: 4.25 us -> 3.28 us
    all_to_all x1 -> x0, other arithmetic: 0.99 us -> none  [local(): lax.all_to_all(chunks, 'elem', split_axis=0, concat_axis=0, tiled=True)]
  transfers between devices with their start and end apart: 5 -> 5, of which waited for: 4 -> 5; matrix products, arithmetic and copies ran while one was open for 8% -> 8% of each run, Pallas kernels for 0% -> 0%
where the time goes in v17:
time: 79.6 us; the launch traced here: 78 us
  waiting for transfers between devices  24.7 us (31%)
  starting transfers between devices  17.2 us (22%)
  blocking collectives  14.3 us (18%)
  Pallas kernels  9.77 us (12%)
  local copies, waits for them, and re-layouts  7.22 us (9%)
  other arithmetic  3.28 us (4%)
  between operations  1.58 us (2%)
    all_to_all x1, waiting for transfers between devices, local(): lax.all_to_all(outgoing, 'elem', split_axis=0, concat_axis=0, tiled=True)  15.7 us
    all_to_all x1, blocking collectives, local(): lax.all_to_all(flat, 'elem', split_axis=0, concat_axis=0, tiled=True)  14.3 us
    all_to_all x1, starting transfers between devices, local(): lax.all_to_all(outgoing, 'elem', split_axis=0, concat_axis=0, tiled=True)  11.8 us
    ppermute x3, waiting for transfers between devices, local(): halfway = halfway + lax.ppermute(piece, 'blk', ring)  6.98 us
    pallas_call x1, Pallas kernels, element_stage(): pl.pallas_call(element_body, out_shape=jax.ShapeDtypeStruct((modes + 8, m...  5.53 us
    ppermute x3, starting transfers between devices, local(): halfway = halfway + lax.ppermute(piece, 'blk', ring)  5.32 us
    pallas_call x1, Pallas kernels, gather_rows(): pl.pallas_call(gather_body, out_shape=jax.ShapeDtypeStruct((n_rows, comps...  4.24 us
    ppermute x1, waiting for transfers between devices, local(): chip_sum = kept + lax.ppermute(sent, 'blk', pair)  2 us
  transfers between devices with their start and end apart: 5, of which 5 were waited for; matrix products, arithmetic and copies ran while one was open for 8% of the time, Pallas kernels for 0%

profile of v17, /device:TPU:2, one launch (start us, length us, event | category | flops | bytes accessed | tf_op | source)
XLA Modules:
  0.0 78.0 jit_solution(17731234197620557732)
XLA Ops:
  0.6 4.2 %shard_map.95 = bf16[256,1536]{1,0:T(8,128)(2,1)} custom-call(bf16[3,1024,512]{2,1,0:T(8,128)(2,1)} %bitcast.28, s32[1,256]{1,0:T(1,128)} %bitcast.32), custom_call_target="tpu_custom_call" | custom-call | tf_op jit(solution)/shard_map/pallas_call | solution.py:125
  4.9 0.0 copy-start.3
  4.9 11.8 %all-to-all-start = ((bf16[32,8,1536]{2,1,0:T(8,128)(2,1)}), bf16[32,8,1536]{2,1,0:T(8,128)(2,1)S(1)}, u32[]{:S(2)}, u32[]{:S(2)}) async-start(bf16[32,8,1536]{2,1,0:T(8,128)(2,1)} %bitcast.30), calls=%async_computation | async-start | bytes 1572864 | tf_op jit(solution)/shard_map/all_to_all | solution.py:142
  16.7 0.6 reduce_sum.18
  18.0 0.6 dynamic_slice.24
  18.6 0.6 fusion.7
  19.3 0.7 copy.27.omega_ref
  20.0 0.7 copy.28.stiff_ref
  20.7 0.9 %reshape.60.slot_ref = s32[512,1]{1,0:T(8,128)} reshape(s32[8,64]{1,0:T(8,128)S(1)} %copy-done.1) | data formatting | bytes 4096 | tf_op jit(solution)/shard_map/reshape | solution.py:107
  21.6 1.7 %fusion.state_ref = bf16[1536,128]{1,0:T(8,128)(2,1)} fusion(s32[1536]{0:T(1024)S(1)} %add_select_fusion, bf16[1536]{0:T(1024)(128)(2,1)S(1)} %broadcast_in_dim.25), kind=kLoop, calls=%fused_computation.1 | loop fusion | flops 393216 | bytes 402432 | tf_op jit(solution)/shard_map/jit(_where)/select_n | solution.py:94
  23.4 15.7 %all-to-all-done = bf16[32,8,1536]{2,1,0:T(8,128)(2,1)S(1)} async-done(((bf16[32,8,1536]{2,1,0:T(8,128)(2,1)}), bf16[32,8,1536]{2,1,0:T(8,128)(2,1)S(1)}, u32[]{:S(2)}, u32[]{:S(2)}) %all-to-all-start) | async-done | bytes 786464 | tf_op jit(solution)/shard_map/all_to_all | solution.py:142
  39.1 0.6 broadcast_in_dim.28.scale_ref
  39.7 0.3 copy-done
  40.0 5.5 %shard_map.96 = f32[520,512]{1,0:T(8,128)} custom-call(bf16[256,1536]{1,0:T(8,128)(2,1)} %bitcast.29, s32[512,1]{1,0:T(8,128)} %reshape.60.slot_ref, bf16[1536,128]{1,0:T(8,128)(2,1)} %fusion.state_ref, f32[64,1]{1,0:T(8,128)} %copy.27.omega_ref, f32[64,1]{1,0:T(8,128)} %copy.28.stiff_ref, f32[8,128]{1,0:T(8,128)} %broadcast_in_dim.28.scale_ref), custom_call_target="tpu_custom_call" | custom-call | tf_op jit(solution)/shard_map/pallas_call | solution.py:98
  45.6 1.6 %copy.29 = f32[520,512]{0,1:T(8,128)S(1)} copy(f32[520,512]{1,0:T(8,128)} %shard_map.96) | data formatting | bytes 2129920 | tf_op jit(solution)/shard_map/pallas_call | solution.py:98
  47.2 0.1 dynamic-slice_bitcast_fusion
  47.3 0.1 collective-permute-start
  47.4 2.0 %collective-permute-done = f32[520,4,64]{0,2,1:T(8,128)S(1)} collective-permute-done((f32[520,4,64]{0,2,1:T(8,128)S(1)}, f32[520,4,64]{0,2,1:T(8,128)S(1)}, u32[]{:S(2)}, u32[]{:S(2)}) %collective-permute-start) | collective-permute-done | bytes 532512 | tf_op jit(solution)/shard_map/ppermute | solution.py:160
  49.4 0.1 bitcast_add_fusion
  49.6 1.7 %collective-permute-start.1 = (f32[520,64]{0,1:T(8,128)S(1)}, f32[520,64]{0,1:T(8,128)S(1)}, u32[]{:S(2)}, u32[]{:S(2)}) collective-permute-start(f32[520,64]{0,1:T(8,128)S(1)} %get-tuple-element.2), channel_id=1, source_target_pairs={{0,2},{1,3},{2,4},{3,5},{4,6},{5,7},{6,0},{7,1},{8,10},{9,11},{10,... | collective-permute-start | bytes 399368 | tf_op jit(solution)/shard_map/ppermute | solution.py:165
  51.3 1.6 %collective-permute-start.3 = (f32[520,64]{0,1:T(8,128)S(1)}, f32[520,64]{0,1:T(8,128)S(1)}, u32[]{:S(2)}, u32[]{:S(2)}) collective-permute-start(f32[520,64]{0,1:T(8,128)S(1)} %get-tuple-element.3), channel_id=1, source_target_pairs={{0,6},{1,7},{2,0},{3,1},{4,2},{5,3},{6,4},{7,5},{8,14},{9,15},{10,... | collective-permute-start | bytes 399368 | tf_op jit(solution)/shard_map/ppermute | solution.py:165
  52.9 2.0 %collective-permute-start.2 = (f32[520,64]{0,1:T(8,128)S(1)}, f32[520,64]{0,1:T(8,128)S(1)}, u32[]{:S(2)}, u32[]{:S(2)}) collective-permute-start(f32[520,64]{0,1:T(8,128)S(1)} %get-tuple-element.4), channel_id=1, source_target_pairs={{0,4},{1,5},{2,6},{3,7},{4,0},{5,1},{6,2},{7,3},{8,12},{9,13},{10,... | collective-permute-start | bytes 399368 | tf_op jit(solution)/shard_map/ppermute | solution.py:165
  54.9 2.3 %collective-permute-done.1 = f32[520,64]{0,1:T(8,128)S(1)} collective-permute-done((f32[520,64]{0,1:T(8,128)S(1)}, f32[520,64]{0,1:T(8,128)S(1)}, u32[]{:S(2)}, u32[]{:S(2)}) %collective-permute-start.1) | collective-permute-done | bytes 133152 | tf_op jit(solution)/shard_map/ppermute | solution.py:165
  57.2 2.9 %collective-permute-done.3 = f32[520,64]{0,1:T(8,128)S(1)} collective-permute-done((f32[520,64]{0,1:T(8,128)S(1)}, f32[520,64]{0,1:T(8,128)S(1)}, u32[]{:S(2)}, u32[]{:S(2)}) %collective-permute-start.3) | collective-permute-done | bytes 133152 | tf_op jit(solution)/shard_map/ppermute | solution.py:165
  60.1 1.8 %collective-permute-done.2 = f32[520,64]{0,1:T(8,128)S(1)} collective-permute-done((f32[520,64]{0,1:T(8,128)S(1)}, f32[520,64]{0,1:T(8,128)S(1)}, u32[]{:S(2)}, u32[]{:S(2)}) %collective-permute-start.2) | collective-permute-done | bytes 133152 | tf_op jit(solution)/shard_map/ppermute | solution.py:165
  61.9 0.1 slice_reduce_fusion
  62.0 0.1 copy.30
  62.3 0.2 all_to_all.18
  62.5 14.3 %all_to_all.21 = f32[32,1,1088]{2,1,0:T(1,128)S(1)} all-to-all(f32[32,1,1088]{2,1,0:T(1,128)S(1)} %all_to_all.18), channel_id=1, replica_groups=mesh['elem'=32,'blk'=8] {'elem'}, dimensions={0} | all-to-all | bytes 278528 | tf_op jit(solution)/shard_map/all_to_all | solution.py:172
  76.7 0.1 reduce_sum.19
  76.8 0.5 slice.32
  77.4 0.7 slice.27
  (22 shorter events, 0.2 us)
Async XLA Ops:
  4.9 11.8 %copy-start.6 = (s32[32]{0:T(128)S(1)}, s32[32]{0:T(128)}, u32[]{:S(2)}) copy-start(s32[32]{0:T(128)} %param.11) | copy-start | bytes 388
  4.9 13.7 %copy-start.2 = (bf16[512]{0:T(512)(128)(2,1)S(1)}, bf16[512]{0:T(512)(128)(2,1)}, u32[]{:S(2)}) copy-start(bf16[512]{0:T(512)(128)(2,1)} %param.14) | copy-start | bytes 3076
  4.9 13.8 %copy-start.4 = (f32[64]{0:T(128)S(1)}, f32[64]{0:T(128)}, u32[]{:S(2)}) copy-start(f32[64]{0:T(128)} %param.12) | copy-start | bytes 772
  4.9 15.1 %copy-start.3 = (f32[64]{0:T(128)S(1)}, f32[64]{0:T(128)}, u32[]{:S(2)}) copy-start(f32[64]{0:T(128)} %param.13) | copy-start | bytes 772
  4.9 15.8 %copy-start.1 = (s32[8,64]{1,0:T(8,128)S(1)}, s32[8,64]{1,0:T(8,128)}, u32[]{:S(2)}) copy-start(s32[8,64]{1,0:T(8,128)} %param.10) | copy-start | bytes 6148
  4.9 34.2 %all-to-all-start = ((bf16[32,8,1536]{2,1,0:T(8,128)(2,1)}), bf16[32,8,1536]{2,1,0:T(8,128)(2,1)S(1)}, u32[]{:S(2)}, u32[]{:S(2)}) async-start(bf16[32,8,1536]{2,1,0:T(8,128)(2,1)} %bitcast.30), calls=%async_computation | async-start | bytes 1572864 | tf_op jit(solution)/shard_map/all_to_all | solution.py:142
  39.1 0.9 %copy-start = (bf16[32,8,1536]{2,1,0:T(8,128)(2,1)}, bf16[32,8,1536]{2,1,0:T(8,128)(2,1)S(1)}, u32[]{:S(2)}) copy-start(bf16[32,8,1536]{2,1,0:T(8,128)(2,1)S(1)} %all-to-all-done) | copy-start | bytes 2359300
  47.3 2.2 %collective-permute-start = (f32[520,4,64]{0,2,1:T(8,128)S(1)}, f32[520,4,64]{0,2,1:T(8,128)S(1)}, u32[]{:S(2)}, u32[]{:S(2)}) collective-permute-start(f32[520,4,64]{0,2,1:T(8,128)S(1)} %dynamic-slice_bitcast_fusion), channel_id=1, source_target_pairs={{0,1},{1,0},{2,3},{3,2},{4,5},{5,4},{6,7},{7,6},{8,9},{9,8},{10,11... | collective-permute-start | bytes 1597448 | tf_op jit(solution)/shard_map/ppermute | solution.py:160
  49.5 12.7 %copy-start.5 = (f32[64]{0:T(128)S(1)}, f32[64]{0:T(128)}, u32[]{:S(2)}) copy-start(f32[64]{0:T(128)} %param.15) | copy-start | bytes 772
  49.6 7.6 %collective-permute-start.1 = (f32[520,64]{0,1:T(8,128)S(1)}, f32[520,64]{0,1:T(8,128)S(1)}, u32[]{:S(2)}, u32[]{:S(2)}) collective-permute-start(f32[520,64]{0,1:T(8,128)S(1)} %get-tuple-element.2), channel_id=1, source_target_pairs={{0,2},{1,3},{2,4},{3,5},{4,6},{5,7},{6,0},{7,1},{8,10},{9,11},{10,... | collective-permute-start | bytes 399368 | tf_op jit(solution)/shard_map/ppermute | solution.py:165
  51.3 8.8 %collective-permute-start.3 = (f32[520,64]{0,1:T(8,128)S(1)}, f32[520,64]{0,1:T(8,128)S(1)}, u32[]{:S(2)}, u32[]{:S(2)}) collective-permute-start(f32[520,64]{0,1:T(8,128)S(1)} %get-tuple-element.3), channel_id=1, source_target_pairs={{0,6},{1,7},{2,0},{3,1},{4,2},{5,3},{6,4},{7,5},{8,14},{9,15},{10,... | collective-permute-start | bytes 399368 | tf_op jit(solution)/shard_map/ppermute | solution.py:165
  52.9 9.0 %collective-permute-start.2 = (f32[520,64]{0,1:T(8,128)S(1)}, f32[520,64]{0,1:T(8,128)S(1)}, u32[]{:S(2)}, u32[]{:S(2)}) collective-permute-start(f32[520,64]{0,1:T(8,128)S(1)} %get-tuple-element.4), channel_id=1, source_target_pairs={{0,4},{1,5},{2,6},{3,7},{4,0},{5,1},{6,2},{7,3},{8,12},{9,13},{10,... | collective-permute-start | bytes 399368 | tf_op jit(solution)/shard_map/ppermute | solution.py:165

commit v18 on v17

--- a/solution.py
+++ b/solution.py
@@ -109,28 +109,26 @@
 
 
 def gather_body(basis_ref, rows_ref, out_ref):
-    nodes = basis_ref.shape[1]
+    comps, nodes, modes = basis_ref.shape
     n_rows = rows_ref.shape[1]
     node = lax.broadcasted_iota(jnp.int32, (nodes, n_rows), 0)
     onehot_t = (node == rows_ref[...]).astype(jnp.bfloat16)
-    picked = lax.dot_general(
-        onehot_t, basis_ref[0], (((0,), (0,)), ((), ())), preferred_element_type=jnp.float32
-    )
-    out_ref[...] = picked.astype(jnp.bfloat16)
+    for c in range(comps):
+        picked = lax.dot_general(
+            onehot_t, basis_ref[c], (((0,), (0,)), ((), ())), preferred_element_type=jnp.float32
+        )
+        out_ref[:, pl.ds(c * modes, modes)] = picked.astype(jnp.bfloat16)
 
 
 def gather_rows(by_component, rows):
     comps, nodes, modes = by_component.shape
     n_rows = rows.shape[0]
+    vmem = pltpu.MemorySpace.VMEM if hasattr(pltpu, "MemorySpace") else pltpu.TPUMemorySpace.VMEM
     return pl.pallas_call(
         gather_body,
         out_shape=jax.ShapeDtypeStruct((n_rows, comps * modes), jnp.bfloat16),
-        grid=(comps,),
-        in_specs=[
-            pl.BlockSpec((1, nodes, modes), lambda c: (c, 0, 0)),
-            pl.BlockSpec((1, n_rows), lambda c: (0, 0)),
-        ],
-        out_specs=pl.BlockSpec((n_rows, modes), lambda c: (0, c)),
+        in_specs=[pl.BlockSpec(memory_space=vmem)] * 2,
+        out_specs=pl.BlockSpec(memory_space=vmem),
     )(by_component, rows.reshape(1, n_rows))
 
 def local(basis, send_rows, elem_slot, set_size, elem_weight, element_stiffening, state, load):

time: 79.6 us -> 79.1 us (level)
  no operation moved by 1% of the time
where the time goes in v18:
time: 79.1 us; the launch traced here: 77.6 us
  waiting for transfers between devices  24.7 us (31%)
  starting transfers between devices  17.1 us (22%)
  blocking collectives  14.3 us (18%)
  Pallas kernels  9.34 us (12%)
  local copies, waits for them, and re-layouts  7.21 us (9%)
  other arithmetic  3.28 us (4%)
  between operations  1.58 us (2%)
    all_to_all x1, waiting for transfers between devices, local(): lax.all_to_all(outgoing, 'elem', split_axis=0, concat_axis=0, tiled=True)  15.7 us
    all_to_all x1, blocking collectives, local(): lax.all_to_all(flat, 'elem', split_axis=0, concat_axis=0, tiled=True)  14.3 us
    all_to_all x1, starting transfers between devices, local(): lax.all_to_all(outgoing, 'elem', split_axis=0, concat_axis=0, tiled=True)  11.8 us
    ppermute x3, waiting for transfers between devices, local(): halfway = halfway + lax.ppermute(piece, 'blk', ring)  6.98 us
    pallas_call x1, Pallas kernels, element_stage(): pl.pallas_call(element_body, out_shape=jax.ShapeDtypeStruct((modes + 8, m...  5.53 us
    ppermute x3, starting transfers between devices, local(): halfway = halfway + lax.ppermute(piece, 'blk', ring)  5.3 us
    pallas_call x1, Pallas kernels, gather_rows(): pl.pallas_call(gather_body, out_shape=jax.ShapeDtypeStruct((n_rows, comps...  3.81 us
    ppermute x1, waiting for transfers between devices, local(): chip_sum = kept + lax.ppermute(sent, 'blk', pair)  2 us
  transfers between devices with their start and end apart: 5, of which 5 were waited for; matrix products, arithmetic and copies ran while one was open for 8% of the time, Pallas kernels for 0%

profile of v18, /device:TPU:2, one launch (start us, length us, event | category | flops | bytes accessed | tf_op | source)
XLA Modules:
  0.0 77.6 jit_solution(16616773720535431726)
XLA Ops:
  0.6 3.8 %shard_map.95 = bf16[256,1536]{1,0:T(8,128)(2,1)} custom-call(bf16[3,1024,512]{2,1,0:T(8,128)(2,1)} %bitcast.28, s32[1,256]{1,0:T(1,128)} %bitcast.32), custom_call_target="tpu_custom_call" | custom-call | tf_op jit(solution)/shard_map/pallas_call | solution.py:127
  4.5 0.0 copy-start.1
  4.5 11.8 %all-to-all-start = ((bf16[32,8,1536]{2,1,0:T(8,128)(2,1)}), bf16[32,8,1536]{2,1,0:T(8,128)(2,1)S(1)}, u32[]{:S(2)}, u32[]{:S(2)}) async-start(bf16[32,8,1536]{2,1,0:T(8,128)(2,1)} %bitcast.30), calls=%async_computation | async-start | bytes 1572864 | tf_op jit(solution)/shard_map/all_to_all | solution.py:140
  16.3 0.6 reduce_sum.18
  17.6 0.6 dynamic_slice.24
  18.2 0.6 fusion.7
  18.9 0.7 copy.27.omega_ref
  19.6 0.7 copy.28.stiff_ref
  20.3 0.9 %reshape.60.slot_ref = s32[512,1]{1,0:T(8,128)} reshape(s32[8,64]{1,0:T(8,128)S(1)} %copy-done.1) | data formatting | bytes 4096 | tf_op jit(solution)/shard_map/reshape | solution.py:107
  21.2 1.7 %fusion.state_ref = bf16[1536,128]{1,0:T(8,128)(2,1)} fusion(s32[1536]{0:T(1024)S(1)} %add_select_fusion, bf16[1536]{0:T(1024)(128)(2,1)S(1)} %broadcast_in_dim.25), kind=kLoop, calls=%fused_computation.1 | loop fusion | flops 393216 | bytes 402432 | tf_op jit(solution)/shard_map/jit(_where)/select_n | solution.py:94
  22.9 15.7 %all-to-all-done = bf16[32,8,1536]{2,1,0:T(8,128)(2,1)S(1)} async-done(((bf16[32,8,1536]{2,1,0:T(8,128)(2,1)}), bf16[32,8,1536]{2,1,0:T(8,128)(2,1)S(1)}, u32[]{:S(2)}, u32[]{:S(2)}) %all-to-all-start) | async-done | bytes 786464 | tf_op jit(solution)/shard_map/all_to_all | solution.py:140
  38.7 0.6 broadcast_in_dim.28.scale_ref
  39.3 0.3 copy-done
  39.6 5.5 %shard_map.96 = f32[520,512]{1,0:T(8,128)} custom-call(bf16[256,1536]{1,0:T(8,128)(2,1)} %bitcast.29, s32[512,1]{1,0:T(8,128)} %reshape.60.slot_ref, bf16[1536,128]{1,0:T(8,128)(2,1)} %fusion.state_ref, f32[64,1]{1,0:T(8,128)} %copy.27.omega_ref, f32[64,1]{1,0:T(8,128)} %copy.28.stiff_ref, f32[8,128]{1,0:T(8,128)} %broadcast_in_dim.28.scale_ref), custom_call_target="tpu_custom_call" | custom-call | tf_op jit(solution)/shard_map/pallas_call | solution.py:98
  45.1 1.6 %copy.29 = f32[520,512]{0,1:T(8,128)S(1)} copy(f32[520,512]{1,0:T(8,128)} %shard_map.96) | data formatting | bytes 2129920 | tf_op jit(solution)/shard_map/pallas_call | solution.py:98
  46.8 0.1 dynamic-slice_bitcast_fusion
  46.8 0.1 collective-permute-start
  47.0 2.0 %collective-permute-done = f32[520,4,64]{0,2,1:T(8,128)S(1)} collective-permute-done((f32[520,4,64]{0,2,1:T(8,128)S(1)}, f32[520,4,64]{0,2,1:T(8,128)S(1)}, u32[]{:S(2)}, u32[]{:S(2)}) %collective-permute-start) | collective-permute-done | bytes 532512 | tf_op jit(solution)/shard_map/ppermute | solution.py:158
  49.0 0.1 bitcast_add_fusion
  49.1 1.7 %collective-permute-start.1 = (f32[520,64]{0,1:T(8,128)S(1)}, f32[520,64]{0,1:T(8,128)S(1)}, u32[]{:S(2)}, u32[]{:S(2)}) collective-permute-start(f32[520,64]{0,1:T(8,128)S(1)} %get-tuple-element.2), channel_id=1, source_target_pairs={{0,2},{1,3},{2,4},{3,5},{4,6},{5,7},{6,0},{7,1},{8,10},{9,11},{10,... | collective-permute-start | bytes 399368 | tf_op jit(solution)/shard_map/ppermute | solution.py:163
  50.8 1.7 %collective-permute-start.3 = (f32[520,64]{0,1:T(8,128)S(1)}, f32[520,64]{0,1:T(8,128)S(1)}, u32[]{:S(2)}, u32[]{:S(2)}) collective-permute-start(f32[520,64]{0,1:T(8,128)S(1)} %get-tuple-element.3), channel_id=1, source_target_pairs={{0,6},{1,7},{2,0},{3,1},{4,2},{5,3},{6,4},{7,5},{8,14},{9,15},{10,... | collective-permute-start | bytes 399368 | tf_op jit(solution)/shard_map/ppermute | solution.py:163
  52.5 2.0 %collective-permute-start.2 = (f32[520,64]{0,1:T(8,128)S(1)}, f32[520,64]{0,1:T(8,128)S(1)}, u32[]{:S(2)}, u32[]{:S(2)}) collective-permute-start(f32[520,64]{0,1:T(8,128)S(1)} %get-tuple-element.4), channel_id=1, source_target_pairs={{0,4},{1,5},{2,6},{3,7},{4,0},{5,1},{6,2},{7,3},{8,12},{9,13},{10,... | collective-permute-start | bytes 399368 | tf_op jit(solution)/shard_map/ppermute | solution.py:163
  54.4 2.3 %collective-permute-done.1 = f32[520,64]{0,1:T(8,128)S(1)} collective-permute-done((f32[520,64]{0,1:T(8,128)S(1)}, f32[520,64]{0,1:T(8,128)S(1)}, u32[]{:S(2)}, u32[]{:S(2)}) %collective-permute-start.1) | collective-permute-done | bytes 133152 | tf_op jit(solution)/shard_map/ppermute | solution.py:163
  56.7 2.9 %collective-permute-done.3 = f32[520,64]{0,1:T(8,128)S(1)} collective-permute-done((f32[520,64]{0,1:T(8,128)S(1)}, f32[520,64]{0,1:T(8,128)S(1)}, u32[]{:S(2)}, u32[]{:S(2)}) %collective-permute-start.3) | collective-permute-done | bytes 133152 | tf_op jit(solution)/shard_map/ppermute | solution.py:163
  59.6 1.8 %collective-permute-done.2 = f32[520,64]{0,1:T(8,128)S(1)} collective-permute-done((f32[520,64]{0,1:T(8,128)S(1)}, f32[520,64]{0,1:T(8,128)S(1)}, u32[]{:S(2)}, u32[]{:S(2)}) %collective-permute-start.2) | collective-permute-done | bytes 133152 | tf_op jit(solution)/shard_map/ppermute | solution.py:163
  61.5 0.1 slice_reduce_fusion
  61.6 0.1 copy.30
  61.8 0.2 all_to_all.18
  62.0 14.3 %all_to_all.21 = f32[32,1,1088]{2,1,0:T(1,128)S(1)} all-to-all(f32[32,1,1088]{2,1,0:T(1,128)S(1)} %all_to_all.18), channel_id=1, replica_groups=mesh['elem'=32,'blk'=8] {'elem'}, dimensions={0} | all-to-all | bytes 278528 | tf_op jit(solution)/shard_map/all_to_all | solution.py:170
  76.3 0.1 reduce_sum.19
  76.4 0.5 slice.32
  76.9 0.7 slice.27
  (22 shorter events, 0.2 us)
Async XLA Ops:
  4.4 11.8 %copy-start.6 = (s32[32]{0:T(128)S(1)}, s32[32]{0:T(128)}, u32[]{:S(2)}) copy-start(s32[32]{0:T(128)} %param.11) | copy-start | bytes 388
  4.4 13.7 %copy-start.2 = (bf16[512]{0:T(512)(128)(2,1)S(1)}, bf16[512]{0:T(512)(128)(2,1)}, u32[]{:S(2)}) copy-start(bf16[512]{0:T(512)(128)(2,1)} %param.14) | copy-start | bytes 3076
  4.4 13.8 %copy-start.4 = (f32[64]{0:T(128)S(1)}, f32[64]{0:T(128)}, u32[]{:S(2)}) copy-start(f32[64]{0:T(128)} %param.12) | copy-start | bytes 772
  4.4 15.1 %copy-start.3 = (f32[64]{0:T(128)S(1)}, f32[64]{0:T(128)}, u32[]{:S(2)}) copy-start(f32[64]{0:T(128)} %param.13) | copy-start | bytes 772
  4.5 15.8 %copy-start.1 = (s32[8,64]{1,0:T(8,128)S(1)}, s32[8,64]{1,0:T(8,128)}, u32[]{:S(2)}) copy-start(s32[8,64]{1,0:T(8,128)} %param.10) | copy-start | bytes 6148
  4.5 34.2 %all-to-all-start = ((bf16[32,8,1536]{2,1,0:T(8,128)(2,1)}), bf16[32,8,1536]{2,1,0:T(8,128)(2,1)S(1)}, u32[]{:S(2)}, u32[]{:S(2)}) async-start(bf16[32,8,1536]{2,1,0:T(8,128)(2,1)} %bitcast.30), calls=%async_computation | async-start | bytes 1572864 | tf_op jit(solution)/shard_map/all_to_all | solution.py:140
  38.7 0.9 %copy-start = (bf16[32,8,1536]{2,1,0:T(8,128)(2,1)}, bf16[32,8,1536]{2,1,0:T(8,128)(2,1)S(1)}, u32[]{:S(2)}) copy-start(bf16[32,8,1536]{2,1,0:T(8,128)(2,1)S(1)} %all-to-all-done) | copy-start | bytes 2359300
  46.8 2.2 %collective-permute-start = (f32[520,4,64]{0,2,1:T(8,128)S(1)}, f32[520,4,64]{0,2,1:T(8,128)S(1)}, u32[]{:S(2)}, u32[]{:S(2)}) collective-permute-start(f32[520,4,64]{0,2,1:T(8,128)S(1)} %dynamic-slice_bitcast_fusion), channel_id=1, source_target_pairs={{0,1},{1,0},{2,3},{3,2},{4,5},{5,4},{6,7},{7,6},{8,9},{9,8},{10,11... | collective-permute-start | bytes 1597448 | tf_op jit(solution)/shard_map/ppermute | solution.py:158
  49.1 12.6 %copy-start.5 = (f32[64]{0:T(128)S(1)}, f32[64]{0:T(128)}, u32[]{:S(2)}) copy-start(f32[64]{0:T(128)} %param.15) | copy-start | bytes 772
  49.1 7.6 %collective-permute-start.1 = (f32[520,64]{0,1:T(8,128)S(1)}, f32[520,64]{0,1:T(8,128)S(1)}, u32[]{:S(2)}, u32[]{:S(2)}) collective-permute-start(f32[520,64]{0,1:T(8,128)S(1)} %get-tuple-element.2), channel_id=1, source_target_pairs={{0,2},{1,3},{2,4},{3,5},{4,6},{5,7},{6,0},{7,1},{8,10},{9,11},{10,... | collective-permute-start | bytes 399368 | tf_op jit(solution)/shard_map/ppermute | solution.py:163
  50.8 8.8 %collective-permute-start.3 = (f32[520,64]{0,1:T(8,128)S(1)}, f32[520,64]{0,1:T(8,128)S(1)}, u32[]{:S(2)}, u32[]{:S(2)}) collective-permute-start(f32[520,64]{0,1:T(8,128)S(1)} %get-tuple-element.3), channel_id=1, source_target_pairs={{0,6},{1,7},{2,0},{3,1},{4,2},{5,3},{6,4},{7,5},{8,14},{9,15},{10,... | collective-permute-start | bytes 399368 | tf_op jit(solution)/shard_map/ppermute | solution.py:163
  52.5 9.0 %collective-permute-start.2 = (f32[520,64]{0,1:T(8,128)S(1)}, f32[520,64]{0,1:T(8,128)S(1)}, u32[]{:S(2)}, u32[]{:S(2)}) collective-permute-start(f32[520,64]{0,1:T(8,128)S(1)} %get-tuple-element.4), channel_id=1, source_target_pairs={{0,4},{1,5},{2,6},{3,7},{4,0},{5,1},{6,2},{7,3},{8,12},{9,13},{10,... | collective-permute-start | bytes 399368 | tf_op jit(solution)/shard_map/ppermute | solution.py:163

commit v19 on v18

--- a/solution.py
+++ b/solution.py
@@ -111,12 +111,11 @@
 def gather_body(basis_ref, rows_ref, out_ref):
     comps, nodes, modes = basis_ref.shape
     n_rows = rows_ref.shape[1]
-    node = lax.broadcasted_iota(jnp.int32, (nodes, n_rows), 0)
-    onehot_t = (node == rows_ref[...]).astype(jnp.bfloat16)
+    rows_col = jnp.transpose(jnp.broadcast_to(rows_ref[...], (8, n_rows)))[:, 0:1]
+    node = lax.broadcasted_iota(jnp.int32, (n_rows, nodes), 1)
+    onehot = (rows_col == node).astype(jnp.bfloat16)
     for c in range(comps):
-        picked = lax.dot_general(
-            onehot_t, basis_ref[c], (((0,), (0,)), ((), ())), preferred_element_type=jnp.float32
-        )
+        picked = jnp.dot(onehot, basis_ref[c], preferred_element_type=jnp.float32)
         out_ref[:, pl.ds(c * modes, modes)] = picked.astype(jnp.bfloat16)
 
 

time: 79.1 us -> 79.2 us (level)
  no operation moved by 1% of the time
where the time goes in v19:
time: 79.2 us; the launch traced here: 77.7 us
  waiting for transfers between devices  24.7 us (31%)
  starting transfers between devices  17.1 us (22%)
  blocking collectives  14.3 us (18%)
  Pallas kernels  9.49 us (12%)
  local copies, waits for them, and re-layouts  7.21 us (9%)
  other arithmetic  3.28 us (4%)
  between operations  1.58 us (2%)
    all_to_all x1, waiting for transfers between devices, local(): lax.all_to_all(outgoing, 'elem', split_axis=0, concat_axis=0, tiled=True)  15.8 us
    all_to_all x1, blocking collectives, local(): lax.all_to_all(flat, 'elem', split_axis=0, concat_axis=0, tiled=True)  14.3 us
    all_to_all x1, starting transfers between devices, local(): lax.all_to_all(outgoing, 'elem', split_axis=0, concat_axis=0, tiled=True)  11.8 us
    ppermute x3, waiting for transfers between devices, local(): halfway = halfway + lax.ppermute(piece, 'blk', ring)  6.98 us
    pallas_call x1, Pallas kernels, element_stage(): pl.pallas_call(element_body, out_shape=jax.ShapeDtypeStruct((modes + 8, m...  5.53 us
    ppermute x3, starting transfers between devices, local(): halfway = halfway + lax.ppermute(piece, 'blk', ring)  5.28 us
    pallas_call x1, Pallas kernels, gather_rows(): pl.pallas_call(gather_body, out_shape=jax.ShapeDtypeStruct((n_rows, comps...  3.96 us
    ppermute x1, waiting for transfers between devices, local(): chip_sum = kept + lax.ppermute(sent, 'blk', pair)  2 us
  transfers between devices with their start and end apart: 5, of which 5 were waited for; matrix products, arithmetic and copies ran while one was open for 8% of the time, Pallas kernels for 0%

profile of v19, /device:TPU:2, one launch (start us, length us, event | category | flops | bytes accessed | tf_op | source)
XLA Modules:
  0.0 77.7 jit_solution(847387258858953368)
XLA Ops:
  0.6 4.0 %shard_map.95 = bf16[256,1536]{1,0:T(8,128)(2,1)} custom-call(bf16[3,1024,512]{2,1,0:T(8,128)(2,1)} %bitcast.28, s32[1,256]{1,0:T(1,128)} %bitcast.32), custom_call_target="tpu_custom_call" | custom-call | tf_op jit(solution)/shard_map/pallas_call | solution.py:126
  4.6 0.0 copy-start.1
  4.6 11.8 %all-to-all-start = ((bf16[32,8,1536]{2,1,0:T(8,128)(2,1)}), bf16[32,8,1536]{2,1,0:T(8,128)(2,1)S(1)}, u32[]{:S(2)}, u32[]{:S(2)}) async-start(bf16[32,8,1536]{2,1,0:T(8,128)(2,1)} %bitcast.30), calls=%async_computation | async-start | bytes 1572864 | tf_op jit(solution)/shard_map/all_to_all | solution.py:139
  16.4 0.6 reduce_sum.18
  17.7 0.6 dynamic_slice.24
  18.3 0.6 fusion.7
  19.0 0.7 copy.27.omega_ref
  19.7 0.7 copy.28.stiff_ref
  20.4 0.9 %reshape.60.slot_ref = s32[512,1]{1,0:T(8,128)} reshape(s32[8,64]{1,0:T(8,128)S(1)} %copy-done.1) | data formatting | bytes 4096 | tf_op jit(solution)/shard_map/reshape | solution.py:107
  21.3 1.7 %fusion.state_ref = bf16[1536,128]{1,0:T(8,128)(2,1)} fusion(s32[1536]{0:T(1024)S(1)} %add_select_fusion, bf16[1536]{0:T(1024)(128)(2,1)S(1)} %broadcast_in_dim.25), kind=kLoop, calls=%fused_computation.1 | loop fusion | flops 393216 | bytes 402432 | tf_op jit(solution)/shard_map/jit(_where)/select_n | solution.py:94
  23.1 15.8 %all-to-all-done = bf16[32,8,1536]{2,1,0:T(8,128)(2,1)S(1)} async-done(((bf16[32,8,1536]{2,1,0:T(8,128)(2,1)}), bf16[32,8,1536]{2,1,0:T(8,128)(2,1)S(1)}, u32[]{:S(2)}, u32[]{:S(2)}) %all-to-all-start) | async-done | bytes 786464 | tf_op jit(solution)/shard_map/all_to_all | solution.py:139
  38.8 0.6 broadcast_in_dim.28.scale_ref
  39.5 0.3 copy-done
  39.8 5.5 %shard_map.96 = f32[520,512]{1,0:T(8,128)} custom-call(bf16[256,1536]{1,0:T(8,128)(2,1)} %bitcast.29, s32[512,1]{1,0:T(8,128)} %reshape.60.slot_ref, bf16[1536,128]{1,0:T(8,128)(2,1)} %fusion.state_ref, f32[64,1]{1,0:T(8,128)} %copy.27.omega_ref, f32[64,1]{1,0:T(8,128)} %copy.28.stiff_ref, f32[8,128]{1,0:T(8,128)} %broadcast_in_dim.28.scale_ref), custom_call_target="tpu_custom_call" | custom-call | tf_op jit(solution)/shard_map/pallas_call | solution.py:98
  45.3 1.6 %copy.29 = f32[520,512]{0,1:T(8,128)S(1)} copy(f32[520,512]{1,0:T(8,128)} %shard_map.96) | data formatting | bytes 2129920 | tf_op jit(solution)/shard_map/pallas_call | solution.py:98
  46.9 0.1 dynamic-slice_bitcast_fusion
  47.0 0.1 collective-permute-start
  47.2 2.0 %collective-permute-done = f32[520,4,64]{0,2,1:T(8,128)S(1)} collective-permute-done((f32[520,4,64]{0,2,1:T(8,128)S(1)}, f32[520,4,64]{0,2,1:T(8,128)S(1)}, u32[]{:S(2)}, u32[]{:S(2)}) %collective-permute-start) | collective-permute-done | bytes 532512 | tf_op jit(solution)/shard_map/ppermute | solution.py:157
  49.2 0.1 bitcast_add_fusion
  49.3 1.6 %collective-permute-start.1 = (f32[520,64]{0,1:T(8,128)S(1)}, f32[520,64]{0,1:T(8,128)S(1)}, u32[]{:S(2)}, u32[]{:S(2)}) collective-permute-start(f32[520,64]{0,1:T(8,128)S(1)} %get-tuple-element.2), channel_id=1, source_target_pairs={{0,2},{1,3},{2,4},{3,5},{4,6},{5,7},{6,0},{7,1},{8,10},{9,11},{10,... | collective-permute-start | bytes 399368 | tf_op jit(solution)/shard_map/ppermute | solution.py:162
  51.0 1.7 %collective-permute-start.3 = (f32[520,64]{0,1:T(8,128)S(1)}, f32[520,64]{0,1:T(8,128)S(1)}, u32[]{:S(2)}, u32[]{:S(2)}) collective-permute-start(f32[520,64]{0,1:T(8,128)S(1)} %get-tuple-element.3), channel_id=1, source_target_pairs={{0,6},{1,7},{2,0},{3,1},{4,2},{5,3},{6,4},{7,5},{8,14},{9,15},{10,... | collective-permute-start | bytes 399368 | tf_op jit(solution)/shard_map/ppermute | solution.py:162
  52.6 2.0 %collective-permute-start.2 = (f32[520,64]{0,1:T(8,128)S(1)}, f32[520,64]{0,1:T(8,128)S(1)}, u32[]{:S(2)}, u32[]{:S(2)}) collective-permute-start(f32[520,64]{0,1:T(8,128)S(1)} %get-tuple-element.4), channel_id=1, source_target_pairs={{0,4},{1,5},{2,6},{3,7},{4,0},{5,1},{6,2},{7,3},{8,12},{9,13},{10,... | collective-permute-start | bytes 399368 | tf_op jit(solution)/shard_map/ppermute | solution.py:162
  54.6 2.3 %collective-permute-done.1 = f32[520,64]{0,1:T(8,128)S(1)} collective-permute-done((f32[520,64]{0,1:T(8,128)S(1)}, f32[520,64]{0,1:T(8,128)S(1)}, u32[]{:S(2)}, u32[]{:S(2)}) %collective-permute-start.1) | collective-permute-done | bytes 133152 | tf_op jit(solution)/shard_map/ppermute | solution.py:162
  56.9 2.9 %collective-permute-done.3 = f32[520,64]{0,1:T(8,128)S(1)} collective-permute-done((f32[520,64]{0,1:T(8,128)S(1)}, f32[520,64]{0,1:T(8,128)S(1)}, u32[]{:S(2)}, u32[]{:S(2)}) %collective-permute-start.3) | collective-permute-done | bytes 133152 | tf_op jit(solution)/shard_map/ppermute | solution.py:162
  59.8 1.8 %collective-permute-done.2 = f32[520,64]{0,1:T(8,128)S(1)} collective-permute-done((f32[520,64]{0,1:T(8,128)S(1)}, f32[520,64]{0,1:T(8,128)S(1)}, u32[]{:S(2)}, u32[]{:S(2)}) %collective-permute-start.2) | collective-permute-done | bytes 133152 | tf_op jit(solution)/shard_map/ppermute | solution.py:162
  61.6 0.1 slice_reduce_fusion
  61.7 0.1 copy.30
  62.0 0.2 all_to_all.18
  62.2 14.3 %all_to_all.21 = f32[32,1,1088]{2,1,0:T(1,128)S(1)} all-to-all(f32[32,1,1088]{2,1,0:T(1,128)S(1)} %all_to_all.18), channel_id=1, replica_groups=mesh['elem'=32,'blk'=8] {'elem'}, dimensions={0} | all-to-all | bytes 278528 | tf_op jit(solution)/shard_map/all_to_all | solution.py:169
  76.4 0.1 reduce_sum.19
  76.5 0.5 slice.32
  77.1 0.7 slice.27
  (22 shorter events, 0.2 us)
Async XLA Ops:
  4.6 11.8 %copy-start.6 = (s32[32]{0:T(128)S(1)}, s32[32]{0:T(128)}, u32[]{:S(2)}) copy-start(s32[32]{0:T(128)} %param.11) | copy-start | bytes 388
  4.6 13.7 %copy-start.2 = (bf16[512]{0:T(512)(128)(2,1)S(1)}, bf16[512]{0:T(512)(128)(2,1)}, u32[]{:S(2)}) copy-start(bf16[512]{0:T(512)(128)(2,1)} %param.14) | copy-start | bytes 3076
  4.6 13.8 %copy-start.4 = (f32[64]{0:T(128)S(1)}, f32[64]{0:T(128)}, u32[]{:S(2)}) copy-start(f32[64]{0:T(128)} %param.12) | copy-start | bytes 772
  4.6 15.1 %copy-start.3 = (f32[64]{0:T(128)S(1)}, f32[64]{0:T(128)}, u32[]{:S(2)}) copy-start(f32[64]{0:T(128)} %param.13) | copy-start | bytes 772
  4.6 15.8 %copy-start.1 = (s32[8,64]{1,0:T(8,128)S(1)}, s32[8,64]{1,0:T(8,128)}, u32[]{:S(2)}) copy-start(s32[8,64]{1,0:T(8,128)} %param.10) | copy-start | bytes 6148
  4.6 34.2 %all-to-all-start = ((bf16[32,8,1536]{2,1,0:T(8,128)(2,1)}), bf16[32,8,1536]{2,1,0:T(8,128)(2,1)S(1)}, u32[]{:S(2)}, u32[]{:S(2)}) async-start(bf16[32,8,1536]{2,1,0:T(8,128)(2,1)} %bitcast.30), calls=%async_computation | async-start | bytes 1572864 | tf_op jit(solution)/shard_map/all_to_all | solution.py:139
  38.8 0.9 %copy-start = (bf16[32,8,1536]{2,1,0:T(8,128)(2,1)}, bf16[32,8,1536]{2,1,0:T(8,128)(2,1)S(1)}, u32[]{:S(2)}) copy-start(bf16[32,8,1536]{2,1,0:T(8,128)(2,1)S(1)} %all-to-all-done) | copy-start | bytes 2359300
  47.0 2.2 %collective-permute-start = (f32[520,4,64]{0,2,1:T(8,128)S(1)}, f32[520,4,64]{0,2,1:T(8,128)S(1)}, u32[]{:S(2)}, u32[]{:S(2)}) collective-permute-start(f32[520,4,64]{0,2,1:T(8,128)S(1)} %dynamic-slice_bitcast_fusion), channel_id=1, source_target_pairs={{0,1},{1,0},{2,3},{3,2},{4,5},{5,4},{6,7},{7,6},{8,9},{9,8},{10,11... | collective-permute-start | bytes 1597448 | tf_op jit(solution)/shard_map/ppermute | solution.py:157
  49.2 12.6 %copy-start.5 = (f32[64]{0:T(128)S(1)}, f32[64]{0:T(128)}, u32[]{:S(2)}) copy-start(f32[64]{0:T(128)} %param.15) | copy-start | bytes 772
  49.3 7.6 %collective-permute-start.1 = (f32[520,64]{0,1:T(8,128)S(1)}, f32[520,64]{0,1:T(8,128)S(1)}, u32[]{:S(2)}, u32[]{:S(2)}) collective-permute-start(f32[520,64]{0,1:T(8,128)S(1)} %get-tuple-element.2), channel_id=1, source_target_pairs={{0,2},{1,3},{2,4},{3,5},{4,6},{5,7},{6,0},{7,1},{8,10},{9,11},{10,... | collective-permute-start | bytes 399368 | tf_op jit(solution)/shard_map/ppermute | solution.py:162
  51.0 8.8 %collective-permute-start.3 = (f32[520,64]{0,1:T(8,128)S(1)}, f32[520,64]{0,1:T(8,128)S(1)}, u32[]{:S(2)}, u32[]{:S(2)}) collective-permute-start(f32[520,64]{0,1:T(8,128)S(1)} %get-tuple-element.3), channel_id=1, source_target_pairs={{0,6},{1,7},{2,0},{3,1},{4,2},{5,3},{6,4},{7,5},{8,14},{9,15},{10,... | collective-permute-start | bytes 399368 | tf_op jit(solution)/shard_map/ppermute | solution.py:162
  52.6 9.0 %collective-permute-start.2 = (f32[520,64]{0,1:T(8,128)S(1)}, f32[520,64]{0,1:T(8,128)S(1)}, u32[]{:S(2)}, u32[]{:S(2)}) collective-permute-start(f32[520,64]{0,1:T(8,128)S(1)} %get-tuple-element.4), channel_id=1, source_target_pairs={{0,4},{1,5},{2,6},{3,7},{4,0},{5,1},{6,2},{7,3},{8,12},{9,13},{10,... | collective-permute-start | bytes 399368 | tf_op jit(solution)/shard_map/ppermute | solution.py:162

commit v20 on v18

--- a/solution.py
+++ b/solution.py
@@ -8,13 +8,10 @@
 G = [[(2 * ((a >> k) & 1) - 1) * 0.25 for k in range(3)] for a in range(8)]
 
 
-def element_body(arrived_ref, slot_ref, state_ref, omega_ref, stiff_ref, scale_ref, out_ref, v_ref, w_ref):
+def element_body(arrived_ref, onehot_ref, signed_ref, state_ref, omega_ref, stiff_ref, scale_ref, out_ref, v_ref, w_ref):
     n_el = omega_ref.shape[0]
-    n_slot = arrived_ref.shape[0]
     modes = out_ref.shape[1]
-    slots = slot_ref[...]
-    lane = lax.broadcasted_iota(jnp.int32, (8 * n_el, n_slot), 1)
-    onehot = (slots == lane).astype(jnp.bfloat16)
+    onehot = onehot_ref[...]
     corners = jnp.dot(onehot, arrived_ref[...], preferred_element_type=jnp.float32).astype(jnp.bfloat16)
     for c in range(3):
         v_ref[pl.ds(c * 8 * n_el, 8 * n_el), :] = corners[:, c * modes:(c + 1) * modes]
@@ -23,15 +20,7 @@
     for a in range(8):
         for c in range(3):
             disp[a, c] = disp_all[a * n_el:(a + 1) * n_el, c:c + 1]
-    lane_el = lane[:n_el]
-    signed_rows = []
-    for k in range(3):
-        signed = None
-        for a in range(8):
-            term = jnp.where(slots[a * n_el:(a + 1) * n_el] == lane_el, G[a][k], 0.0)
-            signed = term if signed is None else signed + term
-        signed_rows.append(signed)
-    signed_all = jnp.concatenate(signed_rows, axis=0).astype(jnp.bfloat16)
+    signed_all = signed_ref[...]
     grad_all = jnp.dot(signed_all, arrived_ref[...], preferred_element_type=jnp.float32)
     grad = {}
     for k in range(3):
@@ -89,6 +78,12 @@
 
 def element_stage(arrived3, slot, state, omega, stiff, scale):
     n_el = slot.shape[1]
+    n_slot = arrived3.shape[0]
+    lane = jnp.arange(n_slot, dtype=jnp.int32)[None, :]
+    onehot = (slot.reshape(8 * n_el, 1) == lane).astype(jnp.bfloat16)
+    signed = jnp.concatenate(
+        [sum(jnp.where(slot[a][:, None] == lane, G[a][k], 0.0) for a in range(8)) for k in range(3)], axis=0
+    ).astype(jnp.bfloat16)
     modes = arrived3.shape[1] // 3
     comp = jnp.arange(3 * modes) // modes
     state_blocks = jnp.where(
@@ -98,13 +93,13 @@
     return pl.pallas_call(
         element_body,
         out_shape=jax.ShapeDtypeStruct((modes + 8, modes), jnp.float32),
-        in_specs=[pl.BlockSpec(memory_space=vmem)] * 6,
+        in_specs=[pl.BlockSpec(memory_space=vmem)] * 7,
         out_specs=pl.BlockSpec(memory_space=vmem),
         scratch_shapes=[
             pltpu.VMEM((24 * n_el, modes), jnp.bfloat16),
             pltpu.VMEM((24 * n_el, modes), jnp.bfloat16),
         ],
-    )(arrived3, slot.reshape(8 * n_el, 1), state_blocks, omega.reshape(n_el, 1), stiff.reshape(n_el, 1),
+    )(arrived3, onehot, signed, state_blocks, omega.reshape(n_el, 1), stiff.reshape(n_el, 1),
       jnp.broadcast_to(scale, (8, 128)))
 
 

time: 79.1 us -> 79 us (level)
  other arithmetic: 3.28 us -> 4.94 us
  waiting for transfers between devices: 24.7 us -> 23.3 us
  local copies, waits for them, and re-layouts: 7.21 us -> 6.4 us
    reshape x1 -> x0, local copies, waits for them, and re-layouts: 0.91 us -> none  [element_stage(): slot.reshape(8 * n_el, 1)]
    all_to_all x1, waiting for transfers between devices: 15.7 us -> 14.9 us  [local(): lax.all_to_all(outgoing, 'elem', split_axis=0, concat_axis=0, tiled=True)]
    convert_element_type x0 -> x1, other arithmetic: none -> 0.85 us  [element_stage(): onehot = (slot.reshape(8 * n_el, 1) == lane).astype(jnp.bfloat16)]
  transfers between devices with their start and end apart: 5 -> 5, of which waited for: 5 -> 4; matrix products, arithmetic and copies ran while one was open for 8% -> 9% of each run, Pallas kernels for 0% -> 0%
where the time goes in v20:
time: 79 us; the launch traced here: 77.5 us
  waiting for transfers between devices  23.3 us (29%)
  starting transfers between devices  17.8 us (23%)
  blocking collectives  14.3 us (18%)
  Pallas kernels  9.27 us (12%)
  local copies, waits for them, and re-layouts  6.4 us (8%)
  other arithmetic  4.94 us (6%)
  between operations  1.62 us (2%)
    all_to_all x1, waiting for transfers between devices, local(): lax.all_to_all(outgoing, 'elem', split_axis=0, concat_axis=0, tiled=True)  14.9 us
    all_to_all x1, blocking collectives, local(): lax.all_to_all(flat, 'elem', split_axis=0, concat_axis=0, tiled=True)  14.3 us
    all_to_all x1, starting transfers between devices, local(): lax.all_to_all(outgoing, 'elem', split_axis=0, concat_axis=0, tiled=True)  11.8 us
    ppermute x3, waiting for transfers between devices, local(): halfway = halfway + lax.ppermute(piece, 'blk', ring)  6.38 us
    ppermute x3, starting transfers between devices, local(): halfway = halfway + lax.ppermute(piece, 'blk', ring)  5.9 us
    pallas_call x1, Pallas kernels, element_stage(): pl.pallas_call(element_body, out_shape=jax.ShapeDtypeStruct((modes + 8, m...  5.47 us
    pallas_call x1, Pallas kernels, gather_rows(): pl.pallas_call(gather_body, out_shape=jax.ShapeDtypeStruct((n_rows, comps...  3.79 us
    ppermute x1, waiting for transfers between devices, local(): chip_sum = kept + lax.ppermute(sent, 'blk', pair)  2 us
  transfers between devices with their start and end apart: 5, of which 4 were waited for; matrix products, arithmetic and copies ran while one was open for 9% of the time, Pallas kernels for 0%

profile of v20, /device:TPU:2, one launch (start us, length us, event | category | flops | bytes accessed | tf_op | source)
XLA Modules:
  0.0 77.5 jit_solution(18083297859372598454)
XLA Ops:
  0.6 3.8 %shard_map.95 = bf16[256,1536]{1,0:T(8,128)(2,1)} custom-call(bf16[3,1024,512]{2,1,0:T(8,128)(2,1)} %bitcast.44, s32[1,256]{1,0:T(1,128)} %bitcast.48), custom_call_target="tpu_custom_call" | custom-call | tf_op jit(solution)/shard_map/pallas_call | solution.py:122
  4.5 11.8 %all-to-all-start = ((bf16[32,8,1536]{2,1,0:T(8,128)(2,1)}), bf16[32,8,1536]{2,1,0:T(8,128)(2,1)S(1)}, u32[]{:S(2)}, u32[]{:S(2)}) async-start(bf16[32,8,1536]{2,1,0:T(8,128)(2,1)} %bitcast.45), calls=%async_computation | async-start | bytes 1572864 | tf_op jit(solution)/shard_map/all_to_all | solution.py:135
  16.2 0.6 reduce_sum.18
  16.9 0.6 dynamic_slice.24
  17.4 0.6 fusion.15
  18.1 0.7 copy.23.omega_ref
  18.8 0.1 eq.84
  18.9 0.7 copy.24.stiff_ref
  20.4 0.2 fusion.10
  20.5 0.6 pad_maximum_fusion.1.signed_ref
  21.2 0.9 %fusion.1.onehot_ref = bf16[512,256]{1,0:T(8,128)(2,1)} fusion(s32[512]{0:T(512)S(1)} %eq.84), kind=kLoop, calls=%fused_computation.5 | loop fusion | flops 262144 | bytes 264192 | tf_op jit(solution)/shard_map/convert_element_type | solution.py:83
  22.0 1.8 %fusion.state_ref = bf16[1536,128]{1,0:T(8,128)(2,1)} fusion(s32[1536]{0:T(1024)S(1)} %add_select_fusion, bf16[1536]{0:T(1024)(128)(2,1)S(1)} %broadcast_in_dim.85), kind=kLoop, calls=%fused_computation.1 | loop fusion | flops 393216 | bytes 402432 | tf_op jit(solution)/shard_map/jit(_where)/select_n | solution.py:89
  23.8 14.9 %all-to-all-done = bf16[32,8,1536]{2,1,0:T(8,128)(2,1)S(1)} async-done(((bf16[32,8,1536]{2,1,0:T(8,128)(2,1)}), bf16[32,8,1536]{2,1,0:T(8,128)(2,1)S(1)}, u32[]{:S(2)}, u32[]{:S(2)}) %all-to-all-start) | async-done | bytes 786464 | tf_op jit(solution)/shard_map/all_to_all | solution.py:135
  38.7 0.6 broadcast_in_dim.88.scale_ref
  39.3 0.3 copy-done
  39.6 5.5 %shard_map.96 = f32[520,512]{1,0:T(8,128)} custom-call(bf16[256,1536]{1,0:T(8,128)(2,1)} %bitcast.46, bf16[512,256]{1,0:T(8,128)(2,1)} %fusion.1.onehot_ref, bf16[192,256]{1,0:T(8,128)(2,1)} %pad_maximum_fusion.1.signed_ref, bf16[1536,128]{1,0:T(8,128)(2,1)} %fusion.state_ref, f32[64,1]{1,0:T(8,128)} %copy.23.omega_ref, f32[64,1]{1,0:T(8,128)} %copy.24.stiff_ref, ...), custom_call_target="tpu_custom_call" | custom-call | tf_op jit(solution)/shard_map/pallas_call | solution.py:93
  45.1 1.6 %copy.25 = f32[520,512]{0,1:T(8,128)S(1)} copy(f32[520,512]{1,0:T(8,128)} %shard_map.96) | data formatting | bytes 2129920 | tf_op jit(solution)/shard_map/pallas_call | solution.py:93
  46.8 0.1 collective-permute-start
  46.9 2.0 %collective-permute-done = f32[520,4,64]{0,2,1:T(8,128)S(1)} collective-permute-done((f32[520,4,64]{0,2,1:T(8,128)S(1)}, f32[520,4,64]{0,2,1:T(8,128)S(1)}, u32[]{:S(2)}, u32[]{:S(2)}) %collective-permute-start) | collective-permute-done | bytes 532512 | tf_op jit(solution)/shard_map/ppermute | solution.py:153
  48.9 0.1 bitcast_add_fusion
  49.1 1.7 %collective-permute-start.1 = (f32[520,64]{0,1:T(8,128)S(1)}, f32[520,64]{0,1:T(8,128)S(1)}, u32[]{:S(2)}, u32[]{:S(2)}) collective-permute-start(f32[520,64]{0,1:T(8,128)S(1)} %get-tuple-element.2), channel_id=1, source_target_pairs={{0,2},{1,3},{2,4},{3,5},{4,6},{5,7},{6,0},{7,1},{8,10},{9,11},{10,... | collective-permute-start | bytes 399368 | tf_op jit(solution)/shard_map/ppermute | solution.py:158
  50.7 2.9 %collective-permute-start.2 = (f32[520,64]{0,1:T(8,128)S(1)}, f32[520,64]{0,1:T(8,128)S(1)}, u32[]{:S(2)}, u32[]{:S(2)}) collective-permute-start(f32[520,64]{0,1:T(8,128)S(1)} %get-tuple-element.4), channel_id=1, source_target_pairs={{0,4},{1,5},{2,6},{3,7},{4,0},{5,1},{6,2},{7,3},{8,12},{9,13},{10,... | collective-permute-start | bytes 399368 | tf_op jit(solution)/shard_map/ppermute | solution.py:158
  53.6 1.3 %collective-permute-start.3 = (f32[520,64]{0,1:T(8,128)S(1)}, f32[520,64]{0,1:T(8,128)S(1)}, u32[]{:S(2)}, u32[]{:S(2)}) collective-permute-start(f32[520,64]{0,1:T(8,128)S(1)} %get-tuple-element.3), channel_id=1, source_target_pairs={{0,6},{1,7},{2,0},{3,1},{4,2},{5,3},{6,4},{7,5},{8,14},{9,15},{10,... | collective-permute-start | bytes 399368 | tf_op jit(solution)/shard_map/ppermute | solution.py:158
  55.0 1.7 %collective-permute-done.1 = f32[520,64]{0,1:T(8,128)S(1)} collective-permute-done((f32[520,64]{0,1:T(8,128)S(1)}, f32[520,64]{0,1:T(8,128)S(1)}, u32[]{:S(2)}, u32[]{:S(2)}) %collective-permute-start.1) | collective-permute-done | bytes 133152 | tf_op jit(solution)/shard_map/ppermute | solution.py:158
  56.7 4.7 %collective-permute-done.2 = f32[520,64]{0,1:T(8,128)S(1)} collective-permute-done((f32[520,64]{0,1:T(8,128)S(1)}, f32[520,64]{0,1:T(8,128)S(1)}, u32[]{:S(2)}, u32[]{:S(2)}) %collective-permute-start.2) | collective-permute-done | bytes 133152 | tf_op jit(solution)/shard_map/ppermute | solution.py:158
  61.4 0.1 slice_reduce_fusion
  61.5 0.1 copy.26
  61.7 0.2 all_to_all.18
  61.9 14.3 %all_to_all.21 = f32[32,1,1088]{2,1,0:T(1,128)S(1)} all-to-all(f32[32,1,1088]{2,1,0:T(1,128)S(1)} %all_to_all.18), channel_id=1, replica_groups=mesh['elem'=32,'blk'=8] {'elem'}, dimensions={0} | all-to-all | bytes 278528 | tf_op jit(solution)/shard_map/all_to_all | solution.py:165
  76.2 0.1 reduce_sum.19
  76.3 0.5 slice.80
  76.8 0.7 slice.75
  (26 shorter events, 0.3 us)
Async XLA Ops:
  4.4 11.8 %copy-start.6 = (s32[32]{0:T(128)S(1)}, s32[32]{0:T(128)}, u32[]{:S(2)}) copy-start(s32[32]{0:T(128)} %param.11) | copy-start | bytes 388
  4.4 13.0 %copy-start.4 = (f32[64]{0:T(128)S(1)}, f32[64]{0:T(128)}, u32[]{:S(2)}) copy-start(f32[64]{0:T(128)} %param.12) | copy-start | bytes 772
  4.4 14.4 %copy-start.2 = (bf16[512]{0:T(512)(128)(2,1)S(1)}, bf16[512]{0:T(512)(128)(2,1)}, u32[]{:S(2)}) copy-start(bf16[512]{0:T(512)(128)(2,1)} %param.14) | copy-start | bytes 3076
  4.4 14.4 %copy-start.1 = (s32[8,64]{1,0:T(8,128)S(1)}, s32[8,64]{1,0:T(8,128)}, u32[]{:S(2)}) copy-start(s32[8,64]{1,0:T(8,128)} %param.10) | copy-start | bytes 6148
  4.4 14.5 %copy-start.3 = (f32[64]{0:T(128)S(1)}, f32[64]{0:T(128)}, u32[]{:S(2)}) copy-start(f32[64]{0:T(128)} %param.13) | copy-start | bytes 772
  4.5 34.2 %all-to-all-start = ((bf16[32,8,1536]{2,1,0:T(8,128)(2,1)}), bf16[32,8,1536]{2,1,0:T(8,128)(2,1)S(1)}, u32[]{:S(2)}, u32[]{:S(2)}) async-start(bf16[32,8,1536]{2,1,0:T(8,128)(2,1)} %bitcast.45), calls=%async_computation | async-start | bytes 1572864 | tf_op jit(solution)/shard_map/all_to_all | solution.py:135
  38.7 0.9 %copy-start = (bf16[32,8,1536]{2,1,0:T(8,128)(2,1)}, bf16[32,8,1536]{2,1,0:T(8,128)(2,1)S(1)}, u32[]{:S(2)}) copy-start(bf16[32,8,1536]{2,1,0:T(8,128)(2,1)S(1)} %all-to-all-done) | copy-start | bytes 2359300
  46.8 2.2 %collective-permute-start = (f32[520,4,64]{0,2,1:T(8,128)S(1)}, f32[520,4,64]{0,2,1:T(8,128)S(1)}, u32[]{:S(2)}, u32[]{:S(2)}) collective-permute-start(f32[520,4,64]{0,2,1:T(8,128)S(1)} %dynamic-slice_bitcast_fusion), channel_id=1, source_target_pairs={{0,1},{1,0},{2,3},{3,2},{4,5},{5,4},{6,7},{7,6},{8,9},{9,8},{10,11... | collective-permute-start | bytes 1597448 | tf_op jit(solution)/shard_map/ppermute | solution.py:153
  49.0 12.7 %copy-start.5 = (f32[64]{0:T(128)S(1)}, f32[64]{0:T(128)}, u32[]{:S(2)}) copy-start(f32[64]{0:T(128)} %param.15) | copy-start | bytes 772
  49.1 7.6 %collective-permute-start.1 = (f32[520,64]{0,1:T(8,128)S(1)}, f32[520,64]{0,1:T(8,128)S(1)}, u32[]{:S(2)}, u32[]{:S(2)}) collective-permute-start(f32[520,64]{0,1:T(8,128)S(1)} %get-tuple-element.2), channel_id=1, source_target_pairs={{0,2},{1,3},{2,4},{3,5},{4,6},{5,7},{6,0},{7,1},{8,10},{9,11},{10,... | collective-permute-start | bytes 399368 | tf_op jit(solution)/shard_map/ppermute | solution.py:158
  50.7 10.6 %collective-permute-start.2 = (f32[520,64]{0,1:T(8,128)S(1)}, f32[520,64]{0,1:T(8,128)S(1)}, u32[]{:S(2)}, u32[]{:S(2)}) collective-permute-start(f32[520,64]{0,1:T(8,128)S(1)} %get-tuple-element.4), channel_id=1, source_target_pairs={{0,4},{1,5},{2,6},{3,7},{4,0},{5,1},{6,2},{7,3},{8,12},{9,13},{10,... | collective-permute-start | bytes 399368 | tf_op jit(solution)/shard_map/ppermute | solution.py:158
  53.6 7.7 %collective-permute-start.3 = (f32[520,64]{0,1:T(8,128)S(1)}, f32[520,64]{0,1:T(8,128)S(1)}, u32[]{:S(2)}, u32[]{:S(2)}) collective-permute-start(f32[520,64]{0,1:T(8,128)S(1)} %get-tuple-element.3), channel_id=1, source_target_pairs={{0,6},{1,7},{2,0},{3,1},{4,2},{5,3},{6,4},{7,5},{8,14},{9,15},{10,... | collective-permute-start | bytes 399368 | tf_op jit(solution)/shard_map/ppermute | solution.py:158

commit v21 on v20

--- a/solution.py
+++ b/solution.py
@@ -152,7 +152,7 @@
     kept = lax.dynamic_index_in_dim(by_dest, core, axis=2, keepdims=False)
     chip_sum = kept + lax.ppermute(sent, "blk", pair)
     halfway = lax.dynamic_index_in_dim(chip_sum, chip, axis=1, keepdims=False)
-    for shift in range(1, n_y):
+    for shift in sorted(range(1, n_y), key=lambda d: -min(d, n_y - d)):
         ring = [(2 * y + c, 2 * ((y + shift) % n_y) + c) for y in range(n_y) for c in range(2)]
         piece = lax.dynamic_index_in_dim(chip_sum, (chip + shift) % n_y, axis=1, keepdims=False)
         halfway = halfway + lax.ppermute(piece, "blk", ring)

time: 79 us -> 78.7 us (level)
  the two profiles are of different devices: /device:TPU:2 before, /device:TPU:8 now
where the time goes in v21:
time: 78.7 us; the launch traced here: 78.3 us
  waiting for transfers between devices  24.5 us (31%)
  starting transfers between devices  16 us (20%)
  blocking collectives  15.7 us (20%)
  Pallas kernels  9.26 us (12%)
  local copies, waits for them, and re-layouts  6.4 us (8%)
  other arithmetic  4.94 us (6%)
  between operations  1.62 us (2%)
    all_to_all x1, blocking collectives, local(): lax.all_to_all(flat, 'elem', split_axis=0, concat_axis=0, tiled=True)  15.7 us
    all_to_all x1, waiting for transfers between devices, local(): lax.all_to_all(outgoing, 'elem', split_axis=0, concat_axis=0, tiled=True)  15.4 us
    all_to_all x1, starting transfers between devices, local(): lax.all_to_all(outgoing, 'elem', split_axis=0, concat_axis=0, tiled=True)  11.5 us
    ppermute x3, waiting for transfers between devices, local(): halfway = halfway + lax.ppermute(piece, 'blk', ring)  7.09 us
    pallas_call x1, Pallas kernels, element_stage(): pl.pallas_call(element_body, out_shape=jax.ShapeDtypeStruct((modes + 8, m...  5.47 us
    ppermute x3, starting transfers between devices, local(): halfway = halfway + lax.ppermute(piece, 'blk', ring)  4.41 us
    pallas_call x1, Pallas kernels, gather_rows(): pl.pallas_call(gather_body, out_shape=jax.ShapeDtypeStruct((n_rows, comps...  3.79 us
    ppermute x1, waiting for transfers between devices, local(): chip_sum = kept + lax.ppermute(sent, 'blk', pair)  2 us
  transfers between devices with their start and end apart: 5, of which 4 were waited for; matrix products, arithmetic and copies ran while one was open for 9% of the time, Pallas kernels for 0%

profile of v21, /device:TPU:8, one launch (start us, length us, event | category | flops | bytes accessed | tf_op | source)
XLA Modules:
  0.0 78.3 jit_solution(3203560319944307922)
XLA Ops:
  0.6 3.8 %shard_map.95 = bf16[256,1536]{1,0:T(8,128)(2,1)} custom-call(bf16[3,1024,512]{2,1,0:T(8,128)(2,1)} %bitcast.44, s32[1,256]{1,0:T(1,128)} %bitcast.48), custom_call_target="tpu_custom_call" | custom-call | tf_op jit(solution)/shard_map/pallas_call | solution.py:122
  4.4 11.5 %all-to-all-start = ((bf16[32,8,1536]{2,1,0:T(8,128)(2,1)}), bf16[32,8,1536]{2,1,0:T(8,128)(2,1)S(1)}, u32[]{:S(2)}, u32[]{:S(2)}) async-start(bf16[32,8,1536]{2,1,0:T(8,128)(2,1)} %bitcast.45), calls=%async_computation | async-start | bytes 1572864 | tf_op jit(solution)/shard_map/all_to_all | solution.py:135
  15.9 0.6 reduce_sum.18
  16.6 0.6 dynamic_slice.24
  17.2 0.6 fusion.15
  17.8 0.7 copy.23.omega_ref
  18.6 0.1 eq.84
  18.6 0.7 copy.24.stiff_ref
  20.1 0.2 fusion.10
  20.2 0.6 pad_maximum_fusion.1.signed_ref
  20.9 0.9 %fusion.1.onehot_ref = bf16[512,256]{1,0:T(8,128)(2,1)} fusion(s32[512]{0:T(512)S(1)} %eq.84), kind=kLoop, calls=%fused_computation.5 | loop fusion | flops 262144 | bytes 264192 | tf_op jit(solution)/shard_map/convert_element_type | solution.py:83
  21.7 1.8 %fusion.state_ref = bf16[1536,128]{1,0:T(8,128)(2,1)} fusion(s32[1536]{0:T(1024)S(1)} %add_select_fusion, bf16[1536]{0:T(1024)(128)(2,1)S(1)} %broadcast_in_dim.85), kind=kLoop, calls=%fused_computation.1 | loop fusion | flops 393216 | bytes 402432 | tf_op jit(solution)/shard_map/jit(_where)/select_n | solution.py:89
  23.5 15.4 %all-to-all-done = bf16[32,8,1536]{2,1,0:T(8,128)(2,1)S(1)} async-done(((bf16[32,8,1536]{2,1,0:T(8,128)(2,1)}), bf16[32,8,1536]{2,1,0:T(8,128)(2,1)S(1)}, u32[]{:S(2)}, u32[]{:S(2)}) %all-to-all-start) | async-done | bytes 786464 | tf_op jit(solution)/shard_map/all_to_all | solution.py:135
  38.9 0.6 broadcast_in_dim.88.scale_ref
  39.5 0.3 copy-done
  39.8 5.5 %shard_map.96 = f32[520,512]{1,0:T(8,128)} custom-call(bf16[256,1536]{1,0:T(8,128)(2,1)} %bitcast.46, bf16[512,256]{1,0:T(8,128)(2,1)} %fusion.1.onehot_ref, bf16[192,256]{1,0:T(8,128)(2,1)} %pad_maximum_fusion.1.signed_ref, bf16[1536,128]{1,0:T(8,128)(2,1)} %fusion.state_ref, f32[64,1]{1,0:T(8,128)} %copy.23.omega_ref, f32[64,1]{1,0:T(8,128)} %copy.24.stiff_ref, ...), custom_call_target="tpu_custom_call" | custom-call | tf_op jit(solution)/shard_map/pallas_call | solution.py:93
  45.2 1.6 %copy.25 = f32[520,512]{0,1:T(8,128)S(1)} copy(f32[520,512]{1,0:T(8,128)} %shard_map.96) | data formatting | bytes 2129920 | tf_op jit(solution)/shard_map/pallas_call | solution.py:93
  46.9 0.1 dynamic-slice_bitcast_fusion
  46.9 0.1 collective-permute-start
  47.1 2.0 %collective-permute-done = f32[520,4,64]{0,2,1:T(8,128)S(1)} collective-permute-done((f32[520,4,64]{0,2,1:T(8,128)S(1)}, f32[520,4,64]{0,2,1:T(8,128)S(1)}, u32[]{:S(2)}, u32[]{:S(2)}) %collective-permute-start) | collective-permute-done | bytes 532512 | tf_op jit(solution)/shard_map/ppermute | solution.py:153
  49.1 0.1 bitcast_add_fusion
  49.3 2.4 %collective-permute-start.1 = (f32[520,64]{0,1:T(8,128)S(1)}, f32[520,64]{0,1:T(8,128)S(1)}, u32[]{:S(2)}, u32[]{:S(2)}) collective-permute-start(f32[520,64]{0,1:T(8,128)S(1)} %get-tuple-element.2), channel_id=1, source_target_pairs={{0,4},{1,5},{2,6},{3,7},{4,0},{5,1},{6,2},{7,3},{8,12},{9,13},{10,... | collective-permute-start | bytes 399368 | tf_op jit(solution)/shard_map/ppermute | solution.py:158
  51.6 2.0 %collective-permute-start.3 = (f32[520,64]{0,1:T(8,128)S(1)}, f32[520,64]{0,1:T(8,128)S(1)}, u32[]{:S(2)}, u32[]{:S(2)}) collective-permute-start(f32[520,64]{0,1:T(8,128)S(1)} %get-tuple-element.3), channel_id=1, source_target_pairs={{0,6},{1,7},{2,0},{3,1},{4,2},{5,3},{6,4},{7,5},{8,14},{9,15},{10,... | collective-permute-start | bytes 399368 | tf_op jit(solution)/shard_map/ppermute | solution.py:158
  53.7 4.3 %collective-permute-done.1 = f32[520,64]{0,1:T(8,128)S(1)} collective-permute-done((f32[520,64]{0,1:T(8,128)S(1)}, f32[520,64]{0,1:T(8,128)S(1)}, u32[]{:S(2)}, u32[]{:S(2)}) %collective-permute-start.1) | collective-permute-done | bytes 133152 | tf_op jit(solution)/shard_map/ppermute | solution.py:158
  57.9 2.8 %collective-permute-done.2 = f32[520,64]{0,1:T(8,128)S(1)} collective-permute-done((f32[520,64]{0,1:T(8,128)S(1)}, f32[520,64]{0,1:T(8,128)S(1)}, u32[]{:S(2)}, u32[]{:S(2)}) %collective-permute-start.2) | collective-permute-done | bytes 133152 | tf_op jit(solution)/shard_map/ppermute | solution.py:158
  60.8 0.1 slice_reduce_fusion
  60.9 0.1 copy.26
  61.2 0.2 all_to_all.18
  61.4 15.7 %all_to_all.21 = f32[32,1,1088]{2,1,0:T(1,128)S(1)} all-to-all(f32[32,1,1088]{2,1,0:T(1,128)S(1)} %all_to_all.18), channel_id=1, replica_groups=mesh['elem'=32,'blk'=8] {'elem'}, dimensions={0} | all-to-all | bytes 278528 | tf_op jit(solution)/shard_map/all_to_all | solution.py:165
  77.0 0.1 reduce_sum.19
  77.2 0.5 slice.80
  77.7 0.7 slice.75
  (26 shorter events, 0.2 us)
Async XLA Ops:
  4.4 11.5 %copy-start.6 = (s32[32]{0:T(128)S(1)}, s32[32]{0:T(128)}, u32[]{:S(2)}) copy-start(s32[32]{0:T(128)} %param.11) | copy-start | bytes 388
  4.4 12.7 %copy-start.4 = (f32[64]{0:T(128)S(1)}, f32[64]{0:T(128)}, u32[]{:S(2)}) copy-start(f32[64]{0:T(128)} %param.12) | copy-start | bytes 772
  4.4 14.1 %copy-start.2 = (bf16[512]{0:T(512)(128)(2,1)S(1)}, bf16[512]{0:T(512)(128)(2,1)}, u32[]{:S(2)}) copy-start(bf16[512]{0:T(512)(128)(2,1)} %param.14) | copy-start | bytes 3076
  4.4 14.1 %copy-start.1 = (s32[8,64]{1,0:T(8,128)S(1)}, s32[8,64]{1,0:T(8,128)}, u32[]{:S(2)}) copy-start(s32[8,64]{1,0:T(8,128)} %param.10) | copy-start | bytes 6148
  4.4 14.2 %copy-start.3 = (f32[64]{0:T(128)S(1)}, f32[64]{0:T(128)}, u32[]{:S(2)}) copy-start(f32[64]{0:T(128)} %param.13) | copy-start | bytes 772
  4.4 34.4 %all-to-all-start = ((bf16[32,8,1536]{2,1,0:T(8,128)(2,1)}), bf16[32,8,1536]{2,1,0:T(8,128)(2,1)S(1)}, u32[]{:S(2)}, u32[]{:S(2)}) async-start(bf16[32,8,1536]{2,1,0:T(8,128)(2,1)} %bitcast.45), calls=%async_computation | async-start | bytes 1572864 | tf_op jit(solution)/shard_map/all_to_all | solution.py:135
  38.9 0.9 %copy-start = (bf16[32,8,1536]{2,1,0:T(8,128)(2,1)}, bf16[32,8,1536]{2,1,0:T(8,128)(2,1)S(1)}, u32[]{:S(2)}) copy-start(bf16[32,8,1536]{2,1,0:T(8,128)(2,1)S(1)} %all-to-all-done) | copy-start | bytes 2359300
  46.9 2.2 %collective-permute-start = (f32[520,4,64]{0,2,1:T(8,128)S(1)}, f32[520,4,64]{0,2,1:T(8,128)S(1)}, u32[]{:S(2)}, u32[]{:S(2)}) collective-permute-start(f32[520,4,64]{0,2,1:T(8,128)S(1)} %dynamic-slice_bitcast_fusion), channel_id=1, source_target_pairs={{0,1},{1,0},{2,3},{3,2},{4,5},{5,4},{6,7},{7,6},{8,9},{9,8},{10,11... | collective-permute-start | bytes 1597448 | tf_op jit(solution)/shard_map/ppermute | solution.py:153
  49.2 11.9 %copy-start.5 = (f32[64]{0:T(128)S(1)}, f32[64]{0:T(128)}, u32[]{:S(2)}) copy-start(f32[64]{0:T(128)} %param.15) | copy-start | bytes 772
  49.3 8.7 %collective-permute-start.1 = (f32[520,64]{0,1:T(8,128)S(1)}, f32[520,64]{0,1:T(8,128)S(1)}, u32[]{:S(2)}, u32[]{:S(2)}) collective-permute-start(f32[520,64]{0,1:T(8,128)S(1)} %get-tuple-element.2), channel_id=1, source_target_pairs={{0,4},{1,5},{2,6},{3,7},{4,0},{5,1},{6,2},{7,3},{8,12},{9,13},{10,... | collective-permute-start | bytes 399368 | tf_op jit(solution)/shard_map/ppermute | solution.py:158
  51.6 9.1 %collective-permute-start.2 = (f32[520,64]{0,1:T(8,128)S(1)}, f32[520,64]{0,1:T(8,128)S(1)}, u32[]{:S(2)}, u32[]{:S(2)}) collective-permute-start(f32[520,64]{0,1:T(8,128)S(1)} %get-tuple-element.4), channel_id=1, source_target_pairs={{0,2},{1,3},{2,4},{3,5},{4,6},{5,7},{6,0},{7,1},{8,10},{9,11},{10,... | collective-permute-start | bytes 399368 | tf_op jit(solution)/shard_map/ppermute | solution.py:158
  51.6 9.1 %collective-permute-start.3 = (f32[520,64]{0,1:T(8,128)S(1)}, f32[520,64]{0,1:T(8,128)S(1)}, u32[]{:S(2)}, u32[]{:S(2)}) collective-permute-start(f32[520,64]{0,1:T(8,128)S(1)} %get-tuple-element.3), channel_id=1, source_target_pairs={{0,6},{1,7},{2,0},{3,1},{4,2},{5,3},{6,4},{7,5},{8,14},{9,15},{10,... | collective-permute-start | bytes 399368 | tf_op jit(solution)/shard_map/ppermute | solution.py:158

commit v22 on v20

--- a/solution.py
+++ b/solution.py
@@ -10,7 +10,7 @@
 
 def element_body(arrived_ref, onehot_ref, signed_ref, state_ref, omega_ref, stiff_ref, scale_ref, out_ref, v_ref, w_ref):
     n_el = omega_ref.shape[0]
-    modes = out_ref.shape[1]
+    modes = out_ref.shape[2] * 2
     onehot = onehot_ref[...]
     corners = jnp.dot(onehot, arrived_ref[...], preferred_element_type=jnp.float32).astype(jnp.bfloat16)
     for c in range(3):
@@ -69,11 +69,16 @@
         v_ref[...], w_ref[...], (((0,), (0,)), ((), ())), preferred_element_type=jnp.float32
     )
     scale = scale_ref[0:1, 0:1]
-    out_ref[pl.ds(0, modes), :] = tangent * scale
-    force_row = jnp.sum(force_acc, axis=0, keepdims=True) * scale
-    out_ref[pl.ds(modes, 8), :] = jnp.concatenate(
-        [force_row, jnp.zeros((7, modes), jnp.float32)], axis=0
+    tangent = tangent * scale
+    force_rows = jnp.concatenate(
+        [jnp.sum(force_acc, axis=0, keepdims=True) * scale, jnp.zeros((7, modes), jnp.float32)], axis=0
     )
+    width = modes // 8
+    for half in range(2):
+        for y in range(4):
+            src = (2 * y + half) * width
+            out_ref[half, pl.ds(0, modes), pl.ds(y * width, width)] = tangent[:, src:src + width]
+            out_ref[half, pl.ds(modes, 8), pl.ds(y * width, width)] = force_rows[:, src:src + width]
 
 
 def element_stage(arrived3, slot, state, omega, stiff, scale):
@@ -92,7 +97,7 @@
     vmem = pltpu.MemorySpace.VMEM if hasattr(pltpu, "MemorySpace") else pltpu.TPUMemorySpace.VMEM
     return pl.pallas_call(
         element_body,
-        out_shape=jax.ShapeDtypeStruct((modes + 8, modes), jnp.float32),
+        out_shape=jax.ShapeDtypeStruct((2, modes + 8, modes // 2), jnp.float32),
         in_specs=[pl.BlockSpec(memory_space=vmem)] * 7,
         out_specs=pl.BlockSpec(memory_space=vmem),
         scratch_shapes=[
@@ -146,11 +151,10 @@
     n_y = n_blk // 2
     core = block_index % 2
     chip = block_index // 2
-    by_dest = stacked.reshape(basis_modes + 8, n_y, 2, cols)
     pair = [(b, b ^ 1) for b in range(n_blk)]
-    sent = lax.dynamic_index_in_dim(by_dest, 1 - core, axis=2, keepdims=False)
-    kept = lax.dynamic_index_in_dim(by_dest, core, axis=2, keepdims=False)
-    chip_sum = kept + lax.ppermute(sent, "blk", pair)
+    sent = lax.dynamic_index_in_dim(stacked, 1 - core, axis=0, keepdims=False)
+    kept = lax.dynamic_index_in_dim(stacked, core, axis=0, keepdims=False)
+    chip_sum = (kept + lax.ppermute(sent, "blk", pair)).reshape(basis_modes + 8, n_y, cols)
     halfway = lax.dynamic_index_in_dim(chip_sum, chip, axis=1, keepdims=False)
     for shift in range(1, n_y):
         ring = [(2 * y + c, 2 * ((y + shift) % n_y) + c) for y in range(n_y) for c in range(2)]

time: 79 us -> 78.7 us (level)
    pallas_call x1 -> x0, local copies, waits for them, and re-layouts: 1.63 us -> none  [element_stage(): pl.pallas_call(element_body, out_shape=jax.ShapeDtypeStruct((modes + 8, m...]
    squeeze x1, local copies, waits for them, and re-layouts: 0.05 us -> 1.17 us  [local(): sent = lax.dynamic_index_in_dim(stacked, 1 - core, axis=0, keepdims=False)]
where the time goes in v22:
time: 78.7 us; the launch traced here: 77.2 us
  waiting for transfers between devices  23.1 us (29%)
  starting transfers between devices  17.8 us (23%)
  blocking collectives  14.3 us (18%)
  Pallas kernels  9.44 us (12%)
  local copies, waits for them, and re-layouts  6.11 us (8%)
  other arithmetic  4.97 us (6%)
  between operations  1.61 us (2%)
    all_to_all x1, waiting for transfers between devices, local(): lax.all_to_all(outgoing, 'elem', split_axis=0, concat_axis=0, tiled=True)  14.9 us
    all_to_all x1, blocking collectives, local(): lax.all_to_all(flat, 'elem', split_axis=0, concat_axis=0, tiled=True)  14.3 us
    all_to_all x1, starting transfers between devices, local(): lax.all_to_all(outgoing, 'elem', split_axis=0, concat_axis=0, tiled=True)  11.8 us
    ppermute x3, waiting for transfers between devices, local(): halfway = halfway + lax.ppermute(piece, 'blk', ring)  6.34 us
    ppermute x3, starting transfers between devices, local(): halfway = halfway + lax.ppermute(piece, 'blk', ring)  5.91 us
    pallas_call x1, Pallas kernels, element_stage(): pl.pallas_call(element_body, out_shape=jax.ShapeDtypeStruct((2, modes + 8...  5.64 us
    pallas_call x1, Pallas kernels, gather_rows(): pl.pallas_call(gather_body, out_shape=jax.ShapeDtypeStruct((n_rows, comps...  3.8 us
    ppermute x1, waiting for transfers between devices, local(): lax.ppermute(sent, 'blk', pair)  1.83 us
  transfers between devices with their start and end apart: 5, of which 4 were waited for; matrix products, arithmetic and copies ran while one was open for 9% of the time, Pallas kernels for 0%

profile of v22, /device:TPU:2, one launch (start us, length us, event | category | flops | bytes accessed | tf_op | source)
XLA Modules:
  0.0 77.2 jit_solution(10005730975460463432)
XLA Ops:
  0.6 3.8 %shard_map.95 = bf16[256,1536]{1,0:T(8,128)(2,1)} custom-call(bf16[3,1024,512]{2,1,0:T(8,128)(2,1)} %bitcast.42, s32[1,256]{1,0:T(1,128)} %bitcast.48), custom_call_target="tpu_custom_call" | custom-call | tf_op jit(solution)/shard_map/pallas_call | solution.py:127
  4.5 11.8 %all-to-all-start = ((bf16[32,8,1536]{2,1,0:T(8,128)(2,1)}), bf16[32,8,1536]{2,1,0:T(8,128)(2,1)S(1)}, u32[]{:S(2)}, u32[]{:S(2)}) async-start(bf16[32,8,1536]{2,1,0:T(8,128)(2,1)} %bitcast.43), calls=%async_computation | async-start | bytes 1572864 | tf_op jit(solution)/shard_map/all_to_all | solution.py:140
  16.2 0.6 reduce_sum.18
  16.9 0.6 dynamic_slice.24
  17.5 0.6 fusion.15
  18.1 0.7 copy.22.omega_ref
  18.9 0.7 copy.23.stiff_ref
  20.4 0.2 fusion.10
  20.5 0.6 pad_maximum_fusion.1.signed_ref
  21.2 0.8 %fusion.1.onehot_ref = bf16[512,256]{1,0:T(8,128)(2,1)} fusion(s32[512]{0:T(512)S(1)} %eq.84), kind=kLoop, calls=%fused_computation.5 | loop fusion | flops 262144 | bytes 264192 | tf_op jit(solution)/shard_map/convert_element_type | solution.py:88
  22.0 1.8 %fusion.state_ref = bf16[1536,128]{1,0:T(8,128)(2,1)} fusion(s32[1536]{0:T(1024)S(1)} %add_select_fusion, bf16[1536]{0:T(1024)(128)(2,1)S(1)} %broadcast_in_dim.85), kind=kLoop, calls=%fused_computation.1 | loop fusion | flops 393216 | bytes 402432 | tf_op jit(solution)/shard_map/jit(_where)/select_n | solution.py:94
  23.8 14.9 %all-to-all-done = bf16[32,8,1536]{2,1,0:T(8,128)(2,1)S(1)} async-done(((bf16[32,8,1536]{2,1,0:T(8,128)(2,1)}), bf16[32,8,1536]{2,1,0:T(8,128)(2,1)S(1)}, u32[]{:S(2)}, u32[]{:S(2)}) %all-to-all-start) | async-done | bytes 786464 | tf_op jit(solution)/shard_map/all_to_all | solution.py:140
  38.7 0.6 broadcast_in_dim.88.scale_ref
  39.3 0.3 copy-done.1
  39.6 5.6 %shard_map.96 = f32[2,520,256]{2,1,0:T(8,128)} custom-call(bf16[256,1536]{1,0:T(8,128)(2,1)} %bitcast.44, bf16[512,256]{1,0:T(8,128)(2,1)} %fusion.1.onehot_ref, bf16[192,256]{1,0:T(8,128)(2,1)} %pad_maximum_fusion.1.signed_ref, bf16[1536,128]{1,0:T(8,128)(2,1)} %fusion.state_ref, f32[64,1]{1,0:T(8,128)} %copy.22.omega_ref, f32[64,1]{1,0:T(8,128)} %copy.23.stiff_ref, ...), custom_call_target="tpu_custom_call" | custom-call | tf_op jit(solution)/shard_map/pallas_call | solution.py:98
  45.2 1.2 %dynamic-slice_bitcast_fusion = f32[520,256]{1,0:T(8,128)S(1)} fusion(f32[2,520,256]{2,1,0:T(8,128)} %shard_map.96, s32[]{:T(128)S(6)} %select_n.145), kind=kLoop, calls=%fused_computation.3 | loop fusion | bytes 1064964 | tf_op jit(solution)/shard_map/jit(dynamic_index_in_dim)/squeeze | solution.py:155
  46.4 0.1 collective-permute-start
  46.6 1.8 %collective-permute-done = f32[520,256]{1,0:T(8,128)S(1)} collective-permute-done((f32[520,256]{1,0:T(8,128)S(1)}, f32[520,256]{1,0:T(8,128)S(1)}, u32[]{:S(2)}, u32[]{:S(2)}) %collective-permute-start) | collective-permute-done | bytes 532512 | tf_op jit(solution)/shard_map/ppermute | solution.py:157
  48.4 0.1 bitcast_add_fusion
  48.5 0.2 copy.24
  48.8 1.6 %collective-permute-start.1 = (f32[520,64]{0,1:T(8,128)S(1)}, f32[520,64]{0,1:T(8,128)S(1)}, u32[]{:S(2)}, u32[]{:S(2)}) collective-permute-start(f32[520,64]{0,1:T(8,128)S(1)} %get-tuple-element.2), channel_id=1, source_target_pairs={{0,2},{1,3},{2,4},{3,5},{4,6},{5,7},{6,0},{7,1},{8,10},{9,11},{10,... | collective-permute-start | bytes 399368 | tf_op jit(solution)/shard_map/ppermute | solution.py:162
  50.5 2.9 %collective-permute-start.2 = (f32[520,64]{0,1:T(8,128)S(1)}, f32[520,64]{0,1:T(8,128)S(1)}, u32[]{:S(2)}, u32[]{:S(2)}) collective-permute-start(f32[520,64]{0,1:T(8,128)S(1)} %get-tuple-element.4), channel_id=1, source_target_pairs={{0,4},{1,5},{2,6},{3,7},{4,0},{5,1},{6,2},{7,3},{8,12},{9,13},{10,... | collective-permute-start | bytes 399368 | tf_op jit(solution)/shard_map/ppermute | solution.py:162
  53.4 1.3 %collective-permute-start.3 = (f32[520,64]{0,1:T(8,128)S(1)}, f32[520,64]{0,1:T(8,128)S(1)}, u32[]{:S(2)}, u32[]{:S(2)}) collective-permute-start(f32[520,64]{0,1:T(8,128)S(1)} %get-tuple-element.3), channel_id=1, source_target_pairs={{0,6},{1,7},{2,0},{3,1},{4,2},{5,3},{6,4},{7,5},{8,14},{9,15},{10,... | collective-permute-start | bytes 399368 | tf_op jit(solution)/shard_map/ppermute | solution.py:162
  54.7 1.7 %collective-permute-done.1 = f32[520,64]{0,1:T(8,128)S(1)} collective-permute-done((f32[520,64]{0,1:T(8,128)S(1)}, f32[520,64]{0,1:T(8,128)S(1)}, u32[]{:S(2)}, u32[]{:S(2)}) %collective-permute-start.1) | collective-permute-done | bytes 133152 | tf_op jit(solution)/shard_map/ppermute | solution.py:162
  56.4 4.7 %collective-permute-done.2 = f32[520,64]{0,1:T(8,128)S(1)} collective-permute-done((f32[520,64]{0,1:T(8,128)S(1)}, f32[520,64]{0,1:T(8,128)S(1)}, u32[]{:S(2)}, u32[]{:S(2)}) %collective-permute-start.2) | collective-permute-done | bytes 133152 | tf_op jit(solution)/shard_map/ppermute | solution.py:162
  61.1 0.1 slice_reduce_fusion
  61.2 0.1 copy.25
  61.5 0.2 all_to_all.18
  61.7 14.3 %all_to_all.21 = f32[32,1,1088]{2,1,0:T(1,128)S(1)} all-to-all(f32[32,1,1088]{2,1,0:T(1,128)S(1)} %all_to_all.18), channel_id=1, replica_groups=mesh['elem'=32,'blk'=8] {'elem'}, dimensions={0} | all-to-all | bytes 278528 | tf_op jit(solution)/shard_map/all_to_all | solution.py:169
  75.9 0.1 reduce_sum.19
  76.0 0.5 slice.80
  76.6 0.7 slice.75
  (28 shorter events, 0.3 us)
Async XLA Ops:
  4.4 11.8 %copy-start.7 = (s32[32]{0:T(128)S(1)}, s32[32]{0:T(128)}, u32[]{:S(2)}) copy-start(s32[32]{0:T(128)} %param.11) | copy-start | bytes 388
  4.4 13.0 %copy-start.5 = (f32[64]{0:T(128)S(1)}, f32[64]{0:T(128)}, u32[]{:S(2)}) copy-start(f32[64]{0:T(128)} %param.12) | copy-start | bytes 772
  4.4 14.4 %copy-start.3 = (bf16[512]{0:T(512)(128)(2,1)S(1)}, bf16[512]{0:T(512)(128)(2,1)}, u32[]{:S(2)}) copy-start(bf16[512]{0:T(512)(128)(2,1)} %param.14) | copy-start | bytes 3076
  4.4 14.4 %copy-start.2 = (s32[8,64]{1,0:T(8,128)S(1)}, s32[8,64]{1,0:T(8,128)}, u32[]{:S(2)}) copy-start(s32[8,64]{1,0:T(8,128)} %param.10) | copy-start | bytes 6148
  4.4 14.5 %copy-start.4 = (f32[64]{0:T(128)S(1)}, f32[64]{0:T(128)}, u32[]{:S(2)}) copy-start(f32[64]{0:T(128)} %param.13) | copy-start | bytes 772
  4.5 34.2 %all-to-all-start = ((bf16[32,8,1536]{2,1,0:T(8,128)(2,1)}), bf16[32,8,1536]{2,1,0:T(8,128)(2,1)S(1)}, u32[]{:S(2)}, u32[]{:S(2)}) async-start(bf16[32,8,1536]{2,1,0:T(8,128)(2,1)} %bitcast.43), calls=%async_computation | async-start | bytes 1572864 | tf_op jit(solution)/shard_map/all_to_all | solution.py:140
  38.7 0.9 %copy-start.1 = (bf16[32,8,1536]{2,1,0:T(8,128)(2,1)}, bf16[32,8,1536]{2,1,0:T(8,128)(2,1)S(1)}, u32[]{:S(2)}) copy-start(bf16[32,8,1536]{2,1,0:T(8,128)(2,1)S(1)} %all-to-all-done) | copy-start | bytes 2359300
  45.2 3.2 %copy-start = (f32[2,520,256]{2,1,0:T(8,128)S(1)}, f32[2,520,256]{2,1,0:T(8,128)}, u32[]{:S(2)}) copy-start(f32[2,520,256]{2,1,0:T(8,128)} %shard_map.96) | copy-start | bytes 3194884
  46.4 2.0 %collective-permute-start = (f32[520,256]{1,0:T(8,128)S(1)}, f32[520,256]{1,0:T(8,128)S(1)}, u32[]{:S(2)}, u32[]{:S(2)}) collective-permute-start(f32[520,256]{1,0:T(8,128)S(1)} %dynamic-slice_bitcast_fusion), channel_id=1, source_target_pairs={{0,1},{1,0},{2,3},{3,2},{4,5},{5,4},{6,7},{7,6},{8,9},{9,8},{10,11... | collective-permute-start | bytes 1597448 | tf_op jit(solution)/shard_map/ppermute | solution.py:157
  48.8 12.6 %copy-start.6 = (f32[64]{0:T(128)S(1)}, f32[64]{0:T(128)}, u32[]{:S(2)}) copy-start(f32[64]{0:T(128)} %param.15) | copy-start | bytes 772
  48.8 7.6 %collective-permute-start.1 = (f32[520,64]{0,1:T(8,128)S(1)}, f32[520,64]{0,1:T(8,128)S(1)}, u32[]{:S(2)}, u32[]{:S(2)}) collective-permute-start(f32[520,64]{0,1:T(8,128)S(1)} %get-tuple-element.2), channel_id=1, source_target_pairs={{0,2},{1,3},{2,4},{3,5},{4,6},{5,7},{6,0},{7,1},{8,10},{9,11},{10,... | collective-permute-start | bytes 399368 | tf_op jit(solution)/shard_map/ppermute | solution.py:162
  50.5 10.6 %collective-permute-start.2 = (f32[520,64]{0,1:T(8,128)S(1)}, f32[520,64]{0,1:T(8,128)S(1)}, u32[]{:S(2)}, u32[]{:S(2)}) collective-permute-start(f32[520,64]{0,1:T(8,128)S(1)} %get-tuple-element.4), channel_id=1, source_target_pairs={{0,4},{1,5},{2,6},{3,7},{4,0},{5,1},{6,2},{7,3},{8,12},{9,13},{10,... | collective-permute-start | bytes 399368 | tf_op jit(solution)/shard_map/ppermute | solution.py:162
  53.4 7.7 %collective-permute-start.3 = (f32[520,64]{0,1:T(8,128)S(1)}, f32[520,64]{0,1:T(8,128)S(1)}, u32[]{:S(2)}, u32[]{:S(2)}) collective-permute-start(f32[520,64]{0,1:T(8,128)S(1)} %get-tuple-element.3), channel_id=1, source_target_pairs={{0,6},{1,7},{2,0},{3,1},{4,2},{5,3},{6,4},{7,5},{8,14},{9,15},{10,... | collective-permute-start | bytes 399368 | tf_op jit(solution)/shard_map/ppermute | solution.py:162

commit v23 on v20

--- a/solution.py
+++ b/solution.py
@@ -87,7 +87,7 @@
     modes = arrived3.shape[1] // 3
     comp = jnp.arange(3 * modes) // modes
     state_blocks = jnp.where(
-        comp[:, None] == jnp.arange(128)[None, :], jnp.tile(state, 3)[:, None], jnp.zeros((), state.dtype)
+        comp[:, None] == jnp.arange(8)[None, :], jnp.tile(state, 3)[:, None], jnp.zeros((), state.dtype)
     )
     vmem = pltpu.MemorySpace.VMEM if hasattr(pltpu, "MemorySpace") else pltpu.TPUMemorySpace.VMEM
     return pl.pallas_call(

time: 79 us -> 79 us (level)
  no operation moved by 1% of the time
where the time goes in v23:
time: 79 us; the launch traced here: 77.5 us
  waiting for transfers between devices  23.3 us (29%)
  starting transfers between devices  17.8 us (23%)
  blocking collectives  14.3 us (18%)
  Pallas kernels  9.27 us (12%)
  local copies, waits for them, and re-layouts  6.4 us (8%)
  other arithmetic  4.94 us (6%)
  between operations  1.62 us (2%)
    all_to_all x1, waiting for transfers between devices, local(): lax.all_to_all(outgoing, 'elem', split_axis=0, concat_axis=0, tiled=True)  14.9 us
    all_to_all x1, blocking collectives, local(): lax.all_to_all(flat, 'elem', split_axis=0, concat_axis=0, tiled=True)  14.3 us
    all_to_all x1, starting transfers between devices, local(): lax.all_to_all(outgoing, 'elem', split_axis=0, concat_axis=0, tiled=True)  11.8 us
    ppermute x3, waiting for transfers between devices, local(): halfway = halfway + lax.ppermute(piece, 'blk', ring)  6.38 us
    ppermute x3, starting transfers between devices, local(): halfway = halfway + lax.ppermute(piece, 'blk', ring)  5.9 us
    pallas_call x1, Pallas kernels, element_stage(): pl.pallas_call(element_body, out_shape=jax.ShapeDtypeStruct((modes + 8, m...  5.47 us
    pallas_call x1, Pallas kernels, gather_rows(): pl.pallas_call(gather_body, out_shape=jax.ShapeDtypeStruct((n_rows, comps...  3.79 us
    ppermute x1, waiting for transfers between devices, local(): chip_sum = kept + lax.ppermute(sent, 'blk', pair)  2 us
  transfers between devices with their start and end apart: 5, of which 4 were waited for; matrix products, arithmetic and copies ran while one was open for 9% of the time, Pallas kernels for 0%

profile of v23, /device:TPU:2, one launch (start us, length us, event | category | flops | bytes accessed | tf_op | source)
XLA Modules:
  0.0 77.5 jit_solution(18083297859372598454)
XLA Ops:
  0.6 3.8 %shard_map.95 = bf16[256,1536]{1,0:T(8,128)(2,1)} custom-call(bf16[3,1024,512]{2,1,0:T(8,128)(2,1)} %bitcast.44, s32[1,256]{1,0:T(1,128)} %bitcast.48), custom_call_target="tpu_custom_call" | custom-call | tf_op jit(solution)/shard_map/pallas_call | solution.py:122
  4.5 11.8 %all-to-all-start = ((bf16[32,8,1536]{2,1,0:T(8,128)(2,1)}), bf16[32,8,1536]{2,1,0:T(8,128)(2,1)S(1)}, u32[]{:S(2)}, u32[]{:S(2)}) async-start(bf16[32,8,1536]{2,1,0:T(8,128)(2,1)} %bitcast.45), calls=%async_computation | async-start | bytes 1572864 | tf_op jit(solution)/shard_map/all_to_all | solution.py:135
  16.2 0.6 reduce_sum.18
  16.9 0.6 dynamic_slice.24
  17.4 0.6 fusion.15
  18.1 0.7 copy.23.omega_ref
  18.8 0.1 eq.84
  18.9 0.7 copy.24.stiff_ref
  20.4 0.2 fusion.10
  20.5 0.6 pad_maximum_fusion.1.signed_ref
  21.2 0.9 %fusion.1.onehot_ref = bf16[512,256]{1,0:T(8,128)(2,1)} fusion(s32[512]{0:T(512)S(1)} %eq.84), kind=kLoop, calls=%fused_computation.5 | loop fusion | flops 262144 | bytes 264192 | tf_op jit(solution)/shard_map/convert_element_type | solution.py:83
  22.0 1.8 %fusion.state_ref = bf16[1536,8]{1,0:T(8,128)(2,1)} fusion(s32[1536]{0:T(1024)S(1)} %add_select_fusion, bf16[1536]{0:T(1024)(128)(2,1)S(1)} %broadcast_in_dim.85), kind=kLoop, calls=%fused_computation.1 | loop fusion | flops 24576 | bytes 33792 | tf_op jit(solution)/shard_map/jit(_where)/select_n | solution.py:89
  23.8 14.9 %all-to-all-done = bf16[32,8,1536]{2,1,0:T(8,128)(2,1)S(1)} async-done(((bf16[32,8,1536]{2,1,0:T(8,128)(2,1)}), bf16[32,8,1536]{2,1,0:T(8,128)(2,1)S(1)}, u32[]{:S(2)}, u32[]{:S(2)}) %all-to-all-start) | async-done | bytes 786464 | tf_op jit(solution)/shard_map/all_to_all | solution.py:135
  38.7 0.6 broadcast_in_dim.88.scale_ref
  39.3 0.3 copy-done
  39.6 5.5 %shard_map.96 = f32[520,512]{1,0:T(8,128)} custom-call(bf16[256,1536]{1,0:T(8,128)(2,1)} %bitcast.46, bf16[512,256]{1,0:T(8,128)(2,1)} %fusion.1.onehot_ref, bf16[192,256]{1,0:T(8,128)(2,1)} %pad_maximum_fusion.1.signed_ref, bf16[1536,8]{1,0:T(8,128)(2,1)} %fusion.state_ref, f32[64,1]{1,0:T(8,128)} %copy.23.omega_ref, f32[64,1]{1,0:T(8,128)} %copy.24.stiff_ref, ...), custom_call_target="tpu_custom_call" | custom-call | tf_op jit(solution)/shard_map/pallas_call | solution.py:93
  45.1 1.6 %copy.25 = f32[520,512]{0,1:T(8,128)S(1)} copy(f32[520,512]{1,0:T(8,128)} %shard_map.96) | data formatting | bytes 2129920 | tf_op jit(solution)/shard_map/pallas_call | solution.py:93
  46.8 0.1 collective-permute-start
  46.9 2.0 %collective-permute-done = f32[520,4,64]{0,2,1:T(8,128)S(1)} collective-permute-done((f32[520,4,64]{0,2,1:T(8,128)S(1)}, f32[520,4,64]{0,2,1:T(8,128)S(1)}, u32[]{:S(2)}, u32[]{:S(2)}) %collective-permute-start) | collective-permute-done | bytes 532512 | tf_op jit(solution)/shard_map/ppermute | solution.py:153
  48.9 0.1 bitcast_add_fusion
  49.1 1.7 %collective-permute-start.1 = (f32[520,64]{0,1:T(8,128)S(1)}, f32[520,64]{0,1:T(8,128)S(1)}, u32[]{:S(2)}, u32[]{:S(2)}) collective-permute-start(f32[520,64]{0,1:T(8,128)S(1)} %get-tuple-element.2), channel_id=1, source_target_pairs={{0,2},{1,3},{2,4},{3,5},{4,6},{5,7},{6,0},{7,1},{8,10},{9,11},{10,... | collective-permute-start | bytes 399368 | tf_op jit(solution)/shard_map/ppermute | solution.py:158
  50.7 2.9 %collective-permute-start.2 = (f32[520,64]{0,1:T(8,128)S(1)}, f32[520,64]{0,1:T(8,128)S(1)}, u32[]{:S(2)}, u32[]{:S(2)}) collective-permute-start(f32[520,64]{0,1:T(8,128)S(1)} %get-tuple-element.4), channel_id=1, source_target_pairs={{0,4},{1,5},{2,6},{3,7},{4,0},{5,1},{6,2},{7,3},{8,12},{9,13},{10,... | collective-permute-start | bytes 399368 | tf_op jit(solution)/shard_map/ppermute | solution.py:158
  53.6 1.3 %collective-permute-start.3 = (f32[520,64]{0,1:T(8,128)S(1)}, f32[520,64]{0,1:T(8,128)S(1)}, u32[]{:S(2)}, u32[]{:S(2)}) collective-permute-start(f32[520,64]{0,1:T(8,128)S(1)} %get-tuple-element.3), channel_id=1, source_target_pairs={{0,6},{1,7},{2,0},{3,1},{4,2},{5,3},{6,4},{7,5},{8,14},{9,15},{10,... | collective-permute-start | bytes 399368 | tf_op jit(solution)/shard_map/ppermute | solution.py:158
  55.0 1.7 %collective-permute-done.1 = f32[520,64]{0,1:T(8,128)S(1)} collective-permute-done((f32[520,64]{0,1:T(8,128)S(1)}, f32[520,64]{0,1:T(8,128)S(1)}, u32[]{:S(2)}, u32[]{:S(2)}) %collective-permute-start.1) | collective-permute-done | bytes 133152 | tf_op jit(solution)/shard_map/ppermute | solution.py:158
  56.7 4.7 %collective-permute-done.2 = f32[520,64]{0,1:T(8,128)S(1)} collective-permute-done((f32[520,64]{0,1:T(8,128)S(1)}, f32[520,64]{0,1:T(8,128)S(1)}, u32[]{:S(2)}, u32[]{:S(2)}) %collective-permute-start.2) | collective-permute-done | bytes 133152 | tf_op jit(solution)/shard_map/ppermute | solution.py:158
  61.4 0.1 slice_reduce_fusion
  61.5 0.1 copy.26
  61.7 0.2 all_to_all.18
  61.9 14.3 %all_to_all.21 = f32[32,1,1088]{2,1,0:T(1,128)S(1)} all-to-all(f32[32,1,1088]{2,1,0:T(1,128)S(1)} %all_to_all.18), channel_id=1, replica_groups=mesh['elem'=32,'blk'=8] {'elem'}, dimensions={0} | all-to-all | bytes 278528 | tf_op jit(solution)/shard_map/all_to_all | solution.py:165
  76.2 0.1 reduce_sum.19
  76.3 0.5 slice.80
  76.8 0.7 slice.75
  (26 shorter events, 0.3 us)
Async XLA Ops:
  4.4 11.8 %copy-start.6 = (s32[32]{0:T(128)S(1)}, s32[32]{0:T(128)}, u32[]{:S(2)}) copy-start(s32[32]{0:T(128)} %param.11) | copy-start | bytes 388
  4.4 13.0 %copy-start.4 = (f32[64]{0:T(128)S(1)}, f32[64]{0:T(128)}, u32[]{:S(2)}) copy-start(f32[64]{0:T(128)} %param.12) | copy-start | bytes 772
  4.4 14.4 %copy-start.2 = (bf16[512]{0:T(512)(128)(2,1)S(1)}, bf16[512]{0:T(512)(128)(2,1)}, u32[]{:S(2)}) copy-start(bf16[512]{0:T(512)(128)(2,1)} %param.14) | copy-start | bytes 3076
  4.4 14.4 %copy-start.1 = (s32[8,64]{1,0:T(8,128)S(1)}, s32[8,64]{1,0:T(8,128)}, u32[]{:S(2)}) copy-start(s32[8,64]{1,0:T(8,128)} %param.10) | copy-start | bytes 6148
  4.4 14.5 %copy-start.3 = (f32[64]{0:T(128)S(1)}, f32[64]{0:T(128)}, u32[]{:S(2)}) copy-start(f32[64]{0:T(128)} %param.13) | copy-start | bytes 772
  4.5 34.2 %all-to-all-start = ((bf16[32,8,1536]{2,1,0:T(8,128)(2,1)}), bf16[32,8,1536]{2,1,0:T(8,128)(2,1)S(1)}, u32[]{:S(2)}, u32[]{:S(2)}) async-start(bf16[32,8,1536]{2,1,0:T(8,128)(2,1)} %bitcast.45), calls=%async_computation | async-start | bytes 1572864 | tf_op jit(solution)/shard_map/all_to_all | solution.py:135
  38.7 0.9 %copy-start = (bf16[32,8,1536]{2,1,0:T(8,128)(2,1)}, bf16[32,8,1536]{2,1,0:T(8,128)(2,1)S(1)}, u32[]{:S(2)}) copy-start(bf16[32,8,1536]{2,1,0:T(8,128)(2,1)S(1)} %all-to-all-done) | copy-start | bytes 2359300
  46.8 2.2 %collective-permute-start = (f32[520,4,64]{0,2,1:T(8,128)S(1)}, f32[520,4,64]{0,2,1:T(8,128)S(1)}, u32[]{:S(2)}, u32[]{:S(2)}) collective-permute-start(f32[520,4,64]{0,2,1:T(8,128)S(1)} %dynamic-slice_bitcast_fusion), channel_id=1, source_target_pairs={{0,1},{1,0},{2,3},{3,2},{4,5},{5,4},{6,7},{7,6},{8,9},{9,8},{10,11... | collective-permute-start | bytes 1597448 | tf_op jit(solution)/shard_map/ppermute | solution.py:153
  49.0 12.7 %copy-start.5 = (f32[64]{0:T(128)S(1)}, f32[64]{0:T(128)}, u32[]{:S(2)}) copy-start(f32[64]{0:T(128)} %param.15) | copy-start | bytes 772
  49.1 7.6 %collective-permute-start.1 = (f32[520,64]{0,1:T(8,128)S(1)}, f32[520,64]{0,1:T(8,128)S(1)}, u32[]{:S(2)}, u32[]{:S(2)}) collective-permute-start(f32[520,64]{0,1:T(8,128)S(1)} %get-tuple-element.2), channel_id=1, source_target_pairs={{0,2},{1,3},{2,4},{3,5},{4,6},{5,7},{6,0},{7,1},{8,10},{9,11},{10,... | collective-permute-start | bytes 399368 | tf_op jit(solution)/shard_map/ppermute | solution.py:158
  50.7 10.6 %collective-permute-start.2 = (f32[520,64]{0,1:T(8,128)S(1)}, f32[520,64]{0,1:T(8,128)S(1)}, u32[]{:S(2)}, u32[]{:S(2)}) collective-permute-start(f32[520,64]{0,1:T(8,128)S(1)} %get-tuple-element.4), channel_id=1, source_target_pairs={{0,4},{1,5},{2,6},{3,7},{4,0},{5,1},{6,2},{7,3},{8,12},{9,13},{10,... | collective-permute-start | bytes 399368 | tf_op jit(solution)/shard_map/ppermute | solution.py:158
  53.6 7.7 %collective-permute-start.3 = (f32[520,64]{0,1:T(8,128)S(1)}, f32[520,64]{0,1:T(8,128)S(1)}, u32[]{:S(2)}, u32[]{:S(2)}) collective-permute-start(f32[520,64]{0,1:T(8,128)S(1)} %get-tuple-element.3), channel_id=1, source_target_pairs={{0,6},{1,7},{2,0},{3,1},{4,2},{5,3},{6,4},{7,5},{8,14},{9,15},{10,... | collective-permute-start | bytes 399368 | tf_op jit(solution)/shard_map/ppermute | solution.py:158
